TPU v7x, 512 devices: a whole 4x4x16 slice. The times are simulated.
512 devices in a mesh: ctx: 64 (over z, y_lo, core), head: 8 (over x, y_hi).
Axes of the slice: x: 4, y: 4 (y_hi: 2, y_lo: 2; y = y_hi * 2 + y_lo), z: 16, core: 2. Of those that a mesh axis runs over, the one named last changes fastest.
Arguments:
- queries_nope: bfloat16 [4096, 8192], P('ctx', 'head'), may hold values from -4 to 4
- queries_rope: bfloat16 [4096, 4096], P('ctx', 'head'), may hold values from -128 to 128
- latents: bfloat16 [4096, 512], P('ctx'), may hold values from -8 to 8
- rope_keys: bfloat16 [4096, 64], P('ctx'), may hold values from -4 to 4
- positions: int32 [4096], P('ctx'), may hold values from 0 to 6143
- key_up: bfloat16 [512, 8192], P(None, 'head'), may hold values from -0.5 to 0.5
- value_up: bfloat16 [512, 8192], P(None, 'head'), may hold values from -0.25 to 0.25
- out_proj: bfloat16 [8192, 3584], P('head', 'ctx'), may hold values from -0.0625 to 0.0625
Outputs:
- attended: bfloat16 [4096, 3584], P('ctx', 'head')
All inputs are finite; a program needn't handle non-finite values.
Results may differ from a plain program's by a relative error of at most 0.014.
The roundings to bfloat16 on the way count: a program that leaves them out, or rounds other values in their place, can miss the bound.
Values may be sent and summed in bfloat16 or wider, within the bound.
No kernel may reach another device: no remote copies, remote signals or barrier semaphores. Data moves between devices by JAX's collectives and lax.ppermute only.
A program may use at most 64 MiB of HBM per device.

v0:
```python
import math

import jax
import jax.numpy as jnp
from jax import lax
from jax.sharding import PartitionSpec as P

LATENT = 512
ROPE = 64
NOPE = 128
VDIM = 128


masked_value = -1e30


def rope_tables(token_pos, width):
    half_width = width // 2
    freqs = jnp.exp(jnp.arange(half_width, dtype=jnp.float32) * (-2.0 * math.log(10000.0) / width))
    angle = token_pos.astype(jnp.float32)[:, None] * freqs[None, :]
    return (jnp.cos(angle), jnp.sin(angle))


def rotate(values, cosine, sine):
    half_width = values.shape[-1] // 2
    first_half = values[..., :half_width]
    second_half = values[..., half_width:]
    cos_part = cosine[:, None, :]
    sin_part = sine[:, None, :]
    return jnp.concatenate(
        [
            first_half * cos_part - second_half * sin_part,
            second_half * cos_part + first_half * sin_part,
        ],
        axis=-1,
    )


def make_update(group, keys, rope_part, key_pos):
    lat_query, rope_query, query_pos = group
    scale = 1.0 / math.sqrt(NOPE + ROPE)

    def update(state):
        peak, totals, summed = state
        scores = jnp.einsum("rl,kl->rk", lat_query, keys, preferred_element_type=jnp.float32)
        scores = scores + jnp.einsum(
            "rl,kl->rk", rope_query, rope_part, preferred_element_type=jnp.float32
        )
        visible = key_pos[None, :] <= query_pos[:, None]
        scores = jnp.where(visible, scores * scale, masked_value)
        new_peak = jnp.maximum(peak, jnp.max(scores, axis=1))
        weights = jnp.where(visible, jnp.exp(scores - new_peak[:, None]), 0.0)
        totals = jnp.sum(weights, axis=1)
        summed = jnp.dot(weights.astype(jnp.bfloat16), keys, preferred_element_type=jnp.float32)
        return (new_peak, totals, summed)

    return update


def unchanged(state):
    return state


def attend(groups, latents, rot_keys, positions):
    initial = tuple(
        (
            (
                jnp.full((group[0].shape[0],), masked_value, jnp.float32),
                jnp.zeros((group[0].shape[0],), jnp.float32),
                jnp.zeros((group[0].shape[0], LATENT), jnp.float32),
            )
            for group in groups
        )
    )
    keys = lax.all_gather(latents, "ctx", axis=0, tiled=True)
    rope_part = lax.all_gather(rot_keys, "ctx", axis=0, tiled=True)
    key_pos = lax.all_gather(positions, "ctx", axis=0, tiled=True)
    earliest = jnp.min(key_pos)
    results = []
    for group, fold_state in zip(groups, initial):
        needed = earliest <= jnp.max(group[2])
        results.append(
            lax.cond(needed, make_update(group, keys, rope_part, key_pos), unchanged, fold_state)
        )
    states = tuple(results)
    return [(state[2] / state[1][:, None]).astype(jnp.bfloat16) for state in states]


def upward(latent_out, value_up, token_count, head_count):
    head_out = jnp.einsum(
        "thl,lhd->thd",
        latent_out.reshape(token_count, head_count, LATENT),
        value_up.reshape(LATENT, head_count, VDIM),
        preferred_element_type=jnp.float32,
    )
    return head_out.astype(jnp.bfloat16).reshape(token_count, head_count * VDIM)


def body(queries_nope, queries_rope, latents, rope_keys, positions, key_up, value_up, out_proj):
    token_count = latents.shape[0]
    head_count = key_up.shape[1] // NOPE
    cosine, sine = rope_tables(positions, ROPE)
    rot_queries = rotate(
        queries_rope.astype(jnp.float32).reshape(token_count, head_count, ROPE), cosine, sine
    ).astype(jnp.bfloat16)
    rot_keys = rotate(rope_keys.astype(jnp.float32)[:, None, :], cosine, sine)[:, 0, :].astype(
        jnp.bfloat16
    )
    lat_queries = jnp.einsum(
        "thn,lhn->thl",
        queries_nope.reshape(token_count, head_count, NOPE),
        key_up.reshape(LATENT, head_count, NOPE),
        preferred_element_type=jnp.float32,
    ).astype(jnp.bfloat16)
    lat_rows = lat_queries.reshape(token_count * head_count, LATENT)
    rope_rows = rot_queries.reshape(token_count * head_count, ROPE)
    groups = [(lat_rows, rope_rows, jnp.repeat(positions, head_count))]
    outcome = attend(groups, latents, rot_keys, positions)
    head_out = upward(outcome[0], value_up, token_count, head_count)
    partial_sums = jnp.dot(
        head_out,
        lax.all_gather(out_proj, "ctx", axis=1, tiled=True),
        preferred_element_type=jnp.float32,
    )
    return lax.psum_scatter(
        partial_sums.astype(jnp.bfloat16), "head", scatter_dimension=1, tiled=True
    )


def solution(mesh):
    in_specs = (
        P("ctx", "head"),
        P("ctx", "head"),
        P("ctx", None),
        P("ctx", None),
        P("ctx"),
        P(None, "head"),
        P(None, "head"),
        P("head", "ctx"),
    )
    out_specs = P("ctx", "head")
    return jax.shard_map(body, mesh=mesh, in_specs=in_specs, out_specs=out_specs, check_vma=False)
```

profile of v0, /device:TPU:6, one launch (start us, length us, event | category | flops | bytes accessed | tf_op | source)
XLA Modules:
  0.0 420.3 jit_solution(58696167406577907)
XLA Ops:
  6.5 0.7 all-gather.4.cloned.1.call-update
  7.3 0.7 all-gather.6.cloned.1.call-update
  8.1 0.7 convert_element_type.38
  8.7 1.0 reshape.142
  9.7 0.8 copy.44
  10.8 75.8 %all-gather = bf16[4096,1,64]{2,1,0:T(2,128)(2,1)S(1)} all-gather(bf16[64,1,64]{2,1,0:T(2,128)(2,1)S(1)} %copy.45), channel_id=2, replica_groups=mesh['ctx'=64,'head'=8] {'ctx'}, dimensions={0}, use_global_device_ids=true | all-gather | bytes 532480 | tf_op jit(solution)/shard_map/all_gather | solution.py:76
  86.6 3.6 copy.46
  90.2 1.3 dynamic-slice
  92.1 0.9 dynamic-update-slice
  93.0 208.8 %all-reduce = s32[4096]{0:T(1024)S(1)} all-reduce(s32[4096]{0:T(1024)S(1)} %dynamic-update-slice), channel_id=1, replica_groups=mesh['ctx'=64,'head'=8] {'ctx'}, use_global_device_ids=true, to_apply=%add | all-reduce | flops 4096 | bytes 32768
  301.8 0.6 reduce_min.9
  302.4 1.4 broadcast_reduce_fusion
  305.2 0.2 multiply_cosine_fusion
  305.7 1.4 fusion.12
  307.2 11.8 %conditional.1 = (f32[512]{0:T(512)S(1)}, f32[512,512]{1,0:T(8,128)S(1)}) conditional(s32[]{:T(128)} %convert_element_type.35, () %tuple.13, (s32[4096]{0:T(1024)S(1)}, s32[64,8]{1,0:T(8,128)S(1)}, bf16[64,8,512]{2,0,1:T(8,128)(2,1)S(1)}, bf16[4096,512]{1,0:T(8,128)(2,1)}, bf16[512,64]{1,0:T(8,128)(2,1)S(1)}, ...), branch_computations={%region_2.0_spmd, %region_3.6_spmd} | conditional | flops 4590665216 | bytes 71440456 | solution.py:83
  307.3 4.7 %fusion.8 = f32[512,4096]{1,0:T(8,128)S(1)} fusion(bf16[4096,512]{1,0:T(8,128)(2,1)} %get-tuple-element.21, bf16[64,8,512]{2,0,1:T(8,128)(2,1)S(1)} %get-tuple-element.60), kind=kOutput, calls=%fused_computation.9 | convolution fusion | flops 2147483648 | bytes 13107200 | tf_op jit(solution)/shard_map/cond/branch_1_fun/rl,kl->rk/dot_general | solution.py:45
  312.0 2.2 fusion.34
  314.2 2.4 fusion.2
  316.6 2.2 fusion.1
  319.2 1.7 fusion.13
  320.9 5.4 %convolution_convert_fusion = bf16[64,3584]{1,0:T(8,128)(2,1)S(1)} fusion(bf16[1024,3584]{0,1:T(8,128)(2,1)} %all-gather.6.cloned.1.call-done, bf16[8,8,8,128]{3,2,1,0:T(8,128)(2,1)S(1)} %fusion.13), kind=kOutput, calls=%fused_computation.14 | convolution fusion | flops 469991424 | bytes 7929856 | tf_op jit(solution)/shard_map/dot_general | solution.py:120
  326.4 1.2 copy.53
  327.6 84.5 %reduce-scatter.4.cloned.1.call-done = bf16[448,64]{1,0:T(8,128)(2,1)} async-done(((bf16[3584,64]{1,0:T(8,128)(2,1)}), bf16[448,64]{1,0:T(8,128)(2,1)}) %reduce-scatter.4.cloned.1.call-update) | async-done | bytes 57360
  412.1 1.6 copy.54
  (26 shorter events, 1.0 us)
Async XLA Ops:
  6.5 299.2 %copy-start = (bf16[512,1024]{1,0:T(8,128)(2,1)S(1)}, bf16[512,1024]{1,0:T(8,128)(2,1)}, u32[]{:S(2)}) copy-start(bf16[512,1024]{1,0:T(8,128)(2,1)} %param.15) | copy-start | bytes 3145732
  6.5 300.6 %copy-start.3 = (s32[64]{0:T(128)S(1)}, s32[64]{0:T(128)}, u32[]{:S(2)}) copy-start(s32[64]{0:T(128)} %param.14) | copy-start | bytes 772
  6.5 300.6 %all-gather.4.cloned.1.call-start = ((), (), s32[]{:S(2)}) async-start(), calls=%async_computation.1 | async-start | bytes 4259840 | tf_op jit(solution)/shard_map/all_gather | solution.py:75
  7.3 313.7 %all-gather.6.cloned.1.call-start = ((), (), s32[]{:S(2)}) async-start(), calls=%async_computation.2 | async-start | bytes 7454720 | tf_op jit(solution)/shard_map/all_gather | solution.py:122
  8.0 404.1 %reduce-scatter.4.cloned.1.call-start = ((), (), s32[]{:S(2)}) async-start(), calls=%async_computation.3 | async-start | bytes 1032192
  307.2 4.8 %copy-start.2 = (bf16[4096,64]{0,1:T(8,128)(2,1)S(1)}, bf16[4096,64]{0,1:T(8,128)(2,1)}, u32[]{:S(2)}) copy-start(bf16[4096,64]{0,1:T(8,128)(2,1)} %get-tuple-element.63) | copy-start | bytes 1572868 | tf_op jit(solution)/shard_map/cond
  312.0 2.2 copy-start.1
Sparse Core Ops, SparseCore 0:
  9.5 128.8 all-gather.3
  140.5 124.4 all-gather.5
  327.7 84.3 reduce-scatter.3
where the time goes:
time: 421 us; the launch traced here: 420 us
  blocking collectives  285 us (68%)
  waiting for transfers between devices  86 us (20%)
  matrix products  17.8 us (4%)
  between operations  15.2 us (4%)
  local copies, waits for them, and re-layouts  10.6 us (3%)
  other arithmetic  5.75 us (1%)
    unnamed x1, blocking collectives  209 us
    unnamed x4, waiting for transfers between devices  85.9 us
    all_gather x1, blocking collectives, attend(): rope_part = lax.all_gather(rot_keys, 'ctx', axis=0, tiled=True)  75.8 us
  transfers between devices with their start and end apart: 3, of which 1 were waited for; matrix products, arithmetic and copies ran while one was open for 6% of the time, Pallas kernels for 0%

commit v1 on v0

v1 whole, which is shorter than its diff:
```python
import math

import jax
import jax.numpy as jnp
from jax import lax
from jax.sharding import PartitionSpec as P

LATENT = 512
ROPE = 64
NOPE = 128
VDIM = 128


masked_value = -1e30


def rope_tables(token_pos, width):
    half_width = width // 2
    freqs = jnp.exp(jnp.arange(half_width, dtype=jnp.float32) * (-2.0 * math.log(10000.0) / width))
    angle = token_pos.astype(jnp.float32)[:, None] * freqs[None, :]
    return (jnp.cos(angle), jnp.sin(angle))


def rotate(values, cosine, sine):
    half_width = values.shape[-1] // 2
    first_half = values[..., :half_width]
    second_half = values[..., half_width:]
    cos_part = cosine[:, None, :]
    sin_part = sine[:, None, :]
    return jnp.concatenate(
        [
            first_half * cos_part - second_half * sin_part,
            second_half * cos_part + first_half * sin_part,
        ],
        axis=-1,
    )


def attend(query_rows, query_index, keys, key_count):
    scale = 1.0 / math.sqrt(NOPE + ROPE)
    scores = jnp.einsum("rl,kl->rk", query_rows, keys, preferred_element_type=jnp.float32)
    key_index = lax.broadcasted_iota(jnp.int32, (1, key_count), 1)
    visible = key_index <= query_index[:, None]
    scores = jnp.where(visible, scores * scale, masked_value)
    peak = jnp.max(scores, axis=1)
    weights = jnp.where(visible, jnp.exp(scores - peak[:, None]), 0.0)
    totals = jnp.sum(weights, axis=1)
    summed = jnp.dot(
        weights.astype(jnp.bfloat16), keys[:, :LATENT], preferred_element_type=jnp.float32
    )
    return (summed / totals[:, None]).astype(jnp.bfloat16)


def upward(latent_out, value_up, token_count, head_count):
    head_out = jnp.einsum(
        "thl,lhd->thd",
        latent_out.reshape(token_count, head_count, LATENT),
        value_up.reshape(LATENT, head_count, VDIM),
        preferred_element_type=jnp.float32,
    )
    return head_out.astype(jnp.bfloat16).reshape(token_count, head_count * VDIM)


def body(queries_nope, queries_rope, latents, rope_keys, positions, key_up, value_up, out_proj):
    token_count = latents.shape[0]
    head_count = key_up.shape[1] // NOPE
    ctx_count = lax.axis_size("ctx")
    cosine, sine = rope_tables(positions, ROPE)
    rot_queries = rotate(
        queries_rope.astype(jnp.float32).reshape(token_count, head_count, ROPE), cosine, sine
    ).astype(jnp.bfloat16)
    rot_keys = rotate(rope_keys.astype(jnp.float32)[:, None, :], cosine, sine)[:, 0, :].astype(
        jnp.bfloat16
    )
    lat_queries = jnp.einsum(
        "thn,lhn->thl",
        queries_nope.reshape(token_count, head_count, NOPE),
        key_up.reshape(LATENT, head_count, NOPE),
        preferred_element_type=jnp.float32,
    ).astype(jnp.bfloat16)
    query_rows = jnp.concatenate([lat_queries, rot_queries], axis=-1).reshape(
        token_count * head_count, LATENT + ROPE
    )
    local_keys = jnp.concatenate([latents, rot_keys], axis=-1)
    keys = lax.all_gather(local_keys, "ctx", axis=0, tiled=True)
    first_token = lax.axis_index("ctx") * token_count
    query_index = jnp.repeat(
        first_token + jnp.arange(token_count, dtype=jnp.int32), head_count
    )
    latent_out = attend(query_rows, query_index, keys, token_count * ctx_count)
    head_out = upward(latent_out, value_up, token_count, head_count)
    partial_sums = jnp.dot(
        head_out,
        lax.all_gather(out_proj, "ctx", axis=1, tiled=True),
        preferred_element_type=jnp.float32,
    )
    return lax.psum_scatter(
        partial_sums.astype(jnp.bfloat16), "head", scatter_dimension=1, tiled=True
    )


def solution(mesh):
    in_specs = (
        P("ctx", "head"),
        P("ctx", "head"),
        P("ctx", None),
        P("ctx", None),
        P("ctx"),
        P(None, "head"),
        P(None, "head"),
        P("head", "ctx"),
    )
    out_specs = P("ctx", "head")
    return jax.shard_map(body, mesh=mesh, in_specs=in_specs, out_specs=out_specs, check_vma=False)
```

time: 421 us -> 366 us (0.87)
  blocking collectives: 285 us -> 0 us
  waiting for transfers between devices: 86 us -> 325 us
  local copies, waits for them, and re-layouts: 10.6 us -> 5.03 us
    unnamed x1 -> x0, blocking collectives: 209 us -> none
    all_gather x1, waiting for transfers between devices: 0.02 us -> 127 us  [body(): keys = lax.all_gather(local_keys, 'ctx', axis=0, tiled=True)]
    all_gather x1, waiting for transfers between devices: 0.02 us -> 114 us  [body(): lax.all_gather(out_proj, 'ctx', axis=1, tiled=True)]
    all_gather x1 -> x0, blocking collectives: 75.8 us -> none  [attend(): rope_part = lax.all_gather(rot_keys, 'ctx', axis=0, tiled=True)]
    dot_general x3 -> x2, matrix products: 9.25 us -> 8.97 us  [the longest x1 6.21 us: attend(): jnp.einsum('rl,kl->rk', query_rows, keys, preferred_element_type=jnp.floa...]
  transfers between devices with their start and end apart: 3 -> 3, of which waited for: 1 -> 3; matrix products, arithmetic and copies ran while one was open for 6% -> 4% of each run, Pallas kernels for 0% -> 0%
where the time goes in v1:
time: 366 us; the launch traced here: 365 us
  waiting for transfers between devices  325 us (89%)
  matrix products  16.2 us (4%)
  between operations  13.2 us (4%)
  other arithmetic  5.66 us (2%)
  local copies, waits for them, and re-layouts  5.03 us (1%)
    all_gather x1, waiting for transfers between devices, body(): keys = lax.all_gather(local_keys, 'ctx', axis=0, tiled=True)  127 us
    all_gather x1, waiting for transfers between devices, body(): lax.all_gather(out_proj, 'ctx', axis=1, tiled=True)  114 us
    unnamed x4, waiting for transfers between devices  84.3 us
  transfers between devices with their start and end apart: 3, of which 3 were waited for; matrix products, arithmetic and copies ran while one was open for 4% of the time, Pallas kernels for 0%

profile of v1, /device:TPU:6, one launch (start us, length us, event | category | flops | bytes accessed | tf_op | source)
XLA Modules:
  0.0 365.4 jit_solution(11109612518860116079)
XLA Ops:
  6.5 0.7 convert_element_type.33
  7.3 0.8 copy.34
  8.1 0.1 fusion.38
  8.3 0.1 copy.35
  8.4 1.5 pad_maximum_fusion.1
  9.9 0.7 all-gather.5.cloned.1.call-update
  10.7 1.0 reshape.133
  11.7 0.1 broadcast_in_dim.24
  11.7 0.1 le.16
  11.8 0.2 multiply_cosine_fusion
  12.0 0.1 fusion.44
  12.2 0.1 subtract_convert_fusion
  12.3 1.4 fusion.10
  13.7 0.1 pad_maximum_fusion
  13.8 126.6 %all-gather.3.cloned.1.call-done = bf16[4096,576]{1,0:T(8,128)(2,1)} async-done(((bf16[64,576]{1,0:T(8,128)(2,1)}), bf16[4096,576]{1,0:T(8,128)(2,1)}) %all-gather.3.cloned.1.call-update) | async-done | bytes 4718608 | tf_op jit(solution)/shard_map/all_gather | solution.py:85
  140.4 6.2 %fusion = (f32[512]{0:T(512)S(1)}, f32[512,4096]{1,0:T(8,128)S(1)}) fusion(s32[512]{0:T(512)S(1)} %le.16, bf16[4096,576]{1,0:T(8,128)(2,1)} %all-gather.3.cloned.1.call-done, bf16[64,8,576]{2,0,1:T(8,128)(2,1)S(1)} %pad_maximum_fusion), kind=kOutput, calls=%fused_computation.3 | convolution fusion | flops 2424307200 | bytes 13701120 | tf_op jit(solution)/shard_map/rl,kl->rk/dot_general | solution.py:41
  146.6 2.8 fusion.1
  149.5 2.8 fusion.20
  152.2 0.5 fusion.11
  152.7 114.3 %all-gather.5.cloned.1.call-done = bf16[1024,3584]{0,1:T(8,128)(2,1)} async-done(((bf16[1024,56]{0,1:T(8,128)(2,1)}), bf16[1024,3584]{0,1:T(8,128)(2,1)}) %all-gather.5.cloned.1.call-update) | async-done | bytes 7340048 | tf_op jit(solution)/shard_map/all_gather | solution.py:94
  267.0 5.4 %convolution_convert_fusion = bf16[64,3584]{1,0:T(8,128)(2,1)S(1)} fusion(bf16[1024,3584]{0,1:T(8,128)(2,1)} %all-gather.5.cloned.1.call-done, bf16[8,8,8,128]{3,2,1,0:T(8,128)(2,1)S(1)} %fusion.11), kind=kOutput, calls=%fused_computation.6 | convolution fusion | flops 469991424 | bytes 7929856 | tf_op jit(solution)/shard_map/dot_general | solution.py:92
  272.4 1.3 copy.39
  273.7 83.6 %reduce-scatter.4.cloned.1.call-done = bf16[448,64]{1,0:T(8,128)(2,1)} async-done(((bf16[3584,64]{1,0:T(8,128)(2,1)}), bf16[448,64]{1,0:T(8,128)(2,1)}) %reduce-scatter.4.cloned.1.call-update) | async-done | bytes 57360
  357.2 1.6 copy.40
  (15 shorter events, 0.2 us)
Async XLA Ops:
  6.5 5.8 %copy-start = (bf16[512,1024]{1,0:T(8,128)(2,1)S(1)}, bf16[512,1024]{1,0:T(8,128)(2,1)}, u32[]{:S(2)}) copy-start(bf16[512,1024]{1,0:T(8,128)(2,1)} %param.13) | copy-start | bytes 3145732
  6.5 133.8 %all-gather.3.cloned.1.call-start = ((), (), s32[]{:S(2)}) async-start(), calls=%async_computation.1 | async-start | bytes 5324800 | tf_op jit(solution)/shard_map/all_gather | solution.py:85
  9.9 257.1 %all-gather.5.cloned.1.call-start = ((), (), s32[]{:S(2)}) async-start(), calls=%async_computation.2 | async-start | bytes 7454720 | tf_op jit(solution)/shard_map/all_gather | solution.py:94
  10.6 346.6 %reduce-scatter.4.cloned.1.call-start = ((), (), s32[]{:S(2)}) async-start(), calls=%async_computation.3 | async-start | bytes 1032192
  146.6 2.9 copy-start.1
  149.5 2.8 copy-start.2
Sparse Core Ops, SparseCore 0:
  10.0 130.3 all-gather.2
  142.5 124.4 all-gather.4
  273.8 83.3 reduce-scatter.3

commit v2 on v1

--- a/solution.py
+++ b/solution.py
@@ -3,6 +3,7 @@
 import jax
 import jax.numpy as jnp
 from jax import lax
+from jax.sharding import Mesh
 from jax.sharding import PartitionSpec as P
 
 LATENT = 512
@@ -51,6 +52,35 @@
     return (summed / totals[:, None]).astype(jnp.bfloat16)
 
 
+def gather_in_order(local, axes):
+    acc = local[None]
+    for axis, size in axes:
+        bit = size // 2
+        while bit >= 1:
+            upper = (lax.axis_index(axis) // bit) % 2 == 1
+            other = lax.ppermute(acc, axis, [(i, i ^ bit) for i in range(size)])
+            first = jnp.where(upper, other, acc)
+            second = jnp.where(upper, acc, other)
+            acc = jnp.stack([first, second], axis=1).reshape((-1,) + local.shape)
+            bit //= 2
+    return acc.reshape((-1,) + local.shape[1:])
+
+
+def scatter_sum(partial, axes):
+    acc = partial
+    for axis, size in axes:
+        bit = size // 2
+        while bit >= 1:
+            upper = (lax.axis_index(axis) // bit) % 2 == 1
+            half = acc.shape[1] // 2
+            low, high = acc[:, :half], acc[:, half:]
+            keep = jnp.where(upper, high, low)
+            send = jnp.where(upper, low, high)
+            acc = keep + lax.ppermute(send, axis, [(i, i ^ bit) for i in range(size)])
+            bit //= 2
+    return acc
+
+
 def upward(latent_out, value_up, token_count, head_count):
     head_out = jnp.einsum(
         "thl,lhd->thd",
@@ -64,7 +94,7 @@
 def body(queries_nope, queries_rope, latents, rope_keys, positions, key_up, value_up, out_proj):
     token_count = latents.shape[0]
     head_count = key_up.shape[1] // NOPE
-    ctx_count = lax.axis_size("ctx")
+    ctx_count = lax.axis_size(CTX)
     cosine, sine = rope_tables(positions, ROPE)
     rot_queries = rotate(
         queries_rope.astype(jnp.float32).reshape(token_count, head_count, ROPE), cosine, sine
@@ -82,8 +112,8 @@
         token_count * head_count, LATENT + ROPE
     )
     local_keys = jnp.concatenate([latents, rot_keys], axis=-1)
-    keys = lax.all_gather(local_keys, "ctx", axis=0, tiled=True)
-    first_token = lax.axis_index("ctx") * token_count
+    keys = gather_in_order(local_keys, CTX_SPLIT)
+    first_token = lax.axis_index(CTX) * token_count
     query_index = jnp.repeat(
         first_token + jnp.arange(token_count, dtype=jnp.int32), head_count
     )
@@ -91,24 +121,30 @@
     head_out = upward(latent_out, value_up, token_count, head_count)
     partial_sums = jnp.dot(
         head_out,
-        lax.all_gather(out_proj, "ctx", axis=1, tiled=True),
+        lax.all_gather(out_proj, CTX, axis=1, tiled=True),
         preferred_element_type=jnp.float32,
     )
-    return lax.psum_scatter(
-        partial_sums.astype(jnp.bfloat16), "head", scatter_dimension=1, tiled=True
-    )
+    return scatter_sum(partial_sums, HEAD_SPLIT).astype(jnp.bfloat16)
+
+
+CTX_SPLIT = (("zh", 8), ("zl", 2), ("yl", 2), ("co", 2))
+HEAD_SPLIT = (("x", 4), ("yh", 2))
+CTX = tuple(name for name, _ in CTX_SPLIT)
+HEAD = tuple(name for name, _ in HEAD_SPLIT)
 
 
 def solution(mesh):
+    sizes = tuple(size for _, size in CTX_SPLIT + HEAD_SPLIT)
+    fine = Mesh(mesh.devices.reshape(sizes), CTX + HEAD)
     in_specs = (
-        P("ctx", "head"),
-        P("ctx", "head"),
-        P("ctx", None),
-        P("ctx", None),
-        P("ctx"),
-        P(None, "head"),
-        P(None, "head"),
-        P("head", "ctx"),
+        P(CTX, HEAD),
+        P(CTX, HEAD),
+        P(CTX, None),
+        P(CTX, None),
+        P(CTX),
+        P(None, HEAD),
+        P(None, HEAD),
+        P(HEAD, CTX),
     )
-    out_specs = P("ctx", "head")
-    return jax.shard_map(body, mesh=mesh, in_specs=in_specs, out_specs=out_specs, check_vma=False)
+    out_specs = P(CTX, HEAD)
+    return jax.shard_map(body, mesh=fine, in_specs=in_specs, out_specs=out_specs, check_vma=False)

time: 366 us -> 223 us (0.61)
  waiting for transfers between devices: 325 us -> 132 us
  starting transfers between devices: 0.08 us -> 45.4 us
  other arithmetic: 5.66 us -> 13.4 us
    all_gather x2 -> x1, waiting for transfers between devices: 241 us -> 0.02 us  [body(): lax.all_gather(out_proj, CTX, axis=1, tiled=True)]
    ppermute x0 -> x9, waiting for transfers between devices: none -> 131 us  [the longest x6 110 us: gather_in_order(): other = lax.ppermute(acc, axis, [(i, i ^ bit) for i in range(size)])]
    unnamed x4 -> x1, waiting for transfers between devices: 84.3 us -> 0.71 us
    ppermute x0 -> x9, starting transfers between devices: none -> 45.4 us  [the longest x6 34 us: gather_in_order(): other = lax.ppermute(acc, axis, [(i, i ^ bit) for i in range(size)])]
    another operation x2 -> x13, other arithmetic: 0.26 us -> 7.53 us  [the longest x11 7.27 us: gather_in_order(): acc = jnp.stack([first, second], axis=1).reshape((-1,) + local.shape)]
  transfers between devices with their start and end apart: 3 -> 10, of which waited for: 3 -> 9; matrix products, arithmetic and copies ran while one was open for 4% -> 11% of each run, Pallas kernels for 0% -> 0%
where the time goes in v2:
time: 223 us; the launch traced here: 222 us
  waiting for transfers between devices  132 us (59%)
  starting transfers between devices  45.4 us (20%)
  between operations  13.9 us (6%)
  other arithmetic  13.4 us (6%)
  matrix products  13.2 us (6%)
  local copies, waits for them, and re-layouts  3.94 us (2%)
    ppermute x6, waiting for transfers between devices, gather_in_order(): other = lax.ppermute(acc, axis, [(i, i ^ bit) for i in range(size)])  110 us
    ppermute x6, starting transfers between devices, gather_in_order(): other = lax.ppermute(acc, axis, [(i, i ^ bit) for i in range(size)])  34 us
    ppermute x3, waiting for transfers between devices, scatter_sum(): acc = keep + lax.ppermute(send, axis, [(i, i ^ bit) for i in range(size)])  21.7 us
    ppermute x3, starting transfers between devices, scatter_sum(): acc = keep + lax.ppermute(send, axis, [(i, i ^ bit) for i in range(size)])  11.3 us
    another operation x11, other arithmetic, gather_in_order(): acc = jnp.stack([first, second], axis=1).reshape((-1,) + local.shape)  7.27 us
    dot_general x1, matrix products, body(): jnp.dot(head_out, lax.all_gather(out_proj, CTX, axis=1, tiled=True), pref...  5.42 us
  transfers between devices with their start and end apart: 10, of which 9 were waited for; matrix products, arithmetic and copies ran while one was open for 11% of the time, Pallas kernels for 0%

profile of v2, /device:TPU:6, one launch (start us, length us, event | category | flops | bytes accessed | tf_op | source)
XLA Modules:
  0.0 222.0 jit_solution(9587533923062762247)
XLA Ops:
  9.9 15.7 %collective-permute-start = (bf16[1,64,576]{2,1,0:T(8,128)(2,1)S(1)}, bf16[1,64,576]{2,1,0:T(8,128)(2,1)S(1)}, u32[]{:S(2)}, u32[]{:S(2)}) collective-permute-start(bf16[1,64,576]{2,1,0:T(8,128)(2,1)S(1)} %maximum_bitcast_fusion.1), channel_id=1, source_target_pairs={{0,256},{64,320},{128,384},{192,448},{256,0},{320,64},{384,128},{4... | collective-permute-start | bytes 221192 | tf_op jit(solution)/shard_map/ppermute | solution.py:61
  25.6 2.7 %collective-permute-done = bf16[1,64,576]{2,1,0:T(8,128)(2,1)S(1)} collective-permute-done((bf16[1,64,576]{2,1,0:T(8,128)(2,1)S(1)}, bf16[1,64,576]{2,1,0:T(8,128)(2,1)S(1)}, u32[]{:S(2)}, u32[]{:S(2)}) %collective-permute-start) | collective-permute-done | bytes 73760 | tf_op jit(solution)/shard_map/ppermute | solution.py:61
  29.2 9.1 %collective-permute-start.1 = (bf16[2,64,576]{2,1,0:T(8,128)(2,1)S(1)}, bf16[2,64,576]{2,1,0:T(8,128)(2,1)S(1)}, u32[]{:S(2)}, u32[]{:S(2)}) collective-permute-start(bf16[2,64,576]{2,1,0:T(8,128)(2,1)S(1)} %maximum_bitcast_fusion), channel_id=1, source_target_pairs={{0,128},{64,192},{128,0},{192,64},{256,384},{320,448},{384,256},{4... | collective-permute-start | bytes 442376 | tf_op jit(solution)/shard_map/ppermute | solution.py:61
  38.4 15.8 %collective-permute-done.1 = bf16[2,64,576]{2,1,0:T(8,128)(2,1)S(1)} collective-permute-done((bf16[2,64,576]{2,1,0:T(8,128)(2,1)S(1)}, bf16[2,64,576]{2,1,0:T(8,128)(2,1)S(1)}, u32[]{:S(2)}, u32[]{:S(2)}) %collective-permute-start.1) | collective-permute-done | bytes 147488 | tf_op jit(solution)/shard_map/ppermute | solution.py:61
  54.4 1.9 collective-permute-start.2
  56.3 19.2 %collective-permute-done.2 = bf16[4,64,576]{2,1,0:T(8,128)(2,1)S(1)} collective-permute-done((bf16[4,64,576]{2,1,0:T(8,128)(2,1)S(1)}, bf16[4,64,576]{2,1,0:T(8,128)(2,1)S(1)}, u32[]{:S(2)}, u32[]{:S(2)}) %collective-permute-start.2) | collective-permute-done | bytes 294944 | tf_op jit(solution)/shard_map/ppermute | solution.py:61
  75.7 1.9 collective-permute-start.3
  77.7 24.6 %collective-permute-done.3 = bf16[8,64,576]{2,1,0:T(8,128)(2,1)S(1)} collective-permute-done((bf16[8,64,576]{2,1,0:T(8,128)(2,1)S(1)}, bf16[8,64,576]{2,1,0:T(8,128)(2,1)S(1)}, u32[]{:S(2)}, u32[]{:S(2)}) %collective-permute-start.3) | collective-permute-done | bytes 589856 | tf_op jit(solution)/shard_map/ppermute | solution.py:61
  102.8 3.4 %collective-permute-start.4 = (bf16[16,64,576]{2,1,0:T(8,128)(2,1)S(1)}, bf16[16,64,576]{2,1,0:T(8,128)(2,1)}, u32[]{:S(2)}, u32[]{:S(2)}) collective-permute-start(bf16[16,64,576]{2,1,0:T(8,128)(2,1)S(1)} %bitcast.96), channel_id=1, source_target_pairs={{0,16},{16,0},{1,17},{17,1},{2,18},{18,2},{3,19},{19,3},{4,20},{20... | collective-permute-start | bytes 3538952 | tf_op jit(solution)/shard_map/ppermute | solution.py:61
  106.2 43.7 %collective-permute-done.4 = bf16[16,64,576]{2,1,0:T(8,128)(2,1)} collective-permute-done((bf16[16,64,576]{2,1,0:T(8,128)(2,1)S(1)}, bf16[16,64,576]{2,1,0:T(8,128)(2,1)}, u32[]{:S(2)}, u32[]{:S(2)}) %collective-permute-start.4) | collective-permute-done | bytes 1179680 | tf_op jit(solution)/shard_map/ppermute | solution.py:61
  151.9 1.8 copy.75
  153.7 1.9 collective-permute-start.5
  157.1 3.8 %collective-permute-done.5 = bf16[32,64,576]{2,1,0:T(8,128)(2,1)} collective-permute-done((bf16[32,64,576]{2,1,0:T(8,128)(2,1)}, bf16[32,64,576]{2,1,0:T(8,128)(2,1)}, u32[]{:S(2)}, u32[]{:S(2)}) %collective-permute-start.5) | collective-permute-done | bytes 2359328 | tf_op jit(solution)/shard_map/ppermute | solution.py:61
  160.8 3.0 %select_bitcast_fusion.1 = (bf16[32,1,64,576]{3,2,0,1:T(8,128)(2,1)S(1)}, bf16[32,1,64,576]{3,2,0,1:T(8,128)(2,1)S(1)}) fusion(bf16[32,64,576]{2,1,0:T(8,128)(2,1)} %collective-permute-done.5, pred[]{:T(512)S(6)} %eq.40, bf16[16,2,64,576]{3,2,1,0:T(8,128)(2,1)} %copy.75), kind=kLoop, calls=%fused_computation.15 | loop fusion | flops 2359296 | bytes 9437185 | tf_op jit(solution)/shard_map/stack | solution.py:64
  165.3 4.1 %fusion = (f32[512]{0:T(512)S(1)}, f32[512,4096]{1,0:T(8,128)S(1)}) fusion(s32[512]{0:T(512)S(1)} %le.16, bf16[4096,576]{1,0:T(8,128)(2,1)S(1)} %bitcast.94, bf16[64,8,576]{2,0,1:T(8,128)(2,1)S(1)} %pad_maximum_fusion.3), kind=kOutput, calls=%fused_computation.3 | convolution fusion | flops 2424307200 | bytes 13701120 | tf_op jit(solution)/shard_map/rl,kl->rk/dot_general | solution.py:42
  169.3 3.0 %fusion.1 = f32[512]{0:T(512)S(1)} fusion(f32[512,4096]{1,0:T(8,128)S(1)} %get-tuple-element.26, f32[512]{0:T(512)S(1)} %get-tuple-element.25, s32[512]{0:T(512)S(1)} %le.16), kind=kLoop, calls=%fused_computation.5 | loop fusion | flops 12582400 | bytes 8394752 | tf_op jit(solution)/shard_map/reduce_sum | solution.py:48
  172.4 2.7 %fusion.20 = bf16[64,8,512]{2,1,0:T(8,128)(2,1)S(1)} fusion(bf16[4096,576]{1,0:T(8,128)(2,1)S(1)} %bitcast.95, f32[512,4096]{1,0:T(8,128)S(1)} %get-tuple-element.26, f32[512]{0:T(512)S(1)} %get-tuple-element.25, s32[512]{0:T(512)S(1)} %le.16, f32[512]{0:T(512)S(1)} %fusion.1), kind=kOutput, calls=%fused_computation.28 | convolution fusion | flops 2160590848 | bytes 13113344 | tf_op jit(solution)/shard_map/dot_general | solution.py:49
  175.6 5.4 %fusion.29 = f32[64,3584]{1,0:T(8,128)S(1)} fusion(bf16[1024,3584]{0,1:T(8,128)(2,1)} %all-gather.2.cloned.1.call-done, bf16[8,8,8,128]{3,2,1,0:T(8,128)(2,1)S(1)} %fusion.11), kind=kOutput, calls=%fused_computation.49 | convolution fusion | flops 469762048 | bytes 8388608 | tf_op jit(solution)/shard_map/dot_general | solution.py:122
  181.1 3.4 %collective-permute-start.6 = (f32[64,1792]{1,0:T(8,128)S(1)}, f32[64,1792]{1,0:T(8,128)S(1)}, u32[]{:S(2)}, u32[]{:S(2)}) collective-permute-start(f32[64,1792]{1,0:T(8,128)S(1)} %slice_select_fusion), channel_id=1, source_target_pairs={{0,4},{2,6},{4,0},{6,2},{1,5},{3,7},{5,1},{7,3},{8,12},{10,14},{12... | collective-permute-start | bytes 1376264 | tf_op jit(solution)/shard_map/ppermute | solution.py:79
  184.5 12.6 %collective-permute-done.6 = f32[64,1792]{1,0:T(8,128)S(1)} collective-permute-done((f32[64,1792]{1,0:T(8,128)S(1)}, f32[64,1792]{1,0:T(8,128)S(1)}, u32[]{:S(2)}, u32[]{:S(2)}) %collective-permute-start.6) | collective-permute-done | bytes 458784 | tf_op jit(solution)/shard_map/ppermute | solution.py:79
  197.2 3.3 %collective-permute-start.7 = (f32[64,896]{1,0:T(8,128)S(1)}, f32[64,896]{1,0:T(8,128)S(1)}, u32[]{:S(2)}, u32[]{:S(2)}) collective-permute-start(f32[64,896]{1,0:T(8,128)S(1)} %slice_select_fusion.1), channel_id=1, source_target_pairs={{0,2},{2,0},{4,6},{6,4},{1,3},{3,1},{5,7},{7,5},{8,10},{10,8},{12,... | collective-permute-start | bytes 688136 | tf_op jit(solution)/shard_map/ppermute | solution.py:79
  200.5 5.5 %collective-permute-done.7 = f32[64,896]{1,0:T(8,128)S(1)} collective-permute-done((f32[64,896]{1,0:T(8,128)S(1)}, f32[64,896]{1,0:T(8,128)S(1)}, u32[]{:S(2)}, u32[]{:S(2)}) %collective-permute-start.7) | collective-permute-done | bytes 229408 | tf_op jit(solution)/shard_map/ppermute | solution.py:79
  206.1 4.7 %collective-permute-start.8 = (f32[64,448]{1,0:T(8,128)S(1)}, f32[64,448]{1,0:T(8,128)S(1)}, u32[]{:S(2)}, u32[]{:S(2)}) collective-permute-start(f32[64,448]{1,0:T(8,128)S(1)} %slice_select_fusion.2), channel_id=1, source_target_pairs={{0,1},{1,0},{2,3},{3,2},{4,5},{5,4},{6,7},{7,6},{8,9},{9,8},{10,11... | collective-permute-start | bytes 344072 | tf_op jit(solution)/shard_map/ppermute | solution.py:79
  210.8 3.7 %collective-permute-done.8 = f32[64,448]{1,0:T(8,128)S(1)} collective-permute-done((f32[64,448]{1,0:T(8,128)S(1)}, f32[64,448]{1,0:T(8,128)S(1)}, u32[]{:S(2)}, u32[]{:S(2)}) %collective-permute-start.8) | collective-permute-done | bytes 114720 | tf_op jit(solution)/shard_map/ppermute | solution.py:79
  (49 shorter events, 11.3 us)
Async XLA Ops:
  6.5 149.9 %copy-start = (bf16[512,1024]{1,0:T(8,128)(2,1)S(1)}, bf16[512,1024]{1,0:T(8,128)(2,1)}, u32[]{:S(2)}) copy-start(bf16[512,1024]{1,0:T(8,128)(2,1)} %param.13) | copy-start | bytes 3145732
  6.5 169.1 %all-gather.2.cloned.1.call-start = ((), (), s32[]{:S(2)}) async-start(), calls=%async_computation | async-start | bytes 7454720 | tf_op jit(solution)/shard_map/all_gather | solution.py:124
  9.9 18.4 %collective-permute-start = (bf16[1,64,576]{2,1,0:T(8,128)(2,1)S(1)}, bf16[1,64,576]{2,1,0:T(8,128)(2,1)S(1)}, u32[]{:S(2)}, u32[]{:S(2)}) collective-permute-start(bf16[1,64,576]{2,1,0:T(8,128)(2,1)S(1)} %maximum_bitcast_fusion.1), channel_id=1, source_target_pairs={{0,256},{64,320},{128,384},{192,448},{256,0},{320,64},{384,128},{4... | collective-permute-start | bytes 221192 | tf_op jit(solution)/shard_map/ppermute | solution.py:61
  29.2 25.0 %collective-permute-start.1 = (bf16[2,64,576]{2,1,0:T(8,128)(2,1)S(1)}, bf16[2,64,576]{2,1,0:T(8,128)(2,1)S(1)}, u32[]{:S(2)}, u32[]{:S(2)}) collective-permute-start(bf16[2,64,576]{2,1,0:T(8,128)(2,1)S(1)} %maximum_bitcast_fusion), channel_id=1, source_target_pairs={{0,128},{64,192},{128,0},{192,64},{256,384},{320,448},{384,256},{4... | collective-permute-start | bytes 442376 | tf_op jit(solution)/shard_map/ppermute | solution.py:61
  54.4 21.1 %collective-permute-start.2 = (bf16[4,64,576]{2,1,0:T(8,128)(2,1)S(1)}, bf16[4,64,576]{2,1,0:T(8,128)(2,1)S(1)}, u32[]{:S(2)}, u32[]{:S(2)}) collective-permute-start(bf16[4,64,576]{2,1,0:T(8,128)(2,1)S(1)} %bitcast.98), channel_id=1, source_target_pairs={{0,64},{64,0},{128,192},{192,128},{256,320},{320,256},{384,448},{4... | collective-permute-start | bytes 884744 | tf_op jit(solution)/shard_map/ppermute | solution.py:61
  75.7 26.5 %collective-permute-start.3 = (bf16[8,64,576]{2,1,0:T(8,128)(2,1)S(1)}, bf16[8,64,576]{2,1,0:T(8,128)(2,1)S(1)}, u32[]{:S(2)}, u32[]{:S(2)}) collective-permute-start(bf16[8,64,576]{2,1,0:T(8,128)(2,1)S(1)} %bitcast.97), channel_id=1, source_target_pairs={{0,32},{32,0},{1,33},{33,1},{2,34},{34,2},{3,35},{35,3},{4,36},{36... | collective-permute-start | bytes 1769480 | tf_op jit(solution)/shard_map/ppermute | solution.py:61
  102.8 47.2 %collective-permute-start.4 = (bf16[16,64,576]{2,1,0:T(8,128)(2,1)S(1)}, bf16[16,64,576]{2,1,0:T(8,128)(2,1)}, u32[]{:S(2)}, u32[]{:S(2)}) collective-permute-start(bf16[16,64,576]{2,1,0:T(8,128)(2,1)S(1)} %bitcast.96), channel_id=1, source_target_pairs={{0,16},{16,0},{1,17},{17,1},{2,18},{18,2},{3,19},{19,3},{4,20},{20... | collective-permute-start | bytes 3538952 | tf_op jit(solution)/shard_map/ppermute | solution.py:61
  151.5 4.4 %copy-start.1 = (bf16[64,512]{1,0:T(8,128)(2,1)S(1)}, bf16[64,512]{1,0:T(8,128)(2,1)}, u32[]{:S(2)}) copy-start(bf16[64,512]{1,0:T(8,128)(2,1)} %param.9) | copy-start | bytes 196612
  151.5 5.0 %copy-start.3 = (bf16[64,1024]{1,0:T(8,128)(2,1)S(1)}, bf16[64,1024]{1,0:T(8,128)(2,1)}, u32[]{:S(2)}) copy-start(bf16[64,1024]{1,0:T(8,128)(2,1)} %param.8) | copy-start | bytes 393220
  153.7 7.1 %collective-permute-start.5 = (bf16[32,64,576]{2,1,0:T(8,128)(2,1)}, bf16[32,64,576]{2,1,0:T(8,128)(2,1)}, u32[]{:S(2)}, u32[]{:S(2)}) collective-permute-start(bf16[32,64,576]{2,1,0:T(8,128)(2,1)} %bitcast.21), channel_id=1, source_target_pairs={{0,8},{8,0},{1,9},{9,1},{2,10},{10,2},{3,11},{11,3},{4,12},{12,4},... | collective-permute-start | bytes 7077896 | tf_op jit(solution)/shard_map/ppermute | solution.py:61
  172.4 2.7 %copy-start.2 = (bf16[512,1024]{1,0:T(8,128)(2,1)S(1)}, bf16[512,1024]{1,0:T(8,128)(2,1)}, u32[]{:S(2)}) copy-start(bf16[512,1024]{1,0:T(8,128)(2,1)} %param.14) | copy-start | bytes 3145732
  181.1 16.0 %collective-permute-start.6 = (f32[64,1792]{1,0:T(8,128)S(1)}, f32[64,1792]{1,0:T(8,128)S(1)}, u32[]{:S(2)}, u32[]{:S(2)}) collective-permute-start(f32[64,1792]{1,0:T(8,128)S(1)} %slice_select_fusion), channel_id=1, source_target_pairs={{0,4},{2,6},{4,0},{6,2},{1,5},{3,7},{5,1},{7,3},{8,12},{10,14},{12... | collective-permute-start | bytes 1376264 | tf_op jit(solution)/shard_map/ppermute | solution.py:79
  197.2 8.8 %collective-permute-start.7 = (f32[64,896]{1,0:T(8,128)S(1)}, f32[64,896]{1,0:T(8,128)S(1)}, u32[]{:S(2)}, u32[]{:S(2)}) collective-permute-start(f32[64,896]{1,0:T(8,128)S(1)} %slice_select_fusion.1), channel_id=1, source_target_pairs={{0,2},{2,0},{4,6},{6,4},{1,3},{3,1},{5,7},{7,5},{8,10},{10,8},{12,... | collective-permute-start | bytes 688136 | tf_op jit(solution)/shard_map/ppermute | solution.py:79
  206.1 8.4 %collective-permute-start.8 = (f32[64,448]{1,0:T(8,128)S(1)}, f32[64,448]{1,0:T(8,128)S(1)}, u32[]{:S(2)}, u32[]{:S(2)}) collective-permute-start(f32[64,448]{1,0:T(8,128)S(1)} %slice_select_fusion.2), channel_id=1, source_target_pairs={{0,1},{1,0},{2,3},{3,2},{4,5},{5,4},{6,7},{7,6},{8,9},{9,8},{10,11... | collective-permute-start | bytes 344072 | tf_op jit(solution)/shard_map/ppermute | solution.py:79
Sparse Core Ops, SparseCore 0:
  9.5 149.2 all-gather.1

commit v3 on v2

--- a/solution.py
+++ b/solution.py
@@ -52,13 +52,23 @@
     return (summed / totals[:, None]).astype(jnp.bfloat16)
 
 
-def gather_in_order(local, axes):
+def exchange(acc, axis, size, bit, same_over_yh):
+    pairs = [(i, i ^ bit) for i in range(size)]
+    if axis != "yl" or not same_over_yh:
+        return lax.ppermute(acc, axis, pairs)
+    half = acc.shape[0] // 2
+    near = lax.ppermute(acc[:half], "yl", pairs)
+    far = lax.ppermute(acc[half:], ("yl", "yh"), [(i, i ^ 3) for i in range(4)])
+    return jnp.concatenate([near, far], axis=0)
+
+
+def gather_in_order(local, axes, same_over_yh):
     acc = local[None]
     for axis, size in axes:
         bit = size // 2
         while bit >= 1:
             upper = (lax.axis_index(axis) // bit) % 2 == 1
-            other = lax.ppermute(acc, axis, [(i, i ^ bit) for i in range(size)])
+            other = exchange(acc, axis, size, bit, same_over_yh)
             first = jnp.where(upper, other, acc)
             second = jnp.where(upper, acc, other)
             acc = jnp.stack([first, second], axis=1).reshape((-1,) + local.shape)
@@ -79,6 +89,13 @@
             acc = keep + lax.ppermute(send, axis, [(i, i ^ bit) for i in range(size)])
             bit //= 2
     return acc
+
+
+def chip_pair_columns(out_proj):
+    blocks = gather_in_order(out_proj.T, (("yl", 2), ("co", 2)), False)
+    return blocks.reshape(-1, out_proj.shape[1], out_proj.shape[0]).transpose(2, 0, 1).reshape(
+        out_proj.shape[0], -1
+    )
 
 
 def upward(latent_out, value_up, token_count, head_count):
@@ -112,7 +129,7 @@
         token_count * head_count, LATENT + ROPE
     )
     local_keys = jnp.concatenate([latents, rot_keys], axis=-1)
-    keys = gather_in_order(local_keys, CTX_SPLIT)
+    keys = gather_in_order(local_keys, CTX_SPLIT, True)
     first_token = lax.axis_index(CTX) * token_count
     query_index = jnp.repeat(
         first_token + jnp.arange(token_count, dtype=jnp.int32), head_count
@@ -121,7 +138,7 @@
     head_out = upward(latent_out, value_up, token_count, head_count)
     partial_sums = jnp.dot(
         head_out,
-        lax.all_gather(out_proj, CTX, axis=1, tiled=True),
+        lax.all_gather(chip_pair_columns(out_proj), ("zh", "zl"), axis=1, tiled=True),
         preferred_element_type=jnp.float32,
     )
     return scatter_sum(partial_sums, HEAD_SPLIT).astype(jnp.bfloat16)

time: 223 us -> 218 us (0.978)
  waiting for transfers between devices: 132 us -> 120 us
  starting transfers between devices: 45.4 us -> 52 us
    ppermute x6 -> x9, waiting for transfers between devices: 110 us -> 95.8 us  [the longest x7 82.8 us: exchange(): return lax.ppermute(acc, axis, pairs)]
    ppermute x6 -> x9, starting transfers between devices: 34 us -> 43.3 us  [the longest x7 36.3 us: exchange(): return lax.ppermute(acc, axis, pairs)]
    ppermute x3, starting transfers between devices: 11.3 us -> 8.7 us  [scatter_sum(): acc = keep + lax.ppermute(send, axis, [(i, i ^ bit) for i in range(size)])]
    ppermute x3, waiting for transfers between devices: 21.7 us -> 24.3 us  [scatter_sum(): acc = keep + lax.ppermute(send, axis, [(i, i ^ bit) for i in range(size)])]
    another operation x11 -> x14, other arithmetic: 7.27 us -> 7.73 us  [gather_in_order(): acc = jnp.stack([first, second], axis=1).reshape((-1,) + local.shape)]
  transfers between devices with their start and end apart: 10 -> 13, of which waited for: 9 -> 12; matrix products, arithmetic and copies ran while one was open for 11% -> 11% of each run, Pallas kernels for 0% -> 0%
where the time goes in v3:
time: 218 us
  waiting for transfers between devices  120 us (55%)
  starting transfers between devices  52 us (24%)
  other arithmetic  14.4 us (7%)
  between operations  14 us (6%)
  matrix products  13.2 us (6%)
  local copies, waits for them, and re-layouts  4.05 us (2%)
    ppermute x7, waiting for transfers between devices, exchange(): return lax.ppermute(acc, axis, pairs)  82.8 us
    ppermute x7, starting transfers between devices, exchange(): return lax.ppermute(acc, axis, pairs)  36.3 us
    ppermute x3, waiting for transfers between devices, scatter_sum(): acc = keep + lax.ppermute(send, axis, [(i, i ^ bit) for i in range(size)])  24.3 us
    ppermute x1, waiting for transfers between devices, exchange(): near = lax.ppermute(acc[:half], 'yl', pairs)  8.89 us
    ppermute x3, starting transfers between devices, scatter_sum(): acc = keep + lax.ppermute(send, axis, [(i, i ^ bit) for i in range(size)])  8.7 us
    another operation x14, other arithmetic, gather_in_order(): acc = jnp.stack([first, second], axis=1).reshape((-1,) + local.shape)  7.73 us
    dot_general x1, matrix products, body(): jnp.dot(head_out, lax.all_gather(chip_pair_columns(out_proj), ('zh', 'zl'...  5.42 us
  transfers between devices with their start and end apart: 13, of which 12 were waited for; matrix products, arithmetic and copies ran while one was open for 11% of the time, Pallas kernels for 0%

profile of v3, /device:TPU:6, one launch (start us, length us, event | category | flops | bytes accessed | tf_op | source)
XLA Modules:
  0.0 217.7 jit_solution(14362665299364328502)
XLA Ops:
  6.5 3.6 %collective-permute-start.7 = (bf16[1,56,1024]{2,1,0:T(8,128)(2,1)}, bf16[1,56,1024]{2,1,0:T(8,128)(2,1)S(1)}, u32[]{:S(2)}, u32[]{:S(2)}) collective-permute-start(bf16[1,56,1024]{2,1,0:T(8,128)(2,1)} %bitcast.129), channel_id=1, source_target_pairs={{0,16},{16,0},{1,17},{17,1},{2,18},{18,2},{3,19},{19,3},{4,20},{20... | collective-permute-start | bytes 344072 | tf_op jit(solution)/shard_map/ppermute | solution.py:58
  10.2 3.5 %collective-permute-done.7 = bf16[1,56,1024]{2,1,0:T(8,128)(2,1)S(1)} collective-permute-done((bf16[1,56,1024]{2,1,0:T(8,128)(2,1)}, bf16[1,56,1024]{2,1,0:T(8,128)(2,1)S(1)}, u32[]{:S(2)}, u32[]{:S(2)}) %collective-permute-start.7) | collective-permute-done | bytes 114720 | tf_op jit(solution)/shard_map/ppermute | solution.py:58
  21.5 15.7 %collective-permute-start = (bf16[1,64,576]{2,1,0:T(8,128)(2,1)S(1)}, bf16[1,64,576]{2,1,0:T(8,128)(2,1)S(1)}, u32[]{:S(2)}, u32[]{:S(2)}) collective-permute-start(bf16[1,64,576]{2,1,0:T(8,128)(2,1)S(1)} %maximum_bitcast_fusion.2), channel_id=1, source_target_pairs={{0,256},{64,320},{128,384},{192,448},{256,0},{320,64},{384,128},{4... | collective-permute-start | bytes 221192 | tf_op jit(solution)/shard_map/ppermute | solution.py:58
  37.3 3.0 %collective-permute-done = bf16[1,64,576]{2,1,0:T(8,128)(2,1)S(1)} collective-permute-done((bf16[1,64,576]{2,1,0:T(8,128)(2,1)S(1)}, bf16[1,64,576]{2,1,0:T(8,128)(2,1)S(1)}, u32[]{:S(2)}, u32[]{:S(2)}) %collective-permute-start) | collective-permute-done | bytes 73760 | tf_op jit(solution)/shard_map/ppermute | solution.py:58
  41.2 9.3 %collective-permute-start.1 = (bf16[2,64,576]{2,1,0:T(8,128)(2,1)S(1)}, bf16[2,64,576]{2,1,0:T(8,128)(2,1)S(1)}, u32[]{:S(2)}, u32[]{:S(2)}) collective-permute-start(bf16[2,64,576]{2,1,0:T(8,128)(2,1)S(1)} %maximum_bitcast_fusion.1), channel_id=1, source_target_pairs={{0,128},{64,192},{128,0},{192,64},{256,384},{320,448},{384,256},{4... | collective-permute-start | bytes 442376 | tf_op jit(solution)/shard_map/ppermute | solution.py:58
  50.5 17.9 %collective-permute-done.1 = bf16[2,64,576]{2,1,0:T(8,128)(2,1)S(1)} collective-permute-done((bf16[2,64,576]{2,1,0:T(8,128)(2,1)S(1)}, bf16[2,64,576]{2,1,0:T(8,128)(2,1)S(1)}, u32[]{:S(2)}, u32[]{:S(2)}) %collective-permute-start.1) | collective-permute-done | bytes 147488 | tf_op jit(solution)/shard_map/ppermute | solution.py:58
  70.4 22.5 %collective-permute-done.2 = bf16[4,64,576]{2,1,0:T(8,128)(2,1)S(1)} collective-permute-done((bf16[4,64,576]{2,1,0:T(8,128)(2,1)S(1)}, bf16[4,64,576]{2,1,0:T(8,128)(2,1)S(1)}, u32[]{:S(2)}, u32[]{:S(2)}) %collective-permute-start.2) | collective-permute-done | bytes 294944 | tf_op jit(solution)/shard_map/ppermute | solution.py:58
  95.2 30.7 %collective-permute-done.3 = bf16[8,64,576]{2,1,0:T(8,128)(2,1)S(1)} collective-permute-done((bf16[8,64,576]{2,1,0:T(8,128)(2,1)S(1)}, bf16[8,64,576]{2,1,0:T(8,128)(2,1)S(1)}, u32[]{:S(2)}, u32[]{:S(2)}) %collective-permute-start.3) | collective-permute-done | bytes 589856 | tf_op jit(solution)/shard_map/ppermute | solution.py:58
  126.4 3.3 %collective-permute-start.4 = (bf16[8,64,576]{2,1,0:T(8,128)(2,1)S(1)}, bf16[8,64,576]{2,1,0:T(8,128)(2,1)S(1)}, u32[]{:S(2)}, u32[]{:S(2)}) collective-permute-start(bf16[8,64,576]{2,1,0:T(8,128)(2,1)S(1)} %bitcast.125), channel_id=1, source_target_pairs={{0,16},{16,0},{1,17},{17,1},{2,18},{18,2},{3,19},{19,3},{4,20},{20... | collective-permute-start | bytes 1769480 | tf_op jit(solution)/shard_map/ppermute | solution.py:60
  129.7 3.8 %collective-permute-start.5 = (bf16[8,64,576]{2,1,0:T(8,128)(2,1)S(1)}, bf16[8,64,576]{2,1,0:T(8,128)(2,1)S(1)}, u32[]{:S(2)}, u32[]{:S(2)}) collective-permute-start(bf16[8,64,576]{2,1,0:T(8,128)(2,1)S(1)} %bitcast.126), channel_id=1, source_target_pairs={{0,17},{1,16},{16,1},{17,0},{2,19},{3,18},{18,3},{19,2},{4,21},{5,... | collective-permute-start | bytes 1769480 | tf_op jit(solution)/shard_map/ppermute | solution.py:61
  133.8 8.9 %collective-permute-done.4 = bf16[8,64,576]{2,1,0:T(8,128)(2,1)S(1)} collective-permute-done((bf16[8,64,576]{2,1,0:T(8,128)(2,1)S(1)}, bf16[8,64,576]{2,1,0:T(8,128)(2,1)S(1)}, u32[]{:S(2)}, u32[]{:S(2)}) %collective-permute-start.4) | collective-permute-done | bytes 589856 | tf_op jit(solution)/shard_map/ppermute | solution.py:60
  142.7 4.1 %collective-permute-done.5 = bf16[8,64,576]{2,1,0:T(8,128)(2,1)S(1)} collective-permute-done((bf16[8,64,576]{2,1,0:T(8,128)(2,1)S(1)}, bf16[8,64,576]{2,1,0:T(8,128)(2,1)S(1)}, u32[]{:S(2)}, u32[]{:S(2)}) %collective-permute-start.5) | collective-permute-done | bytes 589856 | tf_op jit(solution)/shard_map/ppermute | solution.py:61
  152.8 3.8 %collective-permute-done.6 = bf16[32,64,576]{2,1,0:T(8,128)(2,1)} collective-permute-done((bf16[32,64,576]{2,1,0:T(8,128)(2,1)}, bf16[32,64,576]{2,1,0:T(8,128)(2,1)}, u32[]{:S(2)}, u32[]{:S(2)}) %collective-permute-start.6) | collective-permute-done | bytes 2359328 | tf_op jit(solution)/shard_map/ppermute | solution.py:58
  156.6 3.0 %select_bitcast_fusion.1 = (bf16[32,1,64,576]{3,2,0,1:T(8,128)(2,1)S(1)}, bf16[32,1,64,576]{3,2,0,1:T(8,128)(2,1)S(1)}) fusion(bf16[32,64,576]{2,1,0:T(8,128)(2,1)} %collective-permute-done.6, pred[]{:T(512)S(6)} %eq.44, bf16[16,2,64,576]{3,2,1,0:T(8,128)(2,1)} %copy.82), kind=kLoop, calls=%fused_computation.15 | loop fusion | flops 2359296 | bytes 9437185 | tf_op jit(solution)/shard_map/stack | solution.py:74
  161.0 4.1 %fusion = (f32[512]{0:T(512)S(1)}, f32[512,4096]{1,0:T(8,128)S(1)}) fusion(s32[512]{0:T(512)S(1)} %le.16, bf16[4096,576]{1,0:T(8,128)(2,1)S(1)} %bitcast.120, bf16[64,8,576]{2,0,1:T(8,128)(2,1)S(1)} %pad_maximum_fusion.4), kind=kOutput, calls=%fused_computation.3 | convolution fusion | flops 2424307200 | bytes 13701120 | tf_op jit(solution)/shard_map/rl,kl->rk/dot_general | solution.py:42
  165.1 3.0 %fusion.1 = f32[512]{0:T(512)S(1)} fusion(f32[512,4096]{1,0:T(8,128)S(1)} %get-tuple-element.32, f32[512]{0:T(512)S(1)} %get-tuple-element.31, s32[512]{0:T(512)S(1)} %le.16), kind=kLoop, calls=%fused_computation.5 | loop fusion | flops 12582400 | bytes 8394752 | tf_op jit(solution)/shard_map/reduce_sum | solution.py:48
  168.2 2.7 %fusion.20 = bf16[64,8,512]{2,1,0:T(8,128)(2,1)S(1)} fusion(bf16[4096,576]{1,0:T(8,128)(2,1)S(1)} %bitcast.121, f32[512,4096]{1,0:T(8,128)S(1)} %get-tuple-element.32, f32[512]{0:T(512)S(1)} %get-tuple-element.31, s32[512]{0:T(512)S(1)} %le.16, f32[512]{0:T(512)S(1)} %fusion.1), kind=kOutput, calls=%fused_computation.33 | convolution fusion | flops 2160590848 | bytes 13113344 | tf_op jit(solution)/shard_map/dot_general | solution.py:49
  171.4 5.4 %fusion.31 = f32[64,3584]{1,0:T(8,128)S(1)} fusion(bf16[1024,3584]{0,1:T(8,128)(2,1)} %all-gather.2.cloned.1.call-done, bf16[8,8,8,128]{3,2,1,0:T(8,128)(2,1)S(1)} %fusion.11), kind=kOutput, calls=%fused_computation.60 | convolution fusion | flops 469762048 | bytes 8388608 | tf_op jit(solution)/shard_map/dot_general | solution.py:139
  176.9 3.3 %collective-permute-start.9 = (f32[64,1792]{1,0:T(8,128)S(1)}, f32[64,1792]{1,0:T(8,128)S(1)}, u32[]{:S(2)}, u32[]{:S(2)}) collective-permute-start(f32[64,1792]{1,0:T(8,128)S(1)} %slice_select_fusion), channel_id=1, source_target_pairs={{0,4},{2,6},{4,0},{6,2},{1,5},{3,7},{5,1},{7,3},{8,12},{10,14},{12... | collective-permute-start | bytes 1376264 | tf_op jit(solution)/shard_map/ppermute | solution.py:89
  180.2 12.6 %collective-permute-done.9 = f32[64,1792]{1,0:T(8,128)S(1)} collective-permute-done((f32[64,1792]{1,0:T(8,128)S(1)}, f32[64,1792]{1,0:T(8,128)S(1)}, u32[]{:S(2)}, u32[]{:S(2)}) %collective-permute-start.9) | collective-permute-done | bytes 458784 | tf_op jit(solution)/shard_map/ppermute | solution.py:89
  192.9 2.7 %collective-permute-start.10 = (f32[64,896]{1,0:T(8,128)S(1)}, f32[64,896]{1,0:T(8,128)S(1)}, u32[]{:S(2)}, u32[]{:S(2)}) collective-permute-start(f32[64,896]{1,0:T(8,128)S(1)} %slice_select_fusion.1), channel_id=1, source_target_pairs={{0,2},{2,0},{4,6},{6,4},{1,3},{3,1},{5,7},{7,5},{8,10},{10,8},{12,... | collective-permute-start | bytes 688136 | tf_op jit(solution)/shard_map/ppermute | solution.py:89
  195.7 5.9 %collective-permute-done.10 = f32[64,896]{1,0:T(8,128)S(1)} collective-permute-done((f32[64,896]{1,0:T(8,128)S(1)}, f32[64,896]{1,0:T(8,128)S(1)}, u32[]{:S(2)}, u32[]{:S(2)}) %collective-permute-start.10) | collective-permute-done | bytes 229408 | tf_op jit(solution)/shard_map/ppermute | solution.py:89
  201.8 2.7 %collective-permute-start.11 = (f32[64,448]{1,0:T(8,128)S(1)}, f32[64,448]{1,0:T(8,128)S(1)}, u32[]{:S(2)}, u32[]{:S(2)}) collective-permute-start(f32[64,448]{1,0:T(8,128)S(1)} %slice_select_fusion.2), channel_id=1, source_target_pairs={{0,1},{1,0},{2,3},{3,2},{4,5},{5,4},{6,7},{7,6},{8,9},{9,8},{10,11... | collective-permute-start | bytes 344072 | tf_op jit(solution)/shard_map/ppermute | solution.py:89
  204.5 5.7 %collective-permute-done.11 = f32[64,448]{1,0:T(8,128)S(1)} collective-permute-done((f32[64,448]{1,0:T(8,128)S(1)}, f32[64,448]{1,0:T(8,128)S(1)}, u32[]{:S(2)}, u32[]{:S(2)}) %collective-permute-start.11) | collective-permute-done | bytes 114720 | tf_op jit(solution)/shard_map/ppermute | solution.py:89
  (62 shorter events, 22.5 us)
Async XLA Ops:
  6.5 145.7 %copy-start = (bf16[512,1024]{1,0:T(8,128)(2,1)S(1)}, bf16[512,1024]{1,0:T(8,128)(2,1)}, u32[]{:S(2)}) copy-start(bf16[512,1024]{1,0:T(8,128)(2,1)} %param.13) | copy-start | bytes 3145732
  6.5 164.9 %all-gather.2.cloned.1.call-start = ((), (), s32[]{:S(2)}) async-start(), calls=%async_computation | async-start | bytes 7798784 | tf_op jit(solution)/shard_map/all_gather | solution.py:141
  6.5 7.1 %collective-permute-start.7 = (bf16[1,56,1024]{2,1,0:T(8,128)(2,1)}, bf16[1,56,1024]{2,1,0:T(8,128)(2,1)S(1)}, u32[]{:S(2)}, u32[]{:S(2)}) collective-permute-start(bf16[1,56,1024]{2,1,0:T(8,128)(2,1)} %bitcast.129), channel_id=1, source_target_pairs={{0,16},{16,0},{1,17},{17,1},{2,18},{18,2},{3,19},{19,3},{4,20},{20... | collective-permute-start | bytes 344072 | tf_op jit(solution)/shard_map/ppermute | solution.py:58
  14.6 3.4 %collective-permute-start.8 = (bf16[2,56,1024]{2,1,0:T(8,128)(2,1)S(1)}, bf16[2,56,1024]{2,1,0:T(8,128)(2,1)S(1)}, u32[]{:S(2)}, u32[]{:S(2)}) collective-permute-start(bf16[2,56,1024]{2,1,0:T(8,128)(2,1)S(1)} %maximum_bitcast_fusion), channel_id=1, source_target_pairs={{0,8},{8,0},{1,9},{9,1},{2,10},{10,2},{3,11},{11,3},{4,12},{12,4},... | collective-permute-start | bytes 688136 | tf_op jit(solution)/shard_map/ppermute | solution.py:58
  21.5 18.7 %collective-permute-start = (bf16[1,64,576]{2,1,0:T(8,128)(2,1)S(1)}, bf16[1,64,576]{2,1,0:T(8,128)(2,1)S(1)}, u32[]{:S(2)}, u32[]{:S(2)}) collective-permute-start(bf16[1,64,576]{2,1,0:T(8,128)(2,1)S(1)} %maximum_bitcast_fusion.2), channel_id=1, source_target_pairs={{0,256},{64,320},{128,384},{192,448},{256,0},{320,64},{384,128},{4... | collective-permute-start | bytes 221192 | tf_op jit(solution)/shard_map/ppermute | solution.py:58
  41.2 27.2 %collective-permute-start.1 = (bf16[2,64,576]{2,1,0:T(8,128)(2,1)S(1)}, bf16[2,64,576]{2,1,0:T(8,128)(2,1)S(1)}, u32[]{:S(2)}, u32[]{:S(2)}) collective-permute-start(bf16[2,64,576]{2,1,0:T(8,128)(2,1)S(1)} %maximum_bitcast_fusion.1), channel_id=1, source_target_pairs={{0,128},{64,192},{128,0},{192,64},{256,384},{320,448},{384,256},{4... | collective-permute-start | bytes 442376 | tf_op jit(solution)/shard_map/ppermute | solution.py:58
  68.5 24.5 %collective-permute-start.2 = (bf16[4,64,576]{2,1,0:T(8,128)(2,1)S(1)}, bf16[4,64,576]{2,1,0:T(8,128)(2,1)S(1)}, u32[]{:S(2)}, u32[]{:S(2)}) collective-permute-start(bf16[4,64,576]{2,1,0:T(8,128)(2,1)S(1)} %bitcast.124), channel_id=1, source_target_pairs={{0,64},{64,0},{128,192},{192,128},{256,320},{320,256},{384,448},{4... | collective-permute-start | bytes 884744 | tf_op jit(solution)/shard_map/ppermute | solution.py:58
  93.2 32.7 %collective-permute-start.3 = (bf16[8,64,576]{2,1,0:T(8,128)(2,1)S(1)}, bf16[8,64,576]{2,1,0:T(8,128)(2,1)S(1)}, u32[]{:S(2)}, u32[]{:S(2)}) collective-permute-start(bf16[8,64,576]{2,1,0:T(8,128)(2,1)S(1)} %bitcast.122), channel_id=1, source_target_pairs={{0,32},{32,0},{1,33},{33,1},{2,34},{34,2},{3,35},{35,3},{4,36},{36... | collective-permute-start | bytes 1769480 | tf_op jit(solution)/shard_map/ppermute | solution.py:58
  126.4 16.3 %collective-permute-start.4 = (bf16[8,64,576]{2,1,0:T(8,128)(2,1)S(1)}, bf16[8,64,576]{2,1,0:T(8,128)(2,1)S(1)}, u32[]{:S(2)}, u32[]{:S(2)}) collective-permute-start(bf16[8,64,576]{2,1,0:T(8,128)(2,1)S(1)} %bitcast.125), channel_id=1, source_target_pairs={{0,16},{16,0},{1,17},{17,1},{2,18},{18,2},{3,19},{19,3},{4,20},{20... | collective-permute-start | bytes 1769480 | tf_op jit(solution)/shard_map/ppermute | solution.py:60
  129.7 17.1 %collective-permute-start.5 = (bf16[8,64,576]{2,1,0:T(8,128)(2,1)S(1)}, bf16[8,64,576]{2,1,0:T(8,128)(2,1)S(1)}, u32[]{:S(2)}, u32[]{:S(2)}) collective-permute-start(bf16[8,64,576]{2,1,0:T(8,128)(2,1)S(1)} %bitcast.126), channel_id=1, source_target_pairs={{0,17},{1,16},{16,1},{17,0},{2,19},{3,18},{18,3},{19,2},{4,21},{5,... | collective-permute-start | bytes 1769480 | tf_op jit(solution)/shard_map/ppermute | solution.py:61
  147.2 4.4 %copy-start.1 = (bf16[64,512]{1,0:T(8,128)(2,1)S(1)}, bf16[64,512]{1,0:T(8,128)(2,1)}, u32[]{:S(2)}) copy-start(bf16[64,512]{1,0:T(8,128)(2,1)} %param.9) | copy-start | bytes 196612
  147.3 5.0 %copy-start.3 = (bf16[64,1024]{1,0:T(8,128)(2,1)S(1)}, bf16[64,1024]{1,0:T(8,128)(2,1)}, u32[]{:S(2)}) copy-start(bf16[64,1024]{1,0:T(8,128)(2,1)} %param.8) | copy-start | bytes 393220
  149.5 7.1 %collective-permute-start.6 = (bf16[32,64,576]{2,1,0:T(8,128)(2,1)}, bf16[32,64,576]{2,1,0:T(8,128)(2,1)}, u32[]{:S(2)}, u32[]{:S(2)}) collective-permute-start(bf16[32,64,576]{2,1,0:T(8,128)(2,1)} %bitcast.23), channel_id=1, source_target_pairs={{0,8},{8,0},{1,9},{9,1},{2,10},{10,2},{3,11},{11,3},{4,12},{12,4},... | collective-permute-start | bytes 7077896 | tf_op jit(solution)/shard_map/ppermute | solution.py:58
  168.1 2.7 %copy-start.2 = (bf16[512,1024]{1,0:T(8,128)(2,1)S(1)}, bf16[512,1024]{1,0:T(8,128)(2,1)}, u32[]{:S(2)}) copy-start(bf16[512,1024]{1,0:T(8,128)(2,1)} %param.14) | copy-start | bytes 3145732
  176.9 15.9 %collective-permute-start.9 = (f32[64,1792]{1,0:T(8,128)S(1)}, f32[64,1792]{1,0:T(8,128)S(1)}, u32[]{:S(2)}, u32[]{:S(2)}) collective-permute-start(f32[64,1792]{1,0:T(8,128)S(1)} %slice_select_fusion), channel_id=1, source_target_pairs={{0,4},{2,6},{4,0},{6,2},{1,5},{3,7},{5,1},{7,3},{8,12},{10,14},{12... | collective-permute-start | bytes 1376264 | tf_op jit(solution)/shard_map/ppermute | solution.py:89
  192.9 8.7 %collective-permute-start.10 = (f32[64,896]{1,0:T(8,128)S(1)}, f32[64,896]{1,0:T(8,128)S(1)}, u32[]{:S(2)}, u32[]{:S(2)}) collective-permute-start(f32[64,896]{1,0:T(8,128)S(1)} %slice_select_fusion.1), channel_id=1, source_target_pairs={{0,2},{2,0},{4,6},{6,4},{1,3},{3,1},{5,7},{7,5},{8,10},{10,8},{12,... | collective-permute-start | bytes 688136 | tf_op jit(solution)/shard_map/ppermute | solution.py:89
  201.8 8.4 %collective-permute-start.11 = (f32[64,448]{1,0:T(8,128)S(1)}, f32[64,448]{1,0:T(8,128)S(1)}, u32[]{:S(2)}, u32[]{:S(2)}) collective-permute-start(f32[64,448]{1,0:T(8,128)S(1)} %slice_select_fusion.2), channel_id=1, source_target_pairs={{0,1},{1,0},{2,3},{3,2},{4,5},{5,4},{6,7},{7,6},{8,9},{9,8},{10,11... | collective-permute-start | bytes 344072 | tf_op jit(solution)/shard_map/ppermute | solution.py:89
Sparse Core Ops, SparseCore 0:
  19.0 138.2 all-gather.1

commit v4 on v3

--- a/solution.py
+++ b/solution.py
@@ -136,11 +136,16 @@
     )
     latent_out = attend(query_rows, query_index, keys, token_count * ctx_count)
     head_out = upward(latent_out, value_up, token_count, head_count)
-    partial_sums = jnp.dot(
-        head_out,
-        lax.all_gather(chip_pair_columns(out_proj), ("zh", "zl"), axis=1, tiled=True),
-        preferred_element_type=jnp.float32,
+    own = lax.all_gather(out_proj, ("zh", "zl", "yl"), axis=1, tiled=True)
+    swapped = lax.ppermute(own, "co", [(0, 1), (1, 0)])
+    upper = lax.axis_index("co") == 1
+    halves = [jnp.where(upper, swapped, own), jnp.where(upper, own, swapped)]
+    partial_sums = jnp.stack(
+        [jnp.dot(head_out, half, preferred_element_type=jnp.float32) for half in halves], axis=1
     )
+    width = out_proj.shape[1]
+    partial_sums = partial_sums.reshape(token_count, 2, -1, width).transpose(0, 2, 1, 3)
+    partial_sums = partial_sums.reshape(token_count, -1)
     return scatter_sum(partial_sums, HEAD_SPLIT).astype(jnp.bfloat16)
 
 

time: 218 us -> 241 us (1.11)
  local copies, waits for them, and re-layouts: 4.05 us -> 13.2 us
  waiting for transfers between devices: 120 us -> 129 us
  other arithmetic: 14.4 us -> 22.2 us
  matrix products: 13.2 us -> 9.88 us
    ppermute x1, waiting for transfers between devices: 8.89 us -> 32.9 us  [exchange(): near = lax.ppermute(acc[:half], 'yl', pairs)]
    ppermute x7 -> x5, waiting for transfers between devices: 82.8 us -> 59.7 us  [exchange(): return lax.ppermute(acc, axis, pairs)]
    all_gather x1, waiting for transfers between devices: 0.02 us -> 13 us  [body(): own = lax.all_gather(out_proj, ('zh', 'zl', 'yl'), axis=1, tiled=True)]
    ppermute x7 -> x5, starting transfers between devices: 36.3 us -> 30.6 us  [exchange(): return lax.ppermute(acc, axis, pairs)]
    reshape x0 -> x2, local copies, waits for them, and re-layouts: none -> 4.34 us  [the longest x1 4.28 us: body(): partial_sums = partial_sums.reshape(token_count, -1)]
    ppermute x1, waiting for transfers between devices: 4.09 us -> 0.01 us  [exchange(): far = lax.ppermute(acc[half:], ('yl', 'yh'), [(i, i ^ 3) for i in range(4)])]
    transpose x0 -> x1, local copies, waits for them, and re-layouts: none -> 3.84 us  [body(): partial_sums.reshape(token_count, 2, -1, width).transpose(0, 2, 1, 3)]
    select_n x0 -> x1, other arithmetic: none -> 3.64 us  [body(): halves = [jnp.where(upper, swapped, own), jnp.where(upper, own, swapped)]]
  transfers between devices with their start and end apart: 13 -> 12, of which waited for: 12 -> 9; matrix products, arithmetic and copies ran while one was open for 11% -> 11% of each run, Pallas kernels for 0% -> 0%
where the time goes in v4:
time: 241 us; the launch traced here: 240 us
  waiting for transfers between devices  129 us (54%)
  starting transfers between devices  51.7 us (21%)
  other arithmetic  22.2 us (9%)
  between operations  14 us (6%)
  local copies, waits for them, and re-layouts  13.2 us (5%)
  matrix products  9.88 us (4%)
    ppermute x5, waiting for transfers between devices, exchange(): return lax.ppermute(acc, axis, pairs)  59.7 us
    ppermute x1, waiting for transfers between devices, exchange(): near = lax.ppermute(acc[:half], 'yl', pairs)  32.9 us
    ppermute x5, starting transfers between devices, exchange(): return lax.ppermute(acc, axis, pairs)  30.6 us
    ppermute x3, waiting for transfers between devices, scatter_sum(): acc = keep + lax.ppermute(send, axis, [(i, i ^ bit) for i in range(size)])  22.5 us
    all_gather x1, waiting for transfers between devices, body(): own = lax.all_gather(out_proj, ('zh', 'zl', 'yl'), axis=1, tiled=True)  13 us
    ppermute x3, starting transfers between devices, scatter_sum(): acc = keep + lax.ppermute(send, axis, [(i, i ^ bit) for i in range(size)])  11.3 us
    another operation x11, other arithmetic, gather_in_order(): acc = jnp.stack([first, second], axis=1).reshape((-1,) + local.shape)  6.94 us
    ppermute x1, starting transfers between devices, exchange(): far = lax.ppermute(acc[half:], ('yl', 'yh'), [(i, i ^ 3) for i in range(4)])  6.03 us
  transfers between devices with their start and end apart: 12, of which 9 were waited for; matrix products, arithmetic and copies ran while one was open for 11% of the time, Pallas kernels for 0%

profile of v4, /device:TPU:6, one launch (start us, length us, event | category | flops | bytes accessed | tf_op | source)
XLA Modules:
  0.0 239.9 jit_solution(12006451664658267755)
XLA Ops:
  9.9 15.7 %collective-permute-start = (bf16[1,64,576]{2,1,0:T(8,128)(2,1)S(1)}, bf16[1,64,576]{2,1,0:T(8,128)(2,1)S(1)}, u32[]{:S(2)}, u32[]{:S(2)}) collective-permute-start(bf16[1,64,576]{2,1,0:T(8,128)(2,1)S(1)} %maximum_bitcast_fusion.2), channel_id=1, source_target_pairs={{0,256},{64,320},{128,384},{192,448},{256,0},{320,64},{384,128},{4... | collective-permute-start | bytes 221192 | tf_op jit(solution)/shard_map/ppermute | solution.py:58
  25.6 2.7 %collective-permute-done = bf16[1,64,576]{2,1,0:T(8,128)(2,1)S(1)} collective-permute-done((bf16[1,64,576]{2,1,0:T(8,128)(2,1)S(1)}, bf16[1,64,576]{2,1,0:T(8,128)(2,1)S(1)}, u32[]{:S(2)}, u32[]{:S(2)}) %collective-permute-start) | collective-permute-done | bytes 73760 | tf_op jit(solution)/shard_map/ppermute | solution.py:58
  29.2 9.1 %collective-permute-start.1 = (bf16[2,64,576]{2,1,0:T(8,128)(2,1)S(1)}, bf16[2,64,576]{2,1,0:T(8,128)(2,1)S(1)}, u32[]{:S(2)}, u32[]{:S(2)}) collective-permute-start(bf16[2,64,576]{2,1,0:T(8,128)(2,1)S(1)} %maximum_bitcast_fusion.1), channel_id=1, source_target_pairs={{0,128},{64,192},{128,0},{192,64},{256,384},{320,448},{384,256},{4... | collective-permute-start | bytes 442376 | tf_op jit(solution)/shard_map/ppermute | solution.py:58
  38.4 16.3 %collective-permute-done.1 = bf16[2,64,576]{2,1,0:T(8,128)(2,1)S(1)} collective-permute-done((bf16[2,64,576]{2,1,0:T(8,128)(2,1)S(1)}, bf16[2,64,576]{2,1,0:T(8,128)(2,1)S(1)}, u32[]{:S(2)}, u32[]{:S(2)}) %collective-permute-start.1) | collective-permute-done | bytes 147488 | tf_op jit(solution)/shard_map/ppermute | solution.py:58
  56.8 17.8 %collective-permute-done.2 = bf16[4,64,576]{2,1,0:T(8,128)(2,1)S(1)} collective-permute-done((bf16[4,64,576]{2,1,0:T(8,128)(2,1)S(1)}, bf16[4,64,576]{2,1,0:T(8,128)(2,1)S(1)}, u32[]{:S(2)}, u32[]{:S(2)}) %collective-permute-start.2) | collective-permute-done | bytes 294944 | tf_op jit(solution)/shard_map/ppermute | solution.py:58
  74.8 1.9 collective-permute-start.3
  76.8 22.9 %collective-permute-done.3 = bf16[8,64,576]{2,1,0:T(8,128)(2,1)} collective-permute-done((bf16[8,64,576]{2,1,0:T(8,128)(2,1)S(1)}, bf16[8,64,576]{2,1,0:T(8,128)(2,1)}, u32[]{:S(2)}, u32[]{:S(2)}) %collective-permute-start.3) | collective-permute-done | bytes 589856 | tf_op jit(solution)/shard_map/ppermute | solution.py:58
  101.2 1.9 collective-permute-start.4
  104.0 6.0 %collective-permute-start.5 = (bf16[8,64,576]{2,1,0:T(8,128)(2,1)}, bf16[8,64,576]{2,1,0:T(8,128)(2,1)}, u32[]{:S(2)}, u32[]{:S(2)}) collective-permute-start(bf16[8,64,576]{2,1,0:T(8,128)(2,1)} %bitcast.20), channel_id=1, source_target_pairs={{0,17},{1,16},{16,1},{17,0},{2,19},{3,18},{18,3},{19,2},{4,21},{5,... | collective-permute-start | bytes 1769480 | tf_op jit(solution)/shard_map/ppermute | solution.py:61
  110.4 32.9 %collective-permute-done.4 = bf16[8,64,576]{2,1,0:T(8,128)(2,1)} collective-permute-done((bf16[8,64,576]{2,1,0:T(8,128)(2,1)S(1)}, bf16[8,64,576]{2,1,0:T(8,128)(2,1)}, u32[]{:S(2)}, u32[]{:S(2)}) %collective-permute-start.4) | collective-permute-done | bytes 589856 | tf_op jit(solution)/shard_map/ppermute | solution.py:60
  150.7 13.0 %all-gather.2.cloned.1.call-done = bf16[1024,1792]{0,1:T(8,128)(2,1)} async-done(((bf16[1024,56]{0,1:T(8,128)(2,1)}), bf16[1024,1792]{0,1:T(8,128)(2,1)}) %all-gather.2.cloned.1.call-update) | async-done | bytes 3670032 | tf_op jit(solution)/shard_map/all_gather | solution.py:139
  165.7 3.0 %select_bitcast_fusion.1 = (bf16[32,1,64,576]{3,2,0,1:T(8,128)(2,1)S(1)}, bf16[32,1,64,576]{3,2,0,1:T(8,128)(2,1)S(1)}) fusion(bf16[32,64,576]{2,1,0:T(8,128)(2,1)} %collective-permute-done.6, pred[]{:T(512)S(6)} %eq.43, bf16[16,2,64,576]{3,2,1,0:T(8,128)(2,1)} %copy.82), kind=kLoop, calls=%fused_computation.17 | loop fusion | flops 2359296 | bytes 9437185 | tf_op jit(solution)/shard_map/stack | solution.py:74
  170.1 4.0 %fusion = (f32[512]{0:T(512)S(1)}, f32[512,4096]{1,0:T(8,128)S(1)}) fusion(s32[512]{0:T(512)S(1)} %le.16, bf16[4096,576]{1,0:T(8,128)(2,1)S(1)} %bitcast.107, bf16[64,8,576]{2,0,1:T(8,128)(2,1)S(1)} %pad_maximum_fusion.4), kind=kOutput, calls=%fused_computation.3 | convolution fusion | flops 2424307200 | bytes 13701120 | tf_op jit(solution)/shard_map/rl,kl->rk/dot_general | solution.py:42
  174.1 3.0 %fusion.1 = f32[512]{0:T(512)S(1)} fusion(f32[512,4096]{1,0:T(8,128)S(1)} %get-tuple-element.30, f32[512]{0:T(512)S(1)} %get-tuple-element.29, s32[512]{0:T(512)S(1)} %le.16), kind=kLoop, calls=%fused_computation.5 | loop fusion | flops 12582400 | bytes 8394752 | tf_op jit(solution)/shard_map/reduce_sum | solution.py:48
  177.2 2.5 %fusion.20 = bf16[64,8,512]{2,1,0:T(8,128)(2,1)S(1)} fusion(bf16[4096,576]{1,0:T(8,128)(2,1)S(1)} %bitcast.108, f32[512,4096]{1,0:T(8,128)S(1)} %get-tuple-element.30, f32[512]{0:T(512)S(1)} %get-tuple-element.29, s32[512]{0:T(512)S(1)} %le.16, f32[512]{0:T(512)S(1)} %fusion.1), kind=kOutput, calls=%fused_computation.38 | convolution fusion | flops 2160590848 | bytes 13113344 | tf_op jit(solution)/shard_map/dot_general | solution.py:49
  180.3 3.6 %broadcast_select_fusion.1 = (bf16[1024,1792]{0,1:T(8,128)(2,1)S(1)}, bf16[1024,1792]{0,1:T(8,128)(2,1)S(1)}) fusion(bf16[1024,1792]{0,1:T(8,128)(2,1)} %collective-permute-done.7, bf16[1024,1792]{0,1:T(8,128)(2,1)} %all-gather.2.cloned.1.call-done, pred[]{:T(512)S(6)} %eq.49), kind=kLoop, calls=%fused_computation.14 | loop fusion | flops 3670016 | bytes 14680065 | tf_op jit(solution)/shard_map/jit(_where)/select_n | solution.py:142
  187.7 3.8 %copy.87 = f32[64,32,2,56]{3,2,1,0:T(2,128)S(1)} copy(f32[64,32,2,56]{0,3,1,2:T(8,128)} %maximum_bitcast_fusion) | data formatting | bytes 1835008 | tf_op jit(solution)/shard_map/transpose | solution.py:147
  191.6 4.3 %reshape.248 = f32[64,3584]{1,0:T(8,128)} reshape(f32[64,32,2,56]{3,2,1,0:T(2,128)S(1)} %copy.87) | data formatting | bytes 1835008 | tf_op jit(solution)/shard_map/reshape | solution.py:148
  197.1 3.5 %collective-permute-start.8 = (f32[64,1792]{1,0:T(8,128)S(1)}, f32[64,1792]{1,0:T(8,128)S(1)}, u32[]{:S(2)}, u32[]{:S(2)}) collective-permute-start(f32[64,1792]{1,0:T(8,128)S(1)} %slice_select_fusion), channel_id=1, source_target_pairs={{0,4},{2,6},{4,0},{6,2},{1,5},{3,7},{5,1},{7,3},{8,12},{10,14},{12... | collective-permute-start | bytes 1376264 | tf_op jit(solution)/shard_map/ppermute | solution.py:89
  200.6 12.8 %collective-permute-done.8 = f32[64,1792]{1,0:T(8,128)S(1)} collective-permute-done((f32[64,1792]{1,0:T(8,128)S(1)}, f32[64,1792]{1,0:T(8,128)S(1)}, u32[]{:S(2)}, u32[]{:S(2)}) %collective-permute-start.8) | collective-permute-done | bytes 458784 | tf_op jit(solution)/shard_map/ppermute | solution.py:89
  214.7 2.8 %collective-permute-start.9 = (f32[64,896]{1,0:T(8,128)S(1)}, f32[64,896]{1,0:T(8,128)S(1)}, u32[]{:S(2)}, u32[]{:S(2)}) collective-permute-start(f32[64,896]{1,0:T(8,128)S(1)} %slice_select_fusion.1), channel_id=1, source_target_pairs={{0,2},{2,0},{4,6},{6,4},{1,3},{3,1},{5,7},{7,5},{8,10},{10,8},{12,... | collective-permute-start | bytes 688136 | tf_op jit(solution)/shard_map/ppermute | solution.py:89
  217.5 6.3 %collective-permute-done.9 = f32[64,896]{1,0:T(8,128)S(1)} collective-permute-done((f32[64,896]{1,0:T(8,128)S(1)}, f32[64,896]{1,0:T(8,128)S(1)}, u32[]{:S(2)}, u32[]{:S(2)}) %collective-permute-start.9) | collective-permute-done | bytes 229408 | tf_op jit(solution)/shard_map/ppermute | solution.py:89
  223.9 4.9 %collective-permute-start.10 = (f32[64,448]{1,0:T(8,128)S(1)}, f32[64,448]{1,0:T(8,128)S(1)}, u32[]{:S(2)}, u32[]{:S(2)}) collective-permute-start(f32[64,448]{1,0:T(8,128)S(1)} %slice_select_fusion.2), channel_id=1, source_target_pairs={{0,1},{1,0},{2,3},{3,2},{4,5},{5,4},{6,7},{7,6},{8,9},{9,8},{10,11... | collective-permute-start | bytes 344072 | tf_op jit(solution)/shard_map/ppermute | solution.py:89
  228.9 3.4 %collective-permute-done.10 = f32[64,448]{1,0:T(8,128)S(1)} collective-permute-done((f32[64,448]{1,0:T(8,128)S(1)}, f32[64,448]{1,0:T(8,128)S(1)}, u32[]{:S(2)}, u32[]{:S(2)}) %collective-permute-start.10) | collective-permute-done | bytes 114720 | tf_op jit(solution)/shard_map/ppermute | solution.py:89
  (65 shorter events, 27.4 us)
Async XLA Ops:
  6.5 143.5 %copy-start = (bf16[512,1024]{1,0:T(8,128)(2,1)S(1)}, bf16[512,1024]{1,0:T(8,128)(2,1)}, u32[]{:S(2)}) copy-start(bf16[512,1024]{1,0:T(8,128)(2,1)} %param.13) | copy-start | bytes 3145732
  6.5 157.2 %all-gather.2.cloned.1.call-start = ((), (), s32[]{:S(2)}) async-start(), calls=%async_computation | async-start | bytes 3784704 | tf_op jit(solution)/shard_map/all_gather | solution.py:139
  9.9 18.4 %collective-permute-start = (bf16[1,64,576]{2,1,0:T(8,128)(2,1)S(1)}, bf16[1,64,576]{2,1,0:T(8,128)(2,1)S(1)}, u32[]{:S(2)}, u32[]{:S(2)}) collective-permute-start(bf16[1,64,576]{2,1,0:T(8,128)(2,1)S(1)} %maximum_bitcast_fusion.2), channel_id=1, source_target_pairs={{0,256},{64,320},{128,384},{192,448},{256,0},{320,64},{384,128},{4... | collective-permute-start | bytes 221192 | tf_op jit(solution)/shard_map/ppermute | solution.py:58
  29.2 25.5 %collective-permute-start.1 = (bf16[2,64,576]{2,1,0:T(8,128)(2,1)S(1)}, bf16[2,64,576]{2,1,0:T(8,128)(2,1)S(1)}, u32[]{:S(2)}, u32[]{:S(2)}) collective-permute-start(bf16[2,64,576]{2,1,0:T(8,128)(2,1)S(1)} %maximum_bitcast_fusion.1), channel_id=1, source_target_pairs={{0,128},{64,192},{128,0},{192,64},{256,384},{320,448},{384,256},{4... | collective-permute-start | bytes 442376 | tf_op jit(solution)/shard_map/ppermute | solution.py:58
  54.8 19.7 %collective-permute-start.2 = (bf16[4,64,576]{2,1,0:T(8,128)(2,1)S(1)}, bf16[4,64,576]{2,1,0:T(8,128)(2,1)S(1)}, u32[]{:S(2)}, u32[]{:S(2)}) collective-permute-start(bf16[4,64,576]{2,1,0:T(8,128)(2,1)S(1)} %bitcast.110), channel_id=1, source_target_pairs={{0,64},{64,0},{128,192},{192,128},{256,320},{320,256},{384,448},{4... | collective-permute-start | bytes 884744 | tf_op jit(solution)/shard_map/ppermute | solution.py:58
  74.8 24.8 %collective-permute-start.3 = (bf16[8,64,576]{2,1,0:T(8,128)(2,1)S(1)}, bf16[8,64,576]{2,1,0:T(8,128)(2,1)}, u32[]{:S(2)}, u32[]{:S(2)}) collective-permute-start(bf16[8,64,576]{2,1,0:T(8,128)(2,1)S(1)} %bitcast.109), channel_id=1, source_target_pairs={{0,32},{32,0},{1,33},{33,1},{2,34},{34,2},{3,35},{35,3},{4,36},{36... | collective-permute-start | bytes 1769480 | tf_op jit(solution)/shard_map/ppermute | solution.py:58
  101.2 42.2 %collective-permute-start.4 = (bf16[8,64,576]{2,1,0:T(8,128)(2,1)S(1)}, bf16[8,64,576]{2,1,0:T(8,128)(2,1)}, u32[]{:S(2)}, u32[]{:S(2)}) collective-permute-start(bf16[8,64,576]{2,1,0:T(8,128)(2,1)S(1)} %bitcast.111), channel_id=1, source_target_pairs={{0,16},{16,0},{1,17},{17,1},{2,18},{18,2},{3,19},{19,3},{4,20},{20... | collective-permute-start | bytes 1769480 | tf_op jit(solution)/shard_map/ppermute | solution.py:60
  104.0 39.3 %collective-permute-start.5 = (bf16[8,64,576]{2,1,0:T(8,128)(2,1)}, bf16[8,64,576]{2,1,0:T(8,128)(2,1)}, u32[]{:S(2)}, u32[]{:S(2)}) collective-permute-start(bf16[8,64,576]{2,1,0:T(8,128)(2,1)} %bitcast.20), channel_id=1, source_target_pairs={{0,17},{1,16},{16,1},{17,0},{2,19},{3,18},{18,3},{19,2},{4,21},{5,... | collective-permute-start | bytes 1769480 | tf_op jit(solution)/shard_map/ppermute | solution.py:61
  145.5 4.0 %copy-start.2 = (bf16[64,512]{1,0:T(8,128)(2,1)S(1)}, bf16[64,512]{1,0:T(8,128)(2,1)}, u32[]{:S(2)}) copy-start(bf16[64,512]{1,0:T(8,128)(2,1)} %param.9) | copy-start | bytes 196612
  145.5 4.6 %copy-start.4 = (bf16[64,1024]{1,0:T(8,128)(2,1)S(1)}, bf16[64,1024]{1,0:T(8,128)(2,1)}, u32[]{:S(2)}) copy-start(bf16[64,1024]{1,0:T(8,128)(2,1)} %param.8) | copy-start | bytes 393220
  147.3 18.3 %collective-permute-start.6 = (bf16[32,64,576]{2,1,0:T(8,128)(2,1)}, bf16[32,64,576]{2,1,0:T(8,128)(2,1)}, u32[]{:S(2)}, u32[]{:S(2)}) collective-permute-start(bf16[32,64,576]{2,1,0:T(8,128)(2,1)} %bitcast.23), channel_id=1, source_target_pairs={{0,8},{8,0},{1,9},{9,1},{2,10},{10,2},{3,11},{11,3},{4,12},{12,4},... | collective-permute-start | bytes 7077896 | tf_op jit(solution)/shard_map/ppermute | solution.py:58
  163.7 16.6 %collective-permute-start.7 = (bf16[1024,1792]{0,1:T(8,128)(2,1)}, bf16[1024,1792]{0,1:T(8,128)(2,1)}, u32[]{:S(2)}, u32[]{:S(2)}) collective-permute-start(bf16[1024,1792]{0,1:T(8,128)(2,1)} %all-gather.2.cloned.1.call-done), channel_id=1, source_target_pairs={{0,8},{8,0},{1,9},{9,1},{2,10},{10,2},{3,11},{11,3},{4,12},{12,4},... | collective-permute-start | bytes 11010056 | tf_op jit(solution)/shard_map/ppermute | solution.py:140
  177.1 2.5 %copy-start.3 = (bf16[512,1024]{1,0:T(8,128)(2,1)S(1)}, bf16[512,1024]{1,0:T(8,128)(2,1)}, u32[]{:S(2)}) copy-start(bf16[512,1024]{1,0:T(8,128)(2,1)} %param.14) | copy-start | bytes 3145732
  187.7 45.3 %copy-start.1 = (bf16[512,1024]{1,0:T(8,128)(2,1)S(1)}, bf16[512,1024]{1,0:T(8,128)(2,1)}, u32[]{:S(2)}) copy-start(bf16[512,1024]{1,0:T(8,128)(2,1)} %param.13) | copy-start | bytes 3145732
  197.1 16.3 %collective-permute-start.8 = (f32[64,1792]{1,0:T(8,128)S(1)}, f32[64,1792]{1,0:T(8,128)S(1)}, u32[]{:S(2)}, u32[]{:S(2)}) collective-permute-start(f32[64,1792]{1,0:T(8,128)S(1)} %slice_select_fusion), channel_id=1, source_target_pairs={{0,4},{2,6},{4,0},{6,2},{1,5},{3,7},{5,1},{7,3},{8,12},{10,14},{12... | collective-permute-start | bytes 1376264 | tf_op jit(solution)/shard_map/ppermute | solution.py:89
  214.7 9.1 %collective-permute-start.9 = (f32[64,896]{1,0:T(8,128)S(1)}, f32[64,896]{1,0:T(8,128)S(1)}, u32[]{:S(2)}, u32[]{:S(2)}) collective-permute-start(f32[64,896]{1,0:T(8,128)S(1)} %slice_select_fusion.1), channel_id=1, source_target_pairs={{0,2},{2,0},{4,6},{6,4},{1,3},{3,1},{5,7},{7,5},{8,10},{10,8},{12,... | collective-permute-start | bytes 688136 | tf_op jit(solution)/shard_map/ppermute | solution.py:89
  223.9 8.4 %collective-permute-start.10 = (f32[64,448]{1,0:T(8,128)S(1)}, f32[64,448]{1,0:T(8,128)S(1)}, u32[]{:S(2)}, u32[]{:S(2)}) collective-permute-start(f32[64,448]{1,0:T(8,128)S(1)} %slice_select_fusion.2), channel_id=1, source_target_pairs={{0,1},{1,0},{2,3},{3,2},{4,5},{5,4},{6,7},{7,6},{8,9},{9,8},{10,11... | collective-permute-start | bytes 344072 | tf_op jit(solution)/shard_map/ppermute | solution.py:89
Sparse Core Ops, SparseCore 0:
  9.4 154.2 all-gather.1

commit v5 on v4

--- a/solution.py
+++ b/solution.py
@@ -91,13 +91,6 @@
     return acc
 
 
-def chip_pair_columns(out_proj):
-    blocks = gather_in_order(out_proj.T, (("yl", 2), ("co", 2)), False)
-    return blocks.reshape(-1, out_proj.shape[1], out_proj.shape[0]).transpose(2, 0, 1).reshape(
-        out_proj.shape[0], -1
-    )
-
-
 def upward(latent_out, value_up, token_count, head_count):
     head_out = jnp.einsum(
         "thl,lhd->thd",
@@ -136,7 +129,9 @@
     )
     latent_out = attend(query_rows, query_index, keys, token_count * ctx_count)
     head_out = upward(latent_out, value_up, token_count, head_count)
-    own = lax.all_gather(out_proj, ("zh", "zl", "yl"), axis=1, tiled=True)
+    pair = gather_in_order(out_proj.T, (("yl", 2),), False)
+    pair = pair.reshape(2, out_proj.shape[1], -1).transpose(2, 0, 1).reshape(out_proj.shape[0], -1)
+    own = lax.all_gather(pair, ("zh", "zl"), axis=1, tiled=True)
     swapped = lax.ppermute(own, "co", [(0, 1), (1, 0)])
     upper = lax.axis_index("co") == 1
     halves = [jnp.where(upper, swapped, own), jnp.where(upper, own, swapped)]

time: 241 us -> 225 us (0.934)
  waiting for transfers between devices: 129 us -> 115 us
    ppermute x1, waiting for transfers between devices: 32.9 us -> 7.39 us  [exchange(): near = lax.ppermute(acc[:half], 'yl', pairs)]
    ppermute x5 -> x6, waiting for transfers between devices: 59.7 us -> 79.5 us  [exchange(): return lax.ppermute(acc, axis, pairs)]
    all_gather x1, waiting for transfers between devices: 13 us -> 0.02 us  [body(): own = lax.all_gather(pair, ('zh', 'zl'), axis=1, tiled=True)]
    ppermute x1, waiting for transfers between devices: 0.01 us -> 4.65 us  [exchange(): far = lax.ppermute(acc[half:], ('yl', 'yh'), [(i, i ^ 3) for i in range(4)])]
    ppermute x5 -> x6, starting transfers between devices: 30.6 us -> 31.4 us  [exchange(): return lax.ppermute(acc, axis, pairs)]
    another operation x11 -> x13, other arithmetic: 6.94 us -> 7.53 us  [gather_in_order(): acc = jnp.stack([first, second], axis=1).reshape((-1,) + local.shape)]
  transfers between devices with their start and end apart: 12 -> 13, of which waited for: 9 -> 11; matrix products, arithmetic and copies ran while one was open for 11% -> 10% of each run, Pallas kernels for 0% -> 0%
where the time goes in v5:
time: 225 us; the launch traced here: 224 us
  waiting for transfers between devices  115 us (51%)
  starting transfers between devices  51.5 us (23%)
  other arithmetic  21.5 us (10%)
  between operations  14 us (6%)
  local copies, waits for them, and re-layouts  12.4 us (6%)
  matrix products  9.88 us (4%)
    ppermute x6, waiting for transfers between devices, exchange(): return lax.ppermute(acc, axis, pairs)  79.5 us
    ppermute x6, starting transfers between devices, exchange(): return lax.ppermute(acc, axis, pairs)  31.4 us
    ppermute x3, waiting for transfers between devices, scatter_sum(): acc = keep + lax.ppermute(send, axis, [(i, i ^ bit) for i in range(size)])  23.2 us
    ppermute x3, starting transfers between devices, scatter_sum(): acc = keep + lax.ppermute(send, axis, [(i, i ^ bit) for i in range(size)])  9.76 us
    another operation x13, other arithmetic, gather_in_order(): acc = jnp.stack([first, second], axis=1).reshape((-1,) + local.shape)  7.53 us
    ppermute x1, waiting for transfers between devices, exchange(): near = lax.ppermute(acc[:half], 'yl', pairs)  7.39 us
    ppermute x1, waiting for transfers between devices, exchange(): far = lax.ppermute(acc[half:], ('yl', 'yh'), [(i, i ^ 3) for i in range(4)])  4.65 us
  transfers between devices with their start and end apart: 13, of which 11 were waited for; matrix products, arithmetic and copies ran while one was open for 10% of the time, Pallas kernels for 0%

profile of v5, /device:TPU:6, one launch (start us, length us, event | category | flops | bytes accessed | tf_op | source)
XLA Modules:
  0.0 224.0 jit_solution(3224935721370552175)
XLA Ops:
  6.5 3.6 %collective-permute-start.7 = (bf16[1,56,1024]{2,1,0:T(8,128)(2,1)}, bf16[1,56,1024]{2,1,0:T(8,128)(2,1)S(1)}, u32[]{:S(2)}, u32[]{:S(2)}) collective-permute-start(bf16[1,56,1024]{2,1,0:T(8,128)(2,1)} %bitcast.130), channel_id=1, source_target_pairs={{0,16},{16,0},{1,17},{17,1},{2,18},{18,2},{3,19},{19,3},{4,20},{20... | collective-permute-start | bytes 344072 | tf_op jit(solution)/shard_map/ppermute | solution.py:58
  10.2 3.5 %collective-permute-done.7 = bf16[1,56,1024]{2,1,0:T(8,128)(2,1)S(1)} collective-permute-done((bf16[1,56,1024]{2,1,0:T(8,128)(2,1)}, bf16[1,56,1024]{2,1,0:T(8,128)(2,1)S(1)}, u32[]{:S(2)}, u32[]{:S(2)}) %collective-permute-start.7) | collective-permute-done | bytes 114720 | tf_op jit(solution)/shard_map/ppermute | solution.py:58
  17.9 15.7 %collective-permute-start = (bf16[1,64,576]{2,1,0:T(8,128)(2,1)S(1)}, bf16[1,64,576]{2,1,0:T(8,128)(2,1)S(1)}, u32[]{:S(2)}, u32[]{:S(2)}) collective-permute-start(bf16[1,64,576]{2,1,0:T(8,128)(2,1)S(1)} %maximum_bitcast_fusion.2), channel_id=1, source_target_pairs={{0,256},{64,320},{128,384},{192,448},{256,0},{320,64},{384,128},{4... | collective-permute-start | bytes 221192 | tf_op jit(solution)/shard_map/ppermute | solution.py:58
  33.7 4.6 %collective-permute-done = bf16[1,64,576]{2,1,0:T(8,128)(2,1)S(1)} collective-permute-done((bf16[1,64,576]{2,1,0:T(8,128)(2,1)S(1)}, bf16[1,64,576]{2,1,0:T(8,128)(2,1)S(1)}, u32[]{:S(2)}, u32[]{:S(2)}) %collective-permute-start) | collective-permute-done | bytes 73760 | tf_op jit(solution)/shard_map/ppermute | solution.py:58
  39.2 6.3 %collective-permute-start.1 = (bf16[2,64,576]{2,1,0:T(8,128)(2,1)S(1)}, bf16[2,64,576]{2,1,0:T(8,128)(2,1)S(1)}, u32[]{:S(2)}, u32[]{:S(2)}) collective-permute-start(bf16[2,64,576]{2,1,0:T(8,128)(2,1)S(1)} %maximum_bitcast_fusion.1), channel_id=1, source_target_pairs={{0,128},{64,192},{128,0},{192,64},{256,384},{320,448},{384,256},{4... | collective-permute-start | bytes 442376 | tf_op jit(solution)/shard_map/ppermute | solution.py:58
  45.6 17.3 %collective-permute-done.1 = bf16[2,64,576]{2,1,0:T(8,128)(2,1)S(1)} collective-permute-done((bf16[2,64,576]{2,1,0:T(8,128)(2,1)S(1)}, bf16[2,64,576]{2,1,0:T(8,128)(2,1)S(1)}, u32[]{:S(2)}, u32[]{:S(2)}) %collective-permute-start.1) | collective-permute-done | bytes 147488 | tf_op jit(solution)/shard_map/ppermute | solution.py:58
  64.9 22.6 %collective-permute-done.2 = bf16[4,64,576]{2,1,0:T(8,128)(2,1)S(1)} collective-permute-done((bf16[4,64,576]{2,1,0:T(8,128)(2,1)S(1)}, bf16[4,64,576]{2,1,0:T(8,128)(2,1)S(1)}, u32[]{:S(2)}, u32[]{:S(2)}) %collective-permute-start.2) | collective-permute-done | bytes 294944 | tf_op jit(solution)/shard_map/ppermute | solution.py:58
  89.7 30.2 %collective-permute-done.3 = bf16[8,64,576]{2,1,0:T(8,128)(2,1)S(1)} collective-permute-done((bf16[8,64,576]{2,1,0:T(8,128)(2,1)S(1)}, bf16[8,64,576]{2,1,0:T(8,128)(2,1)S(1)}, u32[]{:S(2)}, u32[]{:S(2)}) %collective-permute-start.3) | collective-permute-done | bytes 589856 | tf_op jit(solution)/shard_map/ppermute | solution.py:58
  120.3 3.7 %collective-permute-start.4 = (bf16[8,64,576]{2,1,0:T(8,128)(2,1)S(1)}, bf16[8,64,576]{2,1,0:T(8,128)(2,1)S(1)}, u32[]{:S(2)}, u32[]{:S(2)}) collective-permute-start(bf16[8,64,576]{2,1,0:T(8,128)(2,1)S(1)} %bitcast.126), channel_id=1, source_target_pairs={{0,16},{16,0},{1,17},{17,1},{2,18},{18,2},{3,19},{19,3},{4,20},{20... | collective-permute-start | bytes 1769480 | tf_op jit(solution)/shard_map/ppermute | solution.py:60
  124.1 4.2 %collective-permute-start.5 = (bf16[8,64,576]{2,1,0:T(8,128)(2,1)S(1)}, bf16[8,64,576]{2,1,0:T(8,128)(2,1)S(1)}, u32[]{:S(2)}, u32[]{:S(2)}) collective-permute-start(bf16[8,64,576]{2,1,0:T(8,128)(2,1)S(1)} %bitcast.127), channel_id=1, source_target_pairs={{0,17},{1,16},{16,1},{17,0},{2,19},{3,18},{18,3},{19,2},{4,21},{5,... | collective-permute-start | bytes 1769480 | tf_op jit(solution)/shard_map/ppermute | solution.py:61
  128.7 7.4 %collective-permute-done.4 = bf16[8,64,576]{2,1,0:T(8,128)(2,1)S(1)} collective-permute-done((bf16[8,64,576]{2,1,0:T(8,128)(2,1)S(1)}, bf16[8,64,576]{2,1,0:T(8,128)(2,1)S(1)}, u32[]{:S(2)}, u32[]{:S(2)}) %collective-permute-start.4) | collective-permute-done | bytes 589856 | tf_op jit(solution)/shard_map/ppermute | solution.py:60
  136.1 4.6 %collective-permute-done.5 = bf16[8,64,576]{2,1,0:T(8,128)(2,1)S(1)} collective-permute-done((bf16[8,64,576]{2,1,0:T(8,128)(2,1)S(1)}, bf16[8,64,576]{2,1,0:T(8,128)(2,1)S(1)}, u32[]{:S(2)}, u32[]{:S(2)}) %collective-permute-start.5) | collective-permute-done | bytes 589856 | tf_op jit(solution)/shard_map/ppermute | solution.py:61
  150.6 3.0 %select_bitcast_fusion.1 = (bf16[32,1,64,576]{3,2,0,1:T(8,128)(2,1)S(1)}, bf16[32,1,64,576]{3,2,0,1:T(8,128)(2,1)S(1)}) fusion(bf16[32,64,576]{2,1,0:T(8,128)(2,1)} %collective-permute-done.6, pred[]{:T(512)S(6)} %eq.45, bf16[16,2,64,576]{3,2,1,0:T(8,128)(2,1)} %copy.82), kind=kLoop, calls=%fused_computation.17 | loop fusion | flops 2359296 | bytes 9437185 | tf_op jit(solution)/shard_map/stack | solution.py:74
  155.0 4.0 %fusion = (f32[512]{0:T(512)S(1)}, f32[512,4096]{1,0:T(8,128)S(1)}) fusion(s32[512]{0:T(512)S(1)} %le.16, bf16[4096,576]{1,0:T(8,128)(2,1)S(1)} %bitcast.121, bf16[64,8,576]{2,0,1:T(8,128)(2,1)S(1)} %pad_maximum_fusion.4), kind=kOutput, calls=%fused_computation.3 | convolution fusion | flops 2424307200 | bytes 13701120 | tf_op jit(solution)/shard_map/rl,kl->rk/dot_general | solution.py:42
  159.0 3.0 %fusion.1 = f32[512]{0:T(512)S(1)} fusion(f32[512,4096]{1,0:T(8,128)S(1)} %get-tuple-element.32, f32[512]{0:T(512)S(1)} %get-tuple-element.31, s32[512]{0:T(512)S(1)} %le.16), kind=kLoop, calls=%fused_computation.5 | loop fusion | flops 12582400 | bytes 8394752 | tf_op jit(solution)/shard_map/reduce_sum | solution.py:48
  165.2 3.6 %broadcast_select_fusion.1 = (bf16[1024,1792]{0,1:T(8,128)(2,1)S(1)}, bf16[1024,1792]{0,1:T(8,128)(2,1)S(1)}) fusion(bf16[1024,1792]{0,1:T(8,128)(2,1)} %collective-permute-done.8, bf16[1024,1792]{0,1:T(8,128)(2,1)} %all-gather.2.cloned.1.call-done, pred[]{:T(512)S(6)} %eq.51), kind=kLoop, calls=%fused_computation.14 | loop fusion | flops 3670016 | bytes 14680065 | tf_op jit(solution)/shard_map/jit(_where)/select_n | solution.py:137
  172.6 3.8 %copy.87 = f32[64,32,2,56]{3,2,1,0:T(2,128)S(1)} copy(f32[64,32,2,56]{0,3,1,2:T(8,128)} %maximum_bitcast_fusion) | data formatting | bytes 1835008 | tf_op jit(solution)/shard_map/transpose | solution.py:142
  176.5 4.3 %reshape.252 = f32[64,3584]{1,0:T(8,128)} reshape(f32[64,32,2,56]{3,2,1,0:T(2,128)S(1)} %copy.87) | data formatting | bytes 1835008 | tf_op jit(solution)/shard_map/reshape | solution.py:143
  182.0 3.1 %collective-permute-start.9 = (f32[64,1792]{1,0:T(8,128)S(1)}, f32[64,1792]{1,0:T(8,128)S(1)}, u32[]{:S(2)}, u32[]{:S(2)}) collective-permute-start(f32[64,1792]{1,0:T(8,128)S(1)} %slice_select_fusion), channel_id=1, source_target_pairs={{0,4},{2,6},{4,0},{6,2},{1,5},{3,7},{5,1},{7,3},{8,12},{10,14},{12... | collective-permute-start | bytes 1376264 | tf_op jit(solution)/shard_map/ppermute | solution.py:89
  185.1 12.9 %collective-permute-done.9 = f32[64,1792]{1,0:T(8,128)S(1)} collective-permute-done((f32[64,1792]{1,0:T(8,128)S(1)}, f32[64,1792]{1,0:T(8,128)S(1)}, u32[]{:S(2)}, u32[]{:S(2)}) %collective-permute-start.9) | collective-permute-done | bytes 458784 | tf_op jit(solution)/shard_map/ppermute | solution.py:89
  199.2 2.7 %collective-permute-start.10 = (f32[64,896]{1,0:T(8,128)S(1)}, f32[64,896]{1,0:T(8,128)S(1)}, u32[]{:S(2)}, u32[]{:S(2)}) collective-permute-start(f32[64,896]{1,0:T(8,128)S(1)} %slice_select_fusion.1), channel_id=1, source_target_pairs={{0,2},{2,0},{4,6},{6,4},{1,3},{3,1},{5,7},{7,5},{8,10},{10,8},{12,... | collective-permute-start | bytes 688136 | tf_op jit(solution)/shard_map/ppermute | solution.py:89
  201.9 6.0 %collective-permute-done.10 = f32[64,896]{1,0:T(8,128)S(1)} collective-permute-done((f32[64,896]{1,0:T(8,128)S(1)}, f32[64,896]{1,0:T(8,128)S(1)}, u32[]{:S(2)}, u32[]{:S(2)}) %collective-permute-start.10) | collective-permute-done | bytes 229408 | tf_op jit(solution)/shard_map/ppermute | solution.py:89
  208.1 4.0 %collective-permute-start.11 = (f32[64,448]{1,0:T(8,128)S(1)}, f32[64,448]{1,0:T(8,128)S(1)}, u32[]{:S(2)}, u32[]{:S(2)}) collective-permute-start(f32[64,448]{1,0:T(8,128)S(1)} %slice_select_fusion.2), channel_id=1, source_target_pairs={{0,1},{1,0},{2,3},{3,2},{4,5},{5,4},{6,7},{7,6},{8,9},{9,8},{10,11... | collective-permute-start | bytes 344072 | tf_op jit(solution)/shard_map/ppermute | solution.py:89
  212.1 4.4 %collective-permute-done.11 = f32[64,448]{1,0:T(8,128)S(1)} collective-permute-done((f32[64,448]{1,0:T(8,128)S(1)}, f32[64,448]{1,0:T(8,128)S(1)}, u32[]{:S(2)}, u32[]{:S(2)}) %collective-permute-start.11) | collective-permute-done | bytes 114720 | tf_op jit(solution)/shard_map/ppermute | solution.py:89
  (69 shorter events, 31.4 us)
Async XLA Ops:
  6.5 139.6 %copy-start = (bf16[512,1024]{1,0:T(8,128)(2,1)S(1)}, bf16[512,1024]{1,0:T(8,128)(2,1)}, u32[]{:S(2)}) copy-start(bf16[512,1024]{1,0:T(8,128)(2,1)} %param.13) | copy-start | bytes 3145732
  6.5 140.3 %all-gather.2.cloned.1.call-start = ((), (), s32[]{:S(2)}) async-start(), calls=%async_computation | async-start | bytes 3899392 | tf_op jit(solution)/shard_map/all_gather | solution.py:134
  6.5 7.1 %collective-permute-start.7 = (bf16[1,56,1024]{2,1,0:T(8,128)(2,1)}, bf16[1,56,1024]{2,1,0:T(8,128)(2,1)S(1)}, u32[]{:S(2)}, u32[]{:S(2)}) collective-permute-start(bf16[1,56,1024]{2,1,0:T(8,128)(2,1)} %bitcast.130), channel_id=1, source_target_pairs={{0,16},{16,0},{1,17},{17,1},{2,18},{18,2},{3,19},{19,3},{4,20},{20... | collective-permute-start | bytes 344072 | tf_op jit(solution)/shard_map/ppermute | solution.py:58
  17.9 20.4 %collective-permute-start = (bf16[1,64,576]{2,1,0:T(8,128)(2,1)S(1)}, bf16[1,64,576]{2,1,0:T(8,128)(2,1)S(1)}, u32[]{:S(2)}, u32[]{:S(2)}) collective-permute-start(bf16[1,64,576]{2,1,0:T(8,128)(2,1)S(1)} %maximum_bitcast_fusion.2), channel_id=1, source_target_pairs={{0,256},{64,320},{128,384},{192,448},{256,0},{320,64},{384,128},{4... | collective-permute-start | bytes 221192 | tf_op jit(solution)/shard_map/ppermute | solution.py:58
  39.2 23.7 %collective-permute-start.1 = (bf16[2,64,576]{2,1,0:T(8,128)(2,1)S(1)}, bf16[2,64,576]{2,1,0:T(8,128)(2,1)S(1)}, u32[]{:S(2)}, u32[]{:S(2)}) collective-permute-start(bf16[2,64,576]{2,1,0:T(8,128)(2,1)S(1)} %maximum_bitcast_fusion.1), channel_id=1, source_target_pairs={{0,128},{64,192},{128,0},{192,64},{256,384},{320,448},{384,256},{4... | collective-permute-start | bytes 442376 | tf_op jit(solution)/shard_map/ppermute | solution.py:58
  63.0 24.5 %collective-permute-start.2 = (bf16[4,64,576]{2,1,0:T(8,128)(2,1)S(1)}, bf16[4,64,576]{2,1,0:T(8,128)(2,1)S(1)}, u32[]{:S(2)}, u32[]{:S(2)}) collective-permute-start(bf16[4,64,576]{2,1,0:T(8,128)(2,1)S(1)} %bitcast.124), channel_id=1, source_target_pairs={{0,64},{64,0},{128,192},{192,128},{256,320},{320,256},{384,448},{4... | collective-permute-start | bytes 884744 | tf_op jit(solution)/shard_map/ppermute | solution.py:58
  87.8 32.1 %collective-permute-start.3 = (bf16[8,64,576]{2,1,0:T(8,128)(2,1)S(1)}, bf16[8,64,576]{2,1,0:T(8,128)(2,1)S(1)}, u32[]{:S(2)}, u32[]{:S(2)}) collective-permute-start(bf16[8,64,576]{2,1,0:T(8,128)(2,1)S(1)} %bitcast.123), channel_id=1, source_target_pairs={{0,32},{32,0},{1,33},{33,1},{2,34},{34,2},{3,35},{35,3},{4,36},{36... | collective-permute-start | bytes 1769480 | tf_op jit(solution)/shard_map/ppermute | solution.py:58
  120.3 15.7 %collective-permute-start.4 = (bf16[8,64,576]{2,1,0:T(8,128)(2,1)S(1)}, bf16[8,64,576]{2,1,0:T(8,128)(2,1)S(1)}, u32[]{:S(2)}, u32[]{:S(2)}) collective-permute-start(bf16[8,64,576]{2,1,0:T(8,128)(2,1)S(1)} %bitcast.126), channel_id=1, source_target_pairs={{0,16},{16,0},{1,17},{17,1},{2,18},{18,2},{3,19},{19,3},{4,20},{20... | collective-permute-start | bytes 1769480 | tf_op jit(solution)/shard_map/ppermute | solution.py:60
  124.1 16.6 %collective-permute-start.5 = (bf16[8,64,576]{2,1,0:T(8,128)(2,1)S(1)}, bf16[8,64,576]{2,1,0:T(8,128)(2,1)S(1)}, u32[]{:S(2)}, u32[]{:S(2)}) collective-permute-start(bf16[8,64,576]{2,1,0:T(8,128)(2,1)S(1)} %bitcast.127), channel_id=1, source_target_pairs={{0,17},{1,16},{16,1},{17,0},{2,19},{3,18},{18,3},{19,2},{4,21},{5,... | collective-permute-start | bytes 1769480 | tf_op jit(solution)/shard_map/ppermute | solution.py:61
  141.6 4.0 %copy-start.2 = (bf16[64,512]{1,0:T(8,128)(2,1)S(1)}, bf16[64,512]{1,0:T(8,128)(2,1)}, u32[]{:S(2)}) copy-start(bf16[64,512]{1,0:T(8,128)(2,1)} %param.9) | copy-start | bytes 196612
  141.6 4.6 %copy-start.4 = (bf16[64,1024]{1,0:T(8,128)(2,1)S(1)}, bf16[64,1024]{1,0:T(8,128)(2,1)}, u32[]{:S(2)}) copy-start(bf16[64,1024]{1,0:T(8,128)(2,1)} %param.8) | copy-start | bytes 393220
  143.4 7.1 %collective-permute-start.6 = (bf16[32,64,576]{2,1,0:T(8,128)(2,1)}, bf16[32,64,576]{2,1,0:T(8,128)(2,1)}, u32[]{:S(2)}, u32[]{:S(2)}) collective-permute-start(bf16[32,64,576]{2,1,0:T(8,128)(2,1)} %bitcast.23), channel_id=1, source_target_pairs={{0,8},{8,0},{1,9},{9,1},{2,10},{10,2},{3,11},{11,3},{4,12},{12,4},... | collective-permute-start | bytes 7077896 | tf_op jit(solution)/shard_map/ppermute | solution.py:58
  146.8 18.4 %collective-permute-start.8 = (bf16[1024,1792]{0,1:T(8,128)(2,1)}, bf16[1024,1792]{0,1:T(8,128)(2,1)}, u32[]{:S(2)}, u32[]{:S(2)}) collective-permute-start(bf16[1024,1792]{0,1:T(8,128)(2,1)} %all-gather.2.cloned.1.call-done), channel_id=1, source_target_pairs={{0,8},{8,0},{1,9},{9,1},{2,10},{10,2},{3,11},{11,3},{4,12},{12,4},... | collective-permute-start | bytes 11010056 | tf_op jit(solution)/shard_map/ppermute | solution.py:135
  162.0 2.5 %copy-start.3 = (bf16[512,1024]{1,0:T(8,128)(2,1)S(1)}, bf16[512,1024]{1,0:T(8,128)(2,1)}, u32[]{:S(2)}) copy-start(bf16[512,1024]{1,0:T(8,128)(2,1)} %param.14) | copy-start | bytes 3145732
  172.6 44.6 %copy-start.1 = (bf16[512,1024]{1,0:T(8,128)(2,1)S(1)}, bf16[512,1024]{1,0:T(8,128)(2,1)}, u32[]{:S(2)}) copy-start(bf16[512,1024]{1,0:T(8,128)(2,1)} %param.13) | copy-start | bytes 3145732
  182.0 16.0 %collective-permute-start.9 = (f32[64,1792]{1,0:T(8,128)S(1)}, f32[64,1792]{1,0:T(8,128)S(1)}, u32[]{:S(2)}, u32[]{:S(2)}) collective-permute-start(f32[64,1792]{1,0:T(8,128)S(1)} %slice_select_fusion), channel_id=1, source_target_pairs={{0,4},{2,6},{4,0},{6,2},{1,5},{3,7},{5,1},{7,3},{8,12},{10,14},{12... | collective-permute-start | bytes 1376264 | tf_op jit(solution)/shard_map/ppermute | solution.py:89
  199.2 8.7 %collective-permute-start.10 = (f32[64,896]{1,0:T(8,128)S(1)}, f32[64,896]{1,0:T(8,128)S(1)}, u32[]{:S(2)}, u32[]{:S(2)}) collective-permute-start(f32[64,896]{1,0:T(8,128)S(1)} %slice_select_fusion.1), channel_id=1, source_target_pairs={{0,2},{2,0},{4,6},{6,4},{1,3},{3,1},{5,7},{7,5},{8,10},{10,8},{12,... | collective-permute-start | bytes 688136 | tf_op jit(solution)/shard_map/ppermute | solution.py:89
  208.1 8.4 %collective-permute-start.11 = (f32[64,448]{1,0:T(8,128)S(1)}, f32[64,448]{1,0:T(8,128)S(1)}, u32[]{:S(2)}, u32[]{:S(2)}) collective-permute-start(f32[64,448]{1,0:T(8,128)S(1)} %slice_select_fusion.2), channel_id=1, source_target_pairs={{0,1},{1,0},{2,3},{3,2},{4,5},{5,4},{6,7},{7,6},{8,9},{9,8},{10,11... | collective-permute-start | bytes 344072 | tf_op jit(solution)/shard_map/ppermute | solution.py:89
Sparse Core Ops, SparseCore 0:
  15.4 109.4 all-gather.1

commit v6 on v5

--- a/solution.py
+++ b/solution.py
@@ -37,10 +37,9 @@
     )
 
 
-def attend(query_rows, query_index, keys, key_count):
+def attend(query_rows, query_index, keys, key_index):
     scale = 1.0 / math.sqrt(NOPE + ROPE)
     scores = jnp.einsum("rl,kl->rk", query_rows, keys, preferred_element_type=jnp.float32)
-    key_index = lax.broadcasted_iota(jnp.int32, (1, key_count), 1)
     visible = key_index <= query_index[:, None]
     scores = jnp.where(visible, scores * scale, masked_value)
     peak = jnp.max(scores, axis=1)
@@ -76,19 +75,38 @@
     return acc.reshape((-1,) + local.shape[1:])
 
 
-def scatter_sum(partial, axes):
-    acc = partial
-    for axis, size in axes:
-        bit = size // 2
-        while bit >= 1:
-            upper = (lax.axis_index(axis) // bit) % 2 == 1
-            half = acc.shape[1] // 2
-            low, high = acc[:, :half], acc[:, half:]
-            keep = jnp.where(upper, high, low)
-            send = jnp.where(upper, low, high)
-            acc = keep + lax.ppermute(send, axis, [(i, i ^ bit) for i in range(size)])
-            bit //= 2
-    return acc
+ABSENT = 1 << 20
+
+
+def gather_earlier_keys(local):
+    cubes = lax.axis_size("zh")
+    cube = lax.axis_index("zh")
+    within = lax.axis_index(("zl", "yl", "co"))
+    per_cube = lax.axis_size(("zl", "yl", "co"))
+    blocks = [local]
+    for shift in range(1, cubes):
+        blocks.append(lax.ppermute(local, "zh", [(i, i + shift) for i in range(cubes - shift)]))
+    acc = jnp.stack(blocks)
+    source = cube - jnp.arange(cubes, dtype=jnp.int32)
+    index = jnp.where(source >= 0, source * per_cube + within, ABSENT)
+    for axis, size in (("zl", 2), ("yl", 2), ("co", 2)):
+        step = per_cube // size
+        per_cube = step
+        other = exchange(acc, axis, size, 1, True)
+        acc = jnp.concatenate([acc, other], axis=0)
+        index = jnp.concatenate([index, jnp.where(index < ABSENT, index ^ step, ABSENT)])
+    return acc, index
+
+
+def scatter_sum(blocks):
+    groups = lax.axis_size(HEAD)
+    me = lax.axis_index(HEAD)
+    total = blocks[me]
+    for shift in range(1, groups):
+        total = total + lax.ppermute(
+            blocks[me ^ shift], HEAD, [(i, i ^ shift) for i in range(groups)]
+        )
+    return total
 
 
 def upward(latent_out, value_up, token_count, head_count):
@@ -104,7 +122,6 @@
 def body(queries_nope, queries_rope, latents, rope_keys, positions, key_up, value_up, out_proj):
     token_count = latents.shape[0]
     head_count = key_up.shape[1] // NOPE
-    ctx_count = lax.axis_size(CTX)
     cosine, sine = rope_tables(positions, ROPE)
     rot_queries = rotate(
         queries_rope.astype(jnp.float32).reshape(token_count, head_count, ROPE), cosine, sine
@@ -122,12 +139,16 @@
         token_count * head_count, LATENT + ROPE
     )
     local_keys = jnp.concatenate([latents, rot_keys], axis=-1)
-    keys = gather_in_order(local_keys, CTX_SPLIT, True)
+    key_blocks, block_index = gather_earlier_keys(local_keys)
+    keys = key_blocks.reshape(-1, LATENT + ROPE)
+    key_index = (
+        block_index[:, None] * token_count + jnp.arange(token_count, dtype=jnp.int32)[None, :]
+    ).reshape(1, -1)
     first_token = lax.axis_index(CTX) * token_count
     query_index = jnp.repeat(
         first_token + jnp.arange(token_count, dtype=jnp.int32), head_count
     )
-    latent_out = attend(query_rows, query_index, keys, token_count * ctx_count)
+    latent_out = attend(query_rows, query_index, keys, key_index)
     head_out = upward(latent_out, value_up, token_count, head_count)
     pair = gather_in_order(out_proj.T, (("yl", 2),), False)
     pair = pair.reshape(2, out_proj.shape[1], -1).transpose(2, 0, 1).reshape(out_proj.shape[0], -1)
@@ -135,13 +156,20 @@
     swapped = lax.ppermute(own, "co", [(0, 1), (1, 0)])
     upper = lax.axis_index("co") == 1
     halves = [jnp.where(upper, swapped, own), jnp.where(upper, own, swapped)]
-    partial_sums = jnp.stack(
-        [jnp.dot(head_out, half, preferred_element_type=jnp.float32) for half in halves], axis=1
-    )
+    groups = lax.axis_size(HEAD)
+    partial_sums = jnp.concatenate(
+        [
+            jnp.dot(head_out, half, preferred_element_type=jnp.float32).reshape(
+                token_count, groups, -1
+            )
+            for half in halves
+        ],
+        axis=2,
+    ).transpose(1, 0, 2)
+    mine = scatter_sum(partial_sums)
     width = out_proj.shape[1]
-    partial_sums = partial_sums.reshape(token_count, 2, -1, width).transpose(0, 2, 1, 3)
-    partial_sums = partial_sums.reshape(token_count, -1)
-    return scatter_sum(partial_sums, HEAD_SPLIT).astype(jnp.bfloat16)
+    mine = mine.reshape(token_count, 2, -1, width).transpose(0, 2, 1, 3)
+    return mine.reshape(token_count, -1).astype(jnp.bfloat16)
 
 
 CTX_SPLIT = (("zh", 8), ("zl", 2), ("yl", 2), ("co", 2))

time: 225 us -> 201 us (0.89)
  the two profiles are of different devices: /device:TPU:6 before, /device:TPU:40 now
where the time goes in v6:
time: 201 us; the launch traced here: 200 us
  starting transfers between devices  75.8 us (38%)
  waiting for transfers between devices  69.3 us (34%)
  local copies, waits for them, and re-layouts  16 us (8%)
  between operations  13.9 us (7%)
  other arithmetic  13 us (6%)
  matrix products  12.4 us (6%)
    ppermute x3, waiting for transfers between devices, exchange(): return lax.ppermute(acc, axis, pairs)  31.5 us
    ppermute x7, starting transfers between devices, gather_earlier_keys(): lax.ppermute(local, 'zh', [(i, i + shift) for i in range(cubes - shift)])  28.4 us
    ppermute x7, starting transfers between devices, scatter_sum(): lax.ppermute(blocks[me ^ shift], HEAD, [(i, i ^ shift) for i in range(gro...  27.7 us
    ppermute x7, waiting for transfers between devices, gather_earlier_keys(): lax.ppermute(local, 'zh', [(i, i + shift) for i in range(cubes - shift)])  17.5 us
    ppermute x1, waiting for transfers between devices, exchange(): far = lax.ppermute(acc[half:], ('yl', 'yh'), [(i, i ^ 3) for i in range(4)])  11.7 us
    ppermute x3, starting transfers between devices, exchange(): return lax.ppermute(acc, axis, pairs)  11.3 us
    unnamed x24, local copies, waits for them, and re-layouts  9.76 us
    ppermute x7, waiting for transfers between devices, scatter_sum(): lax.ppermute(blocks[me ^ shift], HEAD, [(i, i ^ shift) for i in range(gro...  8.53 us
  transfers between devices with their start and end apart: 21, of which 10 were waited for; matrix products, arithmetic and copies ran while one was open for 15% of the time, Pallas kernels for 0%

profile of v6, /device:TPU:40, one launch (start us, length us, event | category | flops | bytes accessed | tf_op | source)
XLA Modules:
  0.0 200.5 jit_solution(9371784948281864973)
XLA Ops:
  9.0 4.6 %collective-permute-done.11 = bf16[1,56,1024]{2,1,0:T(8,128)(2,1)S(1)} collective-permute-done((bf16[1,56,1024]{2,1,0:T(8,128)(2,1)}, bf16[1,56,1024]{2,1,0:T(8,128)(2,1)S(1)}, u32[]{:S(2)}, u32[]{:S(2)}) %collective-permute-start.11) | collective-permute-done | bytes 114720 | tf_op jit(solution)/shard_map/ppermute | solution.py:57
  17.9 5.2 %collective-permute-start = (bf16[64,576]{1,0:T(8,128)(2,1)S(1)}, bf16[64,576]{1,0:T(8,128)(2,1)S(1)}, u32[]{:S(2)}, u32[]{:S(2)}) collective-permute-start(bf16[64,576]{1,0:T(8,128)(2,1)S(1)} %pad_maximum_fusion.2), channel_id=1, source_target_pairs={{0,64},{64,128},{128,192},{192,256},{256,320},{320,384},{384,448},... | collective-permute-start | bytes 221192 | tf_op jit(solution)/shard_map/ppermute | solution.py:88
  23.1 9.1 %collective-permute-start.1 = (bf16[64,576]{1,0:T(8,128)(2,1)S(1)}, bf16[64,576]{1,0:T(8,128)(2,1)S(1)}, u32[]{:S(2)}, u32[]{:S(2)}) collective-permute-start(bf16[64,576]{1,0:T(8,128)(2,1)S(1)} %pad_maximum_fusion.2), channel_id=1, source_target_pairs={{0,128},{64,192},{128,256},{192,320},{256,384},{320,448},{1,129},{... | collective-permute-start | bytes 221192 | tf_op jit(solution)/shard_map/ppermute | solution.py:88
  32.2 7.3 %collective-permute-start.2 = (bf16[64,576]{1,0:T(8,128)(2,1)S(1)}, bf16[64,576]{1,0:T(8,128)(2,1)S(1)}, u32[]{:S(2)}, u32[]{:S(2)}) collective-permute-start(bf16[64,576]{1,0:T(8,128)(2,1)S(1)} %pad_maximum_fusion.2), channel_id=1, source_target_pairs={{0,192},{64,256},{128,320},{192,384},{256,448},{1,193},{65,257},{1... | collective-permute-start | bytes 221192 | tf_op jit(solution)/shard_map/ppermute | solution.py:88
  39.5 2.8 %collective-permute-start.3 = (bf16[64,576]{1,0:T(8,128)(2,1)S(1)}, bf16[64,576]{1,0:T(8,128)(2,1)S(1)}, u32[]{:S(2)}, u32[]{:S(2)}) collective-permute-start(bf16[64,576]{1,0:T(8,128)(2,1)S(1)} %pad_maximum_fusion.2), channel_id=1, source_target_pairs={{0,256},{64,320},{128,384},{192,448},{1,257},{65,321},{129,385},{1... | collective-permute-start | bytes 221192 | tf_op jit(solution)/shard_map/ppermute | solution.py:88
  49.8 8.9 %collective-permute-done.3 = bf16[64,576]{1,0:T(8,128)(2,1)S(1)} collective-permute-done((bf16[64,576]{1,0:T(8,128)(2,1)S(1)}, bf16[64,576]{1,0:T(8,128)(2,1)S(1)}, u32[]{:S(2)}, u32[]{:S(2)}) %collective-permute-start.3) | collective-permute-done | bytes 73760 | tf_op jit(solution)/shard_map/ppermute | solution.py:88
  59.4 3.0 %collective-permute-done.4 = bf16[64,576]{1,0:T(8,128)(2,1)S(1)} collective-permute-done((bf16[64,576]{1,0:T(8,128)(2,1)S(1)}, bf16[64,576]{1,0:T(8,128)(2,1)S(1)}, u32[]{:S(2)}, u32[]{:S(2)}) %collective-permute-start.4) | collective-permute-done | bytes 73760 | tf_op jit(solution)/shard_map/ppermute | solution.py:88
  63.0 2.8 %collective-permute-done.5 = bf16[64,576]{1,0:T(8,128)(2,1)S(1)} collective-permute-done((bf16[64,576]{1,0:T(8,128)(2,1)S(1)}, bf16[64,576]{1,0:T(8,128)(2,1)S(1)}, u32[]{:S(2)}, u32[]{:S(2)}) %collective-permute-start.5) | collective-permute-done | bytes 73760 | tf_op jit(solution)/shard_map/ppermute | solution.py:88
  66.5 2.8 %collective-permute-done.6 = bf16[64,576]{1,0:T(8,128)(2,1)S(1)} collective-permute-done((bf16[64,576]{1,0:T(8,128)(2,1)S(1)}, bf16[64,576]{1,0:T(8,128)(2,1)S(1)}, u32[]{:S(2)}, u32[]{:S(2)}) %collective-permute-start.6) | collective-permute-done | bytes 73760 | tf_op jit(solution)/shard_map/ppermute | solution.py:88
  70.0 6.9 %collective-permute-start.7 = (bf16[8,64,576]{2,1,0:T(8,128)(2,1)S(1)}, bf16[8,64,576]{2,1,0:T(8,128)(2,1)S(1)}, u32[]{:S(2)}, u32[]{:S(2)}) collective-permute-start(bf16[8,64,576]{2,1,0:T(8,128)(2,1)S(1)} %get-tuple-element.29), channel_id=1, source_target_pairs={{0,32},{32,0},{1,33},{33,1},{2,34},{34,2},{3,35},{35,3},{4,36},{36... | collective-permute-start | bytes 1769480 | tf_op jit(solution)/shard_map/ppermute | solution.py:57
  79.3 26.2 %collective-permute-done.7 = bf16[8,64,576]{2,1,0:T(8,128)(2,1)S(1)} collective-permute-done((bf16[8,64,576]{2,1,0:T(8,128)(2,1)S(1)}, bf16[8,64,576]{2,1,0:T(8,128)(2,1)S(1)}, u32[]{:S(2)}, u32[]{:S(2)}) %collective-permute-start.7) | collective-permute-done | bytes 589856 | tf_op jit(solution)/shard_map/ppermute | solution.py:57
  105.5 3.5 %collective-permute-start.9 = (bf16[8,64,576]{2,1,0:T(8,128)(2,1)S(1)}, bf16[8,64,576]{2,1,0:T(8,128)(2,1)S(1)}, u32[]{:S(2)}, u32[]{:S(2)}) collective-permute-start(bf16[8,64,576]{2,1,0:T(8,128)(2,1)S(1)} %collective-permute-done.7), channel_id=1, source_target_pairs={{0,17},{1,16},{16,1},{17,0},{2,19},{3,18},{18,3},{19,2},{4,21},{5,... | collective-permute-start | bytes 1769480 | tf_op jit(solution)/shard_map/ppermute | solution.py:60
  111.0 11.7 %collective-permute-done.9 = bf16[8,64,576]{2,1,0:T(8,128)(2,1)S(1)} collective-permute-done((bf16[8,64,576]{2,1,0:T(8,128)(2,1)S(1)}, bf16[8,64,576]{2,1,0:T(8,128)(2,1)S(1)}, u32[]{:S(2)}, u32[]{:S(2)}) %collective-permute-start.9) | collective-permute-done | bytes 589856 | tf_op jit(solution)/shard_map/ppermute | solution.py:60
  129.0 2.6 %collective-permute-start.12 = (bf16[1024,1792]{0,1:T(8,128)(2,1)}, bf16[1024,1792]{0,1:T(8,128)(2,1)}, u32[]{:S(2)}, u32[]{:S(2)}) collective-permute-start(bf16[1024,1792]{0,1:T(8,128)(2,1)} %all-gather.2.cloned.1.call-done), channel_id=1, source_target_pairs={{0,8},{8,0},{1,9},{9,1},{2,10},{10,2},{3,11},{11,3},{4,12},{12,4},... | collective-permute-start | bytes 11010056 | tf_op jit(solution)/shard_map/ppermute | solution.py:156
  133.2 3.5 %constant_dynamic-update-slice_fusion.3 = bf16[64,64,576]{2,1,0:T(8,128)(2,1)} fusion(bf16[64,64,576]{2,1,0:T(8,128)(2,1)} %copy-done.2, bf16[32,64,576]{2,1,0:T(8,128)(2,1)} %collective-permute-done.10), kind=kLoop, calls=%fused_computation.104 | loop fusion | bytes 5242880 | tf_op jit(solution)/shard_map/concatenate | solution.py:96
  136.7 6.4 %fusion = (f32[512]{0:T(512)S(1)}, f32[512,4096]{1,0:T(8,128)S(1)}) fusion(s32[4096]{0:T(1024)S(1)} %add.113, s32[512]{0:T(512)S(1)} %le.16, bf16[4096,576]{1,0:T(8,128)(2,1)} %bitcast.133, bf16[64,8,576]{2,0,1:T(8,128)(2,1)S(1)} %pad_maximum_fusion), kind=kOutput, calls=%fused_computation.2 | convolution fusion | flops 2424307200 | bytes 13717504 | tf_op jit(solution)/shard_map/rl,kl->rk/dot_general | solution.py:42
  143.1 2.6 %fusion.1 = f32[512]{0:T(512)S(1)} fusion(f32[512,4096]{1,0:T(8,128)S(1)} %get-tuple-element.56, f32[512]{0:T(512)S(1)} %get-tuple-element.55, s32[4096]{0:T(1024)S(1)} %add.113, s32[512]{0:T(512)S(1)} %le.16), kind=kLoop, calls=%fused_computation.3 | loop fusion | flops 12582400 | bytes 8411136 | tf_op jit(solution)/shard_map/reduce_sum | solution.py:47
  149.0 3.6 %broadcast_select_fusion = (bf16[1024,1792]{0,1:T(8,128)(2,1)S(1)}, bf16[1024,1792]{0,1:T(8,128)(2,1)S(1)}) fusion(bf16[1024,1792]{0,1:T(8,128)(2,1)} %all-gather.2.cloned.1.call-done, bf16[1024,1792]{0,1:T(8,128)(2,1)} %collective-permute-done.12, pred[]{:T(512)S(6)} %eq.8), kind=kLoop, calls=%fused_computation.12 | loop fusion | flops 3670016 | bytes 14680065 | tf_op jit(solution)/shard_map/jit(_where)/select_n | solution.py:158
  156.1 5.5 %collective-permute-start.13 = (f32[64,448]{1,0:T(8,128)S(1)}, f32[64,448]{1,0:T(8,128)S(1)}, u32[]{:S(2)}, u32[]{:S(2)}) collective-permute-start(f32[64,448]{1,0:T(8,128)S(1)} %get-tuple-element.9), channel_id=1, source_target_pairs={{0,1},{1,0},{2,3},{3,2},{4,5},{5,4},{6,7},{7,6},{8,9},{9,8},{10,11... | collective-permute-start | bytes 344072 | tf_op jit(solution)/shard_map/ppermute | solution.py:106
  161.6 3.4 %collective-permute-start.14 = (f32[64,448]{1,0:T(8,128)S(1)}, f32[64,448]{1,0:T(8,128)S(1)}, u32[]{:S(2)}, u32[]{:S(2)}) collective-permute-start(f32[64,448]{1,0:T(8,128)S(1)} %get-tuple-element.10), channel_id=1, source_target_pairs={{0,2},{1,3},{2,0},{3,1},{4,6},{5,7},{6,4},{7,5},{8,10},{9,11},{10,... | collective-permute-start | bytes 344072 | tf_op jit(solution)/shard_map/ppermute | solution.py:106
  166.9 4.9 %collective-permute-start.16 = (f32[64,448]{1,0:T(8,128)}, f32[64,448]{1,0:T(8,128)S(1)}, u32[]{:S(2)}, u32[]{:S(2)}) collective-permute-start(f32[64,448]{1,0:T(8,128)} %get-tuple-element.12), channel_id=1, source_target_pairs={{0,4},{1,5},{2,6},{3,7},{4,0},{5,1},{6,2},{7,3},{8,12},{9,13},{10,... | collective-permute-start | bytes 344072 | tf_op jit(solution)/shard_map/ppermute | solution.py:106
  171.8 5.4 %collective-permute-start.17 = (f32[64,448]{1,0:T(8,128)S(1)}, f32[64,448]{1,0:T(8,128)S(1)}, u32[]{:S(2)}, u32[]{:S(2)}) collective-permute-start(f32[64,448]{1,0:T(8,128)S(1)} %get-tuple-element.13), channel_id=1, source_target_pairs={{0,5},{1,4},{2,7},{3,6},{4,1},{5,0},{6,3},{7,2},{8,13},{9,12},{10,... | collective-permute-start | bytes 344072 | tf_op jit(solution)/shard_map/ppermute | solution.py:106
  177.3 4.7 %collective-permute-start.18 = (f32[64,448]{1,0:T(8,128)S(1)}, f32[64,448]{1,0:T(8,128)S(1)}, u32[]{:S(2)}, u32[]{:S(2)}) collective-permute-start(f32[64,448]{1,0:T(8,128)S(1)} %get-tuple-element.14), channel_id=1, source_target_pairs={{0,6},{1,7},{2,4},{3,5},{4,2},{5,3},{6,0},{7,1},{8,14},{9,15},{10,... | collective-permute-start | bytes 344072 | tf_op jit(solution)/shard_map/ppermute | solution.py:106
  185.9 6.5 %collective-permute-done.19 = f32[64,448]{1,0:T(8,128)S(1)} collective-permute-done((f32[64,448]{1,0:T(8,128)S(1)}, f32[64,448]{1,0:T(8,128)S(1)}, u32[]{:S(2)}, u32[]{:S(2)}) %collective-permute-start.19) | collective-permute-done | bytes 114720 | tf_op jit(solution)/shard_map/ppermute | solution.py:106
  (86 shorter events, 42.6 us)
Async XLA Ops:
  6.5 125.4 %copy-start = (bf16[512,1024]{1,0:T(8,128)(2,1)S(1)}, bf16[512,1024]{1,0:T(8,128)(2,1)}, u32[]{:S(2)}) copy-start(bf16[512,1024]{1,0:T(8,128)(2,1)} %param.13) | copy-start | bytes 3145732
  6.5 121.5 %copy-start.1 = (bf16[64,512]{1,0:T(8,128)(2,1)S(1)}, bf16[64,512]{1,0:T(8,128)(2,1)}, u32[]{:S(2)}) copy-start(bf16[64,512]{1,0:T(8,128)(2,1)} %param.9) | copy-start | bytes 196612
  6.5 122.4 %all-gather.2.cloned.1.call-start = ((), (), s32[]{:S(2)}) async-start(), calls=%async_computation | async-start | bytes 3899392 | tf_op jit(solution)/shard_map/all_gather | solution.py:155
  6.5 7.1 %collective-permute-start.11 = (bf16[1,56,1024]{2,1,0:T(8,128)(2,1)}, bf16[1,56,1024]{2,1,0:T(8,128)(2,1)S(1)}, u32[]{:S(2)}, u32[]{:S(2)}) collective-permute-start(bf16[1,56,1024]{2,1,0:T(8,128)(2,1)} %bitcast.132), channel_id=1, source_target_pairs={{0,16},{16,0},{1,17},{17,1},{2,18},{18,2},{3,19},{19,3},{4,20},{20... | collective-permute-start | bytes 344072 | tf_op jit(solution)/shard_map/ppermute | solution.py:57
  17.9 27.2 %collective-permute-start = (bf16[64,576]{1,0:T(8,128)(2,1)S(1)}, bf16[64,576]{1,0:T(8,128)(2,1)S(1)}, u32[]{:S(2)}, u32[]{:S(2)}) collective-permute-start(bf16[64,576]{1,0:T(8,128)(2,1)S(1)} %pad_maximum_fusion.2), channel_id=1, source_target_pairs={{0,64},{64,128},{128,192},{192,256},{256,320},{320,384},{384,448},... | collective-permute-start | bytes 221192 | tf_op jit(solution)/shard_map/ppermute | solution.py:88
  23.1 24.0 %collective-permute-start.1 = (bf16[64,576]{1,0:T(8,128)(2,1)S(1)}, bf16[64,576]{1,0:T(8,128)(2,1)S(1)}, u32[]{:S(2)}, u32[]{:S(2)}) collective-permute-start(bf16[64,576]{1,0:T(8,128)(2,1)S(1)} %pad_maximum_fusion.2), channel_id=1, source_target_pairs={{0,128},{64,192},{128,256},{192,320},{256,384},{320,448},{1,129},{... | collective-permute-start | bytes 221192 | tf_op jit(solution)/shard_map/ppermute | solution.py:88
  32.2 17.0 %collective-permute-start.2 = (bf16[64,576]{1,0:T(8,128)(2,1)S(1)}, bf16[64,576]{1,0:T(8,128)(2,1)S(1)}, u32[]{:S(2)}, u32[]{:S(2)}) collective-permute-start(bf16[64,576]{1,0:T(8,128)(2,1)S(1)} %pad_maximum_fusion.2), channel_id=1, source_target_pairs={{0,192},{64,256},{128,320},{192,384},{256,448},{1,193},{65,257},{1... | collective-permute-start | bytes 221192 | tf_op jit(solution)/shard_map/ppermute | solution.py:88
  39.5 19.2 %collective-permute-start.3 = (bf16[64,576]{1,0:T(8,128)(2,1)S(1)}, bf16[64,576]{1,0:T(8,128)(2,1)S(1)}, u32[]{:S(2)}, u32[]{:S(2)}) collective-permute-start(bf16[64,576]{1,0:T(8,128)(2,1)S(1)} %pad_maximum_fusion.2), channel_id=1, source_target_pairs={{0,256},{64,320},{128,384},{192,448},{1,257},{65,321},{129,385},{1... | collective-permute-start | bytes 221192 | tf_op jit(solution)/shard_map/ppermute | solution.py:88
  42.4 20.0 %collective-permute-start.4 = (bf16[64,576]{1,0:T(8,128)(2,1)S(1)}, bf16[64,576]{1,0:T(8,128)(2,1)S(1)}, u32[]{:S(2)}, u32[]{:S(2)}) collective-permute-start(bf16[64,576]{1,0:T(8,128)(2,1)S(1)} %pad_maximum_fusion.2), channel_id=1, source_target_pairs={{0,320},{64,384},{128,448},{1,321},{65,385},{129,449},{2,322},{66,... | collective-permute-start | bytes 221192 | tf_op jit(solution)/shard_map/ppermute | solution.py:88
  45.2 20.7 %collective-permute-start.5 = (bf16[64,576]{1,0:T(8,128)(2,1)S(1)}, bf16[64,576]{1,0:T(8,128)(2,1)S(1)}, u32[]{:S(2)}, u32[]{:S(2)}) collective-permute-start(bf16[64,576]{1,0:T(8,128)(2,1)S(1)} %pad_maximum_fusion.2), channel_id=1, source_target_pairs={{0,384},{64,448},{1,385},{65,449},{2,386},{66,450},{3,387},{67,451... | collective-permute-start | bytes 221192 | tf_op jit(solution)/shard_map/ppermute | solution.py:88
  47.1 84.8 %copy-start.4 = (bf16[64,1024]{1,0:T(8,128)(2,1)S(1)}, bf16[64,1024]{1,0:T(8,128)(2,1)}, u32[]{:S(2)}) copy-start(bf16[64,1024]{1,0:T(8,128)(2,1)} %param.8) | copy-start | bytes 393220
  47.1 22.2 %collective-permute-start.6 = (bf16[64,576]{1,0:T(8,128)(2,1)S(1)}, bf16[64,576]{1,0:T(8,128)(2,1)S(1)}, u32[]{:S(2)}, u32[]{:S(2)}) collective-permute-start(bf16[64,576]{1,0:T(8,128)(2,1)S(1)} %pad_maximum_fusion.2), channel_id=1, source_target_pairs={{0,448},{1,449},{2,450},{3,451},{4,452},{5,453},{6,454},{7,455},{8... | collective-permute-start | bytes 221192 | tf_op jit(solution)/shard_map/ppermute | solution.py:88
  70.0 35.5 %collective-permute-start.7 = (bf16[8,64,576]{2,1,0:T(8,128)(2,1)S(1)}, bf16[8,64,576]{2,1,0:T(8,128)(2,1)S(1)}, u32[]{:S(2)}, u32[]{:S(2)}) collective-permute-start(bf16[8,64,576]{2,1,0:T(8,128)(2,1)S(1)} %get-tuple-element.29), channel_id=1, source_target_pairs={{0,32},{32,0},{1,33},{33,1},{2,34},{34,2},{3,35},{35,3},{4,36},{36... | collective-permute-start | bytes 1769480 | tf_op jit(solution)/shard_map/ppermute | solution.py:57
  76.9 33.1 %collective-permute-start.8 = (bf16[8,64,576]{2,1,0:T(8,128)(2,1)S(1)}, bf16[8,64,576]{2,1,0:T(8,128)(2,1)S(1)}, u32[]{:S(2)}, u32[]{:S(2)}) collective-permute-start(bf16[8,64,576]{2,1,0:T(8,128)(2,1)S(1)} %get-tuple-element.29), channel_id=1, source_target_pairs={{0,16},{16,0},{1,17},{17,1},{2,18},{18,2},{3,19},{19,3},{4,20},{20... | collective-permute-start | bytes 1769480 | tf_op jit(solution)/shard_map/ppermute | solution.py:59
  105.5 17.2 %collective-permute-start.9 = (bf16[8,64,576]{2,1,0:T(8,128)(2,1)S(1)}, bf16[8,64,576]{2,1,0:T(8,128)(2,1)S(1)}, u32[]{:S(2)}, u32[]{:S(2)}) collective-permute-start(bf16[8,64,576]{2,1,0:T(8,128)(2,1)S(1)} %collective-permute-done.7), channel_id=1, source_target_pairs={{0,17},{1,16},{16,1},{17,0},{2,19},{3,18},{18,3},{19,2},{4,21},{5,... | collective-permute-start | bytes 1769480 | tf_op jit(solution)/shard_map/ppermute | solution.py:60
  126.1 7.1 %collective-permute-start.10 = (bf16[32,64,576]{2,1,0:T(8,128)(2,1)}, bf16[32,64,576]{2,1,0:T(8,128)(2,1)}, u32[]{:S(2)}, u32[]{:S(2)}) collective-permute-start(bf16[32,64,576]{2,1,0:T(8,128)(2,1)} %get-tuple-element.15), channel_id=1, source_target_pairs={{0,8},{8,0},{1,9},{9,1},{2,10},{10,2},{3,11},{11,3},{4,12},{12,4},... | collective-permute-start | bytes 7077896 | tf_op jit(solution)/shard_map/ppermute | solution.py:57
  129.0 20.0 %collective-permute-start.12 = (bf16[1024,1792]{0,1:T(8,128)(2,1)}, bf16[1024,1792]{0,1:T(8,128)(2,1)}, u32[]{:S(2)}, u32[]{:S(2)}) collective-permute-start(bf16[1024,1792]{0,1:T(8,128)(2,1)} %all-gather.2.cloned.1.call-done), channel_id=1, source_target_pairs={{0,8},{8,0},{1,9},{9,1},{2,10},{10,2},{3,11},{11,3},{4,12},{12,4},... | collective-permute-start | bytes 11010056 | tf_op jit(solution)/shard_map/ppermute | solution.py:156
  156.1 21.2 %collective-permute-start.13 = (f32[64,448]{1,0:T(8,128)S(1)}, f32[64,448]{1,0:T(8,128)S(1)}, u32[]{:S(2)}, u32[]{:S(2)}) collective-permute-start(f32[64,448]{1,0:T(8,128)S(1)} %get-tuple-element.9), channel_id=1, source_target_pairs={{0,1},{1,0},{2,3},{3,2},{4,5},{5,4},{6,7},{7,6},{8,9},{9,8},{10,11... | collective-permute-start | bytes 344072 | tf_op jit(solution)/shard_map/ppermute | solution.py:106
  161.6 20.4 %collective-permute-start.14 = (f32[64,448]{1,0:T(8,128)S(1)}, f32[64,448]{1,0:T(8,128)S(1)}, u32[]{:S(2)}, u32[]{:S(2)}) collective-permute-start(f32[64,448]{1,0:T(8,128)S(1)} %get-tuple-element.10), channel_id=1, source_target_pairs={{0,2},{1,3},{2,0},{3,1},{4,6},{5,7},{6,4},{7,5},{8,10},{9,11},{10,... | collective-permute-start | bytes 344072 | tf_op jit(solution)/shard_map/ppermute | solution.py:106
  165.0 18.9 %collective-permute-start.15 = (f32[64,448]{1,0:T(8,128)}, f32[64,448]{1,0:T(8,128)S(1)}, u32[]{:S(2)}, u32[]{:S(2)}) collective-permute-start(f32[64,448]{1,0:T(8,128)} %get-tuple-element.11), channel_id=1, source_target_pairs={{0,3},{1,2},{2,1},{3,0},{4,7},{5,6},{6,5},{7,4},{8,11},{9,10},{10,... | collective-permute-start | bytes 344072 | tf_op jit(solution)/shard_map/ppermute | solution.py:106
  166.9 17.0 %collective-permute-start.16 = (f32[64,448]{1,0:T(8,128)}, f32[64,448]{1,0:T(8,128)S(1)}, u32[]{:S(2)}, u32[]{:S(2)}) collective-permute-start(f32[64,448]{1,0:T(8,128)} %get-tuple-element.12), channel_id=1, source_target_pairs={{0,4},{1,5},{2,6},{3,7},{4,0},{5,1},{6,2},{7,3},{8,12},{9,13},{10,... | collective-permute-start | bytes 344072 | tf_op jit(solution)/shard_map/ppermute | solution.py:106
  171.8 12.1 %collective-permute-start.17 = (f32[64,448]{1,0:T(8,128)S(1)}, f32[64,448]{1,0:T(8,128)S(1)}, u32[]{:S(2)}, u32[]{:S(2)}) collective-permute-start(f32[64,448]{1,0:T(8,128)S(1)} %get-tuple-element.13), channel_id=1, source_target_pairs={{0,5},{1,4},{2,7},{3,6},{4,1},{5,0},{6,3},{7,2},{8,13},{9,12},{10,... | collective-permute-start | bytes 344072 | tf_op jit(solution)/shard_map/ppermute | solution.py:106
  177.3 8.6 %collective-permute-start.18 = (f32[64,448]{1,0:T(8,128)S(1)}, f32[64,448]{1,0:T(8,128)S(1)}, u32[]{:S(2)}, u32[]{:S(2)}) collective-permute-start(f32[64,448]{1,0:T(8,128)S(1)} %get-tuple-element.14), channel_id=1, source_target_pairs={{0,6},{1,7},{2,4},{3,5},{4,2},{5,3},{6,0},{7,1},{8,14},{9,15},{10,... | collective-permute-start | bytes 344072 | tf_op jit(solution)/shard_map/ppermute | solution.py:106
  182.0 10.5 %collective-permute-start.19 = (f32[64,448]{1,0:T(8,128)S(1)}, f32[64,448]{1,0:T(8,128)S(1)}, u32[]{:S(2)}, u32[]{:S(2)}) collective-permute-start(f32[64,448]{1,0:T(8,128)S(1)} %fusion.31), channel_id=1, source_target_pairs={{0,7},{1,6},{2,5},{3,4},{4,3},{5,2},{6,1},{7,0},{8,15},{9,14},{10,... | collective-permute-start | bytes 344072 | tf_op jit(solution)/shard_map/ppermute | solution.py:106
  (4 other events, 23.0 us)
Sparse Core Ops, SparseCore 0:
  15.4 109.6 all-gather.1

commit v7 on v6

--- a/solution.py
+++ b/solution.py
@@ -37,7 +37,7 @@
     )
 
 
-def attend(query_rows, query_index, keys, key_index):
+def attend_part(query_rows, query_index, keys, key_index):
     scale = 1.0 / math.sqrt(NOPE + ROPE)
     scores = jnp.einsum("rl,kl->rk", query_rows, keys, preferred_element_type=jnp.float32)
     visible = key_index <= query_index[:, None]
@@ -48,6 +48,19 @@
     summed = jnp.dot(
         weights.astype(jnp.bfloat16), keys[:, :LATENT], preferred_element_type=jnp.float32
     )
+    return peak, totals, summed
+
+
+def merge_parts(parts):
+    peak = parts[0][0]
+    for part in parts[1:]:
+        peak = jnp.maximum(peak, part[0])
+    totals = 0.0
+    summed = 0.0
+    for part_peak, part_totals, part_summed in parts:
+        factor = jnp.exp(part_peak - peak)
+        totals = totals + factor * part_totals
+        summed = summed + factor[:, None] * part_summed
     return (summed / totals[:, None]).astype(jnp.bfloat16)
 
 
@@ -89,13 +102,16 @@
     acc = jnp.stack(blocks)
     source = cube - jnp.arange(cubes, dtype=jnp.int32)
     index = jnp.where(source >= 0, source * per_cube + within, ABSENT)
+    chunks = [(acc, index)]
     for axis, size in (("zl", 2), ("yl", 2), ("co", 2)):
         step = per_cube // size
         per_cube = step
         other = exchange(acc, axis, size, 1, True)
+        other_index = jnp.where(index < ABSENT, index ^ step, ABSENT)
+        chunks.append((other, other_index))
         acc = jnp.concatenate([acc, other], axis=0)
-        index = jnp.concatenate([index, jnp.where(index < ABSENT, index ^ step, ABSENT)])
-    return acc, index
+        index = jnp.concatenate([index, other_index])
+    return chunks
 
 
 def scatter_sum(blocks):
@@ -139,16 +155,18 @@
         token_count * head_count, LATENT + ROPE
     )
     local_keys = jnp.concatenate([latents, rot_keys], axis=-1)
-    key_blocks, block_index = gather_earlier_keys(local_keys)
-    keys = key_blocks.reshape(-1, LATENT + ROPE)
-    key_index = (
-        block_index[:, None] * token_count + jnp.arange(token_count, dtype=jnp.int32)[None, :]
-    ).reshape(1, -1)
     first_token = lax.axis_index(CTX) * token_count
     query_index = jnp.repeat(
         first_token + jnp.arange(token_count, dtype=jnp.int32), head_count
     )
-    latent_out = attend(query_rows, query_index, keys, key_index)
+    parts = []
+    for key_blocks, block_index in gather_earlier_keys(local_keys):
+        keys = key_blocks.reshape(-1, LATENT + ROPE)
+        key_index = (
+            block_index[:, None] * token_count + jnp.arange(token_count, dtype=jnp.int32)[None, :]
+        ).reshape(1, -1)
+        parts.append(attend_part(query_rows, query_index, keys, key_index))
+    latent_out = merge_parts(parts)
     head_out = upward(latent_out, value_up, token_count, head_count)
     pair = gather_in_order(out_proj.T, (("yl", 2),), False)
     pair = pair.reshape(2, out_proj.shape[1], -1).transpose(2, 0, 1).reshape(out_proj.shape[0], -1)

time: 201 us -> 203 us (level)
  the two profiles are of different devices: /device:TPU:40 before, /device:TPU:6 now
where the time goes in v7:
time: 203 us; the launch traced here: 199 us
  starting transfers between devices  75.2 us (37%)
  waiting for transfers between devices  65.7 us (32%)
  matrix products  19.2 us (9%)
  other arithmetic  14.1 us (7%)
  between operations  14 us (7%)
  local copies, waits for them, and re-layouts  10.9 us (5%)
    ppermute x7, starting transfers between devices, gather_earlier_keys(): lax.ppermute(local, 'zh', [(i, i + shift) for i in range(cubes - shift)])  29.2 us
    ppermute x3, waiting for transfers between devices, exchange(): return lax.ppermute(acc, axis, pairs)  28.3 us
    ppermute x7, starting transfers between devices, scatter_sum(): lax.ppermute(blocks[me ^ shift], HEAD, [(i, i ^ shift) for i in range(gro...  27.5 us
    ppermute x7, waiting for transfers between devices, gather_earlier_keys(): lax.ppermute(local, 'zh', [(i, i + shift) for i in range(cubes - shift)])  21.3 us
    ppermute x1, waiting for transfers between devices, exchange(): far = lax.ppermute(acc[half:], ('yl', 'yh'), [(i, i ^ 3) for i in range(4)])  11.2 us
    dot_general x4, matrix products, attend_part(): jnp.einsum('rl,kl->rk', query_rows, keys, preferred_element_type=jnp.floa...  9.5 us
    ppermute x3, starting transfers between devices, exchange(): return lax.ppermute(acc, axis, pairs)  7.42 us
    unnamed x33, local copies, waits for them, and re-layouts  7.29 us
  transfers between devices with their start and end apart: 21, of which 8 were waited for; matrix products, arithmetic and copies ran while one was open for 17% of the time, Pallas kernels for 0%

profile of v7, /device:TPU:6, one launch (start us, length us, event | category | flops | bytes accessed | tf_op | source)
XLA Modules:
  0.0 199.0 jit_solution(9647773870249673474)
XLA Ops:
  6.5 3.6 %collective-permute-start.11 = (bf16[1,56,1024]{2,1,0:T(8,128)(2,1)}, bf16[1,56,1024]{2,1,0:T(8,128)(2,1)S(1)}, u32[]{:S(2)}, u32[]{:S(2)}) collective-permute-start(bf16[1,56,1024]{2,1,0:T(8,128)(2,1)} %bitcast.146), channel_id=1, source_target_pairs={{0,16},{16,0},{1,17},{17,1},{2,18},{18,2},{3,19},{19,3},{4,20},{20... | collective-permute-start | bytes 344072 | tf_op jit(solution)/shard_map/ppermute | solution.py:70
  10.2 3.5 %collective-permute-done.11 = bf16[1,56,1024]{2,1,0:T(8,128)(2,1)S(1)} collective-permute-done((bf16[1,56,1024]{2,1,0:T(8,128)(2,1)}, bf16[1,56,1024]{2,1,0:T(8,128)(2,1)S(1)}, u32[]{:S(2)}, u32[]{:S(2)}) %collective-permute-start.11) | collective-permute-done | bytes 114720 | tf_op jit(solution)/shard_map/ppermute | solution.py:70
  17.9 5.2 %collective-permute-start = (bf16[64,576]{1,0:T(8,128)(2,1)S(1)}, bf16[64,576]{1,0:T(8,128)(2,1)S(1)}, u32[]{:S(2)}, u32[]{:S(2)}) collective-permute-start(bf16[64,576]{1,0:T(8,128)(2,1)S(1)} %pad_maximum_fusion.3), channel_id=1, source_target_pairs={{0,64},{64,128},{128,192},{192,256},{256,320},{320,384},{384,448},... | collective-permute-start | bytes 221192 | tf_op jit(solution)/shard_map/ppermute | solution.py:101
  23.1 9.1 %collective-permute-start.1 = (bf16[64,576]{1,0:T(8,128)(2,1)S(1)}, bf16[64,576]{1,0:T(8,128)(2,1)S(1)}, u32[]{:S(2)}, u32[]{:S(2)}) collective-permute-start(bf16[64,576]{1,0:T(8,128)(2,1)S(1)} %pad_maximum_fusion.3), channel_id=1, source_target_pairs={{0,128},{64,192},{128,256},{192,320},{256,384},{320,448},{1,129},{... | collective-permute-start | bytes 221192 | tf_op jit(solution)/shard_map/ppermute | solution.py:101
  32.2 8.2 %collective-permute-start.2 = (bf16[64,576]{1,0:T(8,128)(2,1)S(1)}, bf16[64,576]{1,0:T(8,128)(2,1)S(1)}, u32[]{:S(2)}, u32[]{:S(2)}) collective-permute-start(bf16[64,576]{1,0:T(8,128)(2,1)S(1)} %pad_maximum_fusion.3), channel_id=1, source_target_pairs={{0,192},{64,256},{128,320},{192,384},{256,448},{1,193},{65,257},{1... | collective-permute-start | bytes 221192 | tf_op jit(solution)/shard_map/ppermute | solution.py:101
  40.4 2.8 %collective-permute-start.3 = (bf16[64,576]{1,0:T(8,128)(2,1)S(1)}, bf16[64,576]{1,0:T(8,128)(2,1)S(1)}, u32[]{:S(2)}, u32[]{:S(2)}) collective-permute-start(bf16[64,576]{1,0:T(8,128)(2,1)S(1)} %pad_maximum_fusion.3), channel_id=1, source_target_pairs={{0,256},{64,320},{128,384},{192,448},{1,257},{65,321},{129,385},{1... | collective-permute-start | bytes 221192 | tf_op jit(solution)/shard_map/ppermute | solution.py:101
  51.6 12.1 %collective-permute-done.4 = bf16[64,576]{1,0:T(8,128)(2,1)S(1)} collective-permute-done((bf16[64,576]{1,0:T(8,128)(2,1)S(1)}, bf16[64,576]{1,0:T(8,128)(2,1)S(1)}, u32[]{:S(2)}, u32[]{:S(2)}) %collective-permute-start.4) | collective-permute-done | bytes 73760 | tf_op jit(solution)/shard_map/ppermute | solution.py:101
  64.4 5.2 %collective-permute-done.5 = bf16[64,576]{1,0:T(8,128)(2,1)S(1)} collective-permute-done((bf16[64,576]{1,0:T(8,128)(2,1)S(1)}, bf16[64,576]{1,0:T(8,128)(2,1)S(1)}, u32[]{:S(2)}, u32[]{:S(2)}) %collective-permute-start.5) | collective-permute-done | bytes 73760 | tf_op jit(solution)/shard_map/ppermute | solution.py:101
  70.3 4.0 %collective-permute-done.6 = bf16[64,576]{1,0:T(8,128)(2,1)S(1)} collective-permute-done((bf16[64,576]{1,0:T(8,128)(2,1)S(1)}, bf16[64,576]{1,0:T(8,128)(2,1)S(1)}, u32[]{:S(2)}, u32[]{:S(2)}) %collective-permute-start.6) | collective-permute-done | bytes 73760 | tf_op jit(solution)/shard_map/ppermute | solution.py:101
  77.1 3.5 %collective-permute-start.8 = (bf16[8,64,576]{2,1,0:T(8,128)(2,1)}, bf16[8,64,576]{2,1,0:T(8,128)(2,1)S(1)}, u32[]{:S(2)}, u32[]{:S(2)}) collective-permute-start(bf16[8,64,576]{2,1,0:T(8,128)(2,1)} %get-tuple-element.30), channel_id=1, source_target_pairs={{0,16},{16,0},{1,17},{17,1},{2,18},{18,2},{3,19},{19,3},{4,20},{20... | collective-permute-start | bytes 1769480 | tf_op jit(solution)/shard_map/ppermute | solution.py:72
  80.6 24.8 %collective-permute-done.7 = bf16[8,64,576]{2,1,0:T(8,128)(2,1)S(1)} collective-permute-done((bf16[8,64,576]{2,1,0:T(8,128)(2,1)}, bf16[8,64,576]{2,1,0:T(8,128)(2,1)S(1)}, u32[]{:S(2)}, u32[]{:S(2)}) %collective-permute-start.7) | collective-permute-done | bytes 589856 | tf_op jit(solution)/shard_map/ppermute | solution.py:70
  105.4 5.1 %collective-permute-start.9 = (bf16[8,64,576]{2,1,0:T(8,128)(2,1)S(1)}, bf16[8,64,576]{2,1,0:T(8,128)(2,1)S(1)}, u32[]{:S(2)}, u32[]{:S(2)}) collective-permute-start(bf16[8,64,576]{2,1,0:T(8,128)(2,1)S(1)} %collective-permute-done.7), channel_id=1, source_target_pairs={{0,17},{1,16},{16,1},{17,0},{2,19},{3,18},{18,3},{19,2},{4,21},{5,... | collective-permute-start | bytes 1769480 | tf_op jit(solution)/shard_map/ppermute | solution.py:73
  113.1 11.2 %collective-permute-done.9 = bf16[8,64,576]{2,1,0:T(8,128)(2,1)S(1)} collective-permute-done((bf16[8,64,576]{2,1,0:T(8,128)(2,1)S(1)}, bf16[8,64,576]{2,1,0:T(8,128)(2,1)S(1)}, u32[]{:S(2)}, u32[]{:S(2)}) %collective-permute-start.9) | collective-permute-done | bytes 589856 | tf_op jit(solution)/shard_map/ppermute | solution.py:73
  135.4 2.8 %fusion.11 = (f32[512]{0:T(512)S(1)}, f32[512,1024]{1,0:T(8,128)S(1)}) fusion(s32[1024]{0:T(1024)S(1)} %add.229, s32[512]{0:T(512)S(1)} %le.25, bf16[1024,576]{1,0:T(8,128)(2,1)} %bitcast.142, bf16[64,8,576]{2,0,1:T(8,128)(2,1)} %copy-done.7), kind=kOutput, calls=%fused_computation.32 | convolution fusion | flops 606076416 | bytes 3874816 | tf_op jit(solution)/shard_map/rl,kl->rk/dot_general | solution.py:42
  138.9 3.9 %fusion = (f32[512]{0:T(512)S(1)}, f32[512,2048]{1,0:T(8,128)S(1)}) fusion(s32[2048]{0:T(1024)S(1)} %add.233, s32[512]{0:T(512)S(1)} %le.25, bf16[2048,576]{1,0:T(8,128)(2,1)} %bitcast.16, bf16[64,8,576]{2,0,1:T(8,128)(2,1)S(1)} %copy-done.8), kind=kOutput, calls=%fused_computation.4 | convolution fusion | flops 1212153344 | bytes 7155712 | tf_op jit(solution)/shard_map/rl,kl->rk/dot_general | solution.py:42
  146.4 3.1 %fusion.17 = f32[512,512]{1,0:T(8,128)S(1)} fusion(bf16[2048,576]{1,0:T(8,128)(2,1)} %bitcast.16, f32[512,2048]{1,0:T(8,128)S(1)} %get-tuple-element.53, f32[512]{0:T(512)S(1)} %get-tuple-element.52, s32[2048]{0:T(1024)S(1)} %add.233, s32[512]{0:T(512)S(1)} %le.25, f32[512]{0:T(512)S(1)} %get-tuple-element.11), kind=kOutput, calls=%fused_computation.43 | convolution fusion | flops 1080295424 | bytes 7354368 | tf_op jit(solution)/shard_map/dot_general | solution.py:48
  151.4 3.6 %broadcast_select_fusion = (bf16[1024,1792]{0,1:T(8,128)(2,1)S(1)}, bf16[1024,1792]{0,1:T(8,128)(2,1)S(1)}) fusion(bf16[1024,1792]{0,1:T(8,128)(2,1)} %all-gather.2.cloned.1.call-done, bf16[1024,1792]{0,1:T(8,128)(2,1)} %collective-permute-done.12, pred[]{:T(512)S(6)} %eq.8), kind=kLoop, calls=%fused_computation.2 | loop fusion | flops 3670016 | bytes 14680065 | tf_op jit(solution)/shard_map/jit(_where)/select_n | solution.py:176
  158.4 3.9 %collective-permute-start.13 = (f32[64,448]{1,0:T(8,128)S(1)}, f32[64,448]{1,0:T(8,128)S(1)}, u32[]{:S(2)}, u32[]{:S(2)}) collective-permute-start(f32[64,448]{1,0:T(8,128)S(1)} %get-tuple-element.18), channel_id=1, source_target_pairs={{0,1},{1,0},{2,3},{3,2},{4,5},{5,4},{6,7},{7,6},{8,9},{9,8},{10,11... | collective-permute-start | bytes 344072 | tf_op jit(solution)/shard_map/ppermute | solution.py:122
  162.3 2.7 %collective-permute-start.14 = (f32[64,448]{1,0:T(8,128)S(1)}, f32[64,448]{1,0:T(8,128)S(1)}, u32[]{:S(2)}, u32[]{:S(2)}) collective-permute-start(f32[64,448]{1,0:T(8,128)S(1)} %get-tuple-element.19), channel_id=1, source_target_pairs={{0,2},{1,3},{2,0},{3,1},{4,6},{5,7},{6,4},{7,5},{8,10},{9,11},{10,... | collective-permute-start | bytes 344072 | tf_op jit(solution)/shard_map/ppermute | solution.py:122
  165.1 4.1 %collective-permute-start.15 = (f32[64,448]{1,0:T(8,128)}, f32[64,448]{1,0:T(8,128)S(1)}, u32[]{:S(2)}, u32[]{:S(2)}) collective-permute-start(f32[64,448]{1,0:T(8,128)} %get-tuple-element.20), channel_id=1, source_target_pairs={{0,3},{1,2},{2,1},{3,0},{4,7},{5,6},{6,5},{7,4},{8,11},{9,10},{10,... | collective-permute-start | bytes 344072 | tf_op jit(solution)/shard_map/ppermute | solution.py:122
  169.2 3.3 %collective-permute-start.16 = (f32[64,448]{1,0:T(8,128)}, f32[64,448]{1,0:T(8,128)S(1)}, u32[]{:S(2)}, u32[]{:S(2)}) collective-permute-start(f32[64,448]{1,0:T(8,128)} %get-tuple-element.21), channel_id=1, source_target_pairs={{0,4},{1,5},{2,6},{3,7},{4,0},{5,1},{6,2},{7,3},{8,12},{9,13},{10,... | collective-permute-start | bytes 344072 | tf_op jit(solution)/shard_map/ppermute | solution.py:122
  172.5 5.5 %collective-permute-start.17 = (f32[64,448]{1,0:T(8,128)S(1)}, f32[64,448]{1,0:T(8,128)S(1)}, u32[]{:S(2)}, u32[]{:S(2)}) collective-permute-start(f32[64,448]{1,0:T(8,128)S(1)} %get-tuple-element.22), channel_id=1, source_target_pairs={{0,5},{1,4},{2,7},{3,6},{4,1},{5,0},{6,3},{7,2},{8,13},{9,12},{10,... | collective-permute-start | bytes 344072 | tf_op jit(solution)/shard_map/ppermute | solution.py:122
  180.5 5.6 %collective-permute-start.19 = (f32[64,448]{1,0:T(8,128)S(1)}, f32[64,448]{1,0:T(8,128)S(1)}, u32[]{:S(2)}, u32[]{:S(2)}) collective-permute-start(f32[64,448]{1,0:T(8,128)S(1)} %fusion.69), channel_id=1, source_target_pairs={{0,7},{1,6},{2,5},{3,4},{4,3},{5,2},{6,1},{7,0},{8,15},{9,14},{10,... | collective-permute-start | bytes 344072 | tf_op jit(solution)/shard_map/ppermute | solution.py:122
  186.9 4.1 %collective-permute-done.19 = f32[64,448]{1,0:T(8,128)S(1)} collective-permute-done((f32[64,448]{1,0:T(8,128)S(1)}, f32[64,448]{1,0:T(8,128)S(1)}, u32[]{:S(2)}, u32[]{:S(2)}) %collective-permute-start.19) | collective-permute-done | bytes 114720 | tf_op jit(solution)/shard_map/ppermute | solution.py:122
  (110 shorter events, 44.3 us)
Async XLA Ops:
  6.5 120.9 %copy-start = (bf16[512,1024]{1,0:T(8,128)(2,1)S(1)}, bf16[512,1024]{1,0:T(8,128)(2,1)}, u32[]{:S(2)}) copy-start(bf16[512,1024]{1,0:T(8,128)(2,1)} %param.13) | copy-start | bytes 3145732
  6.5 104.2 %copy-start.9 = (bf16[64,512]{1,0:T(8,128)(2,1)S(1)}, bf16[64,512]{1,0:T(8,128)(2,1)}, u32[]{:S(2)}) copy-start(bf16[64,512]{1,0:T(8,128)(2,1)} %param.9) | copy-start | bytes 196612
  6.5 126.3 %all-gather.2.cloned.1.call-start = ((), (), s32[]{:S(2)}) async-start(), calls=%async_computation | async-start | bytes 3899392 | tf_op jit(solution)/shard_map/all_gather | solution.py:173
  6.5 7.1 %collective-permute-start.11 = (bf16[1,56,1024]{2,1,0:T(8,128)(2,1)}, bf16[1,56,1024]{2,1,0:T(8,128)(2,1)S(1)}, u32[]{:S(2)}, u32[]{:S(2)}) collective-permute-start(bf16[1,56,1024]{2,1,0:T(8,128)(2,1)} %bitcast.146), channel_id=1, source_target_pairs={{0,16},{16,0},{1,17},{17,1},{2,18},{18,2},{3,19},{19,3},{4,20},{20... | collective-permute-start | bytes 344072 | tf_op jit(solution)/shard_map/ppermute | solution.py:70
  17.9 28.3 %collective-permute-start = (bf16[64,576]{1,0:T(8,128)(2,1)S(1)}, bf16[64,576]{1,0:T(8,128)(2,1)S(1)}, u32[]{:S(2)}, u32[]{:S(2)}) collective-permute-start(bf16[64,576]{1,0:T(8,128)(2,1)S(1)} %pad_maximum_fusion.3), channel_id=1, source_target_pairs={{0,64},{64,128},{128,192},{192,256},{256,320},{320,384},{384,448},... | collective-permute-start | bytes 221192 | tf_op jit(solution)/shard_map/ppermute | solution.py:101
  23.1 25.2 %collective-permute-start.1 = (bf16[64,576]{1,0:T(8,128)(2,1)S(1)}, bf16[64,576]{1,0:T(8,128)(2,1)S(1)}, u32[]{:S(2)}, u32[]{:S(2)}) collective-permute-start(bf16[64,576]{1,0:T(8,128)(2,1)S(1)} %pad_maximum_fusion.3), channel_id=1, source_target_pairs={{0,128},{64,192},{128,256},{192,320},{256,384},{320,448},{1,129},{... | collective-permute-start | bytes 221192 | tf_op jit(solution)/shard_map/ppermute | solution.py:101
  32.2 18.0 %collective-permute-start.2 = (bf16[64,576]{1,0:T(8,128)(2,1)S(1)}, bf16[64,576]{1,0:T(8,128)(2,1)S(1)}, u32[]{:S(2)}, u32[]{:S(2)}) collective-permute-start(bf16[64,576]{1,0:T(8,128)(2,1)S(1)} %pad_maximum_fusion.3), channel_id=1, source_target_pairs={{0,192},{64,256},{128,320},{192,384},{256,448},{1,193},{65,257},{1... | collective-permute-start | bytes 221192 | tf_op jit(solution)/shard_map/ppermute | solution.py:101
  40.4 10.5 %collective-permute-start.3 = (bf16[64,576]{1,0:T(8,128)(2,1)S(1)}, bf16[64,576]{1,0:T(8,128)(2,1)S(1)}, u32[]{:S(2)}, u32[]{:S(2)}) collective-permute-start(bf16[64,576]{1,0:T(8,128)(2,1)S(1)} %pad_maximum_fusion.3), channel_id=1, source_target_pairs={{0,256},{64,320},{128,384},{192,448},{1,257},{65,321},{129,385},{1... | collective-permute-start | bytes 221192 | tf_op jit(solution)/shard_map/ppermute | solution.py:101
  43.2 20.4 %collective-permute-start.4 = (bf16[64,576]{1,0:T(8,128)(2,1)S(1)}, bf16[64,576]{1,0:T(8,128)(2,1)S(1)}, u32[]{:S(2)}, u32[]{:S(2)}) collective-permute-start(bf16[64,576]{1,0:T(8,128)(2,1)S(1)} %pad_maximum_fusion.3), channel_id=1, source_target_pairs={{0,320},{64,384},{128,448},{1,321},{65,385},{129,449},{2,322},{66,... | collective-permute-start | bytes 221192 | tf_op jit(solution)/shard_map/ppermute | solution.py:101
  46.3 23.3 %collective-permute-start.5 = (bf16[64,576]{1,0:T(8,128)(2,1)S(1)}, bf16[64,576]{1,0:T(8,128)(2,1)S(1)}, u32[]{:S(2)}, u32[]{:S(2)}) collective-permute-start(bf16[64,576]{1,0:T(8,128)(2,1)S(1)} %pad_maximum_fusion.3), channel_id=1, source_target_pairs={{0,384},{64,448},{1,385},{65,449},{2,386},{66,450},{3,387},{67,451... | collective-permute-start | bytes 221192 | tf_op jit(solution)/shard_map/ppermute | solution.py:101
  48.2 26.0 %collective-permute-start.6 = (bf16[64,576]{1,0:T(8,128)(2,1)S(1)}, bf16[64,576]{1,0:T(8,128)(2,1)S(1)}, u32[]{:S(2)}, u32[]{:S(2)}) collective-permute-start(bf16[64,576]{1,0:T(8,128)(2,1)S(1)} %pad_maximum_fusion.3), channel_id=1, source_target_pairs={{0,448},{1,449},{2,450},{3,451},{4,452},{5,453},{6,454},{7,455},{8... | collective-permute-start | bytes 221192 | tf_op jit(solution)/shard_map/ppermute | solution.py:101
  74.9 30.5 %collective-permute-start.7 = (bf16[8,64,576]{2,1,0:T(8,128)(2,1)}, bf16[8,64,576]{2,1,0:T(8,128)(2,1)S(1)}, u32[]{:S(2)}, u32[]{:S(2)}) collective-permute-start(bf16[8,64,576]{2,1,0:T(8,128)(2,1)} %get-tuple-element.30), channel_id=1, source_target_pairs={{0,32},{32,0},{1,33},{33,1},{2,34},{34,2},{3,35},{35,3},{4,36},{36... | collective-permute-start | bytes 1769480 | tf_op jit(solution)/shard_map/ppermute | solution.py:70
  77.1 35.1 %collective-permute-start.8 = (bf16[8,64,576]{2,1,0:T(8,128)(2,1)}, bf16[8,64,576]{2,1,0:T(8,128)(2,1)S(1)}, u32[]{:S(2)}, u32[]{:S(2)}) collective-permute-start(bf16[8,64,576]{2,1,0:T(8,128)(2,1)} %get-tuple-element.30), channel_id=1, source_target_pairs={{0,16},{16,0},{1,17},{17,1},{2,18},{18,2},{3,19},{19,3},{4,20},{20... | collective-permute-start | bytes 1769480 | tf_op jit(solution)/shard_map/ppermute | solution.py:72
  105.4 19.8 %copy-start.1 = (bf16[8,64,576]{2,1,0:T(8,128)(2,1)}, bf16[8,64,576]{2,1,0:T(8,128)(2,1)S(1)}, u32[]{:S(2)}) copy-start(bf16[8,64,576]{2,1,0:T(8,128)(2,1)S(1)} %collective-permute-done.7) | copy-start | bytes 1769476
  105.4 18.8 %collective-permute-start.9 = (bf16[8,64,576]{2,1,0:T(8,128)(2,1)S(1)}, bf16[8,64,576]{2,1,0:T(8,128)(2,1)S(1)}, u32[]{:S(2)}, u32[]{:S(2)}) collective-permute-start(bf16[8,64,576]{2,1,0:T(8,128)(2,1)S(1)} %collective-permute-done.7), channel_id=1, source_target_pairs={{0,17},{1,16},{16,1},{17,0},{2,19},{3,18},{18,3},{19,2},{4,21},{5,... | collective-permute-start | bytes 1769480 | tf_op jit(solution)/shard_map/ppermute | solution.py:73
  125.2 13.7 %collective-permute-start.10 = (bf16[32,64,576]{2,1,0:T(8,128)(2,1)}, bf16[32,64,576]{2,1,0:T(8,128)(2,1)}, u32[]{:S(2)}, u32[]{:S(2)}) collective-permute-start(bf16[32,64,576]{2,1,0:T(8,128)(2,1)} %constant_dynamic-update-slice_fusion), channel_id=1, source_target_pairs={{0,8},{8,0},{1,9},{9,1},{2,10},{10,2},{3,11},{11,3},{4,12},{12,4},... | collective-permute-start | bytes 7077896 | tf_op jit(solution)/shard_map/ppermute | solution.py:70
  132.8 18.5 %collective-permute-start.12 = (bf16[1024,1792]{0,1:T(8,128)(2,1)}, bf16[1024,1792]{0,1:T(8,128)(2,1)}, u32[]{:S(2)}, u32[]{:S(2)}) collective-permute-start(bf16[1024,1792]{0,1:T(8,128)(2,1)} %all-gather.2.cloned.1.call-done), channel_id=1, source_target_pairs={{0,8},{8,0},{1,9},{9,1},{2,10},{10,2},{3,11},{11,3},{4,12},{12,4},... | collective-permute-start | bytes 11010056 | tf_op jit(solution)/shard_map/ppermute | solution.py:174
  158.4 19.7 %collective-permute-start.13 = (f32[64,448]{1,0:T(8,128)S(1)}, f32[64,448]{1,0:T(8,128)S(1)}, u32[]{:S(2)}, u32[]{:S(2)}) collective-permute-start(f32[64,448]{1,0:T(8,128)S(1)} %get-tuple-element.18), channel_id=1, source_target_pairs={{0,1},{1,0},{2,3},{3,2},{4,5},{5,4},{6,7},{7,6},{8,9},{9,8},{10,11... | collective-permute-start | bytes 344072 | tf_op jit(solution)/shard_map/ppermute | solution.py:122
  162.3 18.2 %collective-permute-start.14 = (f32[64,448]{1,0:T(8,128)S(1)}, f32[64,448]{1,0:T(8,128)S(1)}, u32[]{:S(2)}, u32[]{:S(2)}) collective-permute-start(f32[64,448]{1,0:T(8,128)S(1)} %get-tuple-element.19), channel_id=1, source_target_pairs={{0,2},{1,3},{2,0},{3,1},{4,6},{5,7},{6,4},{7,5},{8,10},{9,11},{10,... | collective-permute-start | bytes 344072 | tf_op jit(solution)/shard_map/ppermute | solution.py:122
  165.1 21.0 %collective-permute-start.15 = (f32[64,448]{1,0:T(8,128)}, f32[64,448]{1,0:T(8,128)S(1)}, u32[]{:S(2)}, u32[]{:S(2)}) collective-permute-start(f32[64,448]{1,0:T(8,128)} %get-tuple-element.20), channel_id=1, source_target_pairs={{0,3},{1,2},{2,1},{3,0},{4,7},{5,6},{6,5},{7,4},{8,11},{9,10},{10,... | collective-permute-start | bytes 344072 | tf_op jit(solution)/shard_map/ppermute | solution.py:122
  169.2 17.0 %collective-permute-start.16 = (f32[64,448]{1,0:T(8,128)}, f32[64,448]{1,0:T(8,128)S(1)}, u32[]{:S(2)}, u32[]{:S(2)}) collective-permute-start(f32[64,448]{1,0:T(8,128)} %get-tuple-element.21), channel_id=1, source_target_pairs={{0,4},{1,5},{2,6},{3,7},{4,0},{5,1},{6,2},{7,3},{8,12},{9,13},{10,... | collective-permute-start | bytes 344072 | tf_op jit(solution)/shard_map/ppermute | solution.py:122
  172.5 13.7 %collective-permute-start.17 = (f32[64,448]{1,0:T(8,128)S(1)}, f32[64,448]{1,0:T(8,128)S(1)}, u32[]{:S(2)}, u32[]{:S(2)}) collective-permute-start(f32[64,448]{1,0:T(8,128)S(1)} %get-tuple-element.22), channel_id=1, source_target_pairs={{0,5},{1,4},{2,7},{3,6},{4,1},{5,0},{6,3},{7,2},{8,13},{9,12},{10,... | collective-permute-start | bytes 344072 | tf_op jit(solution)/shard_map/ppermute | solution.py:122
  178.1 8.8 %collective-permute-start.18 = (f32[64,448]{1,0:T(8,128)S(1)}, f32[64,448]{1,0:T(8,128)S(1)}, u32[]{:S(2)}, u32[]{:S(2)}) collective-permute-start(f32[64,448]{1,0:T(8,128)S(1)} %get-tuple-element.23), channel_id=1, source_target_pairs={{0,6},{1,7},{2,4},{3,5},{4,2},{5,3},{6,0},{7,1},{8,14},{9,15},{10,... | collective-permute-start | bytes 344072 | tf_op jit(solution)/shard_map/ppermute | solution.py:122
  180.5 10.5 %collective-permute-start.19 = (f32[64,448]{1,0:T(8,128)S(1)}, f32[64,448]{1,0:T(8,128)S(1)}, u32[]{:S(2)}, u32[]{:S(2)}) collective-permute-start(f32[64,448]{1,0:T(8,128)S(1)} %fusion.69), channel_id=1, source_target_pairs={{0,7},{1,6},{2,5},{3,4},{4,3},{5,2},{6,1},{7,0},{8,15},{9,14},{10,... | collective-permute-start | bytes 344072 | tf_op jit(solution)/shard_map/ppermute | solution.py:122
  (9 other events, 33.1 us)
Sparse Core Ops, SparseCore 0:
  15.4 109.7 all-gather.1

commit v8 on v6

--- a/solution.py
+++ b/solution.py
@@ -99,12 +99,20 @@
 
 
 def scatter_sum(blocks):
-    groups = lax.axis_size(HEAD)
-    me = lax.axis_index(HEAD)
-    total = blocks[me]
-    for shift in range(1, groups):
+    rows = lax.axis_size("yh")
+    columns = lax.axis_size("x")
+    x = lax.axis_index("x")
+    yh = lax.axis_index("yh")
+    blocks = blocks.reshape((columns, rows) + blocks.shape[1:])
+    row_sums = blocks[x]
+    for shift in range(1, columns):
+        row_sums = row_sums + lax.ppermute(
+            blocks[x ^ shift], "x", [(i, i ^ shift) for i in range(columns)]
+        )
+    total = row_sums[yh]
+    for shift in range(1, rows):
         total = total + lax.ppermute(
-            blocks[me ^ shift], HEAD, [(i, i ^ shift) for i in range(groups)]
+            row_sums[yh ^ shift], "yh", [(i, i ^ shift) for i in range(rows)]
         )
     return total
 

time: 201 us -> 199 us (0.990)
  the two profiles are of different devices: /device:TPU:40 before, /device:TPU:6 now
where the time goes in v8:
time: 199 us; the launch traced here: 195 us
  waiting for transfers between devices  78.1 us (39%)
  starting transfers between devices  61.8 us (31%)
  local copies, waits for them, and re-layouts  16.1 us (8%)
  between operations  13.9 us (7%)
  other arithmetic  13.1 us (7%)
  matrix products  12.4 us (6%)
    ppermute x7, starting transfers between devices, gather_earlier_keys(): lax.ppermute(local, 'zh', [(i, i + shift) for i in range(cubes - shift)])  29.3 us
    ppermute x3, waiting for transfers between devices, exchange(): return lax.ppermute(acc, axis, pairs)  29 us
    ppermute x7, waiting for transfers between devices, gather_earlier_keys(): lax.ppermute(local, 'zh', [(i, i + shift) for i in range(cubes - shift)])  21.6 us
    ppermute x1, waiting for transfers between devices, exchange(): far = lax.ppermute(acc[half:], ('yl', 'yh'), [(i, i ^ 3) for i in range(4)])  11.5 us
    ppermute x3, waiting for transfers between devices, scatter_sum(): lax.ppermute(blocks[x ^ shift], 'x', [(i, i ^ shift) for i in range(colum...  11 us
    ppermute x3, starting transfers between devices, scatter_sum(): lax.ppermute(blocks[x ^ shift], 'x', [(i, i ^ shift) for i in range(colum...  10.4 us
    unnamed x24, local copies, waits for them, and re-layouts  9.72 us
    ppermute x3, starting transfers between devices, exchange(): return lax.ppermute(acc, axis, pairs)  7.42 us
  transfers between devices with their start and end apart: 18, of which 11 were waited for; matrix products, arithmetic and copies ran while one was open for 15% of the time, Pallas kernels for 0%

profile of v8, /device:TPU:6, one launch (start us, length us, event | category | flops | bytes accessed | tf_op | source)
XLA Modules:
  0.0 195.4 jit_solution(2276236218822765204)
XLA Ops:
  6.5 3.6 %collective-permute-start.11 = (bf16[1,56,1024]{2,1,0:T(8,128)(2,1)}, bf16[1,56,1024]{2,1,0:T(8,128)(2,1)S(1)}, u32[]{:S(2)}, u32[]{:S(2)}) collective-permute-start(bf16[1,56,1024]{2,1,0:T(8,128)(2,1)} %bitcast.123), channel_id=1, source_target_pairs={{0,16},{16,0},{1,17},{17,1},{2,18},{18,2},{3,19},{19,3},{4,20},{20... | collective-permute-start | bytes 344072 | tf_op jit(solution)/shard_map/ppermute | solution.py:57
  10.2 3.5 %collective-permute-done.11 = bf16[1,56,1024]{2,1,0:T(8,128)(2,1)S(1)} collective-permute-done((bf16[1,56,1024]{2,1,0:T(8,128)(2,1)}, bf16[1,56,1024]{2,1,0:T(8,128)(2,1)S(1)}, u32[]{:S(2)}, u32[]{:S(2)}) %collective-permute-start.11) | collective-permute-done | bytes 114720 | tf_op jit(solution)/shard_map/ppermute | solution.py:57
  17.9 5.2 %collective-permute-start = (bf16[64,576]{1,0:T(8,128)(2,1)S(1)}, bf16[64,576]{1,0:T(8,128)(2,1)S(1)}, u32[]{:S(2)}, u32[]{:S(2)}) collective-permute-start(bf16[64,576]{1,0:T(8,128)(2,1)S(1)} %pad_maximum_fusion.3), channel_id=1, source_target_pairs={{0,64},{64,128},{128,192},{192,256},{256,320},{320,384},{384,448},... | collective-permute-start | bytes 221192 | tf_op jit(solution)/shard_map/ppermute | solution.py:88
  23.1 9.1 %collective-permute-start.1 = (bf16[64,576]{1,0:T(8,128)(2,1)S(1)}, bf16[64,576]{1,0:T(8,128)(2,1)S(1)}, u32[]{:S(2)}, u32[]{:S(2)}) collective-permute-start(bf16[64,576]{1,0:T(8,128)(2,1)S(1)} %pad_maximum_fusion.3), channel_id=1, source_target_pairs={{0,128},{64,192},{128,256},{192,320},{256,384},{320,448},{1,129},{... | collective-permute-start | bytes 221192 | tf_op jit(solution)/shard_map/ppermute | solution.py:88
  32.2 8.2 %collective-permute-start.2 = (bf16[64,576]{1,0:T(8,128)(2,1)S(1)}, bf16[64,576]{1,0:T(8,128)(2,1)S(1)}, u32[]{:S(2)}, u32[]{:S(2)}) collective-permute-start(bf16[64,576]{1,0:T(8,128)(2,1)S(1)} %pad_maximum_fusion.3), channel_id=1, source_target_pairs={{0,192},{64,256},{128,320},{192,384},{256,448},{1,193},{65,257},{1... | collective-permute-start | bytes 221192 | tf_op jit(solution)/shard_map/ppermute | solution.py:88
  40.4 2.8 %collective-permute-start.3 = (bf16[64,576]{1,0:T(8,128)(2,1)S(1)}, bf16[64,576]{1,0:T(8,128)(2,1)S(1)}, u32[]{:S(2)}, u32[]{:S(2)}) collective-permute-start(bf16[64,576]{1,0:T(8,128)(2,1)S(1)} %pad_maximum_fusion.3), channel_id=1, source_target_pairs={{0,256},{64,320},{128,384},{192,448},{1,257},{65,321},{129,385},{1... | collective-permute-start | bytes 221192 | tf_op jit(solution)/shard_map/ppermute | solution.py:88
  51.4 12.3 %collective-permute-done.4 = bf16[64,576]{1,0:T(8,128)(2,1)S(1)} collective-permute-done((bf16[64,576]{1,0:T(8,128)(2,1)S(1)}, bf16[64,576]{1,0:T(8,128)(2,1)S(1)}, u32[]{:S(2)}, u32[]{:S(2)}) %collective-permute-start.4) | collective-permute-done | bytes 73760 | tf_op jit(solution)/shard_map/ppermute | solution.py:88
  64.3 5.3 %collective-permute-done.5 = bf16[64,576]{1,0:T(8,128)(2,1)S(1)} collective-permute-done((bf16[64,576]{1,0:T(8,128)(2,1)S(1)}, bf16[64,576]{1,0:T(8,128)(2,1)S(1)}, u32[]{:S(2)}, u32[]{:S(2)}) %collective-permute-start.5) | collective-permute-done | bytes 73760 | tf_op jit(solution)/shard_map/ppermute | solution.py:88
  70.3 4.0 %collective-permute-done.6 = bf16[64,576]{1,0:T(8,128)(2,1)S(1)} collective-permute-done((bf16[64,576]{1,0:T(8,128)(2,1)S(1)}, bf16[64,576]{1,0:T(8,128)(2,1)S(1)}, u32[]{:S(2)}, u32[]{:S(2)}) %collective-permute-start.6) | collective-permute-done | bytes 73760 | tf_op jit(solution)/shard_map/ppermute | solution.py:88
  76.8 3.5 %collective-permute-start.8 = (bf16[8,64,576]{2,1,0:T(8,128)(2,1)S(1)}, bf16[8,64,576]{2,1,0:T(8,128)(2,1)S(1)}, u32[]{:S(2)}, u32[]{:S(2)}) collective-permute-start(bf16[8,64,576]{2,1,0:T(8,128)(2,1)S(1)} %get-tuple-element.26), channel_id=1, source_target_pairs={{0,16},{16,0},{1,17},{17,1},{2,18},{18,2},{3,19},{19,3},{4,20},{20... | collective-permute-start | bytes 1769480 | tf_op jit(solution)/shard_map/ppermute | solution.py:59
  80.3 24.7 %collective-permute-done.7 = bf16[8,64,576]{2,1,0:T(8,128)(2,1)S(1)} collective-permute-done((bf16[8,64,576]{2,1,0:T(8,128)(2,1)S(1)}, bf16[8,64,576]{2,1,0:T(8,128)(2,1)S(1)}, u32[]{:S(2)}, u32[]{:S(2)}) %collective-permute-start.7) | collective-permute-done | bytes 589856 | tf_op jit(solution)/shard_map/ppermute | solution.py:57
  105.0 4.8 %collective-permute-start.9 = (bf16[8,64,576]{2,1,0:T(8,128)(2,1)S(1)}, bf16[8,64,576]{2,1,0:T(8,128)(2,1)S(1)}, u32[]{:S(2)}, u32[]{:S(2)}) collective-permute-start(bf16[8,64,576]{2,1,0:T(8,128)(2,1)S(1)} %collective-permute-done.7), channel_id=1, source_target_pairs={{0,17},{1,16},{16,1},{17,0},{2,19},{3,18},{18,3},{19,2},{4,21},{5,... | collective-permute-start | bytes 1769480 | tf_op jit(solution)/shard_map/ppermute | solution.py:60
  111.9 11.5 %collective-permute-done.9 = bf16[8,64,576]{2,1,0:T(8,128)(2,1)S(1)} collective-permute-done((bf16[8,64,576]{2,1,0:T(8,128)(2,1)S(1)}, bf16[8,64,576]{2,1,0:T(8,128)(2,1)S(1)}, u32[]{:S(2)}, u32[]{:S(2)}) %collective-permute-start.9) | collective-permute-done | bytes 589856 | tf_op jit(solution)/shard_map/ppermute | solution.py:60
  133.9 3.5 %constant_dynamic-update-slice_fusion.3 = bf16[64,64,576]{2,1,0:T(8,128)(2,1)} fusion(bf16[64,64,576]{2,1,0:T(8,128)(2,1)} %copy-done.2, bf16[32,64,576]{2,1,0:T(8,128)(2,1)} %collective-permute-done.10), kind=kLoop, calls=%fused_computation.74 | loop fusion | bytes 5242880 | tf_op jit(solution)/shard_map/concatenate | solution.py:96
  137.4 6.4 %fusion = (f32[512]{0:T(512)S(1)}, f32[512,4096]{1,0:T(8,128)S(1)}) fusion(s32[4096]{0:T(1024)S(1)} %add.95, s32[512]{0:T(512)S(1)} %le.16, bf16[4096,576]{1,0:T(8,128)(2,1)} %bitcast.124, bf16[64,8,576]{2,0,1:T(8,128)(2,1)S(1)} %pad_maximum_fusion.1), kind=kOutput, calls=%fused_computation.2 | convolution fusion | flops 2424307200 | bytes 13717504 | tf_op jit(solution)/shard_map/rl,kl->rk/dot_general | solution.py:42
  143.8 2.6 %fusion.1 = f32[512]{0:T(512)S(1)} fusion(f32[512,4096]{1,0:T(8,128)S(1)} %get-tuple-element.53, f32[512]{0:T(512)S(1)} %get-tuple-element.52, s32[4096]{0:T(1024)S(1)} %add.95, s32[512]{0:T(512)S(1)} %le.16), kind=kLoop, calls=%fused_computation.3 | loop fusion | flops 12582400 | bytes 8411136 | tf_op jit(solution)/shard_map/reduce_sum | solution.py:47
  149.6 3.6 %broadcast_select_fusion.1 = (bf16[1024,1792]{0,1:T(8,128)(2,1)S(1)}, bf16[1024,1792]{0,1:T(8,128)(2,1)S(1)}) fusion(bf16[1024,1792]{0,1:T(8,128)(2,1)} %collective-permute-done.12, bf16[1024,1792]{0,1:T(8,128)(2,1)} %all-gather.2.cloned.1.call-done, pred[]{:T(512)S(6)} %eq.8), kind=kLoop, calls=%fused_computation.13 | loop fusion | flops 3670016 | bytes 14680065 | tf_op jit(solution)/shard_map/jit(_where)/select_n | solution.py:166
  156.2 2.7 %collective-permute-start.13 = (f32[2,64,448]{2,1,0:T(8,128)S(1)}, f32[2,64,448]{2,1,0:T(8,128)S(1)}, u32[]{:S(2)}, u32[]{:S(2)}) collective-permute-start(f32[2,64,448]{2,1,0:T(8,128)S(1)} %get-tuple-element.9), channel_id=1, source_target_pairs={{0,2},{2,0},{4,6},{6,4},{1,3},{3,1},{5,7},{7,5},{8,10},{10,8},{12,... | collective-permute-start | bytes 688136 | tf_op jit(solution)/shard_map/ppermute | solution.py:109
  158.9 3.0 %collective-permute-start.14 = (f32[2,64,448]{2,1,0:T(8,128)S(1)}, f32[2,64,448]{2,1,0:T(8,128)S(1)}, u32[]{:S(2)}, u32[]{:S(2)}) collective-permute-start(f32[2,64,448]{2,1,0:T(8,128)S(1)} %get-tuple-element.11), channel_id=1, source_target_pairs={{0,4},{2,6},{4,0},{6,2},{1,5},{3,7},{5,1},{7,3},{8,12},{10,14},{12... | collective-permute-start | bytes 688136 | tf_op jit(solution)/shard_map/ppermute | solution.py:109
  161.9 4.7 %collective-permute-start.15 = (f32[2,64,448]{2,1,0:T(8,128)S(1)}, f32[2,64,448]{2,1,0:T(8,128)}, u32[]{:S(2)}, u32[]{:S(2)}) collective-permute-start(f32[2,64,448]{2,1,0:T(8,128)S(1)} %get-tuple-element.10), channel_id=1, source_target_pairs={{0,6},{2,4},{4,2},{6,0},{1,7},{3,5},{5,3},{7,1},{8,14},{10,12},{12... | collective-permute-start | bytes 688136 | tf_op jit(solution)/shard_map/ppermute | solution.py:109
  167.2 4.8 %collective-permute-done.14 = f32[2,64,448]{2,1,0:T(8,128)S(1)} collective-permute-done((f32[2,64,448]{2,1,0:T(8,128)S(1)}, f32[2,64,448]{2,1,0:T(8,128)S(1)}, u32[]{:S(2)}, u32[]{:S(2)}) %collective-permute-start.14) | collective-permute-done | bytes 229408 | tf_op jit(solution)/shard_map/ppermute | solution.py:109
  172.0 5.6 %collective-permute-done.15 = f32[2,64,448]{2,1,0:T(8,128)} collective-permute-done((f32[2,64,448]{2,1,0:T(8,128)S(1)}, f32[2,64,448]{2,1,0:T(8,128)}, u32[]{:S(2)}, u32[]{:S(2)}) %collective-permute-start.15) | collective-permute-done | bytes 229408 | tf_op jit(solution)/shard_map/ppermute | solution.py:109
  178.7 3.8 %collective-permute-start.16 = (f32[64,448]{1,0:T(8,128)S(1)}, f32[64,448]{1,0:T(8,128)S(1)}, u32[]{:S(2)}, u32[]{:S(2)}) collective-permute-start(f32[64,448]{1,0:T(8,128)S(1)} %dynamic-slice_bitcast_fusion.3), channel_id=1, source_target_pairs={{0,1},{1,0},{2,3},{3,2},{4,5},{5,4},{6,7},{7,6},{8,9},{9,8},{10,11... | collective-permute-start | bytes 344072 | tf_op jit(solution)/shard_map/ppermute | solution.py:114
  182.5 5.1 %collective-permute-done.16 = f32[64,448]{1,0:T(8,128)S(1)} collective-permute-done((f32[64,448]{1,0:T(8,128)S(1)}, f32[64,448]{1,0:T(8,128)S(1)}, u32[]{:S(2)}, u32[]{:S(2)}) %collective-permute-start.16) | collective-permute-done | bytes 114720 | tf_op jit(solution)/shard_map/ppermute | solution.py:114
  (82 shorter events, 37.3 us)
Async XLA Ops:
  6.5 126.0 %copy-start = (bf16[512,1024]{1,0:T(8,128)(2,1)S(1)}, bf16[512,1024]{1,0:T(8,128)(2,1)}, u32[]{:S(2)}) copy-start(bf16[512,1024]{1,0:T(8,128)(2,1)} %param.13) | copy-start | bytes 3145732
  6.5 122.1 %copy-start.1 = (bf16[64,512]{1,0:T(8,128)(2,1)S(1)}, bf16[64,512]{1,0:T(8,128)(2,1)}, u32[]{:S(2)}) copy-start(bf16[64,512]{1,0:T(8,128)(2,1)} %param.9) | copy-start | bytes 196612
  6.5 123.1 %all-gather.2.cloned.1.call-start = ((), (), s32[]{:S(2)}) async-start(), calls=%async_computation | async-start | bytes 3899392 | tf_op jit(solution)/shard_map/all_gather | solution.py:163
  6.5 7.1 %collective-permute-start.11 = (bf16[1,56,1024]{2,1,0:T(8,128)(2,1)}, bf16[1,56,1024]{2,1,0:T(8,128)(2,1)S(1)}, u32[]{:S(2)}, u32[]{:S(2)}) collective-permute-start(bf16[1,56,1024]{2,1,0:T(8,128)(2,1)} %bitcast.123), channel_id=1, source_target_pairs={{0,16},{16,0},{1,17},{17,1},{2,18},{18,2},{3,19},{19,3},{4,20},{20... | collective-permute-start | bytes 344072 | tf_op jit(solution)/shard_map/ppermute | solution.py:57
  17.9 28.1 %collective-permute-start = (bf16[64,576]{1,0:T(8,128)(2,1)S(1)}, bf16[64,576]{1,0:T(8,128)(2,1)S(1)}, u32[]{:S(2)}, u32[]{:S(2)}) collective-permute-start(bf16[64,576]{1,0:T(8,128)(2,1)S(1)} %pad_maximum_fusion.3), channel_id=1, source_target_pairs={{0,64},{64,128},{128,192},{192,256},{256,320},{320,384},{384,448},... | collective-permute-start | bytes 221192 | tf_op jit(solution)/shard_map/ppermute | solution.py:88
  23.1 24.9 %collective-permute-start.1 = (bf16[64,576]{1,0:T(8,128)(2,1)S(1)}, bf16[64,576]{1,0:T(8,128)(2,1)S(1)}, u32[]{:S(2)}, u32[]{:S(2)}) collective-permute-start(bf16[64,576]{1,0:T(8,128)(2,1)S(1)} %pad_maximum_fusion.3), channel_id=1, source_target_pairs={{0,128},{64,192},{128,256},{192,320},{256,384},{320,448},{1,129},{... | collective-permute-start | bytes 221192 | tf_op jit(solution)/shard_map/ppermute | solution.py:88
  32.2 17.9 %collective-permute-start.2 = (bf16[64,576]{1,0:T(8,128)(2,1)S(1)}, bf16[64,576]{1,0:T(8,128)(2,1)S(1)}, u32[]{:S(2)}, u32[]{:S(2)}) collective-permute-start(bf16[64,576]{1,0:T(8,128)(2,1)S(1)} %pad_maximum_fusion.3), channel_id=1, source_target_pairs={{0,192},{64,256},{128,320},{192,384},{256,448},{1,193},{65,257},{1... | collective-permute-start | bytes 221192 | tf_op jit(solution)/shard_map/ppermute | solution.py:88
  40.4 10.3 %collective-permute-start.3 = (bf16[64,576]{1,0:T(8,128)(2,1)S(1)}, bf16[64,576]{1,0:T(8,128)(2,1)S(1)}, u32[]{:S(2)}, u32[]{:S(2)}) collective-permute-start(bf16[64,576]{1,0:T(8,128)(2,1)S(1)} %pad_maximum_fusion.3), channel_id=1, source_target_pairs={{0,256},{64,320},{128,384},{192,448},{1,257},{65,321},{129,385},{1... | collective-permute-start | bytes 221192 | tf_op jit(solution)/shard_map/ppermute | solution.py:88
  43.3 20.4 %collective-permute-start.4 = (bf16[64,576]{1,0:T(8,128)(2,1)S(1)}, bf16[64,576]{1,0:T(8,128)(2,1)S(1)}, u32[]{:S(2)}, u32[]{:S(2)}) collective-permute-start(bf16[64,576]{1,0:T(8,128)(2,1)S(1)} %pad_maximum_fusion.3), channel_id=1, source_target_pairs={{0,320},{64,384},{128,448},{1,321},{65,385},{129,449},{2,322},{66,... | collective-permute-start | bytes 221192 | tf_op jit(solution)/shard_map/ppermute | solution.py:88
  46.0 23.6 %collective-permute-start.5 = (bf16[64,576]{1,0:T(8,128)(2,1)S(1)}, bf16[64,576]{1,0:T(8,128)(2,1)S(1)}, u32[]{:S(2)}, u32[]{:S(2)}) collective-permute-start(bf16[64,576]{1,0:T(8,128)(2,1)S(1)} %pad_maximum_fusion.3), channel_id=1, source_target_pairs={{0,384},{64,448},{1,385},{65,449},{2,386},{66,450},{3,387},{67,451... | collective-permute-start | bytes 221192 | tf_op jit(solution)/shard_map/ppermute | solution.py:88
  48.0 84.5 %copy-start.4 = (bf16[64,1024]{1,0:T(8,128)(2,1)S(1)}, bf16[64,1024]{1,0:T(8,128)(2,1)}, u32[]{:S(2)}) copy-start(bf16[64,1024]{1,0:T(8,128)(2,1)} %param.8) | copy-start | bytes 393220
  48.0 26.2 %collective-permute-start.6 = (bf16[64,576]{1,0:T(8,128)(2,1)S(1)}, bf16[64,576]{1,0:T(8,128)(2,1)S(1)}, u32[]{:S(2)}, u32[]{:S(2)}) collective-permute-start(bf16[64,576]{1,0:T(8,128)(2,1)S(1)} %pad_maximum_fusion.3), channel_id=1, source_target_pairs={{0,448},{1,449},{2,450},{3,451},{4,452},{5,453},{6,454},{7,455},{8... | collective-permute-start | bytes 221192 | tf_op jit(solution)/shard_map/ppermute | solution.py:88
  74.9 30.2 %collective-permute-start.7 = (bf16[8,64,576]{2,1,0:T(8,128)(2,1)S(1)}, bf16[8,64,576]{2,1,0:T(8,128)(2,1)S(1)}, u32[]{:S(2)}, u32[]{:S(2)}) collective-permute-start(bf16[8,64,576]{2,1,0:T(8,128)(2,1)S(1)} %get-tuple-element.26), channel_id=1, source_target_pairs={{0,32},{32,0},{1,33},{33,1},{2,34},{34,2},{3,35},{35,3},{4,36},{36... | collective-permute-start | bytes 1769480 | tf_op jit(solution)/shard_map/ppermute | solution.py:57
  76.8 34.1 %collective-permute-start.8 = (bf16[8,64,576]{2,1,0:T(8,128)(2,1)S(1)}, bf16[8,64,576]{2,1,0:T(8,128)(2,1)S(1)}, u32[]{:S(2)}, u32[]{:S(2)}) collective-permute-start(bf16[8,64,576]{2,1,0:T(8,128)(2,1)S(1)} %get-tuple-element.26), channel_id=1, source_target_pairs={{0,16},{16,0},{1,17},{17,1},{2,18},{18,2},{3,19},{19,3},{4,20},{20... | collective-permute-start | bytes 1769480 | tf_op jit(solution)/shard_map/ppermute | solution.py:59
  105.0 18.4 %collective-permute-start.9 = (bf16[8,64,576]{2,1,0:T(8,128)(2,1)S(1)}, bf16[8,64,576]{2,1,0:T(8,128)(2,1)S(1)}, u32[]{:S(2)}, u32[]{:S(2)}) collective-permute-start(bf16[8,64,576]{2,1,0:T(8,128)(2,1)S(1)} %collective-permute-done.7), channel_id=1, source_target_pairs={{0,17},{1,16},{16,1},{17,0},{2,19},{3,18},{18,3},{19,2},{4,21},{5,... | collective-permute-start | bytes 1769480 | tf_op jit(solution)/shard_map/ppermute | solution.py:60
  126.7 7.1 %collective-permute-start.10 = (bf16[32,64,576]{2,1,0:T(8,128)(2,1)}, bf16[32,64,576]{2,1,0:T(8,128)(2,1)}, u32[]{:S(2)}, u32[]{:S(2)}) collective-permute-start(bf16[32,64,576]{2,1,0:T(8,128)(2,1)} %get-tuple-element.12), channel_id=1, source_target_pairs={{0,8},{8,0},{1,9},{9,1},{2,10},{10,2},{3,11},{11,3},{4,12},{12,4},... | collective-permute-start | bytes 7077896 | tf_op jit(solution)/shard_map/ppermute | solution.py:57
  129.6 20.0 %collective-permute-start.12 = (bf16[1024,1792]{0,1:T(8,128)(2,1)}, bf16[1024,1792]{0,1:T(8,128)(2,1)}, u32[]{:S(2)}, u32[]{:S(2)}) collective-permute-start(bf16[1024,1792]{0,1:T(8,128)(2,1)} %all-gather.2.cloned.1.call-done), channel_id=1, source_target_pairs={{0,8},{8,0},{1,9},{9,1},{2,10},{10,2},{3,11},{11,3},{4,12},{12,4},... | collective-permute-start | bytes 11010056 | tf_op jit(solution)/shard_map/ppermute | solution.py:164
  137.4 9.0 %slice-start = ((s8[5242880]{0:T(1024)(128)(4,1)}), s8[4194304]{0:T(1024)(128)(4,1)S(1)}, s32[]{:S(2)}) async-start(s8[5242880]{0:T(1024)(128)(4,1)} %bitcast.125), calls=%async_computation.1 | async-start | bytes 8388608
  137.4 9.0 %slice-start.1 = ((s8[5242880]{0:T(1024)(128)(4,1)}), s8[1048576]{0:T(1024)(128)(4,1)S(1)}, s32[]{:S(2)}) async-start(s8[5242880]{0:T(1024)(128)(4,1)} %bitcast.125), calls=%async_computation.2 | async-start | bytes 2097152
  146.4 2.6 %copy-start.3 = (bf16[512,1024]{1,0:T(8,128)(2,1)S(1)}, bf16[512,1024]{1,0:T(8,128)(2,1)}, u32[]{:S(2)}) copy-start(bf16[512,1024]{1,0:T(8,128)(2,1)} %param.14) | copy-start | bytes 3145732
  156.2 11.1 %collective-permute-start.13 = (f32[2,64,448]{2,1,0:T(8,128)S(1)}, f32[2,64,448]{2,1,0:T(8,128)S(1)}, u32[]{:S(2)}, u32[]{:S(2)}) collective-permute-start(f32[2,64,448]{2,1,0:T(8,128)S(1)} %get-tuple-element.9), channel_id=1, source_target_pairs={{0,2},{2,0},{4,6},{6,4},{1,3},{3,1},{5,7},{7,5},{8,10},{10,8},{12,... | collective-permute-start | bytes 688136 | tf_op jit(solution)/shard_map/ppermute | solution.py:109
  158.9 13.1 %collective-permute-start.14 = (f32[2,64,448]{2,1,0:T(8,128)S(1)}, f32[2,64,448]{2,1,0:T(8,128)S(1)}, u32[]{:S(2)}, u32[]{:S(2)}) collective-permute-start(f32[2,64,448]{2,1,0:T(8,128)S(1)} %get-tuple-element.11), channel_id=1, source_target_pairs={{0,4},{2,6},{4,0},{6,2},{1,5},{3,7},{5,1},{7,3},{8,12},{10,14},{12... | collective-permute-start | bytes 688136 | tf_op jit(solution)/shard_map/ppermute | solution.py:109
  161.9 15.7 %collective-permute-start.15 = (f32[2,64,448]{2,1,0:T(8,128)S(1)}, f32[2,64,448]{2,1,0:T(8,128)}, u32[]{:S(2)}, u32[]{:S(2)}) collective-permute-start(f32[2,64,448]{2,1,0:T(8,128)S(1)} %get-tuple-element.10), channel_id=1, source_target_pairs={{0,6},{2,4},{4,2},{6,0},{1,7},{3,5},{5,3},{7,1},{8,14},{10,12},{12... | collective-permute-start | bytes 688136 | tf_op jit(solution)/shard_map/ppermute | solution.py:109
  178.7 8.8 %collective-permute-start.16 = (f32[64,448]{1,0:T(8,128)S(1)}, f32[64,448]{1,0:T(8,128)S(1)}, u32[]{:S(2)}, u32[]{:S(2)}) collective-permute-start(f32[64,448]{1,0:T(8,128)S(1)} %dynamic-slice_bitcast_fusion.3), channel_id=1, source_target_pairs={{0,1},{1,0},{2,3},{3,2},{4,5},{5,4},{6,7},{7,6},{8,9},{9,8},{10,11... | collective-permute-start | bytes 344072 | tf_op jit(solution)/shard_map/ppermute | solution.py:114
  (1 other events, 2.3 us)
Sparse Core Ops, SparseCore 0:
  15.4 109.5 all-gather.1

commit v9 on v8

--- a/solution.py
+++ b/solution.py
@@ -3,6 +3,7 @@
 import jax
 import jax.numpy as jnp
 from jax import lax
+from jax.experimental import pallas as pl
 from jax.sharding import Mesh
 from jax.sharding import PartitionSpec as P
 
@@ -37,18 +38,53 @@
     )
 
 
-def attend(query_rows, query_index, keys, key_index):
+def attention_kernel(q_ref, qi_ref, ka_ref, ia_ref, kb_ref, ib_ref, o_ref):
     scale = 1.0 / math.sqrt(NOPE + ROPE)
-    scores = jnp.einsum("rl,kl->rk", query_rows, keys, preferred_element_type=jnp.float32)
-    visible = key_index <= query_index[:, None]
-    scores = jnp.where(visible, scores * scale, masked_value)
-    peak = jnp.max(scores, axis=1)
-    weights = jnp.where(visible, jnp.exp(scores - peak[:, None]), 0.0)
-    totals = jnp.sum(weights, axis=1)
+    queries = q_ref[...]
+    query_index = qi_ref[...]
+
+    def masked_scores(k_ref, i_ref):
+        scores = lax.dot_general(
+            queries, k_ref[...], (((1,), (1,)), ((), ())), preferred_element_type=jnp.float32
+        )
+        visible = i_ref[...] <= query_index
+        return jnp.where(visible, scores * scale, masked_value), visible
+
+    scores_a, visible_a = masked_scores(ka_ref, ia_ref)
+    scores_b, visible_b = masked_scores(kb_ref, ib_ref)
+    peak = jnp.maximum(
+        jnp.max(scores_a, axis=1, keepdims=True), jnp.max(scores_b, axis=1, keepdims=True)
+    )
+    weights_a = jnp.where(visible_a, jnp.exp(scores_a - peak), 0.0)
+    weights_b = jnp.where(visible_b, jnp.exp(scores_b - peak), 0.0)
+    totals = jnp.sum(weights_a, axis=1, keepdims=True) + jnp.sum(weights_b, axis=1, keepdims=True)
     summed = jnp.dot(
-        weights.astype(jnp.bfloat16), keys[:, :LATENT], preferred_element_type=jnp.float32
-    )
-    return (summed / totals[:, None]).astype(jnp.bfloat16)
+        weights_a.astype(jnp.bfloat16), ka_ref[:, :LATENT], preferred_element_type=jnp.float32
+    )
+    summed = summed + jnp.dot(
+        weights_b.astype(jnp.bfloat16), kb_ref[:, :LATENT], preferred_element_type=jnp.float32
+    )
+    o_ref[...] = (summed / totals).astype(jnp.bfloat16)
+
+
+def attend(query_rows, query_index, halves):
+    rows = query_rows.shape[0]
+    operands = [query_rows, query_index.reshape(rows, 1)]
+    key_count = 0
+    for keys, key_index in halves:
+        operands += [keys, key_index]
+        key_count += keys.shape[0]
+    width = query_rows.shape[1]
+    cost = pl.CostEstimate(
+        flops=2 * rows * key_count * (width + LATENT),
+        transcendentals=rows * key_count,
+        bytes_accessed=2 * (rows * width + key_count * width + rows * LATENT),
+    )
+    return pl.pallas_call(
+        attention_kernel,
+        out_shape=jax.ShapeDtypeStruct((rows, LATENT), jnp.bfloat16),
+        cost_estimate=cost,
+    )(*operands)
 
 
 def exchange(acc, axis, size, bit, same_over_yh):
@@ -89,13 +125,16 @@
     acc = jnp.stack(blocks)
     source = cube - jnp.arange(cubes, dtype=jnp.int32)
     index = jnp.where(source >= 0, source * per_cube + within, ABSENT)
-    for axis, size in (("zl", 2), ("yl", 2), ("co", 2)):
+    rounds = (("zl", 2), ("yl", 2), ("co", 2))
+    for number, (axis, size) in enumerate(rounds):
         step = per_cube // size
         per_cube = step
         other = exchange(acc, axis, size, 1, True)
+        other_index = jnp.where(index < ABSENT, index ^ step, ABSENT)
+        if number == len(rounds) - 1:
+            return (acc, index), (other, other_index)
         acc = jnp.concatenate([acc, other], axis=0)
-        index = jnp.concatenate([index, jnp.where(index < ABSENT, index ^ step, ABSENT)])
-    return acc, index
+        index = jnp.concatenate([index, other_index])
 
 
 def scatter_sum(blocks):
@@ -147,16 +186,18 @@
         token_count * head_count, LATENT + ROPE
     )
     local_keys = jnp.concatenate([latents, rot_keys], axis=-1)
-    key_blocks, block_index = gather_earlier_keys(local_keys)
-    keys = key_blocks.reshape(-1, LATENT + ROPE)
-    key_index = (
-        block_index[:, None] * token_count + jnp.arange(token_count, dtype=jnp.int32)[None, :]
-    ).reshape(1, -1)
+    halves = []
+    for key_blocks, block_index in gather_earlier_keys(local_keys):
+        keys = key_blocks.reshape(-1, LATENT + ROPE)
+        key_index = (
+            block_index[:, None] * token_count + jnp.arange(token_count, dtype=jnp.int32)[None, :]
+        ).reshape(1, -1)
+        halves.append((keys, key_index))
     first_token = lax.axis_index(CTX) * token_count
     query_index = jnp.repeat(
         first_token + jnp.arange(token_count, dtype=jnp.int32), head_count
     )
-    latent_out = attend(query_rows, query_index, keys, key_index)
+    latent_out = attend(query_rows, query_index, halves)
     head_out = upward(latent_out, value_up, token_count, head_count)
     pair = gather_in_order(out_proj.T, (("yl", 2),), False)
     pair = pair.reshape(2, out_proj.shape[1], -1).transpose(2, 0, 1).reshape(out_proj.shape[0], -1)

time: 199 us -> 200 us (level)
  Pallas kernels: 0 us -> 11.7 us
  matrix products: 12.4 us -> 4.49 us
  local copies, waits for them, and re-layouts: 16.1 us -> 13.5 us
  other arithmetic: 13.1 us -> 10.5 us
    all_gather x1, waiting for transfers between devices: 0.02 us -> 14.7 us  [body(): own = lax.all_gather(pair, ('zh', 'zl'), axis=1, tiled=True)]
    pallas_call x0 -> x1, Pallas kernels: none -> 11.7 us  [attend(): pl.pallas_call(attention_kernel, out_shape=jax.ShapeDtypeStruct((rows, LA...]
    ppermute x1, waiting for transfers between devices: 11.5 us -> 0.01 us  [exchange(): far = lax.ppermute(acc[half:], ('yl', 'yh'), [(i, i ^ 3) for i in range(4)])]
    dot_general x2 -> x0, matrix products: 8.96 us -> none  [the longest x1 6.4 us: attend(): jnp.einsum('rl,kl->rk', query_rows, keys, preferred_element_type=jnp.floa...]
    concatenate x2 -> x1, local copies, waits for them, and re-layouts: 4.51 us -> 0.93 us  [gather_earlier_keys(): acc = jnp.concatenate([acc, other], axis=0)]
    unnamed x24 -> x17, local copies, waits for them, and re-layouts: 9.72 us -> 6.76 us
    reduce_sum x1 -> x0, other arithmetic: 2.62 us -> none  [attend(): totals = jnp.sum(weights, axis=1)]
  transfers between devices with their start and end apart: 18 -> 18, of which waited for: 11 -> 11; matrix products, arithmetic and copies ran while one was open for 15% -> 9% of each run, Pallas kernels for 0% -> 6%
where the time goes in v9:
time: 200 us; the launch traced here: 197 us
  waiting for transfers between devices  79.4 us (40%)
  starting transfers between devices  63.2 us (32%)
  between operations  13.8 us (7%)
  local copies, waits for them, and re-layouts  13.5 us (7%)
  Pallas kernels  11.7 us (6%)
  other arithmetic  10.5 us (5%)
  matrix products  4.49 us (2%)
    ppermute x7, starting transfers between devices, gather_earlier_keys(): lax.ppermute(local, 'zh', [(i, i + shift) for i in range(cubes - shift)])  29.2 us
    ppermute x3, waiting for transfers between devices, exchange(): return lax.ppermute(acc, axis, pairs)  28.8 us
    ppermute x7, waiting for transfers between devices, gather_earlier_keys(): lax.ppermute(local, 'zh', [(i, i + shift) for i in range(cubes - shift)])  21.4 us
    all_gather x1, waiting for transfers between devices, body(): own = lax.all_gather(pair, ('zh', 'zl'), axis=1, tiled=True)  14.7 us
    pallas_call x1, Pallas kernels, attend(): pl.pallas_call(attention_kernel, out_shape=jax.ShapeDtypeStruct((rows, LA...  11.7 us
    ppermute x3, waiting for transfers between devices, scatter_sum(): lax.ppermute(blocks[x ^ shift], 'x', [(i, i ^ shift) for i in range(colum...  10.8 us
    ppermute x3, starting transfers between devices, scatter_sum(): lax.ppermute(blocks[x ^ shift], 'x', [(i, i ^ shift) for i in range(colum...  10.4 us
    ppermute x3, starting transfers between devices, exchange(): return lax.ppermute(acc, axis, pairs)  7.91 us
  transfers between devices with their start and end apart: 18, of which 11 were waited for; matrix products, arithmetic and copies ran while one was open for 9% of the time, Pallas kernels for 6%

profile of v9, /device:TPU:6, one launch (start us, length us, event | category | flops | bytes accessed | tf_op | source)
XLA Modules:
  0.0 196.5 jit_solution(16226004786080220029)
XLA Ops:
  6.5 3.6 %collective-permute-start.11 = (bf16[1,56,1024]{2,1,0:T(8,128)(2,1)}, bf16[1,56,1024]{2,1,0:T(8,128)(2,1)S(1)}, u32[]{:S(2)}, u32[]{:S(2)}) collective-permute-start(bf16[1,56,1024]{2,1,0:T(8,128)(2,1)} %bitcast.113), channel_id=1, source_target_pairs={{0,16},{16,0},{1,17},{17,1},{2,18},{18,2},{3,19},{19,3},{4,20},{20... | collective-permute-start | bytes 344072 | tf_op jit(solution)/shard_map/ppermute | solution.py:93
  10.2 3.5 %collective-permute-done.11 = bf16[1,56,1024]{2,1,0:T(8,128)(2,1)S(1)} collective-permute-done((bf16[1,56,1024]{2,1,0:T(8,128)(2,1)}, bf16[1,56,1024]{2,1,0:T(8,128)(2,1)S(1)}, u32[]{:S(2)}, u32[]{:S(2)}) %collective-permute-start.11) | collective-permute-done | bytes 114720 | tf_op jit(solution)/shard_map/ppermute | solution.py:93
  17.9 5.2 %collective-permute-start = (bf16[64,576]{1,0:T(8,128)(2,1)S(1)}, bf16[64,576]{1,0:T(8,128)(2,1)S(1)}, u32[]{:S(2)}, u32[]{:S(2)}) collective-permute-start(bf16[64,576]{1,0:T(8,128)(2,1)S(1)} %pad_maximum_fusion.3), channel_id=1, source_target_pairs={{0,64},{64,128},{128,192},{192,256},{256,320},{320,384},{384,448},... | collective-permute-start | bytes 221192 | tf_op jit(solution)/shard_map/ppermute | solution.py:124
  23.1 9.1 %collective-permute-start.1 = (bf16[64,576]{1,0:T(8,128)(2,1)S(1)}, bf16[64,576]{1,0:T(8,128)(2,1)S(1)}, u32[]{:S(2)}, u32[]{:S(2)}) collective-permute-start(bf16[64,576]{1,0:T(8,128)(2,1)S(1)} %pad_maximum_fusion.3), channel_id=1, source_target_pairs={{0,128},{64,192},{128,256},{192,320},{256,384},{320,448},{1,129},{... | collective-permute-start | bytes 221192 | tf_op jit(solution)/shard_map/ppermute | solution.py:124
  32.2 8.2 %collective-permute-start.2 = (bf16[64,576]{1,0:T(8,128)(2,1)S(1)}, bf16[64,576]{1,0:T(8,128)(2,1)S(1)}, u32[]{:S(2)}, u32[]{:S(2)}) collective-permute-start(bf16[64,576]{1,0:T(8,128)(2,1)S(1)} %pad_maximum_fusion.3), channel_id=1, source_target_pairs={{0,192},{64,256},{128,320},{192,384},{256,448},{1,193},{65,257},{1... | collective-permute-start | bytes 221192 | tf_op jit(solution)/shard_map/ppermute | solution.py:124
  40.4 2.8 %collective-permute-start.3 = (bf16[64,576]{1,0:T(8,128)(2,1)S(1)}, bf16[64,576]{1,0:T(8,128)(2,1)S(1)}, u32[]{:S(2)}, u32[]{:S(2)}) collective-permute-start(bf16[64,576]{1,0:T(8,128)(2,1)S(1)} %pad_maximum_fusion.3), channel_id=1, source_target_pairs={{0,256},{64,320},{128,384},{192,448},{1,257},{65,321},{129,385},{1... | collective-permute-start | bytes 221192 | tf_op jit(solution)/shard_map/ppermute | solution.py:124
  51.4 12.3 %collective-permute-done.4 = bf16[64,576]{1,0:T(8,128)(2,1)S(1)} collective-permute-done((bf16[64,576]{1,0:T(8,128)(2,1)S(1)}, bf16[64,576]{1,0:T(8,128)(2,1)S(1)}, u32[]{:S(2)}, u32[]{:S(2)}) %collective-permute-start.4) | collective-permute-done | bytes 73760 | tf_op jit(solution)/shard_map/ppermute | solution.py:124
  64.4 5.2 %collective-permute-done.5 = bf16[64,576]{1,0:T(8,128)(2,1)S(1)} collective-permute-done((bf16[64,576]{1,0:T(8,128)(2,1)S(1)}, bf16[64,576]{1,0:T(8,128)(2,1)S(1)}, u32[]{:S(2)}, u32[]{:S(2)}) %collective-permute-start.5) | collective-permute-done | bytes 73760 | tf_op jit(solution)/shard_map/ppermute | solution.py:124
  70.3 3.9 %collective-permute-done.6 = bf16[64,576]{1,0:T(8,128)(2,1)S(1)} collective-permute-done((bf16[64,576]{1,0:T(8,128)(2,1)S(1)}, bf16[64,576]{1,0:T(8,128)(2,1)S(1)}, u32[]{:S(2)}, u32[]{:S(2)}) %collective-permute-start.6) | collective-permute-done | bytes 73760 | tf_op jit(solution)/shard_map/ppermute | solution.py:124
  76.8 3.5 %collective-permute-start.8 = (bf16[8,64,576]{2,1,0:T(8,128)(2,1)}, bf16[8,64,576]{2,1,0:T(8,128)(2,1)S(1)}, u32[]{:S(2)}, u32[]{:S(2)}) collective-permute-start(bf16[8,64,576]{2,1,0:T(8,128)(2,1)} %get-tuple-element.20), channel_id=1, source_target_pairs={{0,16},{16,0},{1,17},{17,1},{2,18},{18,2},{3,19},{19,3},{4,20},{20... | collective-permute-start | bytes 1769480 | tf_op jit(solution)/shard_map/ppermute | solution.py:95
  80.3 25.1 %collective-permute-done.7 = bf16[8,64,576]{2,1,0:T(8,128)(2,1)S(1)} collective-permute-done((bf16[8,64,576]{2,1,0:T(8,128)(2,1)}, bf16[8,64,576]{2,1,0:T(8,128)(2,1)S(1)}, u32[]{:S(2)}, u32[]{:S(2)}) %collective-permute-start.7) | collective-permute-done | bytes 589856 | tf_op jit(solution)/shard_map/ppermute | solution.py:93
  105.4 5.1 %collective-permute-start.9 = (bf16[8,64,576]{2,1,0:T(8,128)(2,1)S(1)}, bf16[8,64,576]{2,1,0:T(8,128)(2,1)S(1)}, u32[]{:S(2)}, u32[]{:S(2)}) collective-permute-start(bf16[8,64,576]{2,1,0:T(8,128)(2,1)S(1)} %collective-permute-done.7), channel_id=1, source_target_pairs={{0,17},{1,16},{16,1},{17,0},{2,19},{3,18},{18,3},{19,2},{4,21},{5,... | collective-permute-start | bytes 1769480 | tf_op jit(solution)/shard_map/ppermute | solution.py:96
  110.5 14.7 %all-gather.2.cloned.1.call-done = bf16[1024,1792]{0,1:T(8,128)(2,1)} async-done(((bf16[1024,112]{0,1:T(8,128)(2,1)}), bf16[1024,1792]{0,1:T(8,128)(2,1)}) %all-gather.2.cloned.1.call-update) | async-done | bytes 3670032 | tf_op jit(solution)/shard_map/all_gather | solution.py:204
  125.2 1.9 collective-permute-start.12
  129.9 2.4 %collective-permute-start.10 = (bf16[32,64,576]{2,1,0:T(8,128)(2,1)}, bf16[32,64,576]{2,1,0:T(8,128)(2,1)}, u32[]{:S(2)}, u32[]{:S(2)}) collective-permute-start(bf16[32,64,576]{2,1,0:T(8,128)(2,1)} %constant_dynamic-update-slice_fusion), channel_id=1, source_target_pairs={{0,8},{8,0},{1,9},{9,1},{2,10},{10,2},{3,11},{11,3},{4,12},{12,4},... | collective-permute-start | bytes 7077896 | tf_op jit(solution)/shard_map/ppermute | solution.py:93
  137.6 11.7 %shard_map.82 = bf16[512,512]{1,0:T(8,128)(2,1)} custom-call(bf16[512,576]{1,0:T(8,128)(2,1)} %bitcast.111, s32[512,1]{1,0:T(8,128)} %reshape_reshape.4.qi_ref, bf16[2048,576]{1,0:T(8,128)(2,1)} %bitcast.114, s32[1,2048]{1,0:T(1,128)} %add.130.ia_ref, bf16[2048,576]{1,0:T(8,128)(2,1)} %bitcast.14.kb_ref, s32[1,2048]{1,0:T(1,128)} %add.134.ib_ref), custom_call_target="tpu_custom_call" | custom-call | flops 4563402752 | bytes 5832704 | tf_op jit(solution)/shard_map/pallas_call | solution.py:83
  150.9 3.6 %broadcast_select_fusion.1 = (bf16[1024,1792]{0,1:T(8,128)(2,1)S(1)}, bf16[1024,1792]{0,1:T(8,128)(2,1)S(1)}) fusion(bf16[1024,1792]{0,1:T(8,128)(2,1)} %collective-permute-done.12, bf16[1024,1792]{0,1:T(8,128)(2,1)} %all-gather.2.cloned.1.call-done, pred[]{:T(512)S(6)} %eq.8), kind=kLoop, calls=%fused_computation.1 | loop fusion | flops 3670016 | bytes 14680065 | tf_op jit(solution)/shard_map/jit(_where)/select_n | solution.py:207
  157.5 2.5 %collective-permute-start.13 = (f32[2,64,448]{2,1,0:T(8,128)S(1)}, f32[2,64,448]{2,1,0:T(8,128)S(1)}, u32[]{:S(2)}, u32[]{:S(2)}) collective-permute-start(f32[2,64,448]{2,1,0:T(8,128)S(1)} %get-tuple-element.11), channel_id=1, source_target_pairs={{0,2},{2,0},{4,6},{6,4},{1,3},{3,1},{5,7},{7,5},{8,10},{10,8},{12,... | collective-permute-start | bytes 688136 | tf_op jit(solution)/shard_map/ppermute | solution.py:148
  159.9 3.0 %collective-permute-start.14 = (f32[2,64,448]{2,1,0:T(8,128)S(1)}, f32[2,64,448]{2,1,0:T(8,128)S(1)}, u32[]{:S(2)}, u32[]{:S(2)}) collective-permute-start(f32[2,64,448]{2,1,0:T(8,128)S(1)} %get-tuple-element.13), channel_id=1, source_target_pairs={{0,4},{2,6},{4,0},{6,2},{1,5},{3,7},{5,1},{7,3},{8,12},{10,14},{12... | collective-permute-start | bytes 688136 | tf_op jit(solution)/shard_map/ppermute | solution.py:148
  163.0 4.9 %collective-permute-start.15 = (f32[2,64,448]{2,1,0:T(8,128)S(1)}, f32[2,64,448]{2,1,0:T(8,128)}, u32[]{:S(2)}, u32[]{:S(2)}) collective-permute-start(f32[2,64,448]{2,1,0:T(8,128)S(1)} %get-tuple-element.12), channel_id=1, source_target_pairs={{0,6},{2,4},{4,2},{6,0},{1,7},{3,5},{5,3},{7,1},{8,14},{10,12},{12... | collective-permute-start | bytes 688136 | tf_op jit(solution)/shard_map/ppermute | solution.py:148
  168.5 4.6 %collective-permute-done.14 = f32[2,64,448]{2,1,0:T(8,128)S(1)} collective-permute-done((f32[2,64,448]{2,1,0:T(8,128)S(1)}, f32[2,64,448]{2,1,0:T(8,128)S(1)}, u32[]{:S(2)}, u32[]{:S(2)}) %collective-permute-start.14) | collective-permute-done | bytes 229408 | tf_op jit(solution)/shard_map/ppermute | solution.py:148
  173.1 5.6 %collective-permute-done.15 = f32[2,64,448]{2,1,0:T(8,128)} collective-permute-done((f32[2,64,448]{2,1,0:T(8,128)S(1)}, f32[2,64,448]{2,1,0:T(8,128)}, u32[]{:S(2)}, u32[]{:S(2)}) %collective-permute-start.15) | collective-permute-done | bytes 229408 | tf_op jit(solution)/shard_map/ppermute | solution.py:148
  179.8 5.2 %collective-permute-start.16 = (f32[64,448]{1,0:T(8,128)S(1)}, f32[64,448]{1,0:T(8,128)S(1)}, u32[]{:S(2)}, u32[]{:S(2)}) collective-permute-start(f32[64,448]{1,0:T(8,128)S(1)} %dynamic-slice_bitcast_fusion.3), channel_id=1, source_target_pairs={{0,1},{1,0},{2,3},{3,2},{4,5},{5,4},{6,7},{7,6},{8,9},{9,8},{10,11... | collective-permute-start | bytes 344072 | tf_op jit(solution)/shard_map/ppermute | solution.py:153
  185.0 3.7 %collective-permute-done.16 = f32[64,448]{1,0:T(8,128)S(1)} collective-permute-done((f32[64,448]{1,0:T(8,128)S(1)}, f32[64,448]{1,0:T(8,128)S(1)}, u32[]{:S(2)}, u32[]{:S(2)}) %collective-permute-start.16) | collective-permute-done | bytes 114720 | tf_op jit(solution)/shard_map/ppermute | solution.py:153
  (75 shorter events, 31.5 us)
Async XLA Ops:
  6.5 128.9 %copy-start = (bf16[512,1024]{1,0:T(8,128)(2,1)S(1)}, bf16[512,1024]{1,0:T(8,128)(2,1)}, u32[]{:S(2)}) copy-start(bf16[512,1024]{1,0:T(8,128)(2,1)} %param.13) | copy-start | bytes 3145732
  6.5 118.7 %all-gather.2.cloned.1.call-start = ((), (), s32[]{:S(2)}) async-start(), calls=%async_computation | async-start | bytes 3899392 | tf_op jit(solution)/shard_map/all_gather | solution.py:204
  6.5 7.1 %collective-permute-start.11 = (bf16[1,56,1024]{2,1,0:T(8,128)(2,1)}, bf16[1,56,1024]{2,1,0:T(8,128)(2,1)S(1)}, u32[]{:S(2)}, u32[]{:S(2)}) collective-permute-start(bf16[1,56,1024]{2,1,0:T(8,128)(2,1)} %bitcast.113), channel_id=1, source_target_pairs={{0,16},{16,0},{1,17},{17,1},{2,18},{18,2},{3,19},{19,3},{4,20},{20... | collective-permute-start | bytes 344072 | tf_op jit(solution)/shard_map/ppermute | solution.py:93
  17.9 28.2 %collective-permute-start = (bf16[64,576]{1,0:T(8,128)(2,1)S(1)}, bf16[64,576]{1,0:T(8,128)(2,1)S(1)}, u32[]{:S(2)}, u32[]{:S(2)}) collective-permute-start(bf16[64,576]{1,0:T(8,128)(2,1)S(1)} %pad_maximum_fusion.3), channel_id=1, source_target_pairs={{0,64},{64,128},{128,192},{192,256},{256,320},{320,384},{384,448},... | collective-permute-start | bytes 221192 | tf_op jit(solution)/shard_map/ppermute | solution.py:124
  23.1 25.0 %collective-permute-start.1 = (bf16[64,576]{1,0:T(8,128)(2,1)S(1)}, bf16[64,576]{1,0:T(8,128)(2,1)S(1)}, u32[]{:S(2)}, u32[]{:S(2)}) collective-permute-start(bf16[64,576]{1,0:T(8,128)(2,1)S(1)} %pad_maximum_fusion.3), channel_id=1, source_target_pairs={{0,128},{64,192},{128,256},{192,320},{256,384},{320,448},{1,129},{... | collective-permute-start | bytes 221192 | tf_op jit(solution)/shard_map/ppermute | solution.py:124
  32.2 17.8 %collective-permute-start.2 = (bf16[64,576]{1,0:T(8,128)(2,1)S(1)}, bf16[64,576]{1,0:T(8,128)(2,1)S(1)}, u32[]{:S(2)}, u32[]{:S(2)}) collective-permute-start(bf16[64,576]{1,0:T(8,128)(2,1)S(1)} %pad_maximum_fusion.3), channel_id=1, source_target_pairs={{0,192},{64,256},{128,320},{192,384},{256,448},{1,193},{65,257},{1... | collective-permute-start | bytes 221192 | tf_op jit(solution)/shard_map/ppermute | solution.py:124
  40.4 10.3 %collective-permute-start.3 = (bf16[64,576]{1,0:T(8,128)(2,1)S(1)}, bf16[64,576]{1,0:T(8,128)(2,1)S(1)}, u32[]{:S(2)}, u32[]{:S(2)}) collective-permute-start(bf16[64,576]{1,0:T(8,128)(2,1)S(1)} %pad_maximum_fusion.3), channel_id=1, source_target_pairs={{0,256},{64,320},{128,384},{192,448},{1,257},{65,321},{129,385},{1... | collective-permute-start | bytes 221192 | tf_op jit(solution)/shard_map/ppermute | solution.py:124
  43.2 20.4 %collective-permute-start.4 = (bf16[64,576]{1,0:T(8,128)(2,1)S(1)}, bf16[64,576]{1,0:T(8,128)(2,1)S(1)}, u32[]{:S(2)}, u32[]{:S(2)}) collective-permute-start(bf16[64,576]{1,0:T(8,128)(2,1)S(1)} %pad_maximum_fusion.3), channel_id=1, source_target_pairs={{0,320},{64,384},{128,448},{1,321},{65,385},{129,449},{2,322},{66,... | collective-permute-start | bytes 221192 | tf_op jit(solution)/shard_map/ppermute | solution.py:124
  46.1 23.5 %collective-permute-start.5 = (bf16[64,576]{1,0:T(8,128)(2,1)S(1)}, bf16[64,576]{1,0:T(8,128)(2,1)S(1)}, u32[]{:S(2)}, u32[]{:S(2)}) collective-permute-start(bf16[64,576]{1,0:T(8,128)(2,1)S(1)} %pad_maximum_fusion.3), channel_id=1, source_target_pairs={{0,384},{64,448},{1,385},{65,449},{2,386},{66,450},{3,387},{67,451... | collective-permute-start | bytes 221192 | tf_op jit(solution)/shard_map/ppermute | solution.py:124
  48.1 26.2 %collective-permute-start.6 = (bf16[64,576]{1,0:T(8,128)(2,1)S(1)}, bf16[64,576]{1,0:T(8,128)(2,1)S(1)}, u32[]{:S(2)}, u32[]{:S(2)}) collective-permute-start(bf16[64,576]{1,0:T(8,128)(2,1)S(1)} %pad_maximum_fusion.3), channel_id=1, source_target_pairs={{0,448},{1,449},{2,450},{3,451},{4,452},{5,453},{6,454},{7,455},{8... | collective-permute-start | bytes 221192 | tf_op jit(solution)/shard_map/ppermute | solution.py:124
  51.4 83.5 %copy-start.1 = (bf16[64,512]{1,0:T(8,128)(2,1)S(1)}, bf16[64,512]{1,0:T(8,128)(2,1)}, u32[]{:S(2)}) copy-start(bf16[64,512]{1,0:T(8,128)(2,1)} %param.9) | copy-start | bytes 196612
  74.9 30.5 %collective-permute-start.7 = (bf16[8,64,576]{2,1,0:T(8,128)(2,1)}, bf16[8,64,576]{2,1,0:T(8,128)(2,1)S(1)}, u32[]{:S(2)}, u32[]{:S(2)}) collective-permute-start(bf16[8,64,576]{2,1,0:T(8,128)(2,1)} %get-tuple-element.20), channel_id=1, source_target_pairs={{0,32},{32,0},{1,33},{33,1},{2,34},{34,2},{3,35},{35,3},{4,36},{36... | collective-permute-start | bytes 1769480 | tf_op jit(solution)/shard_map/ppermute | solution.py:93
  76.8 51.2 %collective-permute-start.8 = (bf16[8,64,576]{2,1,0:T(8,128)(2,1)}, bf16[8,64,576]{2,1,0:T(8,128)(2,1)S(1)}, u32[]{:S(2)}, u32[]{:S(2)}) collective-permute-start(bf16[8,64,576]{2,1,0:T(8,128)(2,1)} %get-tuple-element.20), channel_id=1, source_target_pairs={{0,16},{16,0},{1,17},{17,1},{2,18},{18,2},{3,19},{19,3},{4,20},{20... | collective-permute-start | bytes 1769480 | tf_op jit(solution)/shard_map/ppermute | solution.py:95
  105.4 23.5 %collective-permute-start.9 = (bf16[8,64,576]{2,1,0:T(8,128)(2,1)S(1)}, bf16[8,64,576]{2,1,0:T(8,128)(2,1)S(1)}, u32[]{:S(2)}, u32[]{:S(2)}) collective-permute-start(bf16[8,64,576]{2,1,0:T(8,128)(2,1)S(1)} %collective-permute-done.7), channel_id=1, source_target_pairs={{0,17},{1,16},{16,1},{17,0},{2,19},{3,18},{18,3},{19,2},{4,21},{5,... | collective-permute-start | bytes 1769480 | tf_op jit(solution)/shard_map/ppermute | solution.py:96
  125.2 25.7 %collective-permute-start.12 = (bf16[1024,1792]{0,1:T(8,128)(2,1)}, bf16[1024,1792]{0,1:T(8,128)(2,1)}, u32[]{:S(2)}, u32[]{:S(2)}) collective-permute-start(bf16[1024,1792]{0,1:T(8,128)(2,1)} %all-gather.2.cloned.1.call-done), channel_id=1, source_target_pairs={{0,8},{8,0},{1,9},{9,1},{2,10},{10,2},{3,11},{11,3},{4,12},{12,4},... | collective-permute-start | bytes 11010056 | tf_op jit(solution)/shard_map/ppermute | solution.py:205
  128.0 7.5 %copy-start.3 = (bf16[64,1024]{1,0:T(8,128)(2,1)S(1)}, bf16[64,1024]{1,0:T(8,128)(2,1)}, u32[]{:S(2)}) copy-start(bf16[64,1024]{1,0:T(8,128)(2,1)} %param.8) | copy-start | bytes 393220
  129.9 7.7 %collective-permute-start.10 = (bf16[32,64,576]{2,1,0:T(8,128)(2,1)}, bf16[32,64,576]{2,1,0:T(8,128)(2,1)}, u32[]{:S(2)}, u32[]{:S(2)}) collective-permute-start(bf16[32,64,576]{2,1,0:T(8,128)(2,1)} %constant_dynamic-update-slice_fusion), channel_id=1, source_target_pairs={{0,8},{8,0},{1,9},{9,1},{2,10},{10,2},{3,11},{11,3},{4,12},{12,4},... | collective-permute-start | bytes 7077896 | tf_op jit(solution)/shard_map/ppermute | solution.py:93
  137.6 11.7 %copy-start.2 = (bf16[512,1024]{1,0:T(8,128)(2,1)S(1)}, bf16[512,1024]{1,0:T(8,128)(2,1)}, u32[]{:S(2)}) copy-start(bf16[512,1024]{1,0:T(8,128)(2,1)} %param.14) | copy-start | bytes 3145732
  157.5 11.0 %collective-permute-start.13 = (f32[2,64,448]{2,1,0:T(8,128)S(1)}, f32[2,64,448]{2,1,0:T(8,128)S(1)}, u32[]{:S(2)}, u32[]{:S(2)}) collective-permute-start(f32[2,64,448]{2,1,0:T(8,128)S(1)} %get-tuple-element.11), channel_id=1, source_target_pairs={{0,2},{2,0},{4,6},{6,4},{1,3},{3,1},{5,7},{7,5},{8,10},{10,8},{12,... | collective-permute-start | bytes 688136 | tf_op jit(solution)/shard_map/ppermute | solution.py:148
  159.9 13.1 %collective-permute-start.14 = (f32[2,64,448]{2,1,0:T(8,128)S(1)}, f32[2,64,448]{2,1,0:T(8,128)S(1)}, u32[]{:S(2)}, u32[]{:S(2)}) collective-permute-start(f32[2,64,448]{2,1,0:T(8,128)S(1)} %get-tuple-element.13), channel_id=1, source_target_pairs={{0,4},{2,6},{4,0},{6,2},{1,5},{3,7},{5,1},{7,3},{8,12},{10,14},{12... | collective-permute-start | bytes 688136 | tf_op jit(solution)/shard_map/ppermute | solution.py:148
  163.0 15.7 %collective-permute-start.15 = (f32[2,64,448]{2,1,0:T(8,128)S(1)}, f32[2,64,448]{2,1,0:T(8,128)}, u32[]{:S(2)}, u32[]{:S(2)}) collective-permute-start(f32[2,64,448]{2,1,0:T(8,128)S(1)} %get-tuple-element.12), channel_id=1, source_target_pairs={{0,6},{2,4},{4,2},{6,0},{1,7},{3,5},{5,3},{7,1},{8,14},{10,12},{12... | collective-permute-start | bytes 688136 | tf_op jit(solution)/shard_map/ppermute | solution.py:148
  179.8 8.8 %collective-permute-start.16 = (f32[64,448]{1,0:T(8,128)S(1)}, f32[64,448]{1,0:T(8,128)S(1)}, u32[]{:S(2)}, u32[]{:S(2)}) collective-permute-start(f32[64,448]{1,0:T(8,128)S(1)} %dynamic-slice_bitcast_fusion.3), channel_id=1, source_target_pairs={{0,1},{1,0},{2,3},{3,2},{4,5},{5,4},{6,7},{7,6},{8,9},{9,8},{10,11... | collective-permute-start | bytes 344072 | tf_op jit(solution)/shard_map/ppermute | solution.py:153
Sparse Core Ops, SparseCore 0:
  15.4 109.7 all-gather.1

commit v10 on v9

--- a/solution.py
+++ b/solution.py
@@ -145,14 +145,16 @@
     blocks = blocks.reshape((columns, rows) + blocks.shape[1:])
     row_sums = blocks[x]
     for shift in range(1, columns):
+        sent = blocks[x ^ shift].astype(jnp.bfloat16)
         row_sums = row_sums + lax.ppermute(
-            blocks[x ^ shift], "x", [(i, i ^ shift) for i in range(columns)]
-        )
+            sent, "x", [(i, i ^ shift) for i in range(columns)]
+        ).astype(jnp.float32)
     total = row_sums[yh]
     for shift in range(1, rows):
+        sent = row_sums[yh ^ shift].astype(jnp.bfloat16)
         total = total + lax.ppermute(
-            row_sums[yh ^ shift], "yh", [(i, i ^ shift) for i in range(rows)]
-        )
+            sent, "yh", [(i, i ^ shift) for i in range(rows)]
+        ).astype(jnp.float32)
     return total
 
 
@@ -204,16 +206,12 @@
     own = lax.all_gather(pair, ("zh", "zl"), axis=1, tiled=True)
     swapped = lax.ppermute(own, "co", [(0, 1), (1, 0)])
     upper = lax.axis_index("co") == 1
-    halves = [jnp.where(upper, swapped, own), jnp.where(upper, own, swapped)]
     groups = lax.axis_size(HEAD)
+    from_own = jnp.dot(head_out, own, preferred_element_type=jnp.float32)
+    from_swapped = jnp.dot(head_out, swapped, preferred_element_type=jnp.float32)
+    halves = [jnp.where(upper, from_swapped, from_own), jnp.where(upper, from_own, from_swapped)]
     partial_sums = jnp.concatenate(
-        [
-            jnp.dot(head_out, half, preferred_element_type=jnp.float32).reshape(
-                token_count, groups, -1
-            )
-            for half in halves
-        ],
-        axis=2,
+        [half.reshape(token_count, groups, -1) for half in halves], axis=2
     ).transpose(1, 0, 2)
     mine = scatter_sum(partial_sums)
     width = out_proj.shape[1]

time: 200 us -> 192 us (0.960)
  waiting for transfers between devices: 79.4 us -> 70.7 us
  other arithmetic: 10.5 us -> 5.92 us
  matrix products: 4.49 us -> 8.53 us
    ppermute x4, waiting for transfers between devices: 14.4 us -> 5.74 us  [the longest x3 3.46 us: scatter_sum(): lax.ppermute(sent, 'x', [(i, i ^ shift) for i in range(columns)])]
    dot_general x2, matrix products: 2.52 us -> 6.55 us  [the longest x1 3.28 us: body(): jnp.dot(head_out, swapped, preferred_element_type=jnp.float32)]
    select_n x1 -> x0, other arithmetic: 3.64 us -> none  [body(): halves = [jnp.where(upper, swapped, own), jnp.where(upper, own, swapped)]]
  transfers between devices with their start and end apart: 18 -> 18, of which waited for: 11 -> 10; matrix products, arithmetic and copies ran while one was open for 9% -> 11% of each run, Pallas kernels for 6% -> 6%
where the time goes in v10:
time: 192 us; the launch traced here: 189 us
  waiting for transfers between devices  70.7 us (37%)
  starting transfers between devices  63.4 us (33%)
  local copies, waits for them, and re-layouts  14.6 us (8%)
  between operations  13.8 us (7%)
  Pallas kernels  11.7 us (6%)
  matrix products  8.53 us (4%)
  other arithmetic  5.92 us (3%)
    ppermute x7, starting transfers between devices, gather_earlier_keys(): lax.ppermute(local, 'zh', [(i, i + shift) for i in range(cubes - shift)])  29.2 us
    ppermute x3, waiting for transfers between devices, exchange(): return lax.ppermute(acc, axis, pairs)  28.8 us
    ppermute x7, waiting for transfers between devices, gather_earlier_keys(): lax.ppermute(local, 'zh', [(i, i + shift) for i in range(cubes - shift)])  21.4 us
    all_gather x1, waiting for transfers between devices, body(): own = lax.all_gather(pair, ('zh', 'zl'), axis=1, tiled=True)  14.7 us
    pallas_call x1, Pallas kernels, attend(): pl.pallas_call(attention_kernel, out_shape=jax.ShapeDtypeStruct((rows, LA...  11.7 us
    ppermute x3, starting transfers between devices, scatter_sum(): lax.ppermute(sent, 'x', [(i, i ^ shift) for i in range(columns)])  10.4 us
    ppermute x3, starting transfers between devices, exchange(): return lax.ppermute(acc, axis, pairs)  7.91 us
    unnamed x17, local copies, waits for them, and re-layouts  6.76 us
  transfers between devices with their start and end apart: 18, of which 10 were waited for; matrix products, arithmetic and copies ran while one was open for 11% of the time, Pallas kernels for 6%

profile of v10, /device:TPU:6, one launch (start us, length us, event | category | flops | bytes accessed | tf_op | source)
XLA Modules:
  0.0 188.6 jit_solution(13550812060016118050)
XLA Ops:
  6.5 3.6 %collective-permute-start.11 = (bf16[1,56,1024]{2,1,0:T(8,128)(2,1)}, bf16[1,56,1024]{2,1,0:T(8,128)(2,1)S(1)}, u32[]{:S(2)}, u32[]{:S(2)}) collective-permute-start(bf16[1,56,1024]{2,1,0:T(8,128)(2,1)} %bitcast.111), channel_id=1, source_target_pairs={{0,16},{16,0},{1,17},{17,1},{2,18},{18,2},{3,19},{19,3},{4,20},{20... | collective-permute-start | bytes 344072 | tf_op jit(solution)/shard_map/ppermute | solution.py:93
  10.2 3.5 %collective-permute-done.11 = bf16[1,56,1024]{2,1,0:T(8,128)(2,1)S(1)} collective-permute-done((bf16[1,56,1024]{2,1,0:T(8,128)(2,1)}, bf16[1,56,1024]{2,1,0:T(8,128)(2,1)S(1)}, u32[]{:S(2)}, u32[]{:S(2)}) %collective-permute-start.11) | collective-permute-done | bytes 114720 | tf_op jit(solution)/shard_map/ppermute | solution.py:93
  17.9 5.2 %collective-permute-start = (bf16[64,576]{1,0:T(8,128)(2,1)S(1)}, bf16[64,576]{1,0:T(8,128)(2,1)S(1)}, u32[]{:S(2)}, u32[]{:S(2)}) collective-permute-start(bf16[64,576]{1,0:T(8,128)(2,1)S(1)} %pad_maximum_fusion.2), channel_id=1, source_target_pairs={{0,64},{64,128},{128,192},{192,256},{256,320},{320,384},{384,448},... | collective-permute-start | bytes 221192 | tf_op jit(solution)/shard_map/ppermute | solution.py:124
  23.1 9.1 %collective-permute-start.1 = (bf16[64,576]{1,0:T(8,128)(2,1)S(1)}, bf16[64,576]{1,0:T(8,128)(2,1)S(1)}, u32[]{:S(2)}, u32[]{:S(2)}) collective-permute-start(bf16[64,576]{1,0:T(8,128)(2,1)S(1)} %pad_maximum_fusion.2), channel_id=1, source_target_pairs={{0,128},{64,192},{128,256},{192,320},{256,384},{320,448},{1,129},{... | collective-permute-start | bytes 221192 | tf_op jit(solution)/shard_map/ppermute | solution.py:124
  32.2 8.2 %collective-permute-start.2 = (bf16[64,576]{1,0:T(8,128)(2,1)S(1)}, bf16[64,576]{1,0:T(8,128)(2,1)S(1)}, u32[]{:S(2)}, u32[]{:S(2)}) collective-permute-start(bf16[64,576]{1,0:T(8,128)(2,1)S(1)} %pad_maximum_fusion.2), channel_id=1, source_target_pairs={{0,192},{64,256},{128,320},{192,384},{256,448},{1,193},{65,257},{1... | collective-permute-start | bytes 221192 | tf_op jit(solution)/shard_map/ppermute | solution.py:124
  40.4 2.8 %collective-permute-start.3 = (bf16[64,576]{1,0:T(8,128)(2,1)S(1)}, bf16[64,576]{1,0:T(8,128)(2,1)S(1)}, u32[]{:S(2)}, u32[]{:S(2)}) collective-permute-start(bf16[64,576]{1,0:T(8,128)(2,1)S(1)} %pad_maximum_fusion.2), channel_id=1, source_target_pairs={{0,256},{64,320},{128,384},{192,448},{1,257},{65,321},{129,385},{1... | collective-permute-start | bytes 221192 | tf_op jit(solution)/shard_map/ppermute | solution.py:124
  51.4 12.3 %collective-permute-done.4 = bf16[64,576]{1,0:T(8,128)(2,1)S(1)} collective-permute-done((bf16[64,576]{1,0:T(8,128)(2,1)S(1)}, bf16[64,576]{1,0:T(8,128)(2,1)S(1)}, u32[]{:S(2)}, u32[]{:S(2)}) %collective-permute-start.4) | collective-permute-done | bytes 73760 | tf_op jit(solution)/shard_map/ppermute | solution.py:124
  64.4 5.2 %collective-permute-done.5 = bf16[64,576]{1,0:T(8,128)(2,1)S(1)} collective-permute-done((bf16[64,576]{1,0:T(8,128)(2,1)S(1)}, bf16[64,576]{1,0:T(8,128)(2,1)S(1)}, u32[]{:S(2)}, u32[]{:S(2)}) %collective-permute-start.5) | collective-permute-done | bytes 73760 | tf_op jit(solution)/shard_map/ppermute | solution.py:124
  70.3 3.9 %collective-permute-done.6 = bf16[64,576]{1,0:T(8,128)(2,1)S(1)} collective-permute-done((bf16[64,576]{1,0:T(8,128)(2,1)S(1)}, bf16[64,576]{1,0:T(8,128)(2,1)S(1)}, u32[]{:S(2)}, u32[]{:S(2)}) %collective-permute-start.6) | collective-permute-done | bytes 73760 | tf_op jit(solution)/shard_map/ppermute | solution.py:124
  76.8 3.5 %collective-permute-start.8 = (bf16[8,64,576]{2,1,0:T(8,128)(2,1)}, bf16[8,64,576]{2,1,0:T(8,128)(2,1)S(1)}, u32[]{:S(2)}, u32[]{:S(2)}) collective-permute-start(bf16[8,64,576]{2,1,0:T(8,128)(2,1)} %get-tuple-element.20), channel_id=1, source_target_pairs={{0,16},{16,0},{1,17},{17,1},{2,18},{18,2},{3,19},{19,3},{4,20},{20... | collective-permute-start | bytes 1769480 | tf_op jit(solution)/shard_map/ppermute | solution.py:95
  80.3 25.1 %collective-permute-done.7 = bf16[8,64,576]{2,1,0:T(8,128)(2,1)S(1)} collective-permute-done((bf16[8,64,576]{2,1,0:T(8,128)(2,1)}, bf16[8,64,576]{2,1,0:T(8,128)(2,1)S(1)}, u32[]{:S(2)}, u32[]{:S(2)}) %collective-permute-start.7) | collective-permute-done | bytes 589856 | tf_op jit(solution)/shard_map/ppermute | solution.py:93
  105.4 5.1 %collective-permute-start.9 = (bf16[8,64,576]{2,1,0:T(8,128)(2,1)S(1)}, bf16[8,64,576]{2,1,0:T(8,128)(2,1)S(1)}, u32[]{:S(2)}, u32[]{:S(2)}) collective-permute-start(bf16[8,64,576]{2,1,0:T(8,128)(2,1)S(1)} %collective-permute-done.7), channel_id=1, source_target_pairs={{0,17},{1,16},{16,1},{17,0},{2,19},{3,18},{18,3},{19,2},{4,21},{5,... | collective-permute-start | bytes 1769480 | tf_op jit(solution)/shard_map/ppermute | solution.py:96
  110.5 14.7 %all-gather.2.cloned.1.call-done = bf16[1024,1792]{0,1:T(8,128)(2,1)} async-done(((bf16[1024,112]{0,1:T(8,128)(2,1)}), bf16[1024,1792]{0,1:T(8,128)(2,1)}) %all-gather.2.cloned.1.call-update) | async-done | bytes 3670032 | tf_op jit(solution)/shard_map/all_gather | solution.py:206
  125.2 1.9 %collective-permute-start.12 = (bf16[1024,1792]{0,1:T(8,128)(2,1)}, bf16[1024,1792]{0,1:T(8,128)(2,1)}, u32[]{:S(2)}, u32[]{:S(2)}) collective-permute-start(bf16[1024,1792]{0,1:T(8,128)(2,1)} %all-gather.2.cloned.1.call-done), channel_id=1, source_target_pairs={{0,8},{8,0},{1,9},{9,1},{2,10},{10,2},{3,11},{11,3},{4,12},{12,4},... | collective-permute-start | bytes 11010056 | tf_op jit(solution)/shard_map/ppermute | solution.py:207
  129.9 2.4 %collective-permute-start.10 = (bf16[32,64,576]{2,1,0:T(8,128)(2,1)}, bf16[32,64,576]{2,1,0:T(8,128)(2,1)}, u32[]{:S(2)}, u32[]{:S(2)}) collective-permute-start(bf16[32,64,576]{2,1,0:T(8,128)(2,1)} %constant_dynamic-update-slice_fusion), channel_id=1, source_target_pairs={{0,8},{8,0},{1,9},{9,1},{2,10},{10,2},{3,11},{11,3},{4,12},{12,4},... | collective-permute-start | bytes 7077896 | tf_op jit(solution)/shard_map/ppermute | solution.py:93
  137.6 11.7 %shard_map.82 = bf16[512,512]{1,0:T(8,128)(2,1)} custom-call(bf16[512,576]{1,0:T(8,128)(2,1)} %bitcast.109, s32[512,1]{1,0:T(8,128)} %reshape_reshape.4.qi_ref, bf16[2048,576]{1,0:T(8,128)(2,1)} %bitcast.112, s32[1,2048]{1,0:T(1,128)} %add.130.ia_ref, bf16[2048,576]{1,0:T(8,128)(2,1)} %bitcast.14.kb_ref, s32[1,2048]{1,0:T(1,128)} %add.134.ib_ref), custom_call_target="tpu_custom_call" | custom-call | flops 4563402752 | bytes 5832704 | tf_op jit(solution)/shard_map/pallas_call | solution.py:83
  150.8 3.3 %fusion.12 = f32[64,1792]{1,0:T(8,128)S(1)} fusion(bf16[1024,1792]{0,1:T(8,128)(2,1)} %all-gather.2.cloned.1.call-done, bf16[8,8,8,128]{3,2,1,0:T(8,128)(2,1)S(1)} %fusion.1), kind=kOutput, calls=%fused_computation.26 | convolution fusion | flops 234881024 | bytes 4259840 | tf_op jit(solution)/shard_map/dot_general | solution.py:210
  154.1 3.3 %broadcast_select_fusion.1 = (f32[64,1792]{1,0:T(8,128)S(1)}, f32[64,1792]{1,0:T(8,128)S(1)}) fusion(f32[64,1792]{1,0:T(8,128)S(1)} %fusion.12, pred[]{:T(512)S(6)} %eq.8, bf16[1024,1792]{0,1:T(8,128)(2,1)} %collective-permute-done.12, bf16[8,8,8,128]{3,2,1,0:T(8,128)(2,1)S(1)} %fusion.1), kind=kOutput, calls=%fused_computation.22 | convolution fusion | flops 235110400 | bytes 5177345 | tf_op jit(solution)/shard_map/dot_general | solution.py:211
  159.0 2.5 %collective-permute-start.13 = (bf16[2,64,448]{2,1,0:T(8,128)(2,1)S(1)}, bf16[2,64,448]{2,1,0:T(8,128)(2,1)S(1)}, u32[]{:S(2)}, u32[]{:S(2)}) collective-permute-start(bf16[2,64,448]{2,1,0:T(8,128)(2,1)S(1)} %get-tuple-element.9), channel_id=1, source_target_pairs={{0,2},{2,0},{4,6},{6,4},{1,3},{3,1},{5,7},{7,5},{8,10},{10,8},{12,... | collective-permute-start | bytes 344072 | tf_op jit(solution)/shard_map/ppermute | solution.py:149
  161.4 3.0 %collective-permute-start.14 = (bf16[2,64,448]{2,1,0:T(8,128)(2,1)S(1)}, bf16[2,64,448]{2,1,0:T(8,128)(2,1)S(1)}, u32[]{:S(2)}, u32[]{:S(2)}) collective-permute-start(bf16[2,64,448]{2,1,0:T(8,128)(2,1)S(1)} %get-tuple-element.11), channel_id=1, source_target_pairs={{0,4},{2,6},{4,0},{6,2},{1,5},{3,7},{5,1},{7,3},{8,12},{10,14},{12... | collective-permute-start | bytes 344072 | tf_op jit(solution)/shard_map/ppermute | solution.py:149
  164.5 4.9 %collective-permute-start.15 = (bf16[2,64,448]{2,1,0:T(8,128)(2,1)S(1)}, bf16[2,64,448]{2,1,0:T(8,128)(2,1)S(1)}, u32[]{:S(2)}, u32[]{:S(2)}) collective-permute-start(bf16[2,64,448]{2,1,0:T(8,128)(2,1)S(1)} %get-tuple-element.10), channel_id=1, source_target_pairs={{0,6},{2,4},{4,2},{6,0},{1,7},{3,5},{5,3},{7,1},{8,14},{10,12},{12... | collective-permute-start | bytes 344072 | tf_op jit(solution)/shard_map/ppermute | solution.py:149
  170.1 2.8 %collective-permute-done.15 = bf16[2,64,448]{2,1,0:T(8,128)(2,1)S(1)} collective-permute-done((bf16[2,64,448]{2,1,0:T(8,128)(2,1)S(1)}, bf16[2,64,448]{2,1,0:T(8,128)(2,1)S(1)}, u32[]{:S(2)}, u32[]{:S(2)}) %collective-permute-start.15) | collective-permute-done | bytes 114720 | tf_op jit(solution)/shard_map/ppermute | solution.py:149
  173.0 5.4 %collective-permute-start.16 = (bf16[64,448]{1,0:T(8,128)(2,1)S(1)}, bf16[64,448]{1,0:T(8,128)(2,1)S(1)}, u32[]{:S(2)}, u32[]{:S(2)}) collective-permute-start(bf16[64,448]{1,0:T(8,128)(2,1)S(1)} %fusion.21), channel_id=1, source_target_pairs={{0,1},{1,0},{2,3},{3,2},{4,5},{5,4},{6,7},{7,6},{8,9},{9,8},{10,11... | collective-permute-start | bytes 172040 | tf_op jit(solution)/shard_map/ppermute | solution.py:155
  178.4 2.3 %collective-permute-done.16 = bf16[64,448]{1,0:T(8,128)(2,1)S(1)} collective-permute-done((bf16[64,448]{1,0:T(8,128)(2,1)S(1)}, bf16[64,448]{1,0:T(8,128)(2,1)S(1)}, u32[]{:S(2)}, u32[]{:S(2)}) %collective-permute-start.16) | collective-permute-done | bytes 57376 | tf_op jit(solution)/shard_map/ppermute | solution.py:155
  (75 shorter events, 29.2 us)
Async XLA Ops:
  6.5 128.9 %copy-start = (bf16[512,1024]{1,0:T(8,128)(2,1)S(1)}, bf16[512,1024]{1,0:T(8,128)(2,1)}, u32[]{:S(2)}) copy-start(bf16[512,1024]{1,0:T(8,128)(2,1)} %param.13) | copy-start | bytes 3145732
  6.5 118.7 %all-gather.2.cloned.1.call-start = ((), (), s32[]{:S(2)}) async-start(), calls=%async_computation | async-start | bytes 3899392 | tf_op jit(solution)/shard_map/all_gather | solution.py:206
  6.5 7.1 %collective-permute-start.11 = (bf16[1,56,1024]{2,1,0:T(8,128)(2,1)}, bf16[1,56,1024]{2,1,0:T(8,128)(2,1)S(1)}, u32[]{:S(2)}, u32[]{:S(2)}) collective-permute-start(bf16[1,56,1024]{2,1,0:T(8,128)(2,1)} %bitcast.111), channel_id=1, source_target_pairs={{0,16},{16,0},{1,17},{17,1},{2,18},{18,2},{3,19},{19,3},{4,20},{20... | collective-permute-start | bytes 344072 | tf_op jit(solution)/shard_map/ppermute | solution.py:93
  17.9 28.2 %collective-permute-start = (bf16[64,576]{1,0:T(8,128)(2,1)S(1)}, bf16[64,576]{1,0:T(8,128)(2,1)S(1)}, u32[]{:S(2)}, u32[]{:S(2)}) collective-permute-start(bf16[64,576]{1,0:T(8,128)(2,1)S(1)} %pad_maximum_fusion.2), channel_id=1, source_target_pairs={{0,64},{64,128},{128,192},{192,256},{256,320},{320,384},{384,448},... | collective-permute-start | bytes 221192 | tf_op jit(solution)/shard_map/ppermute | solution.py:124
  23.1 25.0 %collective-permute-start.1 = (bf16[64,576]{1,0:T(8,128)(2,1)S(1)}, bf16[64,576]{1,0:T(8,128)(2,1)S(1)}, u32[]{:S(2)}, u32[]{:S(2)}) collective-permute-start(bf16[64,576]{1,0:T(8,128)(2,1)S(1)} %pad_maximum_fusion.2), channel_id=1, source_target_pairs={{0,128},{64,192},{128,256},{192,320},{256,384},{320,448},{1,129},{... | collective-permute-start | bytes 221192 | tf_op jit(solution)/shard_map/ppermute | solution.py:124
  32.2 17.8 %collective-permute-start.2 = (bf16[64,576]{1,0:T(8,128)(2,1)S(1)}, bf16[64,576]{1,0:T(8,128)(2,1)S(1)}, u32[]{:S(2)}, u32[]{:S(2)}) collective-permute-start(bf16[64,576]{1,0:T(8,128)(2,1)S(1)} %pad_maximum_fusion.2), channel_id=1, source_target_pairs={{0,192},{64,256},{128,320},{192,384},{256,448},{1,193},{65,257},{1... | collective-permute-start | bytes 221192 | tf_op jit(solution)/shard_map/ppermute | solution.py:124
  40.4 10.3 %collective-permute-start.3 = (bf16[64,576]{1,0:T(8,128)(2,1)S(1)}, bf16[64,576]{1,0:T(8,128)(2,1)S(1)}, u32[]{:S(2)}, u32[]{:S(2)}) collective-permute-start(bf16[64,576]{1,0:T(8,128)(2,1)S(1)} %pad_maximum_fusion.2), channel_id=1, source_target_pairs={{0,256},{64,320},{128,384},{192,448},{1,257},{65,321},{129,385},{1... | collective-permute-start | bytes 221192 | tf_op jit(solution)/shard_map/ppermute | solution.py:124
  43.2 20.4 %collective-permute-start.4 = (bf16[64,576]{1,0:T(8,128)(2,1)S(1)}, bf16[64,576]{1,0:T(8,128)(2,1)S(1)}, u32[]{:S(2)}, u32[]{:S(2)}) collective-permute-start(bf16[64,576]{1,0:T(8,128)(2,1)S(1)} %pad_maximum_fusion.2), channel_id=1, source_target_pairs={{0,320},{64,384},{128,448},{1,321},{65,385},{129,449},{2,322},{66,... | collective-permute-start | bytes 221192 | tf_op jit(solution)/shard_map/ppermute | solution.py:124
  46.1 23.5 %collective-permute-start.5 = (bf16[64,576]{1,0:T(8,128)(2,1)S(1)}, bf16[64,576]{1,0:T(8,128)(2,1)S(1)}, u32[]{:S(2)}, u32[]{:S(2)}) collective-permute-start(bf16[64,576]{1,0:T(8,128)(2,1)S(1)} %pad_maximum_fusion.2), channel_id=1, source_target_pairs={{0,384},{64,448},{1,385},{65,449},{2,386},{66,450},{3,387},{67,451... | collective-permute-start | bytes 221192 | tf_op jit(solution)/shard_map/ppermute | solution.py:124
  48.1 26.2 %collective-permute-start.6 = (bf16[64,576]{1,0:T(8,128)(2,1)S(1)}, bf16[64,576]{1,0:T(8,128)(2,1)S(1)}, u32[]{:S(2)}, u32[]{:S(2)}) collective-permute-start(bf16[64,576]{1,0:T(8,128)(2,1)S(1)} %pad_maximum_fusion.2), channel_id=1, source_target_pairs={{0,448},{1,449},{2,450},{3,451},{4,452},{5,453},{6,454},{7,455},{8... | collective-permute-start | bytes 221192 | tf_op jit(solution)/shard_map/ppermute | solution.py:124
  51.4 83.5 %copy-start.1 = (bf16[64,512]{1,0:T(8,128)(2,1)S(1)}, bf16[64,512]{1,0:T(8,128)(2,1)}, u32[]{:S(2)}) copy-start(bf16[64,512]{1,0:T(8,128)(2,1)} %param.9) | copy-start | bytes 196612
  74.9 30.5 %collective-permute-start.7 = (bf16[8,64,576]{2,1,0:T(8,128)(2,1)}, bf16[8,64,576]{2,1,0:T(8,128)(2,1)S(1)}, u32[]{:S(2)}, u32[]{:S(2)}) collective-permute-start(bf16[8,64,576]{2,1,0:T(8,128)(2,1)} %get-tuple-element.20), channel_id=1, source_target_pairs={{0,32},{32,0},{1,33},{33,1},{2,34},{34,2},{3,35},{35,3},{4,36},{36... | collective-permute-start | bytes 1769480 | tf_op jit(solution)/shard_map/ppermute | solution.py:93
  76.8 51.2 %collective-permute-start.8 = (bf16[8,64,576]{2,1,0:T(8,128)(2,1)}, bf16[8,64,576]{2,1,0:T(8,128)(2,1)S(1)}, u32[]{:S(2)}, u32[]{:S(2)}) collective-permute-start(bf16[8,64,576]{2,1,0:T(8,128)(2,1)} %get-tuple-element.20), channel_id=1, source_target_pairs={{0,16},{16,0},{1,17},{17,1},{2,18},{18,2},{3,19},{19,3},{4,20},{20... | collective-permute-start | bytes 1769480 | tf_op jit(solution)/shard_map/ppermute | solution.py:95
  105.4 23.5 %collective-permute-start.9 = (bf16[8,64,576]{2,1,0:T(8,128)(2,1)S(1)}, bf16[8,64,576]{2,1,0:T(8,128)(2,1)S(1)}, u32[]{:S(2)}, u32[]{:S(2)}) collective-permute-start(bf16[8,64,576]{2,1,0:T(8,128)(2,1)S(1)} %collective-permute-done.7), channel_id=1, source_target_pairs={{0,17},{1,16},{16,1},{17,0},{2,19},{3,18},{18,3},{19,2},{4,21},{5,... | collective-permute-start | bytes 1769480 | tf_op jit(solution)/shard_map/ppermute | solution.py:96
  125.2 28.9 %collective-permute-start.12 = (bf16[1024,1792]{0,1:T(8,128)(2,1)}, bf16[1024,1792]{0,1:T(8,128)(2,1)}, u32[]{:S(2)}, u32[]{:S(2)}) collective-permute-start(bf16[1024,1792]{0,1:T(8,128)(2,1)} %all-gather.2.cloned.1.call-done), channel_id=1, source_target_pairs={{0,8},{8,0},{1,9},{9,1},{2,10},{10,2},{3,11},{11,3},{4,12},{12,4},... | collective-permute-start | bytes 11010056 | tf_op jit(solution)/shard_map/ppermute | solution.py:207
  128.0 7.5 %copy-start.3 = (bf16[64,1024]{1,0:T(8,128)(2,1)S(1)}, bf16[64,1024]{1,0:T(8,128)(2,1)}, u32[]{:S(2)}) copy-start(bf16[64,1024]{1,0:T(8,128)(2,1)} %param.8) | copy-start | bytes 393220
  129.9 7.7 %collective-permute-start.10 = (bf16[32,64,576]{2,1,0:T(8,128)(2,1)}, bf16[32,64,576]{2,1,0:T(8,128)(2,1)}, u32[]{:S(2)}, u32[]{:S(2)}) collective-permute-start(bf16[32,64,576]{2,1,0:T(8,128)(2,1)} %constant_dynamic-update-slice_fusion), channel_id=1, source_target_pairs={{0,8},{8,0},{1,9},{9,1},{2,10},{10,2},{3,11},{11,3},{4,12},{12,4},... | collective-permute-start | bytes 7077896 | tf_op jit(solution)/shard_map/ppermute | solution.py:93
  137.6 11.7 %copy-start.2 = (bf16[512,1024]{1,0:T(8,128)(2,1)S(1)}, bf16[512,1024]{1,0:T(8,128)(2,1)}, u32[]{:S(2)}) copy-start(bf16[512,1024]{1,0:T(8,128)(2,1)} %param.14) | copy-start | bytes 3145732
  159.0 10.5 %collective-permute-start.13 = (bf16[2,64,448]{2,1,0:T(8,128)(2,1)S(1)}, bf16[2,64,448]{2,1,0:T(8,128)(2,1)S(1)}, u32[]{:S(2)}, u32[]{:S(2)}) collective-permute-start(bf16[2,64,448]{2,1,0:T(8,128)(2,1)S(1)} %get-tuple-element.9), channel_id=1, source_target_pairs={{0,2},{2,0},{4,6},{6,4},{1,3},{3,1},{5,7},{7,5},{8,10},{10,8},{12,... | collective-permute-start | bytes 344072 | tf_op jit(solution)/shard_map/ppermute | solution.py:149
  161.4 8.7 %collective-permute-start.14 = (bf16[2,64,448]{2,1,0:T(8,128)(2,1)S(1)}, bf16[2,64,448]{2,1,0:T(8,128)(2,1)S(1)}, u32[]{:S(2)}, u32[]{:S(2)}) collective-permute-start(bf16[2,64,448]{2,1,0:T(8,128)(2,1)S(1)} %get-tuple-element.11), channel_id=1, source_target_pairs={{0,4},{2,6},{4,0},{6,2},{1,5},{3,7},{5,1},{7,3},{8,12},{10,14},{12... | collective-permute-start | bytes 344072 | tf_op jit(solution)/shard_map/ppermute | solution.py:149
  164.5 8.4 %collective-permute-start.15 = (bf16[2,64,448]{2,1,0:T(8,128)(2,1)S(1)}, bf16[2,64,448]{2,1,0:T(8,128)(2,1)S(1)}, u32[]{:S(2)}, u32[]{:S(2)}) collective-permute-start(bf16[2,64,448]{2,1,0:T(8,128)(2,1)S(1)} %get-tuple-element.10), channel_id=1, source_target_pairs={{0,6},{2,4},{4,2},{6,0},{1,7},{3,5},{5,3},{7,1},{8,14},{10,12},{12... | collective-permute-start | bytes 344072 | tf_op jit(solution)/shard_map/ppermute | solution.py:149
  173.0 7.7 %collective-permute-start.16 = (bf16[64,448]{1,0:T(8,128)(2,1)S(1)}, bf16[64,448]{1,0:T(8,128)(2,1)S(1)}, u32[]{:S(2)}, u32[]{:S(2)}) collective-permute-start(bf16[64,448]{1,0:T(8,128)(2,1)S(1)} %fusion.21), channel_id=1, source_target_pairs={{0,1},{1,0},{2,3},{3,2},{4,5},{5,4},{6,7},{7,6},{8,9},{9,8},{10,11... | collective-permute-start | bytes 172040 | tf_op jit(solution)/shard_map/ppermute | solution.py:155
Sparse Core Ops, SparseCore 0:
  15.4 109.7 all-gather.1

commit v11 on v10

--- a/solution.py
+++ b/solution.py
@@ -207,13 +207,18 @@
     swapped = lax.ppermute(own, "co", [(0, 1), (1, 0)])
     upper = lax.axis_index("co") == 1
     groups = lax.axis_size(HEAD)
-    from_own = jnp.dot(head_out, own, preferred_element_type=jnp.float32)
-    from_swapped = jnp.dot(head_out, swapped, preferred_element_type=jnp.float32)
-    halves = [jnp.where(upper, from_swapped, from_own), jnp.where(upper, from_own, from_swapped)]
-    partial_sums = jnp.concatenate(
-        [half.reshape(token_count, groups, -1) for half in halves], axis=2
-    ).transpose(1, 0, 2)
+    halves = [
+        jnp.dot(head_out, half, preferred_element_type=jnp.float32).reshape(token_count, groups, -1)
+        for half in (own, swapped)
+    ]
+    partial_sums = jnp.concatenate(halves, axis=2).transpose(1, 0, 2)
     mine = scatter_sum(partial_sums)
+    half_width = mine.shape[1] // 2
+    mine = jnp.where(
+        upper,
+        jnp.concatenate([mine[:, half_width:], mine[:, :half_width]], axis=1),
+        mine,
+    )
     width = out_proj.shape[1]
     mine = mine.reshape(token_count, 2, -1, width).transpose(0, 2, 1, 3)
     return mine.reshape(token_count, -1).astype(jnp.bfloat16)

time: 192 us -> 191 us (level)
  no operation moved by 1% of the time
where the time goes in v11:
time: 191 us; the launch traced here: 188 us
  waiting for transfers between devices  70.7 us (37%)
  starting transfers between devices  63.4 us (33%)
  between operations  13.8 us (7%)
  local copies, waits for them, and re-layouts  13.6 us (7%)
  Pallas kernels  11.7 us (6%)
  matrix products  8.57 us (4%)
  other arithmetic  6.02 us (3%)
    ppermute x7, starting transfers between devices, gather_earlier_keys(): lax.ppermute(local, 'zh', [(i, i + shift) for i in range(cubes - shift)])  29.2 us
    ppermute x3, waiting for transfers between devices, exchange(): return lax.ppermute(acc, axis, pairs)  28.8 us
    ppermute x7, waiting for transfers between devices, gather_earlier_keys(): lax.ppermute(local, 'zh', [(i, i + shift) for i in range(cubes - shift)])  21.4 us
    all_gather x1, waiting for transfers between devices, body(): own = lax.all_gather(pair, ('zh', 'zl'), axis=1, tiled=True)  14.7 us
    pallas_call x1, Pallas kernels, attend(): pl.pallas_call(attention_kernel, out_shape=jax.ShapeDtypeStruct((rows, LA...  11.7 us
    ppermute x3, starting transfers between devices, scatter_sum(): lax.ppermute(sent, 'x', [(i, i ^ shift) for i in range(columns)])  10.4 us
    ppermute x3, starting transfers between devices, exchange(): return lax.ppermute(acc, axis, pairs)  7.91 us
    unnamed x17, local copies, waits for them, and re-layouts  6.76 us
  transfers between devices with their start and end apart: 18, of which 10 were waited for; matrix products, arithmetic and copies ran while one was open for 11% of the time, Pallas kernels for 6%

profile of v11, /device:TPU:6, one launch (start us, length us, event | category | flops | bytes accessed | tf_op | source)
XLA Modules:
  0.0 187.7 jit_solution(1195509145300369474)
XLA Ops:
  6.5 3.6 %collective-permute-start.11 = (bf16[1,56,1024]{2,1,0:T(8,128)(2,1)}, bf16[1,56,1024]{2,1,0:T(8,128)(2,1)S(1)}, u32[]{:S(2)}, u32[]{:S(2)}) collective-permute-start(bf16[1,56,1024]{2,1,0:T(8,128)(2,1)} %bitcast.110), channel_id=1, source_target_pairs={{0,16},{16,0},{1,17},{17,1},{2,18},{18,2},{3,19},{19,3},{4,20},{20... | collective-permute-start | bytes 344072 | tf_op jit(solution)/shard_map/ppermute | solution.py:93
  10.2 3.5 %collective-permute-done.11 = bf16[1,56,1024]{2,1,0:T(8,128)(2,1)S(1)} collective-permute-done((bf16[1,56,1024]{2,1,0:T(8,128)(2,1)}, bf16[1,56,1024]{2,1,0:T(8,128)(2,1)S(1)}, u32[]{:S(2)}, u32[]{:S(2)}) %collective-permute-start.11) | collective-permute-done | bytes 114720 | tf_op jit(solution)/shard_map/ppermute | solution.py:93
  17.9 5.2 %collective-permute-start = (bf16[64,576]{1,0:T(8,128)(2,1)S(1)}, bf16[64,576]{1,0:T(8,128)(2,1)S(1)}, u32[]{:S(2)}, u32[]{:S(2)}) collective-permute-start(bf16[64,576]{1,0:T(8,128)(2,1)S(1)} %pad_maximum_fusion.3), channel_id=1, source_target_pairs={{0,64},{64,128},{128,192},{192,256},{256,320},{320,384},{384,448},... | collective-permute-start | bytes 221192 | tf_op jit(solution)/shard_map/ppermute | solution.py:124
  23.1 9.1 %collective-permute-start.1 = (bf16[64,576]{1,0:T(8,128)(2,1)S(1)}, bf16[64,576]{1,0:T(8,128)(2,1)S(1)}, u32[]{:S(2)}, u32[]{:S(2)}) collective-permute-start(bf16[64,576]{1,0:T(8,128)(2,1)S(1)} %pad_maximum_fusion.3), channel_id=1, source_target_pairs={{0,128},{64,192},{128,256},{192,320},{256,384},{320,448},{1,129},{... | collective-permute-start | bytes 221192 | tf_op jit(solution)/shard_map/ppermute | solution.py:124
  32.2 8.2 %collective-permute-start.2 = (bf16[64,576]{1,0:T(8,128)(2,1)S(1)}, bf16[64,576]{1,0:T(8,128)(2,1)S(1)}, u32[]{:S(2)}, u32[]{:S(2)}) collective-permute-start(bf16[64,576]{1,0:T(8,128)(2,1)S(1)} %pad_maximum_fusion.3), channel_id=1, source_target_pairs={{0,192},{64,256},{128,320},{192,384},{256,448},{1,193},{65,257},{1... | collective-permute-start | bytes 221192 | tf_op jit(solution)/shard_map/ppermute | solution.py:124
  40.4 2.8 %collective-permute-start.3 = (bf16[64,576]{1,0:T(8,128)(2,1)S(1)}, bf16[64,576]{1,0:T(8,128)(2,1)S(1)}, u32[]{:S(2)}, u32[]{:S(2)}) collective-permute-start(bf16[64,576]{1,0:T(8,128)(2,1)S(1)} %pad_maximum_fusion.3), channel_id=1, source_target_pairs={{0,256},{64,320},{128,384},{192,448},{1,257},{65,321},{129,385},{1... | collective-permute-start | bytes 221192 | tf_op jit(solution)/shard_map/ppermute | solution.py:124
  51.4 12.3 %collective-permute-done.4 = bf16[64,576]{1,0:T(8,128)(2,1)S(1)} collective-permute-done((bf16[64,576]{1,0:T(8,128)(2,1)S(1)}, bf16[64,576]{1,0:T(8,128)(2,1)S(1)}, u32[]{:S(2)}, u32[]{:S(2)}) %collective-permute-start.4) | collective-permute-done | bytes 73760 | tf_op jit(solution)/shard_map/ppermute | solution.py:124
  64.4 5.2 %collective-permute-done.5 = bf16[64,576]{1,0:T(8,128)(2,1)S(1)} collective-permute-done((bf16[64,576]{1,0:T(8,128)(2,1)S(1)}, bf16[64,576]{1,0:T(8,128)(2,1)S(1)}, u32[]{:S(2)}, u32[]{:S(2)}) %collective-permute-start.5) | collective-permute-done | bytes 73760 | tf_op jit(solution)/shard_map/ppermute | solution.py:124
  70.3 3.9 %collective-permute-done.6 = bf16[64,576]{1,0:T(8,128)(2,1)S(1)} collective-permute-done((bf16[64,576]{1,0:T(8,128)(2,1)S(1)}, bf16[64,576]{1,0:T(8,128)(2,1)S(1)}, u32[]{:S(2)}, u32[]{:S(2)}) %collective-permute-start.6) | collective-permute-done | bytes 73760 | tf_op jit(solution)/shard_map/ppermute | solution.py:124
  76.8 3.5 %collective-permute-start.8 = (bf16[8,64,576]{2,1,0:T(8,128)(2,1)}, bf16[8,64,576]{2,1,0:T(8,128)(2,1)S(1)}, u32[]{:S(2)}, u32[]{:S(2)}) collective-permute-start(bf16[8,64,576]{2,1,0:T(8,128)(2,1)} %get-tuple-element.18), channel_id=1, source_target_pairs={{0,16},{16,0},{1,17},{17,1},{2,18},{18,2},{3,19},{19,3},{4,20},{20... | collective-permute-start | bytes 1769480 | tf_op jit(solution)/shard_map/ppermute | solution.py:95
  80.3 25.1 %collective-permute-done.7 = bf16[8,64,576]{2,1,0:T(8,128)(2,1)S(1)} collective-permute-done((bf16[8,64,576]{2,1,0:T(8,128)(2,1)}, bf16[8,64,576]{2,1,0:T(8,128)(2,1)S(1)}, u32[]{:S(2)}, u32[]{:S(2)}) %collective-permute-start.7) | collective-permute-done | bytes 589856 | tf_op jit(solution)/shard_map/ppermute | solution.py:93
  105.4 5.1 %collective-permute-start.9 = (bf16[8,64,576]{2,1,0:T(8,128)(2,1)S(1)}, bf16[8,64,576]{2,1,0:T(8,128)(2,1)S(1)}, u32[]{:S(2)}, u32[]{:S(2)}) collective-permute-start(bf16[8,64,576]{2,1,0:T(8,128)(2,1)S(1)} %collective-permute-done.7), channel_id=1, source_target_pairs={{0,17},{1,16},{16,1},{17,0},{2,19},{3,18},{18,3},{19,2},{4,21},{5,... | collective-permute-start | bytes 1769480 | tf_op jit(solution)/shard_map/ppermute | solution.py:96
  110.5 14.7 %all-gather.2.cloned.1.call-done = bf16[1024,1792]{0,1:T(8,128)(2,1)} async-done(((bf16[1024,112]{0,1:T(8,128)(2,1)}), bf16[1024,1792]{0,1:T(8,128)(2,1)}) %all-gather.2.cloned.1.call-update) | async-done | bytes 3670032 | tf_op jit(solution)/shard_map/all_gather | solution.py:206
  125.2 1.9 %collective-permute-start.12 = (bf16[1024,1792]{0,1:T(8,128)(2,1)}, bf16[1024,1792]{0,1:T(8,128)(2,1)}, u32[]{:S(2)}, u32[]{:S(2)}) collective-permute-start(bf16[1024,1792]{0,1:T(8,128)(2,1)} %all-gather.2.cloned.1.call-done), channel_id=1, source_target_pairs={{0,8},{8,0},{1,9},{9,1},{2,10},{10,2},{3,11},{11,3},{4,12},{12,4},... | collective-permute-start | bytes 11010056 | tf_op jit(solution)/shard_map/ppermute | solution.py:207
  129.9 2.4 %collective-permute-start.10 = (bf16[32,64,576]{2,1,0:T(8,128)(2,1)}, bf16[32,64,576]{2,1,0:T(8,128)(2,1)}, u32[]{:S(2)}, u32[]{:S(2)}) collective-permute-start(bf16[32,64,576]{2,1,0:T(8,128)(2,1)} %constant_dynamic-update-slice_fusion), channel_id=1, source_target_pairs={{0,8},{8,0},{1,9},{9,1},{2,10},{10,2},{3,11},{11,3},{4,12},{12,4},... | collective-permute-start | bytes 7077896 | tf_op jit(solution)/shard_map/ppermute | solution.py:93
  137.6 11.7 %shard_map.82 = bf16[512,512]{1,0:T(8,128)(2,1)} custom-call(bf16[512,576]{1,0:T(8,128)(2,1)} %bitcast.108, s32[512,1]{1,0:T(8,128)} %reshape_reshape.4.qi_ref, bf16[2048,576]{1,0:T(8,128)(2,1)} %bitcast.111, s32[1,2048]{1,0:T(1,128)} %add.130.ia_ref, bf16[2048,576]{1,0:T(8,128)(2,1)} %bitcast.14.kb_ref, s32[1,2048]{1,0:T(1,128)} %add.134.ib_ref), custom_call_target="tpu_custom_call" | custom-call | flops 4563402752 | bytes 5832704 | tf_op jit(solution)/shard_map/pallas_call | solution.py:83
  150.9 3.3 %fusion.27 = f32[64,8,224]{2,0,1:T(8,128)S(1)} fusion(bf16[64,1024,1]{1,0,2:T(8,128)(2,1)S(1)} %reshape.271, bf16[8,224,1024]{2,1,0:T(8,128)(2,1)} %bitcast.104), kind=kOutput, calls=%fused_computation.81 | convolution fusion | flops 234881024 | bytes 4259840 | tf_op jit(solution)/shard_map/dot_general | solution.py:211
  154.2 3.3 %fusion.28 = f32[64,8,224]{2,0,1:T(8,128)S(1)} fusion(bf16[64,1024,1]{1,0,2:T(8,128)(2,1)S(1)} %reshape.271, bf16[8,224,1024]{2,1,0:T(8,128)(2,1)} %bitcast.28), kind=kOutput, calls=%fused_computation.82 | convolution fusion | flops 234881024 | bytes 4259840 | tf_op jit(solution)/shard_map/dot_general | solution.py:211
  157.9 2.5 %collective-permute-start.13 = (bf16[2,64,448]{2,1,0:T(8,128)(2,1)S(1)}, bf16[2,64,448]{2,1,0:T(8,128)(2,1)S(1)}, u32[]{:S(2)}, u32[]{:S(2)}) collective-permute-start(bf16[2,64,448]{2,1,0:T(8,128)(2,1)S(1)} %get-tuple-element.9), channel_id=1, source_target_pairs={{0,2},{2,0},{4,6},{6,4},{1,3},{3,1},{5,7},{7,5},{8,10},{10,8},{12,... | collective-permute-start | bytes 344072 | tf_op jit(solution)/shard_map/ppermute | solution.py:149
  160.4 3.0 %collective-permute-start.14 = (bf16[2,64,448]{2,1,0:T(8,128)(2,1)S(1)}, bf16[2,64,448]{2,1,0:T(8,128)(2,1)S(1)}, u32[]{:S(2)}, u32[]{:S(2)}) collective-permute-start(bf16[2,64,448]{2,1,0:T(8,128)(2,1)S(1)} %get-tuple-element.11), channel_id=1, source_target_pairs={{0,4},{2,6},{4,0},{6,2},{1,5},{3,7},{5,1},{7,3},{8,12},{10,14},{12... | collective-permute-start | bytes 344072 | tf_op jit(solution)/shard_map/ppermute | solution.py:149
  163.4 4.9 %collective-permute-start.15 = (bf16[2,64,448]{2,1,0:T(8,128)(2,1)S(1)}, bf16[2,64,448]{2,1,0:T(8,128)(2,1)S(1)}, u32[]{:S(2)}, u32[]{:S(2)}) collective-permute-start(bf16[2,64,448]{2,1,0:T(8,128)(2,1)S(1)} %get-tuple-element.10), channel_id=1, source_target_pairs={{0,6},{2,4},{4,2},{6,0},{1,7},{3,5},{5,3},{7,1},{8,14},{10,12},{12... | collective-permute-start | bytes 344072 | tf_op jit(solution)/shard_map/ppermute | solution.py:149
  169.0 2.8 %collective-permute-done.15 = bf16[2,64,448]{2,1,0:T(8,128)(2,1)S(1)} collective-permute-done((bf16[2,64,448]{2,1,0:T(8,128)(2,1)S(1)}, bf16[2,64,448]{2,1,0:T(8,128)(2,1)S(1)}, u32[]{:S(2)}, u32[]{:S(2)}) %collective-permute-start.15) | collective-permute-done | bytes 114720 | tf_op jit(solution)/shard_map/ppermute | solution.py:149
  171.9 5.4 %collective-permute-start.16 = (bf16[64,448]{1,0:T(8,128)(2,1)S(1)}, bf16[64,448]{1,0:T(8,128)(2,1)S(1)}, u32[]{:S(2)}, u32[]{:S(2)}) collective-permute-start(bf16[64,448]{1,0:T(8,128)(2,1)S(1)} %fusion.15), channel_id=1, source_target_pairs={{0,1},{1,0},{2,3},{3,2},{4,5},{5,4},{6,7},{7,6},{8,9},{9,8},{10,11... | collective-permute-start | bytes 172040 | tf_op jit(solution)/shard_map/ppermute | solution.py:155
  177.3 2.3 %collective-permute-done.16 = bf16[64,448]{1,0:T(8,128)(2,1)S(1)} collective-permute-done((bf16[64,448]{1,0:T(8,128)(2,1)S(1)}, bf16[64,448]{1,0:T(8,128)(2,1)S(1)}, u32[]{:S(2)}, u32[]{:S(2)}) %collective-permute-start.16) | collective-permute-done | bytes 57376 | tf_op jit(solution)/shard_map/ppermute | solution.py:155
  (76 shorter events, 28.3 us)
Async XLA Ops:
  6.5 128.9 %copy-start = (bf16[512,1024]{1,0:T(8,128)(2,1)S(1)}, bf16[512,1024]{1,0:T(8,128)(2,1)}, u32[]{:S(2)}) copy-start(bf16[512,1024]{1,0:T(8,128)(2,1)} %param.13) | copy-start | bytes 3145732
  6.5 118.7 %all-gather.2.cloned.1.call-start = ((), (), s32[]{:S(2)}) async-start(), calls=%async_computation | async-start | bytes 3899392 | tf_op jit(solution)/shard_map/all_gather | solution.py:206
  6.5 7.1 %collective-permute-start.11 = (bf16[1,56,1024]{2,1,0:T(8,128)(2,1)}, bf16[1,56,1024]{2,1,0:T(8,128)(2,1)S(1)}, u32[]{:S(2)}, u32[]{:S(2)}) collective-permute-start(bf16[1,56,1024]{2,1,0:T(8,128)(2,1)} %bitcast.110), channel_id=1, source_target_pairs={{0,16},{16,0},{1,17},{17,1},{2,18},{18,2},{3,19},{19,3},{4,20},{20... | collective-permute-start | bytes 344072 | tf_op jit(solution)/shard_map/ppermute | solution.py:93
  17.9 28.2 %collective-permute-start = (bf16[64,576]{1,0:T(8,128)(2,1)S(1)}, bf16[64,576]{1,0:T(8,128)(2,1)S(1)}, u32[]{:S(2)}, u32[]{:S(2)}) collective-permute-start(bf16[64,576]{1,0:T(8,128)(2,1)S(1)} %pad_maximum_fusion.3), channel_id=1, source_target_pairs={{0,64},{64,128},{128,192},{192,256},{256,320},{320,384},{384,448},... | collective-permute-start | bytes 221192 | tf_op jit(solution)/shard_map/ppermute | solution.py:124
  23.1 25.0 %collective-permute-start.1 = (bf16[64,576]{1,0:T(8,128)(2,1)S(1)}, bf16[64,576]{1,0:T(8,128)(2,1)S(1)}, u32[]{:S(2)}, u32[]{:S(2)}) collective-permute-start(bf16[64,576]{1,0:T(8,128)(2,1)S(1)} %pad_maximum_fusion.3), channel_id=1, source_target_pairs={{0,128},{64,192},{128,256},{192,320},{256,384},{320,448},{1,129},{... | collective-permute-start | bytes 221192 | tf_op jit(solution)/shard_map/ppermute | solution.py:124
  32.2 17.8 %collective-permute-start.2 = (bf16[64,576]{1,0:T(8,128)(2,1)S(1)}, bf16[64,576]{1,0:T(8,128)(2,1)S(1)}, u32[]{:S(2)}, u32[]{:S(2)}) collective-permute-start(bf16[64,576]{1,0:T(8,128)(2,1)S(1)} %pad_maximum_fusion.3), channel_id=1, source_target_pairs={{0,192},{64,256},{128,320},{192,384},{256,448},{1,193},{65,257},{1... | collective-permute-start | bytes 221192 | tf_op jit(solution)/shard_map/ppermute | solution.py:124
  40.4 10.3 %collective-permute-start.3 = (bf16[64,576]{1,0:T(8,128)(2,1)S(1)}, bf16[64,576]{1,0:T(8,128)(2,1)S(1)}, u32[]{:S(2)}, u32[]{:S(2)}) collective-permute-start(bf16[64,576]{1,0:T(8,128)(2,1)S(1)} %pad_maximum_fusion.3), channel_id=1, source_target_pairs={{0,256},{64,320},{128,384},{192,448},{1,257},{65,321},{129,385},{1... | collective-permute-start | bytes 221192 | tf_op jit(solution)/shard_map/ppermute | solution.py:124
  43.2 20.4 %collective-permute-start.4 = (bf16[64,576]{1,0:T(8,128)(2,1)S(1)}, bf16[64,576]{1,0:T(8,128)(2,1)S(1)}, u32[]{:S(2)}, u32[]{:S(2)}) collective-permute-start(bf16[64,576]{1,0:T(8,128)(2,1)S(1)} %pad_maximum_fusion.3), channel_id=1, source_target_pairs={{0,320},{64,384},{128,448},{1,321},{65,385},{129,449},{2,322},{66,... | collective-permute-start | bytes 221192 | tf_op jit(solution)/shard_map/ppermute | solution.py:124
  46.1 23.5 %collective-permute-start.5 = (bf16[64,576]{1,0:T(8,128)(2,1)S(1)}, bf16[64,576]{1,0:T(8,128)(2,1)S(1)}, u32[]{:S(2)}, u32[]{:S(2)}) collective-permute-start(bf16[64,576]{1,0:T(8,128)(2,1)S(1)} %pad_maximum_fusion.3), channel_id=1, source_target_pairs={{0,384},{64,448},{1,385},{65,449},{2,386},{66,450},{3,387},{67,451... | collective-permute-start | bytes 221192 | tf_op jit(solution)/shard_map/ppermute | solution.py:124
  48.1 26.2 %collective-permute-start.6 = (bf16[64,576]{1,0:T(8,128)(2,1)S(1)}, bf16[64,576]{1,0:T(8,128)(2,1)S(1)}, u32[]{:S(2)}, u32[]{:S(2)}) collective-permute-start(bf16[64,576]{1,0:T(8,128)(2,1)S(1)} %pad_maximum_fusion.3), channel_id=1, source_target_pairs={{0,448},{1,449},{2,450},{3,451},{4,452},{5,453},{6,454},{7,455},{8... | collective-permute-start | bytes 221192 | tf_op jit(solution)/shard_map/ppermute | solution.py:124
  51.4 83.5 %copy-start.1 = (bf16[64,512]{1,0:T(8,128)(2,1)S(1)}, bf16[64,512]{1,0:T(8,128)(2,1)}, u32[]{:S(2)}) copy-start(bf16[64,512]{1,0:T(8,128)(2,1)} %param.9) | copy-start | bytes 196612
  74.9 30.5 %collective-permute-start.7 = (bf16[8,64,576]{2,1,0:T(8,128)(2,1)}, bf16[8,64,576]{2,1,0:T(8,128)(2,1)S(1)}, u32[]{:S(2)}, u32[]{:S(2)}) collective-permute-start(bf16[8,64,576]{2,1,0:T(8,128)(2,1)} %get-tuple-element.18), channel_id=1, source_target_pairs={{0,32},{32,0},{1,33},{33,1},{2,34},{34,2},{3,35},{35,3},{4,36},{36... | collective-permute-start | bytes 1769480 | tf_op jit(solution)/shard_map/ppermute | solution.py:93
  76.8 51.2 %collective-permute-start.8 = (bf16[8,64,576]{2,1,0:T(8,128)(2,1)}, bf16[8,64,576]{2,1,0:T(8,128)(2,1)S(1)}, u32[]{:S(2)}, u32[]{:S(2)}) collective-permute-start(bf16[8,64,576]{2,1,0:T(8,128)(2,1)} %get-tuple-element.18), channel_id=1, source_target_pairs={{0,16},{16,0},{1,17},{17,1},{2,18},{18,2},{3,19},{19,3},{4,20},{20... | collective-permute-start | bytes 1769480 | tf_op jit(solution)/shard_map/ppermute | solution.py:95
  105.4 23.5 %collective-permute-start.9 = (bf16[8,64,576]{2,1,0:T(8,128)(2,1)S(1)}, bf16[8,64,576]{2,1,0:T(8,128)(2,1)S(1)}, u32[]{:S(2)}, u32[]{:S(2)}) collective-permute-start(bf16[8,64,576]{2,1,0:T(8,128)(2,1)S(1)} %collective-permute-done.7), channel_id=1, source_target_pairs={{0,17},{1,16},{16,1},{17,0},{2,19},{3,18},{18,3},{19,2},{4,21},{5,... | collective-permute-start | bytes 1769480 | tf_op jit(solution)/shard_map/ppermute | solution.py:96
  125.2 29.0 %collective-permute-start.12 = (bf16[1024,1792]{0,1:T(8,128)(2,1)}, bf16[1024,1792]{0,1:T(8,128)(2,1)}, u32[]{:S(2)}, u32[]{:S(2)}) collective-permute-start(bf16[1024,1792]{0,1:T(8,128)(2,1)} %all-gather.2.cloned.1.call-done), channel_id=1, source_target_pairs={{0,8},{8,0},{1,9},{9,1},{2,10},{10,2},{3,11},{11,3},{4,12},{12,4},... | collective-permute-start | bytes 11010056 | tf_op jit(solution)/shard_map/ppermute | solution.py:207
  128.0 7.5 %copy-start.3 = (bf16[64,1024]{1,0:T(8,128)(2,1)S(1)}, bf16[64,1024]{1,0:T(8,128)(2,1)}, u32[]{:S(2)}) copy-start(bf16[64,1024]{1,0:T(8,128)(2,1)} %param.8) | copy-start | bytes 393220
  129.9 7.7 %collective-permute-start.10 = (bf16[32,64,576]{2,1,0:T(8,128)(2,1)}, bf16[32,64,576]{2,1,0:T(8,128)(2,1)}, u32[]{:S(2)}, u32[]{:S(2)}) collective-permute-start(bf16[32,64,576]{2,1,0:T(8,128)(2,1)} %constant_dynamic-update-slice_fusion), channel_id=1, source_target_pairs={{0,8},{8,0},{1,9},{9,1},{2,10},{10,2},{3,11},{11,3},{4,12},{12,4},... | collective-permute-start | bytes 7077896 | tf_op jit(solution)/shard_map/ppermute | solution.py:93
  137.6 11.7 %copy-start.2 = (bf16[512,1024]{1,0:T(8,128)(2,1)S(1)}, bf16[512,1024]{1,0:T(8,128)(2,1)}, u32[]{:S(2)}) copy-start(bf16[512,1024]{1,0:T(8,128)(2,1)} %param.14) | copy-start | bytes 3145732
  157.9 10.5 %collective-permute-start.13 = (bf16[2,64,448]{2,1,0:T(8,128)(2,1)S(1)}, bf16[2,64,448]{2,1,0:T(8,128)(2,1)S(1)}, u32[]{:S(2)}, u32[]{:S(2)}) collective-permute-start(bf16[2,64,448]{2,1,0:T(8,128)(2,1)S(1)} %get-tuple-element.9), channel_id=1, source_target_pairs={{0,2},{2,0},{4,6},{6,4},{1,3},{3,1},{5,7},{7,5},{8,10},{10,8},{12,... | collective-permute-start | bytes 344072 | tf_op jit(solution)/shard_map/ppermute | solution.py:149
  160.4 8.7 %collective-permute-start.14 = (bf16[2,64,448]{2,1,0:T(8,128)(2,1)S(1)}, bf16[2,64,448]{2,1,0:T(8,128)(2,1)S(1)}, u32[]{:S(2)}, u32[]{:S(2)}) collective-permute-start(bf16[2,64,448]{2,1,0:T(8,128)(2,1)S(1)} %get-tuple-element.11), channel_id=1, source_target_pairs={{0,4},{2,6},{4,0},{6,2},{1,5},{3,7},{5,1},{7,3},{8,12},{10,14},{12... | collective-permute-start | bytes 344072 | tf_op jit(solution)/shard_map/ppermute | solution.py:149
  163.4 8.4 %collective-permute-start.15 = (bf16[2,64,448]{2,1,0:T(8,128)(2,1)S(1)}, bf16[2,64,448]{2,1,0:T(8,128)(2,1)S(1)}, u32[]{:S(2)}, u32[]{:S(2)}) collective-permute-start(bf16[2,64,448]{2,1,0:T(8,128)(2,1)S(1)} %get-tuple-element.10), channel_id=1, source_target_pairs={{0,6},{2,4},{4,2},{6,0},{1,7},{3,5},{5,3},{7,1},{8,14},{10,12},{12... | collective-permute-start | bytes 344072 | tf_op jit(solution)/shard_map/ppermute | solution.py:149
  171.9 7.7 %collective-permute-start.16 = (bf16[64,448]{1,0:T(8,128)(2,1)S(1)}, bf16[64,448]{1,0:T(8,128)(2,1)S(1)}, u32[]{:S(2)}, u32[]{:S(2)}) collective-permute-start(bf16[64,448]{1,0:T(8,128)(2,1)S(1)} %fusion.15), channel_id=1, source_target_pairs={{0,1},{1,0},{2,3},{3,2},{4,5},{5,4},{6,7},{7,6},{8,9},{9,8},{10,11... | collective-permute-start | bytes 172040 | tf_op jit(solution)/shard_map/ppermute | solution.py:155
Sparse Core Ops, SparseCore 0:
  15.4 109.7 all-gather.1

commit v12 on v11

--- a/solution.py
+++ b/solution.py
@@ -137,18 +137,18 @@
         index = jnp.concatenate([index, other_index])
 
 
-def scatter_sum(blocks):
+def scatter_sum(head_blocks):
     rows = lax.axis_size("yh")
     columns = lax.axis_size("x")
     x = lax.axis_index("x")
     yh = lax.axis_index("yh")
-    blocks = blocks.reshape((columns, rows) + blocks.shape[1:])
-    row_sums = blocks[x]
+    received = []
     for shift in range(1, columns):
-        sent = blocks[x ^ shift].astype(jnp.bfloat16)
-        row_sums = row_sums + lax.ppermute(
-            sent, "x", [(i, i ^ shift) for i in range(columns)]
-        ).astype(jnp.float32)
+        sent = head_blocks((x ^ shift) * rows, rows).astype(jnp.bfloat16)
+        received.append(lax.ppermute(sent, "x", [(i, i ^ shift) for i in range(columns)]))
+    row_sums = head_blocks(x * rows, rows)
+    for part in received:
+        row_sums = row_sums + part.astype(jnp.float32)
     total = row_sums[yh]
     for shift in range(1, rows):
         sent = row_sums[yh ^ shift].astype(jnp.bfloat16)
@@ -207,12 +207,22 @@
     swapped = lax.ppermute(own, "co", [(0, 1), (1, 0)])
     upper = lax.axis_index("co") == 1
     groups = lax.axis_size(HEAD)
-    halves = [
-        jnp.dot(head_out, half, preferred_element_type=jnp.float32).reshape(token_count, groups, -1)
-        for half in (own, swapped)
-    ]
-    partial_sums = jnp.concatenate(halves, axis=2).transpose(1, 0, 2)
-    mine = scatter_sum(partial_sums)
+    own = own.reshape(own.shape[0], groups, -1)
+    swapped = swapped.reshape(swapped.shape[0], groups, -1)
+
+    def head_blocks(first_head, count):
+        parts = [
+            jnp.einsum(
+                "tk,kjc->jtc",
+                head_out,
+                lax.dynamic_slice_in_dim(half, first_head, count, axis=1),
+                preferred_element_type=jnp.float32,
+            )
+            for half in (own, swapped)
+        ]
+        return jnp.concatenate(parts, axis=2)
+
+    mine = scatter_sum(head_blocks)
     half_width = mine.shape[1] // 2
     mine = jnp.where(
         upper,

time: 191 us -> 192 us (level)
  the two profiles are of different devices: /device:TPU:6 before, /device:TPU:32 now
where the time goes in v12:
time: 192 us; the launch traced here: 191 us
  waiting for transfers between devices  66.3 us (35%)
  starting transfers between devices  65.6 us (34%)
  matrix products  14.7 us (8%)
  between operations  13.8 us (7%)
  local copies, waits for them, and re-layouts  13.2 us (7%)
  Pallas kernels  11.7 us (6%)
  other arithmetic  6.06 us (3%)
    ppermute x3, waiting for transfers between devices, exchange(): return lax.ppermute(acc, axis, pairs)  28.6 us
    ppermute x7, starting transfers between devices, gather_earlier_keys(): lax.ppermute(local, 'zh', [(i, i + shift) for i in range(cubes - shift)])  28.3 us
    ppermute x7, waiting for transfers between devices, gather_earlier_keys(): lax.ppermute(local, 'zh', [(i, i + shift) for i in range(cubes - shift)])  17.7 us
    dot_general x8, matrix products, head_blocks(): jnp.einsum('tk,kjc->jtc', head_out, lax.dynamic_slice_in_dim(half, first_...  12.7 us
    ppermute x3, starting transfers between devices, exchange(): return lax.ppermute(acc, axis, pairs)  12.4 us
    ppermute x1, waiting for transfers between devices, exchange(): far = lax.ppermute(acc[half:], ('yl', 'yh'), [(i, i ^ 3) for i in range(4)])  11.8 us
    pallas_call x1, Pallas kernels, attend(): pl.pallas_call(attention_kernel, out_shape=jax.ShapeDtypeStruct((rows, LA...  11.7 us
    ppermute x3, starting transfers between devices, scatter_sum(): lax.ppermute(sent, 'x', [(i, i ^ shift) for i in range(columns)])  10.4 us
  transfers between devices with their start and end apart: 18, of which 10 were waited for; matrix products, arithmetic and copies ran while one was open for 14% of the time, Pallas kernels for 6%

profile of v12, /device:TPU:32, one launch (start us, length us, event | category | flops | bytes accessed | tf_op | source)
XLA Modules:
  0.0 191.3 jit_solution(11742076042873250723)
XLA Ops:
  6.5 3.6 %collective-permute-start = (bf16[1,56,1024]{2,1,0:T(8,128)(2,1)}, bf16[1,56,1024]{2,1,0:T(8,128)(2,1)S(1)}, u32[]{:S(2)}, u32[]{:S(2)}) collective-permute-start(bf16[1,56,1024]{2,1,0:T(8,128)(2,1)} %bitcast.112), channel_id=1, source_target_pairs={{0,16},{16,0},{1,17},{17,1},{2,18},{18,2},{3,19},{19,3},{4,20},{20... | collective-permute-start | bytes 344072 | tf_op jit(solution)/shard_map/ppermute | solution.py:93
  10.2 3.5 %collective-permute-done = bf16[1,56,1024]{2,1,0:T(8,128)(2,1)S(1)} collective-permute-done((bf16[1,56,1024]{2,1,0:T(8,128)(2,1)}, bf16[1,56,1024]{2,1,0:T(8,128)(2,1)S(1)}, u32[]{:S(2)}, u32[]{:S(2)}) %collective-permute-start) | collective-permute-done | bytes 114720 | tf_op jit(solution)/shard_map/ppermute | solution.py:93
  17.9 5.2 %collective-permute-start.1 = (bf16[64,576]{1,0:T(8,128)(2,1)S(1)}, bf16[64,576]{1,0:T(8,128)(2,1)S(1)}, u32[]{:S(2)}, u32[]{:S(2)}) collective-permute-start(bf16[64,576]{1,0:T(8,128)(2,1)S(1)} %pad_maximum_fusion.5), channel_id=1, source_target_pairs={{0,64},{64,128},{128,192},{192,256},{256,320},{320,384},{384,448},... | collective-permute-start | bytes 221192 | tf_op jit(solution)/shard_map/ppermute | solution.py:124
  23.1 9.1 %collective-permute-start.2 = (bf16[64,576]{1,0:T(8,128)(2,1)S(1)}, bf16[64,576]{1,0:T(8,128)(2,1)S(1)}, u32[]{:S(2)}, u32[]{:S(2)}) collective-permute-start(bf16[64,576]{1,0:T(8,128)(2,1)S(1)} %pad_maximum_fusion.5), channel_id=1, source_target_pairs={{0,128},{64,192},{128,256},{192,320},{256,384},{320,448},{1,129},{... | collective-permute-start | bytes 221192 | tf_op jit(solution)/shard_map/ppermute | solution.py:124
  32.2 7.3 %collective-permute-start.3 = (bf16[64,576]{1,0:T(8,128)(2,1)S(1)}, bf16[64,576]{1,0:T(8,128)(2,1)S(1)}, u32[]{:S(2)}, u32[]{:S(2)}) collective-permute-start(bf16[64,576]{1,0:T(8,128)(2,1)S(1)} %pad_maximum_fusion.5), channel_id=1, source_target_pairs={{0,192},{64,256},{128,320},{192,384},{256,448},{1,193},{65,257},{1... | collective-permute-start | bytes 221192 | tf_op jit(solution)/shard_map/ppermute | solution.py:124
  39.5 2.8 %collective-permute-start.4 = (bf16[64,576]{1,0:T(8,128)(2,1)S(1)}, bf16[64,576]{1,0:T(8,128)(2,1)S(1)}, u32[]{:S(2)}, u32[]{:S(2)}) collective-permute-start(bf16[64,576]{1,0:T(8,128)(2,1)S(1)} %pad_maximum_fusion.5), channel_id=1, source_target_pairs={{0,256},{64,320},{128,384},{192,448},{1,257},{65,321},{129,385},{1... | collective-permute-start | bytes 221192 | tf_op jit(solution)/shard_map/ppermute | solution.py:124
  49.7 9.1 %collective-permute-done.4 = bf16[64,576]{1,0:T(8,128)(2,1)S(1)} collective-permute-done((bf16[64,576]{1,0:T(8,128)(2,1)S(1)}, bf16[64,576]{1,0:T(8,128)(2,1)S(1)}, u32[]{:S(2)}, u32[]{:S(2)}) %collective-permute-start.4) | collective-permute-done | bytes 73760 | tf_op jit(solution)/shard_map/ppermute | solution.py:124
  59.4 3.0 %collective-permute-done.5 = bf16[64,576]{1,0:T(8,128)(2,1)S(1)} collective-permute-done((bf16[64,576]{1,0:T(8,128)(2,1)S(1)}, bf16[64,576]{1,0:T(8,128)(2,1)S(1)}, u32[]{:S(2)}, u32[]{:S(2)}) %collective-permute-start.5) | collective-permute-done | bytes 73760 | tf_op jit(solution)/shard_map/ppermute | solution.py:124
  63.0 2.9 %collective-permute-done.6 = bf16[64,576]{1,0:T(8,128)(2,1)S(1)} collective-permute-done((bf16[64,576]{1,0:T(8,128)(2,1)S(1)}, bf16[64,576]{1,0:T(8,128)(2,1)S(1)}, u32[]{:S(2)}, u32[]{:S(2)}) %collective-permute-start.6) | collective-permute-done | bytes 73760 | tf_op jit(solution)/shard_map/ppermute | solution.py:124
  66.5 2.8 %collective-permute-done.7 = bf16[64,576]{1,0:T(8,128)(2,1)S(1)} collective-permute-done((bf16[64,576]{1,0:T(8,128)(2,1)S(1)}, bf16[64,576]{1,0:T(8,128)(2,1)S(1)}, u32[]{:S(2)}, u32[]{:S(2)}) %collective-permute-start.7) | collective-permute-done | bytes 73760 | tf_op jit(solution)/shard_map/ppermute | solution.py:124
  70.0 6.9 %collective-permute-start.8 = (bf16[8,64,576]{2,1,0:T(8,128)(2,1)S(1)}, bf16[8,64,576]{2,1,0:T(8,128)(2,1)S(1)}, u32[]{:S(2)}, u32[]{:S(2)}) collective-permute-start(bf16[8,64,576]{2,1,0:T(8,128)(2,1)S(1)} %get-tuple-element.15), channel_id=1, source_target_pairs={{0,32},{32,0},{1,33},{33,1},{2,34},{34,2},{3,35},{35,3},{4,36},{36... | collective-permute-start | bytes 1769480 | tf_op jit(solution)/shard_map/ppermute | solution.py:93
  76.9 3.5 %collective-permute-start.9 = (bf16[8,64,576]{2,1,0:T(8,128)(2,1)S(1)}, bf16[8,64,576]{2,1,0:T(8,128)(2,1)S(1)}, u32[]{:S(2)}, u32[]{:S(2)}) collective-permute-start(bf16[8,64,576]{2,1,0:T(8,128)(2,1)S(1)} %get-tuple-element.15), channel_id=1, source_target_pairs={{0,16},{16,0},{1,17},{17,1},{2,18},{18,2},{3,19},{19,3},{4,20},{20... | collective-permute-start | bytes 1769480 | tf_op jit(solution)/shard_map/ppermute | solution.py:95
  80.4 25.1 %collective-permute-done.8 = bf16[8,64,576]{2,1,0:T(8,128)(2,1)S(1)} collective-permute-done((bf16[8,64,576]{2,1,0:T(8,128)(2,1)S(1)}, bf16[8,64,576]{2,1,0:T(8,128)(2,1)S(1)}, u32[]{:S(2)}, u32[]{:S(2)}) %collective-permute-start.8) | collective-permute-done | bytes 589856 | tf_op jit(solution)/shard_map/ppermute | solution.py:93
  105.5 4.9 %collective-permute-start.10 = (bf16[8,64,576]{2,1,0:T(8,128)(2,1)S(1)}, bf16[8,64,576]{2,1,0:T(8,128)(2,1)S(1)}, u32[]{:S(2)}, u32[]{:S(2)}) collective-permute-start(bf16[8,64,576]{2,1,0:T(8,128)(2,1)S(1)} %collective-permute-done.8), channel_id=1, source_target_pairs={{0,17},{1,16},{16,1},{17,0},{2,19},{3,18},{18,3},{19,2},{4,21},{5,... | collective-permute-start | bytes 1769480 | tf_op jit(solution)/shard_map/ppermute | solution.py:96
  112.3 11.8 %collective-permute-done.10 = bf16[8,64,576]{2,1,0:T(8,128)(2,1)S(1)} collective-permute-done((bf16[8,64,576]{2,1,0:T(8,128)(2,1)S(1)}, bf16[8,64,576]{2,1,0:T(8,128)(2,1)S(1)}, u32[]{:S(2)}, u32[]{:S(2)}) %collective-permute-start.10) | collective-permute-done | bytes 589856 | tf_op jit(solution)/shard_map/ppermute | solution.py:96
  125.0 1.9 collective-permute-start.11
  127.0 2.4 %collective-permute-start.12 = (bf16[1024,1792]{0,1:T(8,128)(2,1)}, bf16[1024,1792]{0,1:T(8,128)(2,1)}, u32[]{:S(2)}, u32[]{:S(2)}) collective-permute-start(bf16[1024,1792]{0,1:T(8,128)(2,1)} %all-gather.2.cloned.1.call-done), channel_id=1, source_target_pairs={{0,8},{8,0},{1,9},{9,1},{2,10},{10,2},{3,11},{11,3},{4,12},{12,4},... | collective-permute-start | bytes 11010056 | tf_op jit(solution)/shard_map/ppermute | solution.py:207
  134.4 11.7 %shard_map.82 = bf16[512,512]{1,0:T(8,128)(2,1)} custom-call(bf16[512,576]{1,0:T(8,128)(2,1)} %bitcast.110, s32[512,1]{1,0:T(8,128)} %reshape_reshape.4.qi_ref, bf16[2048,576]{1,0:T(8,128)(2,1)} %bitcast.22.ka_ref, s32[1,2048]{1,0:T(1,128)} %add.136.ia_ref, bf16[2048,576]{1,0:T(8,128)(2,1)} %bitcast.23.kb_ref, s32[1,2048]{1,0:T(1,128)} %add.140.ib_ref), custom_call_target="tpu_custom_call" | custom-call | flops 4563402752 | bytes 5832704 | tf_op jit(solution)/shard_map/pallas_call | solution.py:83
  159.0 3.4 %collective-permute-start.13 = (bf16[2,64,448]{2,1,0:T(8,128)(2,1)S(1)}, bf16[2,64,448]{2,1,0:T(8,128)(2,1)S(1)}, u32[]{:S(2)}, u32[]{:S(2)}) collective-permute-start(bf16[2,64,448]{2,1,0:T(8,128)(2,1)S(1)} %pad_maximum_fusion.2), channel_id=1, source_target_pairs={{0,2},{2,0},{4,6},{6,4},{1,3},{3,1},{5,7},{7,5},{8,10},{10,8},{12,... | collective-permute-start | bytes 344072 | tf_op jit(solution)/shard_map/ppermute | solution.py:148
  162.6 4.7 %collective-permute-start.14 = (bf16[2,64,448]{2,1,0:T(8,128)(2,1)S(1)}, bf16[2,64,448]{2,1,0:T(8,128)(2,1)S(1)}, u32[]{:S(2)}, u32[]{:S(2)}) collective-permute-start(bf16[2,64,448]{2,1,0:T(8,128)(2,1)S(1)} %pad_maximum_fusion.3), channel_id=1, source_target_pairs={{0,4},{2,6},{4,0},{6,2},{1,5},{3,7},{5,1},{7,3},{8,12},{10,14},{12... | collective-permute-start | bytes 344072 | tf_op jit(solution)/shard_map/ppermute | solution.py:148
  167.3 2.4 %collective-permute-start.15 = (bf16[2,64,448]{2,1,0:T(8,128)(2,1)S(1)}, bf16[2,64,448]{2,1,0:T(8,128)(2,1)S(1)}, u32[]{:S(2)}, u32[]{:S(2)}) collective-permute-start(bf16[2,64,448]{2,1,0:T(8,128)(2,1)S(1)} %pad_maximum_fusion.4), channel_id=1, source_target_pairs={{0,6},{2,4},{4,2},{6,0},{1,7},{3,5},{5,3},{7,1},{8,14},{10,12},{12... | collective-permute-start | bytes 344072 | tf_op jit(solution)/shard_map/ppermute | solution.py:148
  171.4 4.0 %collective-permute-done.15 = bf16[2,64,448]{2,1,0:T(8,128)(2,1)S(1)} collective-permute-done((bf16[2,64,448]{2,1,0:T(8,128)(2,1)S(1)}, bf16[2,64,448]{2,1,0:T(8,128)(2,1)S(1)}, u32[]{:S(2)}, u32[]{:S(2)}) %collective-permute-start.15) | collective-permute-done | bytes 114720 | tf_op jit(solution)/shard_map/ppermute | solution.py:148
  175.5 3.6 %collective-permute-start.16 = (bf16[64,448]{1,0:T(8,128)(2,1)S(1)}, bf16[64,448]{1,0:T(8,128)(2,1)S(1)}, u32[]{:S(2)}, u32[]{:S(2)}) collective-permute-start(bf16[64,448]{1,0:T(8,128)(2,1)S(1)} %fusion.26), channel_id=1, source_target_pairs={{0,1},{1,0},{2,3},{3,2},{4,5},{5,4},{6,7},{7,6},{8,9},{9,8},{10,11... | collective-permute-start | bytes 172040 | tf_op jit(solution)/shard_map/ppermute | solution.py:155
  179.2 4.0 %collective-permute-done.16 = bf16[64,448]{1,0:T(8,128)(2,1)S(1)} collective-permute-done((bf16[64,448]{1,0:T(8,128)(2,1)S(1)}, bf16[64,448]{1,0:T(8,128)(2,1)S(1)}, u32[]{:S(2)}, u32[]{:S(2)}) %collective-permute-start.16) | collective-permute-done | bytes 57376 | tf_op jit(solution)/shard_map/ppermute | solution.py:155
  (83 shorter events, 37.9 us)
Async XLA Ops:
  6.5 126.0 %copy-start = (bf16[512,1024]{1,0:T(8,128)(2,1)S(1)}, bf16[512,1024]{1,0:T(8,128)(2,1)}, u32[]{:S(2)}) copy-start(bf16[512,1024]{1,0:T(8,128)(2,1)} %param.13) | copy-start | bytes 3145732
  6.5 120.4 %all-gather.2.cloned.1.call-start = ((), (), s32[]{:S(2)}) async-start(), calls=%async_computation | async-start | bytes 3899392 | tf_op jit(solution)/shard_map/all_gather | solution.py:206
  6.5 7.1 %collective-permute-start = (bf16[1,56,1024]{2,1,0:T(8,128)(2,1)}, bf16[1,56,1024]{2,1,0:T(8,128)(2,1)S(1)}, u32[]{:S(2)}, u32[]{:S(2)}) collective-permute-start(bf16[1,56,1024]{2,1,0:T(8,128)(2,1)} %bitcast.112), channel_id=1, source_target_pairs={{0,16},{16,0},{1,17},{17,1},{2,18},{18,2},{3,19},{19,3},{4,20},{20... | collective-permute-start | bytes 344072 | tf_op jit(solution)/shard_map/ppermute | solution.py:93
  17.9 27.2 %collective-permute-start.1 = (bf16[64,576]{1,0:T(8,128)(2,1)S(1)}, bf16[64,576]{1,0:T(8,128)(2,1)S(1)}, u32[]{:S(2)}, u32[]{:S(2)}) collective-permute-start(bf16[64,576]{1,0:T(8,128)(2,1)S(1)} %pad_maximum_fusion.5), channel_id=1, source_target_pairs={{0,64},{64,128},{128,192},{192,256},{256,320},{320,384},{384,448},... | collective-permute-start | bytes 221192 | tf_op jit(solution)/shard_map/ppermute | solution.py:124
  23.1 24.0 %collective-permute-start.2 = (bf16[64,576]{1,0:T(8,128)(2,1)S(1)}, bf16[64,576]{1,0:T(8,128)(2,1)S(1)}, u32[]{:S(2)}, u32[]{:S(2)}) collective-permute-start(bf16[64,576]{1,0:T(8,128)(2,1)S(1)} %pad_maximum_fusion.5), channel_id=1, source_target_pairs={{0,128},{64,192},{128,256},{192,320},{256,384},{320,448},{1,129},{... | collective-permute-start | bytes 221192 | tf_op jit(solution)/shard_map/ppermute | solution.py:124
  32.2 16.8 %collective-permute-start.3 = (bf16[64,576]{1,0:T(8,128)(2,1)S(1)}, bf16[64,576]{1,0:T(8,128)(2,1)S(1)}, u32[]{:S(2)}, u32[]{:S(2)}) collective-permute-start(bf16[64,576]{1,0:T(8,128)(2,1)S(1)} %pad_maximum_fusion.5), channel_id=1, source_target_pairs={{0,192},{64,256},{128,320},{192,384},{256,448},{1,193},{65,257},{1... | collective-permute-start | bytes 221192 | tf_op jit(solution)/shard_map/ppermute | solution.py:124
  39.5 19.2 %collective-permute-start.4 = (bf16[64,576]{1,0:T(8,128)(2,1)S(1)}, bf16[64,576]{1,0:T(8,128)(2,1)S(1)}, u32[]{:S(2)}, u32[]{:S(2)}) collective-permute-start(bf16[64,576]{1,0:T(8,128)(2,1)S(1)} %pad_maximum_fusion.5), channel_id=1, source_target_pairs={{0,256},{64,320},{128,384},{192,448},{1,257},{65,321},{129,385},{1... | collective-permute-start | bytes 221192 | tf_op jit(solution)/shard_map/ppermute | solution.py:124
  42.3 20.0 %collective-permute-start.5 = (bf16[64,576]{1,0:T(8,128)(2,1)S(1)}, bf16[64,576]{1,0:T(8,128)(2,1)S(1)}, u32[]{:S(2)}, u32[]{:S(2)}) collective-permute-start(bf16[64,576]{1,0:T(8,128)(2,1)S(1)} %pad_maximum_fusion.5), channel_id=1, source_target_pairs={{0,320},{64,384},{128,448},{1,321},{65,385},{129,449},{2,322},{66,... | collective-permute-start | bytes 221192 | tf_op jit(solution)/shard_map/ppermute | solution.py:124
  45.1 20.7 %collective-permute-start.6 = (bf16[64,576]{1,0:T(8,128)(2,1)S(1)}, bf16[64,576]{1,0:T(8,128)(2,1)S(1)}, u32[]{:S(2)}, u32[]{:S(2)}) collective-permute-start(bf16[64,576]{1,0:T(8,128)(2,1)S(1)} %pad_maximum_fusion.5), channel_id=1, source_target_pairs={{0,384},{64,448},{1,385},{65,449},{2,386},{66,450},{3,387},{67,451... | collective-permute-start | bytes 221192 | tf_op jit(solution)/shard_map/ppermute | solution.py:124
  47.1 22.3 %collective-permute-start.7 = (bf16[64,576]{1,0:T(8,128)(2,1)S(1)}, bf16[64,576]{1,0:T(8,128)(2,1)S(1)}, u32[]{:S(2)}, u32[]{:S(2)}) collective-permute-start(bf16[64,576]{1,0:T(8,128)(2,1)S(1)} %pad_maximum_fusion.5), channel_id=1, source_target_pairs={{0,448},{1,449},{2,450},{3,451},{4,452},{5,453},{6,454},{7,455},{8... | collective-permute-start | bytes 221192 | tf_op jit(solution)/shard_map/ppermute | solution.py:124
  59.4 72.6 %copy-start.1 = (bf16[64,512]{1,0:T(8,128)(2,1)S(1)}, bf16[64,512]{1,0:T(8,128)(2,1)}, u32[]{:S(2)}) copy-start(bf16[64,512]{1,0:T(8,128)(2,1)} %param.9) | copy-start | bytes 196612
  70.0 35.6 %collective-permute-start.8 = (bf16[8,64,576]{2,1,0:T(8,128)(2,1)S(1)}, bf16[8,64,576]{2,1,0:T(8,128)(2,1)S(1)}, u32[]{:S(2)}, u32[]{:S(2)}) collective-permute-start(bf16[8,64,576]{2,1,0:T(8,128)(2,1)S(1)} %get-tuple-element.15), channel_id=1, source_target_pairs={{0,32},{32,0},{1,33},{33,1},{2,34},{34,2},{3,35},{35,3},{4,36},{36... | collective-permute-start | bytes 1769480 | tf_op jit(solution)/shard_map/ppermute | solution.py:93
  76.9 34.5 %collective-permute-start.9 = (bf16[8,64,576]{2,1,0:T(8,128)(2,1)S(1)}, bf16[8,64,576]{2,1,0:T(8,128)(2,1)S(1)}, u32[]{:S(2)}, u32[]{:S(2)}) collective-permute-start(bf16[8,64,576]{2,1,0:T(8,128)(2,1)S(1)} %get-tuple-element.15), channel_id=1, source_target_pairs={{0,16},{16,0},{1,17},{17,1},{2,18},{18,2},{3,19},{19,3},{4,20},{20... | collective-permute-start | bytes 1769480 | tf_op jit(solution)/shard_map/ppermute | solution.py:95
  105.5 18.5 %collective-permute-start.10 = (bf16[8,64,576]{2,1,0:T(8,128)(2,1)S(1)}, bf16[8,64,576]{2,1,0:T(8,128)(2,1)S(1)}, u32[]{:S(2)}, u32[]{:S(2)}) collective-permute-start(bf16[8,64,576]{2,1,0:T(8,128)(2,1)S(1)} %collective-permute-done.8), channel_id=1, source_target_pairs={{0,17},{1,16},{16,1},{17,0},{2,19},{3,18},{18,3},{19,2},{4,21},{5,... | collective-permute-start | bytes 1769480 | tf_op jit(solution)/shard_map/ppermute | solution.py:96
  111.3 21.2 %copy-start.3 = (bf16[64,1024]{1,0:T(8,128)(2,1)S(1)}, bf16[64,1024]{1,0:T(8,128)(2,1)}, u32[]{:S(2)}) copy-start(bf16[64,1024]{1,0:T(8,128)(2,1)} %param.8) | copy-start | bytes 393220
  125.0 9.4 %collective-permute-start.11 = (bf16[32,64,576]{2,1,0:T(8,128)(2,1)}, bf16[32,64,576]{2,1,0:T(8,128)(2,1)}, u32[]{:S(2)}, u32[]{:S(2)}) collective-permute-start(bf16[32,64,576]{2,1,0:T(8,128)(2,1)} %constant_dynamic-update-slice_fusion), channel_id=1, source_target_pairs={{0,8},{8,0},{1,9},{9,1},{2,10},{10,2},{3,11},{11,3},{4,12},{12,4},... | collective-permute-start | bytes 7077896 | tf_op jit(solution)/shard_map/ppermute | solution.py:93
  127.0 27.2 %collective-permute-start.12 = (bf16[1024,1792]{0,1:T(8,128)(2,1)}, bf16[1024,1792]{0,1:T(8,128)(2,1)}, u32[]{:S(2)}, u32[]{:S(2)}) collective-permute-start(bf16[1024,1792]{0,1:T(8,128)(2,1)} %all-gather.2.cloned.1.call-done), channel_id=1, source_target_pairs={{0,8},{8,0},{1,9},{9,1},{2,10},{10,2},{3,11},{11,3},{4,12},{12,4},... | collective-permute-start | bytes 11010056 | tf_op jit(solution)/shard_map/ppermute | solution.py:207
  134.4 11.7 %copy-start.2 = (bf16[512,1024]{1,0:T(8,128)(2,1)S(1)}, bf16[512,1024]{1,0:T(8,128)(2,1)}, u32[]{:S(2)}) copy-start(bf16[512,1024]{1,0:T(8,128)(2,1)} %param.14) | copy-start | bytes 3145732
  159.0 12.2 %collective-permute-start.13 = (bf16[2,64,448]{2,1,0:T(8,128)(2,1)S(1)}, bf16[2,64,448]{2,1,0:T(8,128)(2,1)S(1)}, u32[]{:S(2)}, u32[]{:S(2)}) collective-permute-start(bf16[2,64,448]{2,1,0:T(8,128)(2,1)S(1)} %pad_maximum_fusion.2), channel_id=1, source_target_pairs={{0,2},{2,0},{4,6},{6,4},{1,3},{3,1},{5,7},{7,5},{8,10},{10,8},{12,... | collective-permute-start | bytes 344072 | tf_op jit(solution)/shard_map/ppermute | solution.py:148
  162.6 8.8 %collective-permute-start.14 = (bf16[2,64,448]{2,1,0:T(8,128)(2,1)S(1)}, bf16[2,64,448]{2,1,0:T(8,128)(2,1)S(1)}, u32[]{:S(2)}, u32[]{:S(2)}) collective-permute-start(bf16[2,64,448]{2,1,0:T(8,128)(2,1)S(1)} %pad_maximum_fusion.3), channel_id=1, source_target_pairs={{0,4},{2,6},{4,0},{6,2},{1,5},{3,7},{5,1},{7,3},{8,12},{10,14},{12... | collective-permute-start | bytes 344072 | tf_op jit(solution)/shard_map/ppermute | solution.py:148
  167.3 8.1 %collective-permute-start.15 = (bf16[2,64,448]{2,1,0:T(8,128)(2,1)S(1)}, bf16[2,64,448]{2,1,0:T(8,128)(2,1)S(1)}, u32[]{:S(2)}, u32[]{:S(2)}) collective-permute-start(bf16[2,64,448]{2,1,0:T(8,128)(2,1)S(1)} %pad_maximum_fusion.4), channel_id=1, source_target_pairs={{0,6},{2,4},{4,2},{6,0},{1,7},{3,5},{5,3},{7,1},{8,14},{10,12},{12... | collective-permute-start | bytes 344072 | tf_op jit(solution)/shard_map/ppermute | solution.py:148
  175.5 7.7 %collective-permute-start.16 = (bf16[64,448]{1,0:T(8,128)(2,1)S(1)}, bf16[64,448]{1,0:T(8,128)(2,1)S(1)}, u32[]{:S(2)}, u32[]{:S(2)}) collective-permute-start(bf16[64,448]{1,0:T(8,128)(2,1)S(1)} %fusion.26), channel_id=1, source_target_pairs={{0,1},{1,0},{2,3},{3,2},{4,5},{5,4},{6,7},{7,6},{8,9},{9,8},{10,11... | collective-permute-start | bytes 172040 | tf_op jit(solution)/shard_map/ppermute | solution.py:155
Sparse Core Ops, SparseCore 0:
  15.4 109.6 all-gather.1

commit v13 on v11

--- a/solution.py
+++ b/solution.py
@@ -38,53 +38,66 @@
     )
 
 
-def attention_kernel(q_ref, qi_ref, ka_ref, ia_ref, kb_ref, ib_ref, o_ref):
+def masked_scores(queries, query_index, k_ref, i_ref):
     scale = 1.0 / math.sqrt(NOPE + ROPE)
-    queries = q_ref[...]
-    query_index = qi_ref[...]
-
-    def masked_scores(k_ref, i_ref):
-        scores = lax.dot_general(
-            queries, k_ref[...], (((1,), (1,)), ((), ())), preferred_element_type=jnp.float32
+    scores = lax.dot_general(
+        queries, k_ref[...], (((1,), (1,)), ((), ())), preferred_element_type=jnp.float32
+    )
+    visible = i_ref[...] <= query_index
+    return jnp.where(visible, scores * scale, masked_value), visible
+
+
+def first_kernel(q_ref, qi_ref, k_ref, i_ref, peak_ref, totals_ref, summed_ref):
+    scores, visible = masked_scores(q_ref[...], qi_ref[...], k_ref, i_ref)
+    peak = jnp.max(scores, axis=1, keepdims=True)
+    weights = jnp.where(visible, jnp.exp(scores - peak), 0.0)
+    peak_ref[...] = peak
+    totals_ref[...] = jnp.sum(weights, axis=1, keepdims=True)
+    summed_ref[...] = jnp.dot(
+        weights.astype(jnp.bfloat16), k_ref[:, :LATENT], preferred_element_type=jnp.float32
+    )
+
+
+def second_kernel(q_ref, qi_ref, k_ref, i_ref, pa_ref, ta_ref, sa_ref, o_ref):
+    scores, visible = masked_scores(q_ref[...], qi_ref[...], k_ref, i_ref)
+    first_peak = pa_ref[...]
+    peak = jnp.maximum(first_peak, jnp.max(scores, axis=1, keepdims=True))
+    weights = jnp.where(visible, jnp.exp(scores - peak), 0.0)
+    factor = jnp.exp(first_peak - peak)
+    totals = factor * ta_ref[...] + jnp.sum(weights, axis=1, keepdims=True)
+    summed = factor * sa_ref[...] + jnp.dot(
+        weights.astype(jnp.bfloat16), k_ref[:, :LATENT], preferred_element_type=jnp.float32
+    )
+    o_ref[...] = (summed / totals).astype(jnp.bfloat16)
+
+
+def attend(query_rows, query_index, halves):
+    rows, width = query_rows.shape
+    query_index = query_index.reshape(rows, 1)
+    (keys_a, index_a), (keys_b, index_b) = halves
+    f32 = jnp.float32
+
+    def cost(key_count):
+        return pl.CostEstimate(
+            flops=2 * rows * key_count * (width + LATENT),
+            transcendentals=rows * key_count,
+            bytes_accessed=2 * (rows * width + key_count * width) + 4 * rows * LATENT,
         )
-        visible = i_ref[...] <= query_index
-        return jnp.where(visible, scores * scale, masked_value), visible
-
-    scores_a, visible_a = masked_scores(ka_ref, ia_ref)
-    scores_b, visible_b = masked_scores(kb_ref, ib_ref)
-    peak = jnp.maximum(
-        jnp.max(scores_a, axis=1, keepdims=True), jnp.max(scores_b, axis=1, keepdims=True)
-    )
-    weights_a = jnp.where(visible_a, jnp.exp(scores_a - peak), 0.0)
-    weights_b = jnp.where(visible_b, jnp.exp(scores_b - peak), 0.0)
-    totals = jnp.sum(weights_a, axis=1, keepdims=True) + jnp.sum(weights_b, axis=1, keepdims=True)
-    summed = jnp.dot(
-        weights_a.astype(jnp.bfloat16), ka_ref[:, :LATENT], preferred_element_type=jnp.float32
-    )
-    summed = summed + jnp.dot(
-        weights_b.astype(jnp.bfloat16), kb_ref[:, :LATENT], preferred_element_type=jnp.float32
-    )
-    o_ref[...] = (summed / totals).astype(jnp.bfloat16)
-
-
-def attend(query_rows, query_index, halves):
-    rows = query_rows.shape[0]
-    operands = [query_rows, query_index.reshape(rows, 1)]
-    key_count = 0
-    for keys, key_index in halves:
-        operands += [keys, key_index]
-        key_count += keys.shape[0]
-    width = query_rows.shape[1]
-    cost = pl.CostEstimate(
-        flops=2 * rows * key_count * (width + LATENT),
-        transcendentals=rows * key_count,
-        bytes_accessed=2 * (rows * width + key_count * width + rows * LATENT),
-    )
+
+    pieces = pl.pallas_call(
+        first_kernel,
+        out_shape=(
+            jax.ShapeDtypeStruct((rows, 1), f32),
+            jax.ShapeDtypeStruct((rows, 1), f32),
+            jax.ShapeDtypeStruct((rows, LATENT), f32),
+        ),
+        cost_estimate=cost(keys_a.shape[0]),
+    )(query_rows, query_index, keys_a, index_a)
     return pl.pallas_call(
-        attention_kernel,
+        second_kernel,
         out_shape=jax.ShapeDtypeStruct((rows, LATENT), jnp.bfloat16),
-        cost_estimate=cost,
-    )(*operands)
+        cost_estimate=cost(keys_b.shape[0]),
+    )(query_rows, query_index, keys_b, index_b, *pieces)
 
 
 def exchange(acc, axis, size, bit, same_over_yh):

time: 191 us -> 193 us (1.010)
  Pallas kernels: 11.7 us -> 14.3 us
    pallas_call x1 -> x2, Pallas kernels: 11.7 us -> 14.3 us  [the longest x1 7.23 us: attend(): pl.pallas_call(second_kernel, out_shape=jax.ShapeDtypeStruct((rows, LATEN...]
  transfers between devices with their start and end apart: 18 -> 18, of which waited for: 10 -> 9; matrix products, arithmetic and copies ran while one was open for 11% -> 11% of each run, Pallas kernels for 6% -> 8%
where the time goes in v13:
time: 193 us; the launch traced here: 190 us
  waiting for transfers between devices  70.4 us (36%)
  starting transfers between devices  63.4 us (33%)
  Pallas kernels  14.3 us (7%)
  between operations  13.8 us (7%)
  local copies, waits for them, and re-layouts  13.5 us (7%)
  matrix products  8.57 us (4%)
  other arithmetic  6.01 us (3%)
    ppermute x7, starting transfers between devices, gather_earlier_keys(): lax.ppermute(local, 'zh', [(i, i + shift) for i in range(cubes - shift)])  29.2 us
    ppermute x3, waiting for transfers between devices, exchange(): return lax.ppermute(acc, axis, pairs)  28.5 us
    ppermute x7, waiting for transfers between devices, gather_earlier_keys(): lax.ppermute(local, 'zh', [(i, i + shift) for i in range(cubes - shift)])  21.4 us
    all_gather x1, waiting for transfers between devices, body(): own = lax.all_gather(pair, ('zh', 'zl'), axis=1, tiled=True)  14.7 us
    ppermute x3, starting transfers between devices, scatter_sum(): lax.ppermute(sent, 'x', [(i, i ^ shift) for i in range(columns)])  10.4 us
    ppermute x3, starting transfers between devices, exchange(): return lax.ppermute(acc, axis, pairs)  7.91 us
    pallas_call x1, Pallas kernels, attend(): pl.pallas_call(second_kernel, out_shape=jax.ShapeDtypeStruct((rows, LATEN...  7.23 us
    pallas_call x1, Pallas kernels, attend(): pl.pallas_call(first_kernel, out_shape=(jax.ShapeDtypeStruct((rows, 1), f...  7.08 us
  transfers between devices with their start and end apart: 18, of which 9 were waited for; matrix products, arithmetic and copies ran while one was open for 11% of the time, Pallas kernels for 8%

profile of v13, /device:TPU:6, one launch (start us, length us, event | category | flops | bytes accessed | tf_op | source)
XLA Modules:
  0.0 189.9 jit_solution(9538314125136782090)
XLA Ops:
  6.5 3.6 %collective-permute-start.11 = (bf16[1,56,1024]{2,1,0:T(8,128)(2,1)}, bf16[1,56,1024]{2,1,0:T(8,128)(2,1)S(1)}, u32[]{:S(2)}, u32[]{:S(2)}) collective-permute-start(bf16[1,56,1024]{2,1,0:T(8,128)(2,1)} %bitcast.111), channel_id=1, source_target_pairs={{0,16},{16,0},{1,17},{17,1},{2,18},{18,2},{3,19},{19,3},{4,20},{20... | collective-permute-start | bytes 344072 | tf_op jit(solution)/shard_map/ppermute | solution.py:106
  10.2 3.5 %collective-permute-done.11 = bf16[1,56,1024]{2,1,0:T(8,128)(2,1)S(1)} collective-permute-done((bf16[1,56,1024]{2,1,0:T(8,128)(2,1)}, bf16[1,56,1024]{2,1,0:T(8,128)(2,1)S(1)}, u32[]{:S(2)}, u32[]{:S(2)}) %collective-permute-start.11) | collective-permute-done | bytes 114720 | tf_op jit(solution)/shard_map/ppermute | solution.py:106
  17.9 5.2 %collective-permute-start = (bf16[64,576]{1,0:T(8,128)(2,1)S(1)}, bf16[64,576]{1,0:T(8,128)(2,1)S(1)}, u32[]{:S(2)}, u32[]{:S(2)}) collective-permute-start(bf16[64,576]{1,0:T(8,128)(2,1)S(1)} %pad_maximum_fusion.3), channel_id=1, source_target_pairs={{0,64},{64,128},{128,192},{192,256},{256,320},{320,384},{384,448},... | collective-permute-start | bytes 221192 | tf_op jit(solution)/shard_map/ppermute | solution.py:137
  23.1 9.1 %collective-permute-start.1 = (bf16[64,576]{1,0:T(8,128)(2,1)S(1)}, bf16[64,576]{1,0:T(8,128)(2,1)S(1)}, u32[]{:S(2)}, u32[]{:S(2)}) collective-permute-start(bf16[64,576]{1,0:T(8,128)(2,1)S(1)} %pad_maximum_fusion.3), channel_id=1, source_target_pairs={{0,128},{64,192},{128,256},{192,320},{256,384},{320,448},{1,129},{... | collective-permute-start | bytes 221192 | tf_op jit(solution)/shard_map/ppermute | solution.py:137
  32.2 8.2 %collective-permute-start.2 = (bf16[64,576]{1,0:T(8,128)(2,1)S(1)}, bf16[64,576]{1,0:T(8,128)(2,1)S(1)}, u32[]{:S(2)}, u32[]{:S(2)}) collective-permute-start(bf16[64,576]{1,0:T(8,128)(2,1)S(1)} %pad_maximum_fusion.3), channel_id=1, source_target_pairs={{0,192},{64,256},{128,320},{192,384},{256,448},{1,193},{65,257},{1... | collective-permute-start | bytes 221192 | tf_op jit(solution)/shard_map/ppermute | solution.py:137
  40.4 2.8 %collective-permute-start.3 = (bf16[64,576]{1,0:T(8,128)(2,1)S(1)}, bf16[64,576]{1,0:T(8,128)(2,1)S(1)}, u32[]{:S(2)}, u32[]{:S(2)}) collective-permute-start(bf16[64,576]{1,0:T(8,128)(2,1)S(1)} %pad_maximum_fusion.3), channel_id=1, source_target_pairs={{0,256},{64,320},{128,384},{192,448},{1,257},{65,321},{129,385},{1... | collective-permute-start | bytes 221192 | tf_op jit(solution)/shard_map/ppermute | solution.py:137
  51.4 12.3 %collective-permute-done.4 = bf16[64,576]{1,0:T(8,128)(2,1)S(1)} collective-permute-done((bf16[64,576]{1,0:T(8,128)(2,1)S(1)}, bf16[64,576]{1,0:T(8,128)(2,1)S(1)}, u32[]{:S(2)}, u32[]{:S(2)}) %collective-permute-start.4) | collective-permute-done | bytes 73760 | tf_op jit(solution)/shard_map/ppermute | solution.py:137
  64.4 5.2 %collective-permute-done.5 = bf16[64,576]{1,0:T(8,128)(2,1)S(1)} collective-permute-done((bf16[64,576]{1,0:T(8,128)(2,1)S(1)}, bf16[64,576]{1,0:T(8,128)(2,1)S(1)}, u32[]{:S(2)}, u32[]{:S(2)}) %collective-permute-start.5) | collective-permute-done | bytes 73760 | tf_op jit(solution)/shard_map/ppermute | solution.py:137
  70.3 4.0 %collective-permute-done.6 = bf16[64,576]{1,0:T(8,128)(2,1)S(1)} collective-permute-done((bf16[64,576]{1,0:T(8,128)(2,1)S(1)}, bf16[64,576]{1,0:T(8,128)(2,1)S(1)}, u32[]{:S(2)}, u32[]{:S(2)}) %collective-permute-start.6) | collective-permute-done | bytes 73760 | tf_op jit(solution)/shard_map/ppermute | solution.py:137
  76.8 3.5 %collective-permute-start.8 = (bf16[8,64,576]{2,1,0:T(8,128)(2,1)}, bf16[8,64,576]{2,1,0:T(8,128)(2,1)S(1)}, u32[]{:S(2)}, u32[]{:S(2)}) collective-permute-start(bf16[8,64,576]{2,1,0:T(8,128)(2,1)} %get-tuple-element.24), channel_id=1, source_target_pairs={{0,16},{16,0},{1,17},{17,1},{2,18},{18,2},{3,19},{19,3},{4,20},{20... | collective-permute-start | bytes 1769480 | tf_op jit(solution)/shard_map/ppermute | solution.py:108
  80.3 25.1 %collective-permute-done.7 = bf16[8,64,576]{2,1,0:T(8,128)(2,1)S(1)} collective-permute-done((bf16[8,64,576]{2,1,0:T(8,128)(2,1)}, bf16[8,64,576]{2,1,0:T(8,128)(2,1)S(1)}, u32[]{:S(2)}, u32[]{:S(2)}) %collective-permute-start.7) | collective-permute-done | bytes 589856 | tf_op jit(solution)/shard_map/ppermute | solution.py:106
  105.4 5.1 %collective-permute-start.9 = (bf16[8,64,576]{2,1,0:T(8,128)(2,1)S(1)}, bf16[8,64,576]{2,1,0:T(8,128)(2,1)S(1)}, u32[]{:S(2)}, u32[]{:S(2)}) collective-permute-start(bf16[8,64,576]{2,1,0:T(8,128)(2,1)S(1)} %collective-permute-done.7), channel_id=1, source_target_pairs={{0,17},{1,16},{16,1},{17,0},{2,19},{3,18},{18,3},{19,2},{4,21},{5,... | collective-permute-start | bytes 1769480 | tf_op jit(solution)/shard_map/ppermute | solution.py:109
  110.5 14.7 %all-gather.2.cloned.1.call-done = bf16[1024,1792]{0,1:T(8,128)(2,1)} async-done(((bf16[1024,112]{0,1:T(8,128)(2,1)}), bf16[1024,1792]{0,1:T(8,128)(2,1)}) %all-gather.2.cloned.1.call-update) | async-done | bytes 3670032 | tf_op jit(solution)/shard_map/all_gather | solution.py:219
  129.9 2.4 %collective-permute-start.10 = (bf16[32,64,576]{2,1,0:T(8,128)(2,1)}, bf16[32,64,576]{2,1,0:T(8,128)(2,1)}, u32[]{:S(2)}, u32[]{:S(2)}) collective-permute-start(bf16[32,64,576]{2,1,0:T(8,128)(2,1)} %constant_dynamic-update-slice_fusion), channel_id=1, source_target_pairs={{0,8},{8,0},{1,9},{9,1},{2,10},{10,2},{3,11},{11,3},{4,12},{12,4},... | collective-permute-start | bytes 7077896 | tf_op jit(solution)/shard_map/ppermute | solution.py:106
  137.3 7.1 %shard_map.82 = (f32[512,1]{1,0:T(8,128)}, f32[512,1]{1,0:T(8,128)}, f32[512,512]{1,0:T(8,128)}) custom-call(bf16[512,576]{1,0:T(8,128)(2,1)} %bitcast.108, s32[512,1]{1,0:T(8,128)} %reshape_reshape.4.qi_ref, bf16[2048,576]{1,0:T(8,128)(2,1)} %bitcast.112, s32[1,2048]{1,0:T(1,128)} %add.134.i_ref), custom_call_target="tpu_custom_call" | custom-call | flops 2281701376 | bytes 3997696 | tf_op jit(solution)/shard_map/pallas_call | solution.py:87
  144.4 7.2 %shard_map.83 = bf16[512,512]{1,0:T(8,128)(2,1)} custom-call(bf16[512,576]{1,0:T(8,128)(2,1)} %bitcast.109, s32[512,1]{1,0:T(8,128)} %reshape_reshape.4.qi_ref, bf16[2048,576]{1,0:T(8,128)(2,1)} %bitcast.13.k_ref, s32[1,2048]{1,0:T(1,128)} %add.130.i_ref, f32[512,1]{1,0:T(8,128)} %get-tuple-element.8.pa_ref, f32[512,1]{1,0:T(8,128)} %get-tuple-element.9.ta_ref, ...), custom_call_target="tpu_custom_call" | custom-call | flops 2281701376 | bytes 3997696 | tf_op jit(solution)/shard_map/pallas_call | solution.py:96
  153.3 3.3 %fusion.27 = f32[64,8,224]{2,0,1:T(8,128)S(1)} fusion(bf16[64,1024,1]{1,0,2:T(8,128)(2,1)S(1)} %reshape.271, bf16[8,224,1024]{2,1,0:T(8,128)(2,1)} %bitcast.104), kind=kOutput, calls=%fused_computation.81 | convolution fusion | flops 234881024 | bytes 4259840 | tf_op jit(solution)/shard_map/dot_general | solution.py:224
  156.6 3.3 %fusion.28 = f32[64,8,224]{2,0,1:T(8,128)S(1)} fusion(bf16[64,1024,1]{1,0,2:T(8,128)(2,1)S(1)} %reshape.271, bf16[8,224,1024]{2,1,0:T(8,128)(2,1)} %bitcast.28), kind=kOutput, calls=%fused_computation.82 | convolution fusion | flops 234881024 | bytes 4259840 | tf_op jit(solution)/shard_map/dot_general | solution.py:224
  160.2 2.5 %collective-permute-start.13 = (bf16[2,64,448]{2,1,0:T(8,128)(2,1)S(1)}, bf16[2,64,448]{2,1,0:T(8,128)(2,1)S(1)}, u32[]{:S(2)}, u32[]{:S(2)}) collective-permute-start(bf16[2,64,448]{2,1,0:T(8,128)(2,1)S(1)} %get-tuple-element.15), channel_id=1, source_target_pairs={{0,2},{2,0},{4,6},{6,4},{1,3},{3,1},{5,7},{7,5},{8,10},{10,8},{12,... | collective-permute-start | bytes 344072 | tf_op jit(solution)/shard_map/ppermute | solution.py:162
  162.7 3.0 %collective-permute-start.14 = (bf16[2,64,448]{2,1,0:T(8,128)(2,1)S(1)}, bf16[2,64,448]{2,1,0:T(8,128)(2,1)S(1)}, u32[]{:S(2)}, u32[]{:S(2)}) collective-permute-start(bf16[2,64,448]{2,1,0:T(8,128)(2,1)S(1)} %get-tuple-element.17), channel_id=1, source_target_pairs={{0,4},{2,6},{4,0},{6,2},{1,5},{3,7},{5,1},{7,3},{8,12},{10,14},{12... | collective-permute-start | bytes 344072 | tf_op jit(solution)/shard_map/ppermute | solution.py:162
  165.8 4.9 %collective-permute-start.15 = (bf16[2,64,448]{2,1,0:T(8,128)(2,1)S(1)}, bf16[2,64,448]{2,1,0:T(8,128)(2,1)S(1)}, u32[]{:S(2)}, u32[]{:S(2)}) collective-permute-start(bf16[2,64,448]{2,1,0:T(8,128)(2,1)S(1)} %get-tuple-element.16), channel_id=1, source_target_pairs={{0,6},{2,4},{4,2},{6,0},{1,7},{3,5},{5,3},{7,1},{8,14},{10,12},{12... | collective-permute-start | bytes 344072 | tf_op jit(solution)/shard_map/ppermute | solution.py:162
  171.3 2.8 %collective-permute-done.15 = bf16[2,64,448]{2,1,0:T(8,128)(2,1)S(1)} collective-permute-done((bf16[2,64,448]{2,1,0:T(8,128)(2,1)S(1)}, bf16[2,64,448]{2,1,0:T(8,128)(2,1)S(1)}, u32[]{:S(2)}, u32[]{:S(2)}) %collective-permute-start.15) | collective-permute-done | bytes 114720 | tf_op jit(solution)/shard_map/ppermute | solution.py:162
  174.1 5.4 %collective-permute-start.16 = (bf16[64,448]{1,0:T(8,128)(2,1)S(1)}, bf16[64,448]{1,0:T(8,128)(2,1)S(1)}, u32[]{:S(2)}, u32[]{:S(2)}) collective-permute-start(bf16[64,448]{1,0:T(8,128)(2,1)S(1)} %fusion.15), channel_id=1, source_target_pairs={{0,1},{1,0},{2,3},{3,2},{4,5},{5,4},{6,7},{7,6},{8,9},{9,8},{10,11... | collective-permute-start | bytes 172040 | tf_op jit(solution)/shard_map/ppermute | solution.py:168
  179.5 2.3 %collective-permute-done.16 = bf16[64,448]{1,0:T(8,128)(2,1)S(1)} collective-permute-done((bf16[64,448]{1,0:T(8,128)(2,1)S(1)}, bf16[64,448]{1,0:T(8,128)(2,1)S(1)}, u32[]{:S(2)}, u32[]{:S(2)}) %collective-permute-start.16) | collective-permute-done | bytes 57376 | tf_op jit(solution)/shard_map/ppermute | solution.py:168
  (77 shorter events, 29.8 us)
Async XLA Ops:
  6.5 128.2 %copy-start = (bf16[512,1024]{1,0:T(8,128)(2,1)S(1)}, bf16[512,1024]{1,0:T(8,128)(2,1)}, u32[]{:S(2)}) copy-start(bf16[512,1024]{1,0:T(8,128)(2,1)} %param.13) | copy-start | bytes 3145732
  6.5 118.7 %all-gather.2.cloned.1.call-start = ((), (), s32[]{:S(2)}) async-start(), calls=%async_computation | async-start | bytes 3899392 | tf_op jit(solution)/shard_map/all_gather | solution.py:219
  6.5 7.1 %collective-permute-start.11 = (bf16[1,56,1024]{2,1,0:T(8,128)(2,1)}, bf16[1,56,1024]{2,1,0:T(8,128)(2,1)S(1)}, u32[]{:S(2)}, u32[]{:S(2)}) collective-permute-start(bf16[1,56,1024]{2,1,0:T(8,128)(2,1)} %bitcast.111), channel_id=1, source_target_pairs={{0,16},{16,0},{1,17},{17,1},{2,18},{18,2},{3,19},{19,3},{4,20},{20... | collective-permute-start | bytes 344072 | tf_op jit(solution)/shard_map/ppermute | solution.py:106
  17.9 28.2 %collective-permute-start = (bf16[64,576]{1,0:T(8,128)(2,1)S(1)}, bf16[64,576]{1,0:T(8,128)(2,1)S(1)}, u32[]{:S(2)}, u32[]{:S(2)}) collective-permute-start(bf16[64,576]{1,0:T(8,128)(2,1)S(1)} %pad_maximum_fusion.3), channel_id=1, source_target_pairs={{0,64},{64,128},{128,192},{192,256},{256,320},{320,384},{384,448},... | collective-permute-start | bytes 221192 | tf_op jit(solution)/shard_map/ppermute | solution.py:137
  23.1 25.0 %collective-permute-start.1 = (bf16[64,576]{1,0:T(8,128)(2,1)S(1)}, bf16[64,576]{1,0:T(8,128)(2,1)S(1)}, u32[]{:S(2)}, u32[]{:S(2)}) collective-permute-start(bf16[64,576]{1,0:T(8,128)(2,1)S(1)} %pad_maximum_fusion.3), channel_id=1, source_target_pairs={{0,128},{64,192},{128,256},{192,320},{256,384},{320,448},{1,129},{... | collective-permute-start | bytes 221192 | tf_op jit(solution)/shard_map/ppermute | solution.py:137
  32.2 17.9 %collective-permute-start.2 = (bf16[64,576]{1,0:T(8,128)(2,1)S(1)}, bf16[64,576]{1,0:T(8,128)(2,1)S(1)}, u32[]{:S(2)}, u32[]{:S(2)}) collective-permute-start(bf16[64,576]{1,0:T(8,128)(2,1)S(1)} %pad_maximum_fusion.3), channel_id=1, source_target_pairs={{0,192},{64,256},{128,320},{192,384},{256,448},{1,193},{65,257},{1... | collective-permute-start | bytes 221192 | tf_op jit(solution)/shard_map/ppermute | solution.py:137
  40.4 10.3 %collective-permute-start.3 = (bf16[64,576]{1,0:T(8,128)(2,1)S(1)}, bf16[64,576]{1,0:T(8,128)(2,1)S(1)}, u32[]{:S(2)}, u32[]{:S(2)}) collective-permute-start(bf16[64,576]{1,0:T(8,128)(2,1)S(1)} %pad_maximum_fusion.3), channel_id=1, source_target_pairs={{0,256},{64,320},{128,384},{192,448},{1,257},{65,321},{129,385},{1... | collective-permute-start | bytes 221192 | tf_op jit(solution)/shard_map/ppermute | solution.py:137
  43.2 20.4 %collective-permute-start.4 = (bf16[64,576]{1,0:T(8,128)(2,1)S(1)}, bf16[64,576]{1,0:T(8,128)(2,1)S(1)}, u32[]{:S(2)}, u32[]{:S(2)}) collective-permute-start(bf16[64,576]{1,0:T(8,128)(2,1)S(1)} %pad_maximum_fusion.3), channel_id=1, source_target_pairs={{0,320},{64,384},{128,448},{1,321},{65,385},{129,449},{2,322},{66,... | collective-permute-start | bytes 221192 | tf_op jit(solution)/shard_map/ppermute | solution.py:137
  46.1 23.5 %collective-permute-start.5 = (bf16[64,576]{1,0:T(8,128)(2,1)S(1)}, bf16[64,576]{1,0:T(8,128)(2,1)S(1)}, u32[]{:S(2)}, u32[]{:S(2)}) collective-permute-start(bf16[64,576]{1,0:T(8,128)(2,1)S(1)} %pad_maximum_fusion.3), channel_id=1, source_target_pairs={{0,384},{64,448},{1,385},{65,449},{2,386},{66,450},{3,387},{67,451... | collective-permute-start | bytes 221192 | tf_op jit(solution)/shard_map/ppermute | solution.py:137
  48.1 26.2 %collective-permute-start.6 = (bf16[64,576]{1,0:T(8,128)(2,1)S(1)}, bf16[64,576]{1,0:T(8,128)(2,1)S(1)}, u32[]{:S(2)}, u32[]{:S(2)}) collective-permute-start(bf16[64,576]{1,0:T(8,128)(2,1)S(1)} %pad_maximum_fusion.3), channel_id=1, source_target_pairs={{0,448},{1,449},{2,450},{3,451},{4,452},{5,453},{6,454},{7,455},{8... | collective-permute-start | bytes 221192 | tf_op jit(solution)/shard_map/ppermute | solution.py:137
  51.4 82.7 %copy-start.1 = (bf16[64,512]{1,0:T(8,128)(2,1)S(1)}, bf16[64,512]{1,0:T(8,128)(2,1)}, u32[]{:S(2)}) copy-start(bf16[64,512]{1,0:T(8,128)(2,1)} %param.9) | copy-start | bytes 196612
  74.9 30.5 %collective-permute-start.7 = (bf16[8,64,576]{2,1,0:T(8,128)(2,1)}, bf16[8,64,576]{2,1,0:T(8,128)(2,1)S(1)}, u32[]{:S(2)}, u32[]{:S(2)}) collective-permute-start(bf16[8,64,576]{2,1,0:T(8,128)(2,1)} %get-tuple-element.24), channel_id=1, source_target_pairs={{0,32},{32,0},{1,33},{33,1},{2,34},{34,2},{3,35},{35,3},{4,36},{36... | collective-permute-start | bytes 1769480 | tf_op jit(solution)/shard_map/ppermute | solution.py:106
  76.8 51.2 %collective-permute-start.8 = (bf16[8,64,576]{2,1,0:T(8,128)(2,1)}, bf16[8,64,576]{2,1,0:T(8,128)(2,1)S(1)}, u32[]{:S(2)}, u32[]{:S(2)}) collective-permute-start(bf16[8,64,576]{2,1,0:T(8,128)(2,1)} %get-tuple-element.24), channel_id=1, source_target_pairs={{0,16},{16,0},{1,17},{17,1},{2,18},{18,2},{3,19},{19,3},{4,20},{20... | collective-permute-start | bytes 1769480 | tf_op jit(solution)/shard_map/ppermute | solution.py:108
  105.4 23.6 %collective-permute-start.9 = (bf16[8,64,576]{2,1,0:T(8,128)(2,1)S(1)}, bf16[8,64,576]{2,1,0:T(8,128)(2,1)S(1)}, u32[]{:S(2)}, u32[]{:S(2)}) collective-permute-start(bf16[8,64,576]{2,1,0:T(8,128)(2,1)S(1)} %collective-permute-done.7), channel_id=1, source_target_pairs={{0,17},{1,16},{16,1},{17,0},{2,19},{3,18},{18,3},{19,2},{4,21},{5,... | collective-permute-start | bytes 1769480 | tf_op jit(solution)/shard_map/ppermute | solution.py:109
  125.2 31.4 %collective-permute-start.12 = (bf16[1024,1792]{0,1:T(8,128)(2,1)}, bf16[1024,1792]{0,1:T(8,128)(2,1)}, u32[]{:S(2)}, u32[]{:S(2)}) collective-permute-start(bf16[1024,1792]{0,1:T(8,128)(2,1)} %all-gather.2.cloned.1.call-done), channel_id=1, source_target_pairs={{0,8},{8,0},{1,9},{9,1},{2,10},{10,2},{3,11},{11,3},{4,12},{12,4},... | collective-permute-start | bytes 11010056 | tf_op jit(solution)/shard_map/ppermute | solution.py:220
  128.0 6.7 %copy-start.3 = (bf16[64,1024]{1,0:T(8,128)(2,1)S(1)}, bf16[64,1024]{1,0:T(8,128)(2,1)}, u32[]{:S(2)}) copy-start(bf16[64,1024]{1,0:T(8,128)(2,1)} %param.8) | copy-start | bytes 393220
  129.9 14.5 %collective-permute-start.10 = (bf16[32,64,576]{2,1,0:T(8,128)(2,1)}, bf16[32,64,576]{2,1,0:T(8,128)(2,1)}, u32[]{:S(2)}, u32[]{:S(2)}) collective-permute-start(bf16[32,64,576]{2,1,0:T(8,128)(2,1)} %constant_dynamic-update-slice_fusion), channel_id=1, source_target_pairs={{0,8},{8,0},{1,9},{9,1},{2,10},{10,2},{3,11},{11,3},{4,12},{12,4},... | collective-permute-start | bytes 7077896 | tf_op jit(solution)/shard_map/ppermute | solution.py:106
  144.4 7.2 %copy-start.2 = (bf16[512,1024]{1,0:T(8,128)(2,1)S(1)}, bf16[512,1024]{1,0:T(8,128)(2,1)}, u32[]{:S(2)}) copy-start(bf16[512,1024]{1,0:T(8,128)(2,1)} %param.14) | copy-start | bytes 3145732
  160.2 10.5 %collective-permute-start.13 = (bf16[2,64,448]{2,1,0:T(8,128)(2,1)S(1)}, bf16[2,64,448]{2,1,0:T(8,128)(2,1)S(1)}, u32[]{:S(2)}, u32[]{:S(2)}) collective-permute-start(bf16[2,64,448]{2,1,0:T(8,128)(2,1)S(1)} %get-tuple-element.15), channel_id=1, source_target_pairs={{0,2},{2,0},{4,6},{6,4},{1,3},{3,1},{5,7},{7,5},{8,10},{10,8},{12,... | collective-permute-start | bytes 344072 | tf_op jit(solution)/shard_map/ppermute | solution.py:162
  162.7 8.6 %collective-permute-start.14 = (bf16[2,64,448]{2,1,0:T(8,128)(2,1)S(1)}, bf16[2,64,448]{2,1,0:T(8,128)(2,1)S(1)}, u32[]{:S(2)}, u32[]{:S(2)}) collective-permute-start(bf16[2,64,448]{2,1,0:T(8,128)(2,1)S(1)} %get-tuple-element.17), channel_id=1, source_target_pairs={{0,4},{2,6},{4,0},{6,2},{1,5},{3,7},{5,1},{7,3},{8,12},{10,14},{12... | collective-permute-start | bytes 344072 | tf_op jit(solution)/shard_map/ppermute | solution.py:162
  165.8 8.3 %collective-permute-start.15 = (bf16[2,64,448]{2,1,0:T(8,128)(2,1)S(1)}, bf16[2,64,448]{2,1,0:T(8,128)(2,1)S(1)}, u32[]{:S(2)}, u32[]{:S(2)}) collective-permute-start(bf16[2,64,448]{2,1,0:T(8,128)(2,1)S(1)} %get-tuple-element.16), channel_id=1, source_target_pairs={{0,6},{2,4},{4,2},{6,0},{1,7},{3,5},{5,3},{7,1},{8,14},{10,12},{12... | collective-permute-start | bytes 344072 | tf_op jit(solution)/shard_map/ppermute | solution.py:162
  174.1 7.7 %collective-permute-start.16 = (bf16[64,448]{1,0:T(8,128)(2,1)S(1)}, bf16[64,448]{1,0:T(8,128)(2,1)S(1)}, u32[]{:S(2)}, u32[]{:S(2)}) collective-permute-start(bf16[64,448]{1,0:T(8,128)(2,1)S(1)} %fusion.15), channel_id=1, source_target_pairs={{0,1},{1,0},{2,3},{3,2},{4,5},{5,4},{6,7},{7,6},{8,9},{9,8},{10,11... | collective-permute-start | bytes 172040 | tf_op jit(solution)/shard_map/ppermute | solution.py:168
Sparse Core Ops, SparseCore 0:
  15.4 109.7 all-gather.1

commit v14 on v11

--- a/solution.py
+++ b/solution.py
@@ -38,7 +38,7 @@
     )
 
 
-def attention_kernel(q_ref, qi_ref, ka_ref, ia_ref, kb_ref, ib_ref, o_ref):
+def attention_kernel(q_ref, qi_ref, ka_ref, ia_ref, kb_ref, ib_ref, v_ref, o_ref):
     scale = 1.0 / math.sqrt(NOPE + ROPE)
     queries = q_ref[...]
     query_index = qi_ref[...]
@@ -64,10 +64,19 @@
     summed = summed + jnp.dot(
         weights_b.astype(jnp.bfloat16), kb_ref[:, :LATENT], preferred_element_type=jnp.float32
     )
-    o_ref[...] = (summed / totals).astype(jnp.bfloat16)
-
-
-def attend(query_rows, query_index, halves):
+    latent_out = (summed / totals).astype(jnp.bfloat16)
+    head_count = v_ref.shape[1] // VDIM
+    tokens = latent_out.shape[0] // head_count
+    for head in range(head_count):
+        head_out = jnp.dot(
+            latent_out[head * tokens : (head + 1) * tokens],
+            v_ref[:, head * VDIM : (head + 1) * VDIM],
+            preferred_element_type=jnp.float32,
+        )
+        o_ref[:, head * VDIM : (head + 1) * VDIM] = head_out.astype(jnp.bfloat16)
+
+
+def attend(query_rows, query_index, halves, value_up):
     rows = query_rows.shape[0]
     operands = [query_rows, query_index.reshape(rows, 1)]
     key_count = 0
@@ -80,9 +89,11 @@
         transcendentals=rows * key_count,
         bytes_accessed=2 * (rows * width + key_count * width + rows * LATENT),
     )
+    operands.append(value_up)
+    tokens = rows * VDIM // value_up.shape[1]
     return pl.pallas_call(
         attention_kernel,
-        out_shape=jax.ShapeDtypeStruct((rows, LATENT), jnp.bfloat16),
+        out_shape=jax.ShapeDtypeStruct((tokens, value_up.shape[1]), jnp.bfloat16),
         cost_estimate=cost,
     )(*operands)
 
@@ -158,16 +169,6 @@
     return total
 
 
-def upward(latent_out, value_up, token_count, head_count):
-    head_out = jnp.einsum(
-        "thl,lhd->thd",
-        latent_out.reshape(token_count, head_count, LATENT),
-        value_up.reshape(LATENT, head_count, VDIM),
-        preferred_element_type=jnp.float32,
-    )
-    return head_out.astype(jnp.bfloat16).reshape(token_count, head_count * VDIM)
-
-
 def body(queries_nope, queries_rope, latents, rope_keys, positions, key_up, value_up, out_proj):
     token_count = latents.shape[0]
     head_count = key_up.shape[1] // NOPE
@@ -184,8 +185,10 @@
         key_up.reshape(LATENT, head_count, NOPE),
         preferred_element_type=jnp.float32,
     ).astype(jnp.bfloat16)
-    query_rows = jnp.concatenate([lat_queries, rot_queries], axis=-1).reshape(
-        token_count * head_count, LATENT + ROPE
+    query_rows = (
+        jnp.concatenate([lat_queries, rot_queries], axis=-1)
+        .transpose(1, 0, 2)
+        .reshape(head_count * token_count, LATENT + ROPE)
     )
     local_keys = jnp.concatenate([latents, rot_keys], axis=-1)
     halves = []
@@ -196,11 +199,8 @@
         ).reshape(1, -1)
         halves.append((keys, key_index))
     first_token = lax.axis_index(CTX) * token_count
-    query_index = jnp.repeat(
-        first_token + jnp.arange(token_count, dtype=jnp.int32), head_count
-    )
-    latent_out = attend(query_rows, query_index, halves)
-    head_out = upward(latent_out, value_up, token_count, head_count)
+    query_index = jnp.tile(first_token + jnp.arange(token_count, dtype=jnp.int32), head_count)
+    head_out = attend(query_rows, query_index, halves, value_up)
     pair = gather_in_order(out_proj.T, (("yl", 2),), False)
     pair = pair.reshape(2, out_proj.shape[1], -1).transpose(2, 0, 1).reshape(out_proj.shape[0], -1)
     own = lax.all_gather(pair, ("zh", "zl"), axis=1, tiled=True)

time: 191 us -> 191 us (level)
  no operation moved by 1% of the time
where the time goes in v14:
time: 191 us; the launch traced here: 188 us
  waiting for transfers between devices  71.1 us (37%)
  starting transfers between devices  63.4 us (33%)
  between operations  13.8 us (7%)
  local copies, waits for them, and re-layouts  13.4 us (7%)
  Pallas kernels  12 us (6%)
  matrix products  7.11 us (4%)
  other arithmetic  6.87 us (4%)
    ppermute x3, waiting for transfers between devices, exchange(): return lax.ppermute(acc, axis, pairs)  29.2 us
    ppermute x7, starting transfers between devices, gather_earlier_keys(): lax.ppermute(local, 'zh', [(i, i + shift) for i in range(cubes - shift)])  29.2 us
    ppermute x7, waiting for transfers between devices, gather_earlier_keys(): lax.ppermute(local, 'zh', [(i, i + shift) for i in range(cubes - shift)])  21.4 us
    all_gather x1, waiting for transfers between devices, body(): own = lax.all_gather(pair, ('zh', 'zl'), axis=1, tiled=True)  14.7 us
    pallas_call x1, Pallas kernels, attend(): pl.pallas_call(attention_kernel, out_shape=jax.ShapeDtypeStruct((tokens,...  12 us
    ppermute x3, starting transfers between devices, scatter_sum(): lax.ppermute(sent, 'x', [(i, i ^ shift) for i in range(columns)])  10.4 us
    ppermute x3, starting transfers between devices, exchange(): return lax.ppermute(acc, axis, pairs)  7.91 us
    unnamed x17, local copies, waits for them, and re-layouts  6.76 us
  transfers between devices with their start and end apart: 18, of which 10 were waited for; matrix products, arithmetic and copies ran while one was open for 11% of the time, Pallas kernels for 6%

profile of v14, /device:TPU:6, one launch (start us, length us, event | category | flops | bytes accessed | tf_op | source)
XLA Modules:
  0.0 187.6 jit_solution(634078437274837206)
XLA Ops:
  6.5 3.6 %collective-permute-start.11 = (bf16[1,56,1024]{2,1,0:T(8,128)(2,1)}, bf16[1,56,1024]{2,1,0:T(8,128)(2,1)S(1)}, u32[]{:S(2)}, u32[]{:S(2)}) collective-permute-start(bf16[1,56,1024]{2,1,0:T(8,128)(2,1)} %bitcast.93), channel_id=1, source_target_pairs={{0,16},{16,0},{1,17},{17,1},{2,18},{18,2},{3,19},{19,3},{4,20},{20... | collective-permute-start | bytes 344072 | tf_op jit(solution)/shard_map/ppermute | solution.py:104
  10.2 3.5 %collective-permute-done.11 = bf16[1,56,1024]{2,1,0:T(8,128)(2,1)S(1)} collective-permute-done((bf16[1,56,1024]{2,1,0:T(8,128)(2,1)}, bf16[1,56,1024]{2,1,0:T(8,128)(2,1)S(1)}, u32[]{:S(2)}, u32[]{:S(2)}) %collective-permute-start.11) | collective-permute-done | bytes 114720 | tf_op jit(solution)/shard_map/ppermute | solution.py:104
  17.9 5.2 %collective-permute-start = (bf16[64,576]{1,0:T(8,128)(2,1)S(1)}, bf16[64,576]{1,0:T(8,128)(2,1)S(1)}, u32[]{:S(2)}, u32[]{:S(2)}) collective-permute-start(bf16[64,576]{1,0:T(8,128)(2,1)S(1)} %pad_maximum_fusion.2), channel_id=1, source_target_pairs={{0,64},{64,128},{128,192},{192,256},{256,320},{320,384},{384,448},... | collective-permute-start | bytes 221192 | tf_op jit(solution)/shard_map/ppermute | solution.py:135
  23.1 9.1 %collective-permute-start.1 = (bf16[64,576]{1,0:T(8,128)(2,1)S(1)}, bf16[64,576]{1,0:T(8,128)(2,1)S(1)}, u32[]{:S(2)}, u32[]{:S(2)}) collective-permute-start(bf16[64,576]{1,0:T(8,128)(2,1)S(1)} %pad_maximum_fusion.2), channel_id=1, source_target_pairs={{0,128},{64,192},{128,256},{192,320},{256,384},{320,448},{1,129},{... | collective-permute-start | bytes 221192 | tf_op jit(solution)/shard_map/ppermute | solution.py:135
  32.2 8.2 %collective-permute-start.2 = (bf16[64,576]{1,0:T(8,128)(2,1)S(1)}, bf16[64,576]{1,0:T(8,128)(2,1)S(1)}, u32[]{:S(2)}, u32[]{:S(2)}) collective-permute-start(bf16[64,576]{1,0:T(8,128)(2,1)S(1)} %pad_maximum_fusion.2), channel_id=1, source_target_pairs={{0,192},{64,256},{128,320},{192,384},{256,448},{1,193},{65,257},{1... | collective-permute-start | bytes 221192 | tf_op jit(solution)/shard_map/ppermute | solution.py:135
  40.4 2.8 %collective-permute-start.3 = (bf16[64,576]{1,0:T(8,128)(2,1)S(1)}, bf16[64,576]{1,0:T(8,128)(2,1)S(1)}, u32[]{:S(2)}, u32[]{:S(2)}) collective-permute-start(bf16[64,576]{1,0:T(8,128)(2,1)S(1)} %pad_maximum_fusion.2), channel_id=1, source_target_pairs={{0,256},{64,320},{128,384},{192,448},{1,257},{65,321},{129,385},{1... | collective-permute-start | bytes 221192 | tf_op jit(solution)/shard_map/ppermute | solution.py:135
  51.4 12.3 %collective-permute-done.4 = bf16[64,576]{1,0:T(8,128)(2,1)S(1)} collective-permute-done((bf16[64,576]{1,0:T(8,128)(2,1)S(1)}, bf16[64,576]{1,0:T(8,128)(2,1)S(1)}, u32[]{:S(2)}, u32[]{:S(2)}) %collective-permute-start.4) | collective-permute-done | bytes 73760 | tf_op jit(solution)/shard_map/ppermute | solution.py:135
  64.4 5.2 %collective-permute-done.5 = bf16[64,576]{1,0:T(8,128)(2,1)S(1)} collective-permute-done((bf16[64,576]{1,0:T(8,128)(2,1)S(1)}, bf16[64,576]{1,0:T(8,128)(2,1)S(1)}, u32[]{:S(2)}, u32[]{:S(2)}) %collective-permute-start.5) | collective-permute-done | bytes 73760 | tf_op jit(solution)/shard_map/ppermute | solution.py:135
  70.3 3.9 %collective-permute-done.6 = bf16[64,576]{1,0:T(8,128)(2,1)S(1)} collective-permute-done((bf16[64,576]{1,0:T(8,128)(2,1)S(1)}, bf16[64,576]{1,0:T(8,128)(2,1)S(1)}, u32[]{:S(2)}, u32[]{:S(2)}) %collective-permute-start.6) | collective-permute-done | bytes 73760 | tf_op jit(solution)/shard_map/ppermute | solution.py:135
  76.8 3.5 %collective-permute-start.8 = (bf16[8,64,576]{2,1,0:T(8,128)(2,1)}, bf16[8,64,576]{2,1,0:T(8,128)(2,1)S(1)}, u32[]{:S(2)}, u32[]{:S(2)}) collective-permute-start(bf16[8,64,576]{2,1,0:T(8,128)(2,1)} %get-tuple-element.18), channel_id=1, source_target_pairs={{0,16},{16,0},{1,17},{17,1},{2,18},{18,2},{3,19},{19,3},{4,20},{20... | collective-permute-start | bytes 1769480 | tf_op jit(solution)/shard_map/ppermute | solution.py:106
  80.3 25.1 %collective-permute-done.7 = bf16[8,64,576]{2,1,0:T(8,128)(2,1)S(1)} collective-permute-done((bf16[8,64,576]{2,1,0:T(8,128)(2,1)}, bf16[8,64,576]{2,1,0:T(8,128)(2,1)S(1)}, u32[]{:S(2)}, u32[]{:S(2)}) %collective-permute-start.7) | collective-permute-done | bytes 589856 | tf_op jit(solution)/shard_map/ppermute | solution.py:104
  105.4 5.1 %collective-permute-start.9 = (bf16[8,64,576]{2,1,0:T(8,128)(2,1)S(1)}, bf16[8,64,576]{2,1,0:T(8,128)(2,1)S(1)}, u32[]{:S(2)}, u32[]{:S(2)}) collective-permute-start(bf16[8,64,576]{2,1,0:T(8,128)(2,1)S(1)} %collective-permute-done.7), channel_id=1, source_target_pairs={{0,17},{1,16},{16,1},{17,0},{2,19},{3,18},{18,3},{19,2},{4,21},{5,... | collective-permute-start | bytes 1769480 | tf_op jit(solution)/shard_map/ppermute | solution.py:107
  110.5 14.7 %all-gather.2.cloned.1.call-done = bf16[1024,1792]{0,1:T(8,128)(2,1)} async-done(((bf16[1024,112]{0,1:T(8,128)(2,1)}), bf16[1024,1792]{0,1:T(8,128)(2,1)}) %all-gather.2.cloned.1.call-update) | async-done | bytes 3670032 | tf_op jit(solution)/shard_map/all_gather | solution.py:206
  125.2 1.9 %collective-permute-start.12 = (bf16[1024,1792]{0,1:T(8,128)(2,1)}, bf16[1024,1792]{0,1:T(8,128)(2,1)}, u32[]{:S(2)}, u32[]{:S(2)}) collective-permute-start(bf16[1024,1792]{0,1:T(8,128)(2,1)} %all-gather.2.cloned.1.call-done), channel_id=1, source_target_pairs={{0,8},{8,0},{1,9},{9,1},{2,10},{10,2},{3,11},{11,3},{4,12},{12,4},... | collective-permute-start | bytes 11010056 | tf_op jit(solution)/shard_map/ppermute | solution.py:207
  129.9 2.4 %collective-permute-start.10 = (bf16[32,64,576]{2,1,0:T(8,128)(2,1)}, bf16[32,64,576]{2,1,0:T(8,128)(2,1)}, u32[]{:S(2)}, u32[]{:S(2)}) collective-permute-start(bf16[32,64,576]{2,1,0:T(8,128)(2,1)} %constant_dynamic-update-slice_fusion), channel_id=1, source_target_pairs={{0,8},{8,0},{1,9},{9,1},{2,10},{10,2},{3,11},{11,3},{4,12},{12,4},... | collective-permute-start | bytes 7077896 | tf_op jit(solution)/shard_map/ppermute | solution.py:104
  137.6 12.0 %shard_map.82 = bf16[64,1024]{1,0:T(8,128)(2,1)} custom-call(bf16[512,576]{1,0:T(8,128)(2,1)} %bitcast.91, s32[512,1]{1,0:T(8,128)} %reshape_tile.4.qi_ref, bf16[2048,576]{1,0:T(8,128)(2,1)} %bitcast.94, s32[1,2048]{1,0:T(1,128)} %add.134.ia_ref, bf16[2048,576]{1,0:T(8,128)(2,1)} %bitcast.15.kb_ref, s32[1,2048]{1,0:T(1,128)} %add.138.ib_ref, ...), custom_call_target="tpu_custom_call" | custom-call | flops 4563402752 | bytes 5832704 | tf_op jit(solution)/shard_map/pallas_call | solution.py:94
  149.6 3.4 %fusion.23 = f32[64,1792]{1,0:T(8,128)S(1)} fusion(bf16[64,1024]{1,0:T(8,128)(2,1)} %shard_map.82, bf16[1024,1792]{0,1:T(8,128)(2,1)} %all-gather.2.cloned.1.call-done), kind=kOutput, calls=%fused_computation.75 | convolution fusion | flops 234881024 | bytes 4259840 | tf_op jit(solution)/shard_map/dot_general | solution.py:211
  153.3 3.3 %fusion.24 = f32[64,1792]{1,0:T(8,128)S(1)} fusion(bf16[64,1024]{1,0:T(8,128)(2,1)S(1)} %copy-done.1, bf16[1024,1792]{0,1:T(8,128)(2,1)} %collective-permute-done.12), kind=kOutput, calls=%fused_computation.76 | convolution fusion | flops 234881024 | bytes 4259840 | tf_op jit(solution)/shard_map/dot_general | solution.py:211
  157.9 2.5 %collective-permute-start.13 = (bf16[2,64,448]{2,1,0:T(8,128)(2,1)S(1)}, bf16[2,64,448]{2,1,0:T(8,128)(2,1)S(1)}, u32[]{:S(2)}, u32[]{:S(2)}) collective-permute-start(bf16[2,64,448]{2,1,0:T(8,128)(2,1)S(1)} %get-tuple-element.9), channel_id=1, source_target_pairs={{0,2},{2,0},{4,6},{6,4},{1,3},{3,1},{5,7},{7,5},{8,10},{10,8},{12,... | collective-permute-start | bytes 344072 | tf_op jit(solution)/shard_map/ppermute | solution.py:160
  160.3 3.0 %collective-permute-start.14 = (bf16[2,64,448]{2,1,0:T(8,128)(2,1)S(1)}, bf16[2,64,448]{2,1,0:T(8,128)(2,1)S(1)}, u32[]{:S(2)}, u32[]{:S(2)}) collective-permute-start(bf16[2,64,448]{2,1,0:T(8,128)(2,1)S(1)} %get-tuple-element.11), channel_id=1, source_target_pairs={{0,4},{2,6},{4,0},{6,2},{1,5},{3,7},{5,1},{7,3},{8,12},{10,14},{12... | collective-permute-start | bytes 344072 | tf_op jit(solution)/shard_map/ppermute | solution.py:160
  163.4 4.9 %collective-permute-start.15 = (bf16[2,64,448]{2,1,0:T(8,128)(2,1)S(1)}, bf16[2,64,448]{2,1,0:T(8,128)(2,1)S(1)}, u32[]{:S(2)}, u32[]{:S(2)}) collective-permute-start(bf16[2,64,448]{2,1,0:T(8,128)(2,1)S(1)} %get-tuple-element.10), channel_id=1, source_target_pairs={{0,6},{2,4},{4,2},{6,0},{1,7},{3,5},{5,3},{7,1},{8,14},{10,12},{12... | collective-permute-start | bytes 344072 | tf_op jit(solution)/shard_map/ppermute | solution.py:160
  169.0 2.8 %collective-permute-done.15 = bf16[2,64,448]{2,1,0:T(8,128)(2,1)S(1)} collective-permute-done((bf16[2,64,448]{2,1,0:T(8,128)(2,1)S(1)}, bf16[2,64,448]{2,1,0:T(8,128)(2,1)S(1)}, u32[]{:S(2)}, u32[]{:S(2)}) %collective-permute-start.15) | collective-permute-done | bytes 114720 | tf_op jit(solution)/shard_map/ppermute | solution.py:160
  171.9 5.4 %collective-permute-start.16 = (bf16[64,448]{1,0:T(8,128)(2,1)S(1)}, bf16[64,448]{1,0:T(8,128)(2,1)S(1)}, u32[]{:S(2)}, u32[]{:S(2)}) collective-permute-start(bf16[64,448]{1,0:T(8,128)(2,1)S(1)} %fusion.11), channel_id=1, source_target_pairs={{0,1},{1,0},{2,3},{3,2},{4,5},{5,4},{6,7},{7,6},{8,9},{9,8},{10,11... | collective-permute-start | bytes 172040 | tf_op jit(solution)/shard_map/ppermute | solution.py:166
  177.3 2.3 %collective-permute-done.16 = bf16[64,448]{1,0:T(8,128)(2,1)S(1)} collective-permute-done((bf16[64,448]{1,0:T(8,128)(2,1)S(1)}, bf16[64,448]{1,0:T(8,128)(2,1)S(1)}, u32[]{:S(2)}, u32[]{:S(2)}) %collective-permute-start.16) | collective-permute-done | bytes 57376 | tf_op jit(solution)/shard_map/ppermute | solution.py:166
  (75 shorter events, 27.9 us)
Async XLA Ops:
  6.5 128.9 %copy-start = (bf16[512,1024]{1,0:T(8,128)(2,1)S(1)}, bf16[512,1024]{1,0:T(8,128)(2,1)}, u32[]{:S(2)}) copy-start(bf16[512,1024]{1,0:T(8,128)(2,1)} %param.13) | copy-start | bytes 3145732
  6.5 118.7 %all-gather.2.cloned.1.call-start = ((), (), s32[]{:S(2)}) async-start(), calls=%async_computation | async-start | bytes 3899392 | tf_op jit(solution)/shard_map/all_gather | solution.py:206
  6.5 7.1 %collective-permute-start.11 = (bf16[1,56,1024]{2,1,0:T(8,128)(2,1)}, bf16[1,56,1024]{2,1,0:T(8,128)(2,1)S(1)}, u32[]{:S(2)}, u32[]{:S(2)}) collective-permute-start(bf16[1,56,1024]{2,1,0:T(8,128)(2,1)} %bitcast.93), channel_id=1, source_target_pairs={{0,16},{16,0},{1,17},{17,1},{2,18},{18,2},{3,19},{19,3},{4,20},{20... | collective-permute-start | bytes 344072 | tf_op jit(solution)/shard_map/ppermute | solution.py:104
  17.9 28.2 %collective-permute-start = (bf16[64,576]{1,0:T(8,128)(2,1)S(1)}, bf16[64,576]{1,0:T(8,128)(2,1)S(1)}, u32[]{:S(2)}, u32[]{:S(2)}) collective-permute-start(bf16[64,576]{1,0:T(8,128)(2,1)S(1)} %pad_maximum_fusion.2), channel_id=1, source_target_pairs={{0,64},{64,128},{128,192},{192,256},{256,320},{320,384},{384,448},... | collective-permute-start | bytes 221192 | tf_op jit(solution)/shard_map/ppermute | solution.py:135
  23.1 25.0 %collective-permute-start.1 = (bf16[64,576]{1,0:T(8,128)(2,1)S(1)}, bf16[64,576]{1,0:T(8,128)(2,1)S(1)}, u32[]{:S(2)}, u32[]{:S(2)}) collective-permute-start(bf16[64,576]{1,0:T(8,128)(2,1)S(1)} %pad_maximum_fusion.2), channel_id=1, source_target_pairs={{0,128},{64,192},{128,256},{192,320},{256,384},{320,448},{1,129},{... | collective-permute-start | bytes 221192 | tf_op jit(solution)/shard_map/ppermute | solution.py:135
  32.2 17.8 %collective-permute-start.2 = (bf16[64,576]{1,0:T(8,128)(2,1)S(1)}, bf16[64,576]{1,0:T(8,128)(2,1)S(1)}, u32[]{:S(2)}, u32[]{:S(2)}) collective-permute-start(bf16[64,576]{1,0:T(8,128)(2,1)S(1)} %pad_maximum_fusion.2), channel_id=1, source_target_pairs={{0,192},{64,256},{128,320},{192,384},{256,448},{1,193},{65,257},{1... | collective-permute-start | bytes 221192 | tf_op jit(solution)/shard_map/ppermute | solution.py:135
  40.4 10.3 %collective-permute-start.3 = (bf16[64,576]{1,0:T(8,128)(2,1)S(1)}, bf16[64,576]{1,0:T(8,128)(2,1)S(1)}, u32[]{:S(2)}, u32[]{:S(2)}) collective-permute-start(bf16[64,576]{1,0:T(8,128)(2,1)S(1)} %pad_maximum_fusion.2), channel_id=1, source_target_pairs={{0,256},{64,320},{128,384},{192,448},{1,257},{65,321},{129,385},{1... | collective-permute-start | bytes 221192 | tf_op jit(solution)/shard_map/ppermute | solution.py:135
  43.2 20.4 %collective-permute-start.4 = (bf16[64,576]{1,0:T(8,128)(2,1)S(1)}, bf16[64,576]{1,0:T(8,128)(2,1)S(1)}, u32[]{:S(2)}, u32[]{:S(2)}) collective-permute-start(bf16[64,576]{1,0:T(8,128)(2,1)S(1)} %pad_maximum_fusion.2), channel_id=1, source_target_pairs={{0,320},{64,384},{128,448},{1,321},{65,385},{129,449},{2,322},{66,... | collective-permute-start | bytes 221192 | tf_op jit(solution)/shard_map/ppermute | solution.py:135
  46.1 23.5 %collective-permute-start.5 = (bf16[64,576]{1,0:T(8,128)(2,1)S(1)}, bf16[64,576]{1,0:T(8,128)(2,1)S(1)}, u32[]{:S(2)}, u32[]{:S(2)}) collective-permute-start(bf16[64,576]{1,0:T(8,128)(2,1)S(1)} %pad_maximum_fusion.2), channel_id=1, source_target_pairs={{0,384},{64,448},{1,385},{65,449},{2,386},{66,450},{3,387},{67,451... | collective-permute-start | bytes 221192 | tf_op jit(solution)/shard_map/ppermute | solution.py:135
  48.1 26.2 %collective-permute-start.6 = (bf16[64,576]{1,0:T(8,128)(2,1)S(1)}, bf16[64,576]{1,0:T(8,128)(2,1)S(1)}, u32[]{:S(2)}, u32[]{:S(2)}) collective-permute-start(bf16[64,576]{1,0:T(8,128)(2,1)S(1)} %pad_maximum_fusion.2), channel_id=1, source_target_pairs={{0,448},{1,449},{2,450},{3,451},{4,452},{5,453},{6,454},{7,455},{8... | collective-permute-start | bytes 221192 | tf_op jit(solution)/shard_map/ppermute | solution.py:135
  50.7 84.1 %copy-start.2 = (bf16[64,512]{1,0:T(8,128)(2,1)S(1)}, bf16[64,512]{1,0:T(8,128)(2,1)}, u32[]{:S(2)}) copy-start(bf16[64,512]{1,0:T(8,128)(2,1)} %param.9) | copy-start | bytes 196612
  74.9 30.5 %collective-permute-start.7 = (bf16[8,64,576]{2,1,0:T(8,128)(2,1)}, bf16[8,64,576]{2,1,0:T(8,128)(2,1)S(1)}, u32[]{:S(2)}, u32[]{:S(2)}) collective-permute-start(bf16[8,64,576]{2,1,0:T(8,128)(2,1)} %get-tuple-element.18), channel_id=1, source_target_pairs={{0,32},{32,0},{1,33},{33,1},{2,34},{34,2},{3,35},{35,3},{4,36},{36... | collective-permute-start | bytes 1769480 | tf_op jit(solution)/shard_map/ppermute | solution.py:104
  76.8 51.2 %collective-permute-start.8 = (bf16[8,64,576]{2,1,0:T(8,128)(2,1)}, bf16[8,64,576]{2,1,0:T(8,128)(2,1)S(1)}, u32[]{:S(2)}, u32[]{:S(2)}) collective-permute-start(bf16[8,64,576]{2,1,0:T(8,128)(2,1)} %get-tuple-element.18), channel_id=1, source_target_pairs={{0,16},{16,0},{1,17},{17,1},{2,18},{18,2},{3,19},{19,3},{4,20},{20... | collective-permute-start | bytes 1769480 | tf_op jit(solution)/shard_map/ppermute | solution.py:106
  105.4 23.5 %collective-permute-start.9 = (bf16[8,64,576]{2,1,0:T(8,128)(2,1)S(1)}, bf16[8,64,576]{2,1,0:T(8,128)(2,1)S(1)}, u32[]{:S(2)}, u32[]{:S(2)}) collective-permute-start(bf16[8,64,576]{2,1,0:T(8,128)(2,1)S(1)} %collective-permute-done.7), channel_id=1, source_target_pairs={{0,17},{1,16},{16,1},{17,0},{2,19},{3,18},{18,3},{19,2},{4,21},{5,... | collective-permute-start | bytes 1769480 | tf_op jit(solution)/shard_map/ppermute | solution.py:107
  125.2 28.1 %collective-permute-start.12 = (bf16[1024,1792]{0,1:T(8,128)(2,1)}, bf16[1024,1792]{0,1:T(8,128)(2,1)}, u32[]{:S(2)}, u32[]{:S(2)}) collective-permute-start(bf16[1024,1792]{0,1:T(8,128)(2,1)} %all-gather.2.cloned.1.call-done), channel_id=1, source_target_pairs={{0,8},{8,0},{1,9},{9,1},{2,10},{10,2},{3,11},{11,3},{4,12},{12,4},... | collective-permute-start | bytes 11010056 | tf_op jit(solution)/shard_map/ppermute | solution.py:207
  128.0 7.5 %copy-start.3 = (bf16[64,1024]{1,0:T(8,128)(2,1)S(1)}, bf16[64,1024]{1,0:T(8,128)(2,1)}, u32[]{:S(2)}) copy-start(bf16[64,1024]{1,0:T(8,128)(2,1)} %param.8) | copy-start | bytes 393220
  129.9 7.7 %collective-permute-start.10 = (bf16[32,64,576]{2,1,0:T(8,128)(2,1)}, bf16[32,64,576]{2,1,0:T(8,128)(2,1)}, u32[]{:S(2)}, u32[]{:S(2)}) collective-permute-start(bf16[32,64,576]{2,1,0:T(8,128)(2,1)} %constant_dynamic-update-slice_fusion), channel_id=1, source_target_pairs={{0,8},{8,0},{1,9},{9,1},{2,10},{10,2},{3,11},{11,3},{4,12},{12,4},... | collective-permute-start | bytes 7077896 | tf_op jit(solution)/shard_map/ppermute | solution.py:104
  149.6 3.7 %copy-start.1 = (bf16[64,1024]{1,0:T(8,128)(2,1)S(1)}, bf16[64,1024]{1,0:T(8,128)(2,1)}, u32[]{:S(2)}) copy-start(bf16[64,1024]{1,0:T(8,128)(2,1)} %shard_map.82) | copy-start | bytes 393220
  157.9 10.5 %collective-permute-start.13 = (bf16[2,64,448]{2,1,0:T(8,128)(2,1)S(1)}, bf16[2,64,448]{2,1,0:T(8,128)(2,1)S(1)}, u32[]{:S(2)}, u32[]{:S(2)}) collective-permute-start(bf16[2,64,448]{2,1,0:T(8,128)(2,1)S(1)} %get-tuple-element.9), channel_id=1, source_target_pairs={{0,2},{2,0},{4,6},{6,4},{1,3},{3,1},{5,7},{7,5},{8,10},{10,8},{12,... | collective-permute-start | bytes 344072 | tf_op jit(solution)/shard_map/ppermute | solution.py:160
  160.3 8.7 %collective-permute-start.14 = (bf16[2,64,448]{2,1,0:T(8,128)(2,1)S(1)}, bf16[2,64,448]{2,1,0:T(8,128)(2,1)S(1)}, u32[]{:S(2)}, u32[]{:S(2)}) collective-permute-start(bf16[2,64,448]{2,1,0:T(8,128)(2,1)S(1)} %get-tuple-element.11), channel_id=1, source_target_pairs={{0,4},{2,6},{4,0},{6,2},{1,5},{3,7},{5,1},{7,3},{8,12},{10,14},{12... | collective-permute-start | bytes 344072 | tf_op jit(solution)/shard_map/ppermute | solution.py:160
  163.4 8.4 %collective-permute-start.15 = (bf16[2,64,448]{2,1,0:T(8,128)(2,1)S(1)}, bf16[2,64,448]{2,1,0:T(8,128)(2,1)S(1)}, u32[]{:S(2)}, u32[]{:S(2)}) collective-permute-start(bf16[2,64,448]{2,1,0:T(8,128)(2,1)S(1)} %get-tuple-element.10), channel_id=1, source_target_pairs={{0,6},{2,4},{4,2},{6,0},{1,7},{3,5},{5,3},{7,1},{8,14},{10,12},{12... | collective-permute-start | bytes 344072 | tf_op jit(solution)/shard_map/ppermute | solution.py:160
  171.9 7.7 %collective-permute-start.16 = (bf16[64,448]{1,0:T(8,128)(2,1)S(1)}, bf16[64,448]{1,0:T(8,128)(2,1)S(1)}, u32[]{:S(2)}, u32[]{:S(2)}) collective-permute-start(bf16[64,448]{1,0:T(8,128)(2,1)S(1)} %fusion.11), channel_id=1, source_target_pairs={{0,1},{1,0},{2,3},{3,2},{4,5},{5,4},{6,7},{7,6},{8,9},{9,8},{10,11... | collective-permute-start | bytes 172040 | tf_op jit(solution)/shard_map/ppermute | solution.py:166
Sparse Core Ops, SparseCore 0:
  15.4 109.7 all-gather.1

commit v15 on v14

--- a/solution.py
+++ b/solution.py
@@ -201,8 +201,8 @@
     first_token = lax.axis_index(CTX) * token_count
     query_index = jnp.tile(first_token + jnp.arange(token_count, dtype=jnp.int32), head_count)
     head_out = attend(query_rows, query_index, halves, value_up)
-    pair = gather_in_order(out_proj.T, (("yl", 2),), False)
-    pair = pair.reshape(2, out_proj.shape[1], -1).transpose(2, 0, 1).reshape(out_proj.shape[0], -1)
+    partner = lax.ppermute(out_proj, "yl", [(0, 1), (1, 0)])
+    pair = jnp.concatenate([out_proj, partner], axis=1)
     own = lax.all_gather(pair, ("zh", "zl"), axis=1, tiled=True)
     swapped = lax.ppermute(own, "co", [(0, 1), (1, 0)])
     upper = lax.axis_index("co") == 1
@@ -220,7 +220,9 @@
         mine,
     )
     width = out_proj.shape[1]
-    mine = mine.reshape(token_count, 2, -1, width).transpose(0, 2, 1, 3)
+    mine = mine.reshape(token_count, 2, -1, 2, width)
+    mine = jnp.where(lax.axis_index("yl") == 1, mine[:, :, :, ::-1, :], mine)
+    mine = mine.transpose(0, 2, 3, 1, 4)
     return mine.reshape(token_count, -1).astype(jnp.bfloat16)
 
 

time: 191 us -> 192 us (level)
    ppermute x3 -> x2, starting transfers between devices: 7.91 us -> 4.3 us  [exchange(): return lax.ppermute(acc, axis, pairs)]
    ppermute x0 -> x1, starting transfers between devices: none -> 3.6 us  [body(): partner = lax.ppermute(out_proj, 'yl', [(0, 1), (1, 0)])]
    ppermute x0 -> x1, waiting for transfers between devices: none -> 3.5 us  [body(): partner = lax.ppermute(out_proj, 'yl', [(0, 1), (1, 0)])]
    ppermute x3 -> x2, waiting for transfers between devices: 29.2 us -> 25.7 us  [exchange(): return lax.ppermute(acc, axis, pairs)]
where the time goes in v15:
time: 192 us; the launch traced here: 188 us
  waiting for transfers between devices  71.1 us (37%)
  starting transfers between devices  63.4 us (33%)
  local copies, waits for them, and re-layouts  14.2 us (7%)
  between operations  13.8 us (7%)
  Pallas kernels  12 us (6%)
  matrix products  7.11 us (4%)
  other arithmetic  7.02 us (4%)
    ppermute x7, starting transfers between devices, gather_earlier_keys(): lax.ppermute(local, 'zh', [(i, i + shift) for i in range(cubes - shift)])  29.2 us
    ppermute x2, waiting for transfers between devices, exchange(): return lax.ppermute(acc, axis, pairs)  25.7 us
    ppermute x7, waiting for transfers between devices, gather_earlier_keys(): lax.ppermute(local, 'zh', [(i, i + shift) for i in range(cubes - shift)])  21.4 us
    all_gather x1, waiting for transfers between devices, body(): own = lax.all_gather(pair, ('zh', 'zl'), axis=1, tiled=True)  14.7 us
    pallas_call x1, Pallas kernels, attend(): pl.pallas_call(attention_kernel, out_shape=jax.ShapeDtypeStruct((tokens,...  12 us
    ppermute x3, starting transfers between devices, scatter_sum(): lax.ppermute(sent, 'x', [(i, i ^ shift) for i in range(columns)])  10.4 us
    unnamed x17, local copies, waits for them, and re-layouts  6.76 us
    dot_general x2, matrix products, body(): jnp.dot(head_out, half, preferred_element_type=jnp.float32)  6.63 us
  transfers between devices with their start and end apart: 18, of which 10 were waited for; matrix products, arithmetic and copies ran while one was open for 11% of the time, Pallas kernels for 6%

profile of v15, /device:TPU:6, one launch (start us, length us, event | category | flops | bytes accessed | tf_op | source)
XLA Modules:
  0.0 188.5 jit_solution(14336062081708549184)
XLA Ops:
  6.5 3.6 %collective-permute-start.11 = (bf16[1024,56]{0,1:T(8,128)(2,1)}, bf16[1024,56]{0,1:T(8,128)(2,1)S(1)}, u32[]{:S(2)}, u32[]{:S(2)}) collective-permute-start(bf16[1024,56]{0,1:T(8,128)(2,1)} %param.15), channel_id=1, source_target_pairs={{0,16},{16,0},{1,17},{17,1},{2,18},{18,2},{3,19},{19,3},{4,20},{20... | collective-permute-start | bytes 344072 | tf_op jit(solution)/shard_map/ppermute | solution.py:204
  10.2 3.5 %collective-permute-done.11 = bf16[1024,56]{0,1:T(8,128)(2,1)S(1)} collective-permute-done((bf16[1024,56]{0,1:T(8,128)(2,1)}, bf16[1024,56]{0,1:T(8,128)(2,1)S(1)}, u32[]{:S(2)}, u32[]{:S(2)}) %collective-permute-start.11) | collective-permute-done | bytes 114720 | tf_op jit(solution)/shard_map/ppermute | solution.py:204
  17.9 5.2 %collective-permute-start = (bf16[64,576]{1,0:T(8,128)(2,1)S(1)}, bf16[64,576]{1,0:T(8,128)(2,1)S(1)}, u32[]{:S(2)}, u32[]{:S(2)}) collective-permute-start(bf16[64,576]{1,0:T(8,128)(2,1)S(1)} %pad_maximum_fusion.2), channel_id=1, source_target_pairs={{0,64},{64,128},{128,192},{192,256},{256,320},{320,384},{384,448},... | collective-permute-start | bytes 221192 | tf_op jit(solution)/shard_map/ppermute | solution.py:135
  23.1 9.1 %collective-permute-start.1 = (bf16[64,576]{1,0:T(8,128)(2,1)S(1)}, bf16[64,576]{1,0:T(8,128)(2,1)S(1)}, u32[]{:S(2)}, u32[]{:S(2)}) collective-permute-start(bf16[64,576]{1,0:T(8,128)(2,1)S(1)} %pad_maximum_fusion.2), channel_id=1, source_target_pairs={{0,128},{64,192},{128,256},{192,320},{256,384},{320,448},{1,129},{... | collective-permute-start | bytes 221192 | tf_op jit(solution)/shard_map/ppermute | solution.py:135
  32.2 8.2 %collective-permute-start.2 = (bf16[64,576]{1,0:T(8,128)(2,1)S(1)}, bf16[64,576]{1,0:T(8,128)(2,1)S(1)}, u32[]{:S(2)}, u32[]{:S(2)}) collective-permute-start(bf16[64,576]{1,0:T(8,128)(2,1)S(1)} %pad_maximum_fusion.2), channel_id=1, source_target_pairs={{0,192},{64,256},{128,320},{192,384},{256,448},{1,193},{65,257},{1... | collective-permute-start | bytes 221192 | tf_op jit(solution)/shard_map/ppermute | solution.py:135
  40.4 2.8 %collective-permute-start.3 = (bf16[64,576]{1,0:T(8,128)(2,1)S(1)}, bf16[64,576]{1,0:T(8,128)(2,1)S(1)}, u32[]{:S(2)}, u32[]{:S(2)}) collective-permute-start(bf16[64,576]{1,0:T(8,128)(2,1)S(1)} %pad_maximum_fusion.2), channel_id=1, source_target_pairs={{0,256},{64,320},{128,384},{192,448},{1,257},{65,321},{129,385},{1... | collective-permute-start | bytes 221192 | tf_op jit(solution)/shard_map/ppermute | solution.py:135
  51.4 12.3 %collective-permute-done.4 = bf16[64,576]{1,0:T(8,128)(2,1)S(1)} collective-permute-done((bf16[64,576]{1,0:T(8,128)(2,1)S(1)}, bf16[64,576]{1,0:T(8,128)(2,1)S(1)}, u32[]{:S(2)}, u32[]{:S(2)}) %collective-permute-start.4) | collective-permute-done | bytes 73760 | tf_op jit(solution)/shard_map/ppermute | solution.py:135
  64.4 5.2 %collective-permute-done.5 = bf16[64,576]{1,0:T(8,128)(2,1)S(1)} collective-permute-done((bf16[64,576]{1,0:T(8,128)(2,1)S(1)}, bf16[64,576]{1,0:T(8,128)(2,1)S(1)}, u32[]{:S(2)}, u32[]{:S(2)}) %collective-permute-start.5) | collective-permute-done | bytes 73760 | tf_op jit(solution)/shard_map/ppermute | solution.py:135
  70.3 3.9 %collective-permute-done.6 = bf16[64,576]{1,0:T(8,128)(2,1)S(1)} collective-permute-done((bf16[64,576]{1,0:T(8,128)(2,1)S(1)}, bf16[64,576]{1,0:T(8,128)(2,1)S(1)}, u32[]{:S(2)}, u32[]{:S(2)}) %collective-permute-start.6) | collective-permute-done | bytes 73760 | tf_op jit(solution)/shard_map/ppermute | solution.py:135
  76.8 3.5 %collective-permute-start.8 = (bf16[8,64,576]{2,1,0:T(8,128)(2,1)}, bf16[8,64,576]{2,1,0:T(8,128)(2,1)S(1)}, u32[]{:S(2)}, u32[]{:S(2)}) collective-permute-start(bf16[8,64,576]{2,1,0:T(8,128)(2,1)} %get-tuple-element.16), channel_id=1, source_target_pairs={{0,16},{16,0},{1,17},{17,1},{2,18},{18,2},{3,19},{19,3},{4,20},{20... | collective-permute-start | bytes 1769480 | tf_op jit(solution)/shard_map/ppermute | solution.py:106
  80.3 25.1 %collective-permute-done.7 = bf16[8,64,576]{2,1,0:T(8,128)(2,1)S(1)} collective-permute-done((bf16[8,64,576]{2,1,0:T(8,128)(2,1)}, bf16[8,64,576]{2,1,0:T(8,128)(2,1)S(1)}, u32[]{:S(2)}, u32[]{:S(2)}) %collective-permute-start.7) | collective-permute-done | bytes 589856 | tf_op jit(solution)/shard_map/ppermute | solution.py:104
  105.4 5.1 %collective-permute-start.9 = (bf16[8,64,576]{2,1,0:T(8,128)(2,1)S(1)}, bf16[8,64,576]{2,1,0:T(8,128)(2,1)S(1)}, u32[]{:S(2)}, u32[]{:S(2)}) collective-permute-start(bf16[8,64,576]{2,1,0:T(8,128)(2,1)S(1)} %collective-permute-done.7), channel_id=1, source_target_pairs={{0,17},{1,16},{16,1},{17,0},{2,19},{3,18},{18,3},{19,2},{4,21},{5,... | collective-permute-start | bytes 1769480 | tf_op jit(solution)/shard_map/ppermute | solution.py:107
  110.5 14.7 %all-gather.2.cloned.1.call-done = bf16[1024,1792]{0,1:T(8,128)(2,1)} async-done(((bf16[1024,112]{0,1:T(8,128)(2,1)}), bf16[1024,1792]{0,1:T(8,128)(2,1)}) %all-gather.2.cloned.1.call-update) | async-done | bytes 3670032 | tf_op jit(solution)/shard_map/all_gather | solution.py:206
  125.2 1.9 %collective-permute-start.12 = (bf16[1024,1792]{0,1:T(8,128)(2,1)}, bf16[1024,1792]{0,1:T(8,128)(2,1)}, u32[]{:S(2)}, u32[]{:S(2)}) collective-permute-start(bf16[1024,1792]{0,1:T(8,128)(2,1)} %all-gather.2.cloned.1.call-done), channel_id=1, source_target_pairs={{0,8},{8,0},{1,9},{9,1},{2,10},{10,2},{3,11},{11,3},{4,12},{12,4},... | collective-permute-start | bytes 11010056 | tf_op jit(solution)/shard_map/ppermute | solution.py:207
  129.8 2.4 %collective-permute-start.10 = (bf16[32,64,576]{2,1,0:T(8,128)(2,1)}, bf16[32,64,576]{2,1,0:T(8,128)(2,1)}, u32[]{:S(2)}, u32[]{:S(2)}) collective-permute-start(bf16[32,64,576]{2,1,0:T(8,128)(2,1)} %constant_dynamic-update-slice_fusion), channel_id=1, source_target_pairs={{0,8},{8,0},{1,9},{9,1},{2,10},{10,2},{3,11},{11,3},{4,12},{12,4},... | collective-permute-start | bytes 7077896 | tf_op jit(solution)/shard_map/ppermute | solution.py:104
  137.6 12.0 %shard_map.82 = bf16[64,1024]{1,0:T(8,128)(2,1)} custom-call(bf16[512,576]{1,0:T(8,128)(2,1)} %bitcast.77, s32[512,1]{1,0:T(8,128)} %reshape_tile.4.qi_ref, bf16[2048,576]{1,0:T(8,128)(2,1)} %bitcast.78, s32[1,2048]{1,0:T(1,128)} %add.129.ia_ref, bf16[2048,576]{1,0:T(8,128)(2,1)} %bitcast.15.kb_ref, s32[1,2048]{1,0:T(1,128)} %add.133.ib_ref, ...), custom_call_target="tpu_custom_call" | custom-call | flops 4563402752 | bytes 5832704 | tf_op jit(solution)/shard_map/pallas_call | solution.py:94
  149.5 3.4 %fusion.23 = f32[64,1792]{1,0:T(8,128)S(1)} fusion(bf16[64,1024]{1,0:T(8,128)(2,1)} %shard_map.82, bf16[1024,1792]{0,1:T(8,128)(2,1)} %all-gather.2.cloned.1.call-done), kind=kOutput, calls=%fused_computation.74 | convolution fusion | flops 234881024 | bytes 4259840 | tf_op jit(solution)/shard_map/dot_general | solution.py:211
  153.3 3.3 %fusion.24 = f32[64,1792]{1,0:T(8,128)S(1)} fusion(bf16[64,1024]{1,0:T(8,128)(2,1)S(1)} %copy-done.1, bf16[1024,1792]{0,1:T(8,128)(2,1)} %collective-permute-done.12), kind=kOutput, calls=%fused_computation.75 | convolution fusion | flops 234881024 | bytes 4259840 | tf_op jit(solution)/shard_map/dot_general | solution.py:211
  157.8 2.5 %collective-permute-start.13 = (bf16[2,64,448]{2,1,0:T(8,128)(2,1)S(1)}, bf16[2,64,448]{2,1,0:T(8,128)(2,1)S(1)}, u32[]{:S(2)}, u32[]{:S(2)}) collective-permute-start(bf16[2,64,448]{2,1,0:T(8,128)(2,1)S(1)} %get-tuple-element.9), channel_id=1, source_target_pairs={{0,2},{2,0},{4,6},{6,4},{1,3},{3,1},{5,7},{7,5},{8,10},{10,8},{12,... | collective-permute-start | bytes 344072 | tf_op jit(solution)/shard_map/ppermute | solution.py:160
  160.3 2.8 %collective-permute-start.14 = (bf16[2,64,448]{2,1,0:T(8,128)(2,1)S(1)}, bf16[2,64,448]{2,1,0:T(8,128)(2,1)S(1)}, u32[]{:S(2)}, u32[]{:S(2)}) collective-permute-start(bf16[2,64,448]{2,1,0:T(8,128)(2,1)S(1)} %get-tuple-element.11), channel_id=1, source_target_pairs={{0,4},{2,6},{4,0},{6,2},{1,5},{3,7},{5,1},{7,3},{8,12},{10,14},{12... | collective-permute-start | bytes 344072 | tf_op jit(solution)/shard_map/ppermute | solution.py:160
  163.1 5.1 %collective-permute-start.15 = (bf16[2,64,448]{2,1,0:T(8,128)(2,1)S(1)}, bf16[2,64,448]{2,1,0:T(8,128)(2,1)S(1)}, u32[]{:S(2)}, u32[]{:S(2)}) collective-permute-start(bf16[2,64,448]{2,1,0:T(8,128)(2,1)S(1)} %get-tuple-element.10), channel_id=1, source_target_pairs={{0,6},{2,4},{4,2},{6,0},{1,7},{3,5},{5,3},{7,1},{8,14},{10,12},{12... | collective-permute-start | bytes 344072 | tf_op jit(solution)/shard_map/ppermute | solution.py:160
  169.0 2.8 %collective-permute-done.15 = bf16[2,64,448]{2,1,0:T(8,128)(2,1)S(1)} collective-permute-done((bf16[2,64,448]{2,1,0:T(8,128)(2,1)S(1)}, bf16[2,64,448]{2,1,0:T(8,128)(2,1)S(1)}, u32[]{:S(2)}, u32[]{:S(2)}) %collective-permute-start.15) | collective-permute-done | bytes 114720 | tf_op jit(solution)/shard_map/ppermute | solution.py:160
  171.9 5.4 %collective-permute-start.16 = (bf16[64,448]{1,0:T(8,128)(2,1)S(1)}, bf16[64,448]{1,0:T(8,128)(2,1)S(1)}, u32[]{:S(2)}, u32[]{:S(2)}) collective-permute-start(bf16[64,448]{1,0:T(8,128)(2,1)S(1)} %fusion.11), channel_id=1, source_target_pairs={{0,1},{1,0},{2,3},{3,2},{4,5},{5,4},{6,7},{7,6},{8,9},{9,8},{10,11... | collective-permute-start | bytes 172040 | tf_op jit(solution)/shard_map/ppermute | solution.py:166
  177.3 2.3 %collective-permute-done.16 = bf16[64,448]{1,0:T(8,128)(2,1)S(1)} collective-permute-done((bf16[64,448]{1,0:T(8,128)(2,1)S(1)}, bf16[64,448]{1,0:T(8,128)(2,1)S(1)}, u32[]{:S(2)}, u32[]{:S(2)}) %collective-permute-start.16) | collective-permute-done | bytes 57376 | tf_op jit(solution)/shard_map/ppermute | solution.py:166
  (76 shorter events, 28.8 us)
Async XLA Ops:
  6.5 128.9 %copy-start = (bf16[512,1024]{1,0:T(8,128)(2,1)S(1)}, bf16[512,1024]{1,0:T(8,128)(2,1)}, u32[]{:S(2)}) copy-start(bf16[512,1024]{1,0:T(8,128)(2,1)} %param.13) | copy-start | bytes 3145732
  6.5 118.6 %all-gather.2.cloned.1.call-start = ((), (), s32[]{:S(2)}) async-start(), calls=%async_computation | async-start | bytes 3899392 | tf_op jit(solution)/shard_map/all_gather | solution.py:206
  6.5 7.1 %collective-permute-start.11 = (bf16[1024,56]{0,1:T(8,128)(2,1)}, bf16[1024,56]{0,1:T(8,128)(2,1)S(1)}, u32[]{:S(2)}, u32[]{:S(2)}) collective-permute-start(bf16[1024,56]{0,1:T(8,128)(2,1)} %param.15), channel_id=1, source_target_pairs={{0,16},{16,0},{1,17},{17,1},{2,18},{18,2},{3,19},{19,3},{4,20},{20... | collective-permute-start | bytes 344072 | tf_op jit(solution)/shard_map/ppermute | solution.py:204
  17.9 28.2 %collective-permute-start = (bf16[64,576]{1,0:T(8,128)(2,1)S(1)}, bf16[64,576]{1,0:T(8,128)(2,1)S(1)}, u32[]{:S(2)}, u32[]{:S(2)}) collective-permute-start(bf16[64,576]{1,0:T(8,128)(2,1)S(1)} %pad_maximum_fusion.2), channel_id=1, source_target_pairs={{0,64},{64,128},{128,192},{192,256},{256,320},{320,384},{384,448},... | collective-permute-start | bytes 221192 | tf_op jit(solution)/shard_map/ppermute | solution.py:135
  23.1 25.0 %collective-permute-start.1 = (bf16[64,576]{1,0:T(8,128)(2,1)S(1)}, bf16[64,576]{1,0:T(8,128)(2,1)S(1)}, u32[]{:S(2)}, u32[]{:S(2)}) collective-permute-start(bf16[64,576]{1,0:T(8,128)(2,1)S(1)} %pad_maximum_fusion.2), channel_id=1, source_target_pairs={{0,128},{64,192},{128,256},{192,320},{256,384},{320,448},{1,129},{... | collective-permute-start | bytes 221192 | tf_op jit(solution)/shard_map/ppermute | solution.py:135
  32.2 17.8 %collective-permute-start.2 = (bf16[64,576]{1,0:T(8,128)(2,1)S(1)}, bf16[64,576]{1,0:T(8,128)(2,1)S(1)}, u32[]{:S(2)}, u32[]{:S(2)}) collective-permute-start(bf16[64,576]{1,0:T(8,128)(2,1)S(1)} %pad_maximum_fusion.2), channel_id=1, source_target_pairs={{0,192},{64,256},{128,320},{192,384},{256,448},{1,193},{65,257},{1... | collective-permute-start | bytes 221192 | tf_op jit(solution)/shard_map/ppermute | solution.py:135
  40.4 10.3 %collective-permute-start.3 = (bf16[64,576]{1,0:T(8,128)(2,1)S(1)}, bf16[64,576]{1,0:T(8,128)(2,1)S(1)}, u32[]{:S(2)}, u32[]{:S(2)}) collective-permute-start(bf16[64,576]{1,0:T(8,128)(2,1)S(1)} %pad_maximum_fusion.2), channel_id=1, source_target_pairs={{0,256},{64,320},{128,384},{192,448},{1,257},{65,321},{129,385},{1... | collective-permute-start | bytes 221192 | tf_op jit(solution)/shard_map/ppermute | solution.py:135
  43.2 20.4 %collective-permute-start.4 = (bf16[64,576]{1,0:T(8,128)(2,1)S(1)}, bf16[64,576]{1,0:T(8,128)(2,1)S(1)}, u32[]{:S(2)}, u32[]{:S(2)}) collective-permute-start(bf16[64,576]{1,0:T(8,128)(2,1)S(1)} %pad_maximum_fusion.2), channel_id=1, source_target_pairs={{0,320},{64,384},{128,448},{1,321},{65,385},{129,449},{2,322},{66,... | collective-permute-start | bytes 221192 | tf_op jit(solution)/shard_map/ppermute | solution.py:135
  46.1 23.5 %collective-permute-start.5 = (bf16[64,576]{1,0:T(8,128)(2,1)S(1)}, bf16[64,576]{1,0:T(8,128)(2,1)S(1)}, u32[]{:S(2)}, u32[]{:S(2)}) collective-permute-start(bf16[64,576]{1,0:T(8,128)(2,1)S(1)} %pad_maximum_fusion.2), channel_id=1, source_target_pairs={{0,384},{64,448},{1,385},{65,449},{2,386},{66,450},{3,387},{67,451... | collective-permute-start | bytes 221192 | tf_op jit(solution)/shard_map/ppermute | solution.py:135
  48.0 26.2 %collective-permute-start.6 = (bf16[64,576]{1,0:T(8,128)(2,1)S(1)}, bf16[64,576]{1,0:T(8,128)(2,1)S(1)}, u32[]{:S(2)}, u32[]{:S(2)}) collective-permute-start(bf16[64,576]{1,0:T(8,128)(2,1)S(1)} %pad_maximum_fusion.2), channel_id=1, source_target_pairs={{0,448},{1,449},{2,450},{3,451},{4,452},{5,453},{6,454},{7,455},{8... | collective-permute-start | bytes 221192 | tf_op jit(solution)/shard_map/ppermute | solution.py:135
  50.7 84.1 %copy-start.2 = (bf16[64,512]{1,0:T(8,128)(2,1)S(1)}, bf16[64,512]{1,0:T(8,128)(2,1)}, u32[]{:S(2)}) copy-start(bf16[64,512]{1,0:T(8,128)(2,1)} %param.9) | copy-start | bytes 196612
  74.9 30.5 %collective-permute-start.7 = (bf16[8,64,576]{2,1,0:T(8,128)(2,1)}, bf16[8,64,576]{2,1,0:T(8,128)(2,1)S(1)}, u32[]{:S(2)}, u32[]{:S(2)}) collective-permute-start(bf16[8,64,576]{2,1,0:T(8,128)(2,1)} %get-tuple-element.16), channel_id=1, source_target_pairs={{0,32},{32,0},{1,33},{33,1},{2,34},{34,2},{3,35},{35,3},{4,36},{36... | collective-permute-start | bytes 1769480 | tf_op jit(solution)/shard_map/ppermute | solution.py:104
  76.8 51.2 %collective-permute-start.8 = (bf16[8,64,576]{2,1,0:T(8,128)(2,1)}, bf16[8,64,576]{2,1,0:T(8,128)(2,1)S(1)}, u32[]{:S(2)}, u32[]{:S(2)}) collective-permute-start(bf16[8,64,576]{2,1,0:T(8,128)(2,1)} %get-tuple-element.16), channel_id=1, source_target_pairs={{0,16},{16,0},{1,17},{17,1},{2,18},{18,2},{3,19},{19,3},{4,20},{20... | collective-permute-start | bytes 1769480 | tf_op jit(solution)/shard_map/ppermute | solution.py:106
  105.4 23.5 %collective-permute-start.9 = (bf16[8,64,576]{2,1,0:T(8,128)(2,1)S(1)}, bf16[8,64,576]{2,1,0:T(8,128)(2,1)S(1)}, u32[]{:S(2)}, u32[]{:S(2)}) collective-permute-start(bf16[8,64,576]{2,1,0:T(8,128)(2,1)S(1)} %collective-permute-done.7), channel_id=1, source_target_pairs={{0,17},{1,16},{16,1},{17,0},{2,19},{3,18},{18,3},{19,2},{4,21},{5,... | collective-permute-start | bytes 1769480 | tf_op jit(solution)/shard_map/ppermute | solution.py:107
  125.2 28.1 %collective-permute-start.12 = (bf16[1024,1792]{0,1:T(8,128)(2,1)}, bf16[1024,1792]{0,1:T(8,128)(2,1)}, u32[]{:S(2)}, u32[]{:S(2)}) collective-permute-start(bf16[1024,1792]{0,1:T(8,128)(2,1)} %all-gather.2.cloned.1.call-done), channel_id=1, source_target_pairs={{0,8},{8,0},{1,9},{9,1},{2,10},{10,2},{3,11},{11,3},{4,12},{12,4},... | collective-permute-start | bytes 11010056 | tf_op jit(solution)/shard_map/ppermute | solution.py:207
  128.0 7.5 %copy-start.3 = (bf16[64,1024]{1,0:T(8,128)(2,1)S(1)}, bf16[64,1024]{1,0:T(8,128)(2,1)}, u32[]{:S(2)}) copy-start(bf16[64,1024]{1,0:T(8,128)(2,1)} %param.8) | copy-start | bytes 393220
  129.8 7.7 %collective-permute-start.10 = (bf16[32,64,576]{2,1,0:T(8,128)(2,1)}, bf16[32,64,576]{2,1,0:T(8,128)(2,1)}, u32[]{:S(2)}, u32[]{:S(2)}) collective-permute-start(bf16[32,64,576]{2,1,0:T(8,128)(2,1)} %constant_dynamic-update-slice_fusion), channel_id=1, source_target_pairs={{0,8},{8,0},{1,9},{9,1},{2,10},{10,2},{3,11},{11,3},{4,12},{12,4},... | collective-permute-start | bytes 7077896 | tf_op jit(solution)/shard_map/ppermute | solution.py:104
  149.5 3.7 %copy-start.1 = (bf16[64,1024]{1,0:T(8,128)(2,1)S(1)}, bf16[64,1024]{1,0:T(8,128)(2,1)}, u32[]{:S(2)}) copy-start(bf16[64,1024]{1,0:T(8,128)(2,1)} %shard_map.82) | copy-start | bytes 393220
  157.8 10.5 %collective-permute-start.13 = (bf16[2,64,448]{2,1,0:T(8,128)(2,1)S(1)}, bf16[2,64,448]{2,1,0:T(8,128)(2,1)S(1)}, u32[]{:S(2)}, u32[]{:S(2)}) collective-permute-start(bf16[2,64,448]{2,1,0:T(8,128)(2,1)S(1)} %get-tuple-element.9), channel_id=1, source_target_pairs={{0,2},{2,0},{4,6},{6,4},{1,3},{3,1},{5,7},{7,5},{8,10},{10,8},{12,... | collective-permute-start | bytes 344072 | tf_op jit(solution)/shard_map/ppermute | solution.py:160
  160.3 8.7 %collective-permute-start.14 = (bf16[2,64,448]{2,1,0:T(8,128)(2,1)S(1)}, bf16[2,64,448]{2,1,0:T(8,128)(2,1)S(1)}, u32[]{:S(2)}, u32[]{:S(2)}) collective-permute-start(bf16[2,64,448]{2,1,0:T(8,128)(2,1)S(1)} %get-tuple-element.11), channel_id=1, source_target_pairs={{0,4},{2,6},{4,0},{6,2},{1,5},{3,7},{5,1},{7,3},{8,12},{10,14},{12... | collective-permute-start | bytes 344072 | tf_op jit(solution)/shard_map/ppermute | solution.py:160
  163.1 8.6 %collective-permute-start.15 = (bf16[2,64,448]{2,1,0:T(8,128)(2,1)S(1)}, bf16[2,64,448]{2,1,0:T(8,128)(2,1)S(1)}, u32[]{:S(2)}, u32[]{:S(2)}) collective-permute-start(bf16[2,64,448]{2,1,0:T(8,128)(2,1)S(1)} %get-tuple-element.10), channel_id=1, source_target_pairs={{0,6},{2,4},{4,2},{6,0},{1,7},{3,5},{5,3},{7,1},{8,14},{10,12},{12... | collective-permute-start | bytes 344072 | tf_op jit(solution)/shard_map/ppermute | solution.py:160
  171.9 7.7 %collective-permute-start.16 = (bf16[64,448]{1,0:T(8,128)(2,1)S(1)}, bf16[64,448]{1,0:T(8,128)(2,1)S(1)}, u32[]{:S(2)}, u32[]{:S(2)}) collective-permute-start(bf16[64,448]{1,0:T(8,128)(2,1)S(1)} %fusion.11), channel_id=1, source_target_pairs={{0,1},{1,0},{2,3},{3,2},{4,5},{5,4},{6,7},{7,6},{8,9},{9,8},{10,11... | collective-permute-start | bytes 172040 | tf_op jit(solution)/shard_map/ppermute | solution.py:166
Sparse Core Ops, SparseCore 0:
  15.4 109.7 all-gather.1

commit v16 on v14

--- a/solution.py
+++ b/solution.py
@@ -204,6 +204,7 @@
     pair = gather_in_order(out_proj.T, (("yl", 2),), False)
     pair = pair.reshape(2, out_proj.shape[1], -1).transpose(2, 0, 1).reshape(out_proj.shape[0], -1)
     own = lax.all_gather(pair, ("zh", "zl"), axis=1, tiled=True)
+    own, _ = lax.optimization_barrier((own, halves[1][0]))
     swapped = lax.ppermute(own, "co", [(0, 1), (1, 0)])
     upper = lax.axis_index("co") == 1
     groups = lax.axis_size(HEAD)

time: 191 us -> 191 us (level)
  waiting for transfers between devices: 71.1 us -> 81.3 us
  local copies, waits for them, and re-layouts: 13.4 us -> 7.88 us
  starting transfers between devices: 63.4 us -> 61 us
    all_gather x1, waiting for transfers between devices: 14.7 us -> 0.01 us  [body(): own = lax.all_gather(pair, ('zh', 'zl'), axis=1, tiled=True)]
    ppermute x1, waiting for transfers between devices: 0.01 us -> 14 us  [exchange(): far = lax.ppermute(acc[half:], ('yl', 'yh'), [(i, i ^ 3) for i in range(4)])]
    ppermute x7, waiting for transfers between devices: 21.4 us -> 26 us  [gather_earlier_keys(): lax.ppermute(local, 'zh', [(i, i + shift) for i in range(cubes - shift)])]
    unnamed x17 -> x19, local copies, waits for them, and re-layouts: 6.76 us -> 2.7 us
    ppermute x3, waiting for transfers between devices: 29.2 us -> 32.7 us  [exchange(): return lax.ppermute(acc, axis, pairs)]
    ppermute x1, starting transfers between devices: 5.38 us -> 3.35 us  [scatter_sum(): lax.ppermute(sent, 'yh', [(i, i ^ shift) for i in range(rows)])]
    ppermute x1, waiting for transfers between devices: 2.27 us -> 4.3 us  [scatter_sum(): lax.ppermute(sent, 'yh', [(i, i ^ shift) for i in range(rows)])]
  transfers between devices with their start and end apart: 18 -> 18, of which waited for: 10 -> 10; matrix products, arithmetic and copies ran while one was open for 11% -> 6% of each run, Pallas kernels for 6% -> 6%
where the time goes in v16:
time: 191 us; the launch traced here: 189 us
  waiting for transfers between devices  81.3 us (43%)
  starting transfers between devices  61 us (32%)
  between operations  13.9 us (7%)
  Pallas kernels  12 us (6%)
  local copies, waits for them, and re-layouts  7.88 us (4%)
  matrix products  7.11 us (4%)
  other arithmetic  6.21 us (3%)
    ppermute x3, waiting for transfers between devices, exchange(): return lax.ppermute(acc, axis, pairs)  32.7 us
    ppermute x7, starting transfers between devices, gather_earlier_keys(): lax.ppermute(local, 'zh', [(i, i + shift) for i in range(cubes - shift)])  29.2 us
    ppermute x7, waiting for transfers between devices, gather_earlier_keys(): lax.ppermute(local, 'zh', [(i, i + shift) for i in range(cubes - shift)])  26 us
    ppermute x1, waiting for transfers between devices, exchange(): far = lax.ppermute(acc[half:], ('yl', 'yh'), [(i, i ^ 3) for i in range(4)])  14 us
    pallas_call x1, Pallas kernels, attend(): pl.pallas_call(attention_kernel, out_shape=jax.ShapeDtypeStruct((tokens,...  12 us
    ppermute x3, starting transfers between devices, scatter_sum(): lax.ppermute(sent, 'x', [(i, i ^ shift) for i in range(columns)])  9.83 us
    ppermute x3, starting transfers between devices, exchange(): return lax.ppermute(acc, axis, pairs)  7.43 us
    dot_general x2, matrix products, body(): jnp.dot(head_out, half, preferred_element_type=jnp.float32)  6.63 us
  transfers between devices with their start and end apart: 18, of which 10 were waited for; matrix products, arithmetic and copies ran while one was open for 6% of the time, Pallas kernels for 6%

profile of v16, /device:TPU:6, one launch (start us, length us, event | category | flops | bytes accessed | tf_op | source)
XLA Modules:
  0.0 189.4 jit_solution(6956253572887680439)
XLA Ops:
  6.5 3.6 %collective-permute-start.11 = (bf16[1,56,1024]{2,1,0:T(8,128)(2,1)}, bf16[1,56,1024]{2,1,0:T(8,128)(2,1)S(1)}, u32[]{:S(2)}, u32[]{:S(2)}) collective-permute-start(bf16[1,56,1024]{2,1,0:T(8,128)(2,1)} %bitcast.93), channel_id=1, source_target_pairs={{0,16},{16,0},{1,17},{17,1},{2,18},{18,2},{3,19},{19,3},{4,20},{20... | collective-permute-start | bytes 344072 | tf_op jit(solution)/shard_map/ppermute | solution.py:104
  10.2 3.5 %collective-permute-done.11 = bf16[1,56,1024]{2,1,0:T(8,128)(2,1)S(1)} collective-permute-done((bf16[1,56,1024]{2,1,0:T(8,128)(2,1)}, bf16[1,56,1024]{2,1,0:T(8,128)(2,1)S(1)}, u32[]{:S(2)}, u32[]{:S(2)}) %collective-permute-start.11) | collective-permute-done | bytes 114720 | tf_op jit(solution)/shard_map/ppermute | solution.py:104
  17.9 5.2 %collective-permute-start = (bf16[64,576]{1,0:T(8,128)(2,1)S(1)}, bf16[64,576]{1,0:T(8,128)(2,1)S(1)}, u32[]{:S(2)}, u32[]{:S(2)}) collective-permute-start(bf16[64,576]{1,0:T(8,128)(2,1)S(1)} %pad_maximum_fusion.2), channel_id=1, source_target_pairs={{0,64},{64,128},{128,192},{192,256},{256,320},{320,384},{384,448},... | collective-permute-start | bytes 221192 | tf_op jit(solution)/shard_map/ppermute | solution.py:135
  23.1 9.1 %collective-permute-start.1 = (bf16[64,576]{1,0:T(8,128)(2,1)S(1)}, bf16[64,576]{1,0:T(8,128)(2,1)S(1)}, u32[]{:S(2)}, u32[]{:S(2)}) collective-permute-start(bf16[64,576]{1,0:T(8,128)(2,1)S(1)} %pad_maximum_fusion.2), channel_id=1, source_target_pairs={{0,128},{64,192},{128,256},{192,320},{256,384},{320,448},{1,129},{... | collective-permute-start | bytes 221192 | tf_op jit(solution)/shard_map/ppermute | solution.py:135
  32.2 8.2 %collective-permute-start.2 = (bf16[64,576]{1,0:T(8,128)(2,1)S(1)}, bf16[64,576]{1,0:T(8,128)(2,1)S(1)}, u32[]{:S(2)}, u32[]{:S(2)}) collective-permute-start(bf16[64,576]{1,0:T(8,128)(2,1)S(1)} %pad_maximum_fusion.2), channel_id=1, source_target_pairs={{0,192},{64,256},{128,320},{192,384},{256,448},{1,193},{65,257},{1... | collective-permute-start | bytes 221192 | tf_op jit(solution)/shard_map/ppermute | solution.py:135
  40.4 2.8 %collective-permute-start.3 = (bf16[64,576]{1,0:T(8,128)(2,1)S(1)}, bf16[64,576]{1,0:T(8,128)(2,1)S(1)}, u32[]{:S(2)}, u32[]{:S(2)}) collective-permute-start(bf16[64,576]{1,0:T(8,128)(2,1)S(1)} %pad_maximum_fusion.2), channel_id=1, source_target_pairs={{0,256},{64,320},{128,384},{192,448},{1,257},{65,321},{129,385},{1... | collective-permute-start | bytes 221192 | tf_op jit(solution)/shard_map/ppermute | solution.py:135
  48.2 15.5 %collective-permute-done.4 = bf16[64,576]{1,0:T(8,128)(2,1)S(1)} collective-permute-done((bf16[64,576]{1,0:T(8,128)(2,1)S(1)}, bf16[64,576]{1,0:T(8,128)(2,1)S(1)}, u32[]{:S(2)}, u32[]{:S(2)}) %collective-permute-start.4) | collective-permute-done | bytes 73760 | tf_op jit(solution)/shard_map/ppermute | solution.py:135
  63.7 5.9 %collective-permute-done.5 = bf16[64,576]{1,0:T(8,128)(2,1)S(1)} collective-permute-done((bf16[64,576]{1,0:T(8,128)(2,1)S(1)}, bf16[64,576]{1,0:T(8,128)(2,1)S(1)}, u32[]{:S(2)}, u32[]{:S(2)}) %collective-permute-start.5) | collective-permute-done | bytes 73760 | tf_op jit(solution)/shard_map/ppermute | solution.py:135
  69.6 4.6 %collective-permute-done.6 = bf16[64,576]{1,0:T(8,128)(2,1)S(1)} collective-permute-done((bf16[64,576]{1,0:T(8,128)(2,1)S(1)}, bf16[64,576]{1,0:T(8,128)(2,1)S(1)}, u32[]{:S(2)}, u32[]{:S(2)}) %collective-permute-start.6) | collective-permute-done | bytes 73760 | tf_op jit(solution)/shard_map/ppermute | solution.py:135
  76.2 3.5 %collective-permute-start.8 = (bf16[8,64,576]{2,1,0:T(8,128)(2,1)S(1)}, bf16[8,64,576]{2,1,0:T(8,128)(2,1)S(1)}, u32[]{:S(2)}, u32[]{:S(2)}) collective-permute-start(bf16[8,64,576]{2,1,0:T(8,128)(2,1)S(1)} %get-tuple-element.20), channel_id=1, source_target_pairs={{0,16},{16,0},{1,17},{17,1},{2,18},{18,2},{3,19},{19,3},{4,20},{20... | collective-permute-start | bytes 1769480 | tf_op jit(solution)/shard_map/ppermute | solution.py:106
  79.7 24.2 %collective-permute-done.7 = bf16[8,64,576]{2,1,0:T(8,128)(2,1)S(1)} collective-permute-done((bf16[8,64,576]{2,1,0:T(8,128)(2,1)S(1)}, bf16[8,64,576]{2,1,0:T(8,128)(2,1)S(1)}, u32[]{:S(2)}, u32[]{:S(2)}) %collective-permute-start.7) | collective-permute-done | bytes 589856 | tf_op jit(solution)/shard_map/ppermute | solution.py:104
  103.9 5.7 %collective-permute-start.9 = (bf16[8,64,576]{2,1,0:T(8,128)(2,1)S(1)}, bf16[8,64,576]{2,1,0:T(8,128)(2,1)S(1)}, u32[]{:S(2)}, u32[]{:S(2)}) collective-permute-start(bf16[8,64,576]{2,1,0:T(8,128)(2,1)S(1)} %collective-permute-done.7), channel_id=1, source_target_pairs={{0,17},{1,16},{16,1},{17,0},{2,19},{3,18},{18,3},{19,2},{4,21},{5,... | collective-permute-start | bytes 1769480 | tf_op jit(solution)/shard_map/ppermute | solution.py:107
  109.8 14.0 %collective-permute-done.9 = bf16[8,64,576]{2,1,0:T(8,128)(2,1)S(1)} collective-permute-done((bf16[8,64,576]{2,1,0:T(8,128)(2,1)S(1)}, bf16[8,64,576]{2,1,0:T(8,128)(2,1)S(1)}, u32[]{:S(2)}, u32[]{:S(2)}) %collective-permute-start.9) | collective-permute-done | bytes 589856 | tf_op jit(solution)/shard_map/ppermute | solution.py:107
  127.3 5.0 %collective-permute-done.10 = bf16[32,64,576]{2,1,0:T(8,128)(2,1)} collective-permute-done((bf16[32,64,576]{2,1,0:T(8,128)(2,1)S(1)}, bf16[32,64,576]{2,1,0:T(8,128)(2,1)}, u32[]{:S(2)}, u32[]{:S(2)}) %collective-permute-start.10) | collective-permute-done | bytes 2359328 | tf_op jit(solution)/shard_map/ppermute | solution.py:104
  132.3 2.0 %collective-permute-start.12 = (bf16[1024,1792]{0,1:T(8,128)(2,1)}, bf16[1024,1792]{0,1:T(8,128)(2,1)}, u32[]{:S(2)}, u32[]{:S(2)}) collective-permute-start(bf16[1024,1792]{0,1:T(8,128)(2,1)} %all-gather.2.cloned.1.call-done), channel_id=1, source_target_pairs={{0,8},{8,0},{1,9},{9,1},{2,10},{10,2},{3,11},{11,3},{4,12},{12,4},... | collective-permute-start | bytes 11010056 | tf_op jit(solution)/shard_map/ppermute | solution.py:208
  139.1 12.0 %shard_map.82 = bf16[64,1024]{1,0:T(8,128)(2,1)} custom-call(bf16[512,576]{1,0:T(8,128)(2,1)} %bitcast.91, s32[512,1]{1,0:T(8,128)} %reshape_tile.4.qi_ref, bf16[2048,576]{1,0:T(8,128)(2,1)} %bitcast.94, s32[1,2048]{1,0:T(1,128)} %add.134.ia_ref, bf16[2048,576]{1,0:T(8,128)(2,1)} %bitcast.15.kb_ref, s32[1,2048]{1,0:T(1,128)} %add.138.ib_ref, ...), custom_call_target="tpu_custom_call" | custom-call | flops 4563402752 | bytes 5832704 | tf_op jit(solution)/shard_map/pallas_call | solution.py:94
  151.0 3.4 %fusion.23 = f32[64,1792]{1,0:T(8,128)S(1)} fusion(bf16[64,1024]{1,0:T(8,128)(2,1)} %shard_map.82, bf16[1024,1792]{0,1:T(8,128)(2,1)} %all-gather.2.cloned.1.call-done), kind=kOutput, calls=%fused_computation.75 | convolution fusion | flops 234881024 | bytes 4259840 | tf_op jit(solution)/shard_map/dot_general | solution.py:212
  154.8 3.3 %fusion.24 = f32[64,1792]{1,0:T(8,128)S(1)} fusion(bf16[64,1024]{1,0:T(8,128)(2,1)S(1)} %copy-done.1, bf16[1024,1792]{0,1:T(8,128)(2,1)} %collective-permute-done.12), kind=kOutput, calls=%fused_computation.76 | convolution fusion | flops 234881024 | bytes 4259840 | tf_op jit(solution)/shard_map/dot_general | solution.py:212
  159.4 2.2 %collective-permute-start.15 = (bf16[2,64,448]{2,1,0:T(8,128)(2,1)S(1)}, bf16[2,64,448]{2,1,0:T(8,128)(2,1)S(1)}, u32[]{:S(2)}, u32[]{:S(2)}) collective-permute-start(bf16[2,64,448]{2,1,0:T(8,128)(2,1)S(1)} %get-tuple-element.12), channel_id=1, source_target_pairs={{0,6},{2,4},{4,2},{6,0},{1,7},{3,5},{5,3},{7,1},{8,14},{10,12},{12... | collective-permute-start | bytes 344072 | tf_op jit(solution)/shard_map/ppermute | solution.py:160
  161.6 4.5 %collective-permute-start.14 = (bf16[2,64,448]{2,1,0:T(8,128)(2,1)S(1)}, bf16[2,64,448]{2,1,0:T(8,128)(2,1)S(1)}, u32[]{:S(2)}, u32[]{:S(2)}) collective-permute-start(bf16[2,64,448]{2,1,0:T(8,128)(2,1)S(1)} %get-tuple-element.13), channel_id=1, source_target_pairs={{0,4},{2,6},{4,0},{6,2},{1,5},{3,7},{5,1},{7,3},{8,12},{10,14},{12... | collective-permute-start | bytes 344072 | tf_op jit(solution)/shard_map/ppermute | solution.py:160
  166.0 3.2 %collective-permute-start.13 = (bf16[2,64,448]{2,1,0:T(8,128)(2,1)S(1)}, bf16[2,64,448]{2,1,0:T(8,128)(2,1)S(1)}, u32[]{:S(2)}, u32[]{:S(2)}) collective-permute-start(bf16[2,64,448]{2,1,0:T(8,128)(2,1)S(1)} %get-tuple-element.11), channel_id=1, source_target_pairs={{0,2},{2,0},{4,6},{6,4},{1,3},{3,1},{5,7},{7,5},{8,10},{10,8},{12,... | collective-permute-start | bytes 344072 | tf_op jit(solution)/shard_map/ppermute | solution.py:160
  171.0 2.5 %collective-permute-done.13 = bf16[2,64,448]{2,1,0:T(8,128)(2,1)S(1)} collective-permute-done((bf16[2,64,448]{2,1,0:T(8,128)(2,1)S(1)}, bf16[2,64,448]{2,1,0:T(8,128)(2,1)S(1)}, u32[]{:S(2)}, u32[]{:S(2)}) %collective-permute-start.13) | collective-permute-done | bytes 114720 | tf_op jit(solution)/shard_map/ppermute | solution.py:160
  173.6 3.4 %collective-permute-start.16 = (bf16[64,448]{1,0:T(8,128)(2,1)S(1)}, bf16[64,448]{1,0:T(8,128)(2,1)S(1)}, u32[]{:S(2)}, u32[]{:S(2)}) collective-permute-start(bf16[64,448]{1,0:T(8,128)(2,1)S(1)} %fusion.11), channel_id=1, source_target_pairs={{0,1},{1,0},{2,3},{3,2},{4,5},{5,4},{6,7},{7,6},{8,9},{9,8},{10,11... | collective-permute-start | bytes 172040 | tf_op jit(solution)/shard_map/ppermute | solution.py:166
  177.0 4.3 %collective-permute-done.16 = bf16[64,448]{1,0:T(8,128)(2,1)S(1)} collective-permute-done((bf16[64,448]{1,0:T(8,128)(2,1)S(1)}, bf16[64,448]{1,0:T(8,128)(2,1)S(1)}, u32[]{:S(2)}, u32[]{:S(2)}) %collective-permute-start.16) | collective-permute-done | bytes 57376 | tf_op jit(solution)/shard_map/ppermute | solution.py:166
  (77 shorter events, 24.1 us)
Async XLA Ops:
  6.5 131.1 %copy-start = (bf16[512,1024]{1,0:T(8,128)(2,1)S(1)}, bf16[512,1024]{1,0:T(8,128)(2,1)}, u32[]{:S(2)}) copy-start(bf16[512,1024]{1,0:T(8,128)(2,1)} %param.13) | copy-start | bytes 3145732
  6.5 125.8 %all-gather.2.cloned.1.call-start = ((), (), s32[]{:S(2)}) async-start(), calls=%async_computation | async-start | bytes 3899392 | tf_op jit(solution)/shard_map/all_gather | solution.py:206
  6.5 7.1 %collective-permute-start.11 = (bf16[1,56,1024]{2,1,0:T(8,128)(2,1)}, bf16[1,56,1024]{2,1,0:T(8,128)(2,1)S(1)}, u32[]{:S(2)}, u32[]{:S(2)}) collective-permute-start(bf16[1,56,1024]{2,1,0:T(8,128)(2,1)} %bitcast.93), channel_id=1, source_target_pairs={{0,16},{16,0},{1,17},{17,1},{2,18},{18,2},{3,19},{19,3},{4,20},{20... | collective-permute-start | bytes 344072 | tf_op jit(solution)/shard_map/ppermute | solution.py:104
  17.9 27.5 %collective-permute-start = (bf16[64,576]{1,0:T(8,128)(2,1)S(1)}, bf16[64,576]{1,0:T(8,128)(2,1)S(1)}, u32[]{:S(2)}, u32[]{:S(2)}) collective-permute-start(bf16[64,576]{1,0:T(8,128)(2,1)S(1)} %pad_maximum_fusion.2), channel_id=1, source_target_pairs={{0,64},{64,128},{128,192},{192,256},{256,320},{320,384},{384,448},... | collective-permute-start | bytes 221192 | tf_op jit(solution)/shard_map/ppermute | solution.py:135
  23.1 23.7 %collective-permute-start.1 = (bf16[64,576]{1,0:T(8,128)(2,1)S(1)}, bf16[64,576]{1,0:T(8,128)(2,1)S(1)}, u32[]{:S(2)}, u32[]{:S(2)}) collective-permute-start(bf16[64,576]{1,0:T(8,128)(2,1)S(1)} %pad_maximum_fusion.2), channel_id=1, source_target_pairs={{0,128},{64,192},{128,256},{192,320},{256,384},{320,448},{1,129},{... | collective-permute-start | bytes 221192 | tf_op jit(solution)/shard_map/ppermute | solution.py:135
  32.2 15.9 %collective-permute-start.2 = (bf16[64,576]{1,0:T(8,128)(2,1)S(1)}, bf16[64,576]{1,0:T(8,128)(2,1)S(1)}, u32[]{:S(2)}, u32[]{:S(2)}) collective-permute-start(bf16[64,576]{1,0:T(8,128)(2,1)S(1)} %pad_maximum_fusion.2), channel_id=1, source_target_pairs={{0,192},{64,256},{128,320},{192,384},{256,448},{1,193},{65,257},{1... | collective-permute-start | bytes 221192 | tf_op jit(solution)/shard_map/ppermute | solution.py:135
  40.4 7.7 %collective-permute-start.3 = (bf16[64,576]{1,0:T(8,128)(2,1)S(1)}, bf16[64,576]{1,0:T(8,128)(2,1)S(1)}, u32[]{:S(2)}, u32[]{:S(2)}) collective-permute-start(bf16[64,576]{1,0:T(8,128)(2,1)S(1)} %pad_maximum_fusion.2), channel_id=1, source_target_pairs={{0,256},{64,320},{128,384},{192,448},{1,257},{65,321},{129,385},{1... | collective-permute-start | bytes 221192 | tf_op jit(solution)/shard_map/ppermute | solution.py:135
  43.3 20.4 %collective-permute-start.4 = (bf16[64,576]{1,0:T(8,128)(2,1)S(1)}, bf16[64,576]{1,0:T(8,128)(2,1)S(1)}, u32[]{:S(2)}, u32[]{:S(2)}) collective-permute-start(bf16[64,576]{1,0:T(8,128)(2,1)S(1)} %pad_maximum_fusion.2), channel_id=1, source_target_pairs={{0,320},{64,384},{128,448},{1,321},{65,385},{129,449},{2,322},{66,... | collective-permute-start | bytes 221192 | tf_op jit(solution)/shard_map/ppermute | solution.py:135
  45.4 24.2 %collective-permute-start.5 = (bf16[64,576]{1,0:T(8,128)(2,1)S(1)}, bf16[64,576]{1,0:T(8,128)(2,1)S(1)}, u32[]{:S(2)}, u32[]{:S(2)}) collective-permute-start(bf16[64,576]{1,0:T(8,128)(2,1)S(1)} %pad_maximum_fusion.2), channel_id=1, source_target_pairs={{0,384},{64,448},{1,385},{65,449},{2,386},{66,450},{3,387},{67,451... | collective-permute-start | bytes 221192 | tf_op jit(solution)/shard_map/ppermute | solution.py:135
  46.8 27.5 %collective-permute-start.6 = (bf16[64,576]{1,0:T(8,128)(2,1)S(1)}, bf16[64,576]{1,0:T(8,128)(2,1)S(1)}, u32[]{:S(2)}, u32[]{:S(2)}) collective-permute-start(bf16[64,576]{1,0:T(8,128)(2,1)S(1)} %pad_maximum_fusion.2), channel_id=1, source_target_pairs={{0,448},{1,449},{2,450},{3,451},{4,452},{5,453},{6,454},{7,455},{8... | collective-permute-start | bytes 221192 | tf_op jit(solution)/shard_map/ppermute | solution.py:135
  48.1 86.3 %copy-start.2 = (bf16[64,512]{1,0:T(8,128)(2,1)S(1)}, bf16[64,512]{1,0:T(8,128)(2,1)}, u32[]{:S(2)}) copy-start(bf16[64,512]{1,0:T(8,128)(2,1)} %param.9) | copy-start | bytes 196612
  74.3 29.6 %collective-permute-start.7 = (bf16[8,64,576]{2,1,0:T(8,128)(2,1)S(1)}, bf16[8,64,576]{2,1,0:T(8,128)(2,1)S(1)}, u32[]{:S(2)}, u32[]{:S(2)}) collective-permute-start(bf16[8,64,576]{2,1,0:T(8,128)(2,1)S(1)} %get-tuple-element.20), channel_id=1, source_target_pairs={{0,32},{32,0},{1,33},{33,1},{2,34},{34,2},{3,35},{35,3},{4,36},{36... | collective-permute-start | bytes 1769480 | tf_op jit(solution)/shard_map/ppermute | solution.py:104
  76.2 33.5 %collective-permute-start.8 = (bf16[8,64,576]{2,1,0:T(8,128)(2,1)S(1)}, bf16[8,64,576]{2,1,0:T(8,128)(2,1)S(1)}, u32[]{:S(2)}, u32[]{:S(2)}) collective-permute-start(bf16[8,64,576]{2,1,0:T(8,128)(2,1)S(1)} %get-tuple-element.20), channel_id=1, source_target_pairs={{0,16},{16,0},{1,17},{17,1},{2,18},{18,2},{3,19},{19,3},{4,20},{20... | collective-permute-start | bytes 1769480 | tf_op jit(solution)/shard_map/ppermute | solution.py:106
  103.9 19.8 %collective-permute-start.9 = (bf16[8,64,576]{2,1,0:T(8,128)(2,1)S(1)}, bf16[8,64,576]{2,1,0:T(8,128)(2,1)S(1)}, u32[]{:S(2)}, u32[]{:S(2)}) collective-permute-start(bf16[8,64,576]{2,1,0:T(8,128)(2,1)S(1)} %collective-permute-done.7), channel_id=1, source_target_pairs={{0,17},{1,16},{16,1},{17,0},{2,19},{3,18},{18,3},{19,2},{4,21},{5,... | collective-permute-start | bytes 1769480 | tf_op jit(solution)/shard_map/ppermute | solution.py:107
  109.7 27.9 %copy-start.4 = (bf16[64,1024]{1,0:T(8,128)(2,1)S(1)}, bf16[64,1024]{1,0:T(8,128)(2,1)}, u32[]{:S(2)}) copy-start(bf16[64,1024]{1,0:T(8,128)(2,1)} %param.8) | copy-start | bytes 393220
  123.9 1.6 copy-start.3
  125.4 6.9 %collective-permute-start.10 = (bf16[32,64,576]{2,1,0:T(8,128)(2,1)S(1)}, bf16[32,64,576]{2,1,0:T(8,128)(2,1)}, u32[]{:S(2)}, u32[]{:S(2)}) collective-permute-start(bf16[32,64,576]{2,1,0:T(8,128)(2,1)S(1)} %constant_dynamic-update-slice_fusion), channel_id=1, source_target_pairs={{0,8},{8,0},{1,9},{9,1},{2,10},{10,2},{3,11},{11,3},{4,12},{12,4},... | collective-permute-start | bytes 7077896 | tf_op jit(solution)/shard_map/ppermute | solution.py:104
  132.3 22.4 %collective-permute-start.12 = (bf16[1024,1792]{0,1:T(8,128)(2,1)}, bf16[1024,1792]{0,1:T(8,128)(2,1)}, u32[]{:S(2)}, u32[]{:S(2)}) collective-permute-start(bf16[1024,1792]{0,1:T(8,128)(2,1)} %all-gather.2.cloned.1.call-done), channel_id=1, source_target_pairs={{0,8},{8,0},{1,9},{9,1},{2,10},{10,2},{3,11},{11,3},{4,12},{12,4},... | collective-permute-start | bytes 11010056 | tf_op jit(solution)/shard_map/ppermute | solution.py:208
  151.0 3.7 %copy-start.1 = (bf16[64,1024]{1,0:T(8,128)(2,1)S(1)}, bf16[64,1024]{1,0:T(8,128)(2,1)}, u32[]{:S(2)}) copy-start(bf16[64,1024]{1,0:T(8,128)(2,1)} %shard_map.82) | copy-start | bytes 393220
  159.4 11.7 %collective-permute-start.15 = (bf16[2,64,448]{2,1,0:T(8,128)(2,1)S(1)}, bf16[2,64,448]{2,1,0:T(8,128)(2,1)S(1)}, u32[]{:S(2)}, u32[]{:S(2)}) collective-permute-start(bf16[2,64,448]{2,1,0:T(8,128)(2,1)S(1)} %get-tuple-element.12), channel_id=1, source_target_pairs={{0,6},{2,4},{4,2},{6,0},{1,7},{3,5},{5,3},{7,1},{8,14},{10,12},{12... | collective-permute-start | bytes 344072 | tf_op jit(solution)/shard_map/ppermute | solution.py:160
  161.6 9.5 %collective-permute-start.14 = (bf16[2,64,448]{2,1,0:T(8,128)(2,1)S(1)}, bf16[2,64,448]{2,1,0:T(8,128)(2,1)S(1)}, u32[]{:S(2)}, u32[]{:S(2)}) collective-permute-start(bf16[2,64,448]{2,1,0:T(8,128)(2,1)S(1)} %get-tuple-element.13), channel_id=1, source_target_pairs={{0,4},{2,6},{4,0},{6,2},{1,5},{3,7},{5,1},{7,3},{8,12},{10,14},{12... | collective-permute-start | bytes 344072 | tf_op jit(solution)/shard_map/ppermute | solution.py:160
  166.0 7.5 %collective-permute-start.13 = (bf16[2,64,448]{2,1,0:T(8,128)(2,1)S(1)}, bf16[2,64,448]{2,1,0:T(8,128)(2,1)S(1)}, u32[]{:S(2)}, u32[]{:S(2)}) collective-permute-start(bf16[2,64,448]{2,1,0:T(8,128)(2,1)S(1)} %get-tuple-element.11), channel_id=1, source_target_pairs={{0,2},{2,0},{4,6},{6,4},{1,3},{3,1},{5,7},{7,5},{8,10},{10,8},{12,... | collective-permute-start | bytes 344072 | tf_op jit(solution)/shard_map/ppermute | solution.py:160
  173.6 7.7 %collective-permute-start.16 = (bf16[64,448]{1,0:T(8,128)(2,1)S(1)}, bf16[64,448]{1,0:T(8,128)(2,1)S(1)}, u32[]{:S(2)}, u32[]{:S(2)}) collective-permute-start(bf16[64,448]{1,0:T(8,128)(2,1)S(1)} %fusion.11), channel_id=1, source_target_pairs={{0,1},{1,0},{2,3},{3,2},{4,5},{5,4},{6,7},{7,6},{8,9},{9,8},{10,11... | collective-permute-start | bytes 172040 | tf_op jit(solution)/shard_map/ppermute | solution.py:166
Sparse Core Ops, SparseCore 0:
  15.4 109.9 all-gather.1

commit v17 on v14

--- a/solution.py
+++ b/solution.py
@@ -130,10 +130,10 @@
     cube = lax.axis_index("zh")
     within = lax.axis_index(("zl", "yl", "co"))
     per_cube = lax.axis_size(("zl", "yl", "co"))
-    blocks = [local]
-    for shift in range(1, cubes):
-        blocks.append(lax.ppermute(local, "zh", [(i, i + shift) for i in range(cubes - shift)]))
-    acc = jnp.stack(blocks)
+    sent = {}
+    for shift in sorted(range(1, cubes), key=lambda d: -min(d, cubes - d)):
+        sent[shift] = lax.ppermute(local, "zh", [(i, i + shift) for i in range(cubes - shift)])
+    acc = jnp.stack([local] + [sent[shift] for shift in range(1, cubes)])
     source = cube - jnp.arange(cubes, dtype=jnp.int32)
     index = jnp.where(source >= 0, source * per_cube + within, ABSENT)
     rounds = (("zl", 2), ("yl", 2), ("co", 2))

time: 191 us -> 191 us (level)
  no operation moved by 1% of the time
where the time goes in v17:
time: 191 us; the launch traced here: 188 us
  waiting for transfers between devices  71.1 us (37%)
  starting transfers between devices  63.4 us (33%)
  between operations  13.8 us (7%)
  local copies, waits for them, and re-layouts  13.4 us (7%)
  Pallas kernels  12 us (6%)
  matrix products  7.11 us (4%)
  other arithmetic  6.87 us (4%)
    ppermute x3, waiting for transfers between devices, exchange(): return lax.ppermute(acc, axis, pairs)  29.2 us
    ppermute x7, starting transfers between devices, gather_earlier_keys(): lax.ppermute(local, 'zh', [(i, i + shift) for i in range(cubes - shift)])  29.2 us
    ppermute x7, waiting for transfers between devices, gather_earlier_keys(): lax.ppermute(local, 'zh', [(i, i + shift) for i in range(cubes - shift)])  21.4 us
    all_gather x1, waiting for transfers between devices, body(): own = lax.all_gather(pair, ('zh', 'zl'), axis=1, tiled=True)  14.7 us
    pallas_call x1, Pallas kernels, attend(): pl.pallas_call(attention_kernel, out_shape=jax.ShapeDtypeStruct((tokens,...  12 us
    ppermute x3, starting transfers between devices, scatter_sum(): lax.ppermute(sent, 'x', [(i, i ^ shift) for i in range(columns)])  10.4 us
    ppermute x3, starting transfers between devices, exchange(): return lax.ppermute(acc, axis, pairs)  7.91 us
    unnamed x17, local copies, waits for them, and re-layouts  6.76 us
  transfers between devices with their start and end apart: 18, of which 10 were waited for; matrix products, arithmetic and copies ran while one was open for 11% of the time, Pallas kernels for 6%

profile of v17, /device:TPU:6, one launch (start us, length us, event | category | flops | bytes accessed | tf_op | source)
XLA Modules:
  0.0 187.6 jit_solution(634078437274837206)
XLA Ops:
  6.5 3.6 %collective-permute-start.11 = (bf16[1,56,1024]{2,1,0:T(8,128)(2,1)}, bf16[1,56,1024]{2,1,0:T(8,128)(2,1)S(1)}, u32[]{:S(2)}, u32[]{:S(2)}) collective-permute-start(bf16[1,56,1024]{2,1,0:T(8,128)(2,1)} %bitcast.93), channel_id=1, source_target_pairs={{0,16},{16,0},{1,17},{17,1},{2,18},{18,2},{3,19},{19,3},{4,20},{20... | collective-permute-start | bytes 344072 | tf_op jit(solution)/shard_map/ppermute | solution.py:104
  10.2 3.5 %collective-permute-done.11 = bf16[1,56,1024]{2,1,0:T(8,128)(2,1)S(1)} collective-permute-done((bf16[1,56,1024]{2,1,0:T(8,128)(2,1)}, bf16[1,56,1024]{2,1,0:T(8,128)(2,1)S(1)}, u32[]{:S(2)}, u32[]{:S(2)}) %collective-permute-start.11) | collective-permute-done | bytes 114720 | tf_op jit(solution)/shard_map/ppermute | solution.py:104
  17.9 5.2 %collective-permute-start = (bf16[64,576]{1,0:T(8,128)(2,1)S(1)}, bf16[64,576]{1,0:T(8,128)(2,1)S(1)}, u32[]{:S(2)}, u32[]{:S(2)}) collective-permute-start(bf16[64,576]{1,0:T(8,128)(2,1)S(1)} %pad_maximum_fusion.2), channel_id=1, source_target_pairs={{0,64},{64,128},{128,192},{192,256},{256,320},{320,384},{384,448},... | collective-permute-start | bytes 221192 | tf_op jit(solution)/shard_map/ppermute | solution.py:135
  23.1 9.1 %collective-permute-start.1 = (bf16[64,576]{1,0:T(8,128)(2,1)S(1)}, bf16[64,576]{1,0:T(8,128)(2,1)S(1)}, u32[]{:S(2)}, u32[]{:S(2)}) collective-permute-start(bf16[64,576]{1,0:T(8,128)(2,1)S(1)} %pad_maximum_fusion.2), channel_id=1, source_target_pairs={{0,128},{64,192},{128,256},{192,320},{256,384},{320,448},{1,129},{... | collective-permute-start | bytes 221192 | tf_op jit(solution)/shard_map/ppermute | solution.py:135
  32.2 8.2 %collective-permute-start.2 = (bf16[64,576]{1,0:T(8,128)(2,1)S(1)}, bf16[64,576]{1,0:T(8,128)(2,1)S(1)}, u32[]{:S(2)}, u32[]{:S(2)}) collective-permute-start(bf16[64,576]{1,0:T(8,128)(2,1)S(1)} %pad_maximum_fusion.2), channel_id=1, source_target_pairs={{0,192},{64,256},{128,320},{192,384},{256,448},{1,193},{65,257},{1... | collective-permute-start | bytes 221192 | tf_op jit(solution)/shard_map/ppermute | solution.py:135
  40.4 2.8 %collective-permute-start.3 = (bf16[64,576]{1,0:T(8,128)(2,1)S(1)}, bf16[64,576]{1,0:T(8,128)(2,1)S(1)}, u32[]{:S(2)}, u32[]{:S(2)}) collective-permute-start(bf16[64,576]{1,0:T(8,128)(2,1)S(1)} %pad_maximum_fusion.2), channel_id=1, source_target_pairs={{0,256},{64,320},{128,384},{192,448},{1,257},{65,321},{129,385},{1... | collective-permute-start | bytes 221192 | tf_op jit(solution)/shard_map/ppermute | solution.py:135
  51.4 12.3 %collective-permute-done.4 = bf16[64,576]{1,0:T(8,128)(2,1)S(1)} collective-permute-done((bf16[64,576]{1,0:T(8,128)(2,1)S(1)}, bf16[64,576]{1,0:T(8,128)(2,1)S(1)}, u32[]{:S(2)}, u32[]{:S(2)}) %collective-permute-start.4) | collective-permute-done | bytes 73760 | tf_op jit(solution)/shard_map/ppermute | solution.py:135
  64.4 5.2 %collective-permute-done.5 = bf16[64,576]{1,0:T(8,128)(2,1)S(1)} collective-permute-done((bf16[64,576]{1,0:T(8,128)(2,1)S(1)}, bf16[64,576]{1,0:T(8,128)(2,1)S(1)}, u32[]{:S(2)}, u32[]{:S(2)}) %collective-permute-start.5) | collective-permute-done | bytes 73760 | tf_op jit(solution)/shard_map/ppermute | solution.py:135
  70.3 3.9 %collective-permute-done.6 = bf16[64,576]{1,0:T(8,128)(2,1)S(1)} collective-permute-done((bf16[64,576]{1,0:T(8,128)(2,1)S(1)}, bf16[64,576]{1,0:T(8,128)(2,1)S(1)}, u32[]{:S(2)}, u32[]{:S(2)}) %collective-permute-start.6) | collective-permute-done | bytes 73760 | tf_op jit(solution)/shard_map/ppermute | solution.py:135
  76.8 3.5 %collective-permute-start.8 = (bf16[8,64,576]{2,1,0:T(8,128)(2,1)}, bf16[8,64,576]{2,1,0:T(8,128)(2,1)S(1)}, u32[]{:S(2)}, u32[]{:S(2)}) collective-permute-start(bf16[8,64,576]{2,1,0:T(8,128)(2,1)} %get-tuple-element.18), channel_id=1, source_target_pairs={{0,16},{16,0},{1,17},{17,1},{2,18},{18,2},{3,19},{19,3},{4,20},{20... | collective-permute-start | bytes 1769480 | tf_op jit(solution)/shard_map/ppermute | solution.py:106
  80.3 25.1 %collective-permute-done.7 = bf16[8,64,576]{2,1,0:T(8,128)(2,1)S(1)} collective-permute-done((bf16[8,64,576]{2,1,0:T(8,128)(2,1)}, bf16[8,64,576]{2,1,0:T(8,128)(2,1)S(1)}, u32[]{:S(2)}, u32[]{:S(2)}) %collective-permute-start.7) | collective-permute-done | bytes 589856 | tf_op jit(solution)/shard_map/ppermute | solution.py:104
  105.4 5.1 %collective-permute-start.9 = (bf16[8,64,576]{2,1,0:T(8,128)(2,1)S(1)}, bf16[8,64,576]{2,1,0:T(8,128)(2,1)S(1)}, u32[]{:S(2)}, u32[]{:S(2)}) collective-permute-start(bf16[8,64,576]{2,1,0:T(8,128)(2,1)S(1)} %collective-permute-done.7), channel_id=1, source_target_pairs={{0,17},{1,16},{16,1},{17,0},{2,19},{3,18},{18,3},{19,2},{4,21},{5,... | collective-permute-start | bytes 1769480 | tf_op jit(solution)/shard_map/ppermute | solution.py:107
  110.5 14.7 %all-gather.2.cloned.1.call-done = bf16[1024,1792]{0,1:T(8,128)(2,1)} async-done(((bf16[1024,112]{0,1:T(8,128)(2,1)}), bf16[1024,1792]{0,1:T(8,128)(2,1)}) %all-gather.2.cloned.1.call-update) | async-done | bytes 3670032 | tf_op jit(solution)/shard_map/all_gather | solution.py:206
  125.2 1.9 %collective-permute-start.12 = (bf16[1024,1792]{0,1:T(8,128)(2,1)}, bf16[1024,1792]{0,1:T(8,128)(2,1)}, u32[]{:S(2)}, u32[]{:S(2)}) collective-permute-start(bf16[1024,1792]{0,1:T(8,128)(2,1)} %all-gather.2.cloned.1.call-done), channel_id=1, source_target_pairs={{0,8},{8,0},{1,9},{9,1},{2,10},{10,2},{3,11},{11,3},{4,12},{12,4},... | collective-permute-start | bytes 11010056 | tf_op jit(solution)/shard_map/ppermute | solution.py:207
  129.9 2.4 %collective-permute-start.10 = (bf16[32,64,576]{2,1,0:T(8,128)(2,1)}, bf16[32,64,576]{2,1,0:T(8,128)(2,1)}, u32[]{:S(2)}, u32[]{:S(2)}) collective-permute-start(bf16[32,64,576]{2,1,0:T(8,128)(2,1)} %constant_dynamic-update-slice_fusion), channel_id=1, source_target_pairs={{0,8},{8,0},{1,9},{9,1},{2,10},{10,2},{3,11},{11,3},{4,12},{12,4},... | collective-permute-start | bytes 7077896 | tf_op jit(solution)/shard_map/ppermute | solution.py:104
  137.6 12.0 %shard_map.82 = bf16[64,1024]{1,0:T(8,128)(2,1)} custom-call(bf16[512,576]{1,0:T(8,128)(2,1)} %bitcast.91, s32[512,1]{1,0:T(8,128)} %reshape_tile.4.qi_ref, bf16[2048,576]{1,0:T(8,128)(2,1)} %bitcast.94, s32[1,2048]{1,0:T(1,128)} %add.134.ia_ref, bf16[2048,576]{1,0:T(8,128)(2,1)} %bitcast.15.kb_ref, s32[1,2048]{1,0:T(1,128)} %add.138.ib_ref, ...), custom_call_target="tpu_custom_call" | custom-call | flops 4563402752 | bytes 5832704 | tf_op jit(solution)/shard_map/pallas_call | solution.py:94
  149.6 3.4 %fusion.23 = f32[64,1792]{1,0:T(8,128)S(1)} fusion(bf16[64,1024]{1,0:T(8,128)(2,1)} %shard_map.82, bf16[1024,1792]{0,1:T(8,128)(2,1)} %all-gather.2.cloned.1.call-done), kind=kOutput, calls=%fused_computation.75 | convolution fusion | flops 234881024 | bytes 4259840 | tf_op jit(solution)/shard_map/dot_general | solution.py:211
  153.3 3.3 %fusion.24 = f32[64,1792]{1,0:T(8,128)S(1)} fusion(bf16[64,1024]{1,0:T(8,128)(2,1)S(1)} %copy-done.1, bf16[1024,1792]{0,1:T(8,128)(2,1)} %collective-permute-done.12), kind=kOutput, calls=%fused_computation.76 | convolution fusion | flops 234881024 | bytes 4259840 | tf_op jit(solution)/shard_map/dot_general | solution.py:211
  157.9 2.5 %collective-permute-start.13 = (bf16[2,64,448]{2,1,0:T(8,128)(2,1)S(1)}, bf16[2,64,448]{2,1,0:T(8,128)(2,1)S(1)}, u32[]{:S(2)}, u32[]{:S(2)}) collective-permute-start(bf16[2,64,448]{2,1,0:T(8,128)(2,1)S(1)} %get-tuple-element.9), channel_id=1, source_target_pairs={{0,2},{2,0},{4,6},{6,4},{1,3},{3,1},{5,7},{7,5},{8,10},{10,8},{12,... | collective-permute-start | bytes 344072 | tf_op jit(solution)/shard_map/ppermute | solution.py:160
  160.3 3.0 %collective-permute-start.14 = (bf16[2,64,448]{2,1,0:T(8,128)(2,1)S(1)}, bf16[2,64,448]{2,1,0:T(8,128)(2,1)S(1)}, u32[]{:S(2)}, u32[]{:S(2)}) collective-permute-start(bf16[2,64,448]{2,1,0:T(8,128)(2,1)S(1)} %get-tuple-element.11), channel_id=1, source_target_pairs={{0,4},{2,6},{4,0},{6,2},{1,5},{3,7},{5,1},{7,3},{8,12},{10,14},{12... | collective-permute-start | bytes 344072 | tf_op jit(solution)/shard_map/ppermute | solution.py:160
  163.4 4.9 %collective-permute-start.15 = (bf16[2,64,448]{2,1,0:T(8,128)(2,1)S(1)}, bf16[2,64,448]{2,1,0:T(8,128)(2,1)S(1)}, u32[]{:S(2)}, u32[]{:S(2)}) collective-permute-start(bf16[2,64,448]{2,1,0:T(8,128)(2,1)S(1)} %get-tuple-element.10), channel_id=1, source_target_pairs={{0,6},{2,4},{4,2},{6,0},{1,7},{3,5},{5,3},{7,1},{8,14},{10,12},{12... | collective-permute-start | bytes 344072 | tf_op jit(solution)/shard_map/ppermute | solution.py:160
  169.0 2.8 %collective-permute-done.15 = bf16[2,64,448]{2,1,0:T(8,128)(2,1)S(1)} collective-permute-done((bf16[2,64,448]{2,1,0:T(8,128)(2,1)S(1)}, bf16[2,64,448]{2,1,0:T(8,128)(2,1)S(1)}, u32[]{:S(2)}, u32[]{:S(2)}) %collective-permute-start.15) | collective-permute-done | bytes 114720 | tf_op jit(solution)/shard_map/ppermute | solution.py:160
  171.9 5.4 %collective-permute-start.16 = (bf16[64,448]{1,0:T(8,128)(2,1)S(1)}, bf16[64,448]{1,0:T(8,128)(2,1)S(1)}, u32[]{:S(2)}, u32[]{:S(2)}) collective-permute-start(bf16[64,448]{1,0:T(8,128)(2,1)S(1)} %fusion.11), channel_id=1, source_target_pairs={{0,1},{1,0},{2,3},{3,2},{4,5},{5,4},{6,7},{7,6},{8,9},{9,8},{10,11... | collective-permute-start | bytes 172040 | tf_op jit(solution)/shard_map/ppermute | solution.py:166
  177.3 2.3 %collective-permute-done.16 = bf16[64,448]{1,0:T(8,128)(2,1)S(1)} collective-permute-done((bf16[64,448]{1,0:T(8,128)(2,1)S(1)}, bf16[64,448]{1,0:T(8,128)(2,1)S(1)}, u32[]{:S(2)}, u32[]{:S(2)}) %collective-permute-start.16) | collective-permute-done | bytes 57376 | tf_op jit(solution)/shard_map/ppermute | solution.py:166
  (75 shorter events, 27.9 us)
Async XLA Ops:
  6.5 128.9 %copy-start = (bf16[512,1024]{1,0:T(8,128)(2,1)S(1)}, bf16[512,1024]{1,0:T(8,128)(2,1)}, u32[]{:S(2)}) copy-start(bf16[512,1024]{1,0:T(8,128)(2,1)} %param.13) | copy-start | bytes 3145732
  6.5 118.7 %all-gather.2.cloned.1.call-start = ((), (), s32[]{:S(2)}) async-start(), calls=%async_computation | async-start | bytes 3899392 | tf_op jit(solution)/shard_map/all_gather | solution.py:206
  6.5 7.1 %collective-permute-start.11 = (bf16[1,56,1024]{2,1,0:T(8,128)(2,1)}, bf16[1,56,1024]{2,1,0:T(8,128)(2,1)S(1)}, u32[]{:S(2)}, u32[]{:S(2)}) collective-permute-start(bf16[1,56,1024]{2,1,0:T(8,128)(2,1)} %bitcast.93), channel_id=1, source_target_pairs={{0,16},{16,0},{1,17},{17,1},{2,18},{18,2},{3,19},{19,3},{4,20},{20... | collective-permute-start | bytes 344072 | tf_op jit(solution)/shard_map/ppermute | solution.py:104
  17.9 28.2 %collective-permute-start = (bf16[64,576]{1,0:T(8,128)(2,1)S(1)}, bf16[64,576]{1,0:T(8,128)(2,1)S(1)}, u32[]{:S(2)}, u32[]{:S(2)}) collective-permute-start(bf16[64,576]{1,0:T(8,128)(2,1)S(1)} %pad_maximum_fusion.2), channel_id=1, source_target_pairs={{0,64},{64,128},{128,192},{192,256},{256,320},{320,384},{384,448},... | collective-permute-start | bytes 221192 | tf_op jit(solution)/shard_map/ppermute | solution.py:135
  23.1 25.0 %collective-permute-start.1 = (bf16[64,576]{1,0:T(8,128)(2,1)S(1)}, bf16[64,576]{1,0:T(8,128)(2,1)S(1)}, u32[]{:S(2)}, u32[]{:S(2)}) collective-permute-start(bf16[64,576]{1,0:T(8,128)(2,1)S(1)} %pad_maximum_fusion.2), channel_id=1, source_target_pairs={{0,128},{64,192},{128,256},{192,320},{256,384},{320,448},{1,129},{... | collective-permute-start | bytes 221192 | tf_op jit(solution)/shard_map/ppermute | solution.py:135
  32.2 17.8 %collective-permute-start.2 = (bf16[64,576]{1,0:T(8,128)(2,1)S(1)}, bf16[64,576]{1,0:T(8,128)(2,1)S(1)}, u32[]{:S(2)}, u32[]{:S(2)}) collective-permute-start(bf16[64,576]{1,0:T(8,128)(2,1)S(1)} %pad_maximum_fusion.2), channel_id=1, source_target_pairs={{0,192},{64,256},{128,320},{192,384},{256,448},{1,193},{65,257},{1... | collective-permute-start | bytes 221192 | tf_op jit(solution)/shard_map/ppermute | solution.py:135
  40.4 10.3 %collective-permute-start.3 = (bf16[64,576]{1,0:T(8,128)(2,1)S(1)}, bf16[64,576]{1,0:T(8,128)(2,1)S(1)}, u32[]{:S(2)}, u32[]{:S(2)}) collective-permute-start(bf16[64,576]{1,0:T(8,128)(2,1)S(1)} %pad_maximum_fusion.2), channel_id=1, source_target_pairs={{0,256},{64,320},{128,384},{192,448},{1,257},{65,321},{129,385},{1... | collective-permute-start | bytes 221192 | tf_op jit(solution)/shard_map/ppermute | solution.py:135
  43.2 20.4 %collective-permute-start.4 = (bf16[64,576]{1,0:T(8,128)(2,1)S(1)}, bf16[64,576]{1,0:T(8,128)(2,1)S(1)}, u32[]{:S(2)}, u32[]{:S(2)}) collective-permute-start(bf16[64,576]{1,0:T(8,128)(2,1)S(1)} %pad_maximum_fusion.2), channel_id=1, source_target_pairs={{0,320},{64,384},{128,448},{1,321},{65,385},{129,449},{2,322},{66,... | collective-permute-start | bytes 221192 | tf_op jit(solution)/shard_map/ppermute | solution.py:135
  46.1 23.5 %collective-permute-start.5 = (bf16[64,576]{1,0:T(8,128)(2,1)S(1)}, bf16[64,576]{1,0:T(8,128)(2,1)S(1)}, u32[]{:S(2)}, u32[]{:S(2)}) collective-permute-start(bf16[64,576]{1,0:T(8,128)(2,1)S(1)} %pad_maximum_fusion.2), channel_id=1, source_target_pairs={{0,384},{64,448},{1,385},{65,449},{2,386},{66,450},{3,387},{67,451... | collective-permute-start | bytes 221192 | tf_op jit(solution)/shard_map/ppermute | solution.py:135
  48.1 26.2 %collective-permute-start.6 = (bf16[64,576]{1,0:T(8,128)(2,1)S(1)}, bf16[64,576]{1,0:T(8,128)(2,1)S(1)}, u32[]{:S(2)}, u32[]{:S(2)}) collective-permute-start(bf16[64,576]{1,0:T(8,128)(2,1)S(1)} %pad_maximum_fusion.2), channel_id=1, source_target_pairs={{0,448},{1,449},{2,450},{3,451},{4,452},{5,453},{6,454},{7,455},{8... | collective-permute-start | bytes 221192 | tf_op jit(solution)/shard_map/ppermute | solution.py:135
  50.7 84.1 %copy-start.2 = (bf16[64,512]{1,0:T(8,128)(2,1)S(1)}, bf16[64,512]{1,0:T(8,128)(2,1)}, u32[]{:S(2)}) copy-start(bf16[64,512]{1,0:T(8,128)(2,1)} %param.9) | copy-start | bytes 196612
  74.9 30.5 %collective-permute-start.7 = (bf16[8,64,576]{2,1,0:T(8,128)(2,1)}, bf16[8,64,576]{2,1,0:T(8,128)(2,1)S(1)}, u32[]{:S(2)}, u32[]{:S(2)}) collective-permute-start(bf16[8,64,576]{2,1,0:T(8,128)(2,1)} %get-tuple-element.18), channel_id=1, source_target_pairs={{0,32},{32,0},{1,33},{33,1},{2,34},{34,2},{3,35},{35,3},{4,36},{36... | collective-permute-start | bytes 1769480 | tf_op jit(solution)/shard_map/ppermute | solution.py:104
  76.8 51.2 %collective-permute-start.8 = (bf16[8,64,576]{2,1,0:T(8,128)(2,1)}, bf16[8,64,576]{2,1,0:T(8,128)(2,1)S(1)}, u32[]{:S(2)}, u32[]{:S(2)}) collective-permute-start(bf16[8,64,576]{2,1,0:T(8,128)(2,1)} %get-tuple-element.18), channel_id=1, source_target_pairs={{0,16},{16,0},{1,17},{17,1},{2,18},{18,2},{3,19},{19,3},{4,20},{20... | collective-permute-start | bytes 1769480 | tf_op jit(solution)/shard_map/ppermute | solution.py:106
  105.4 23.5 %collective-permute-start.9 = (bf16[8,64,576]{2,1,0:T(8,128)(2,1)S(1)}, bf16[8,64,576]{2,1,0:T(8,128)(2,1)S(1)}, u32[]{:S(2)}, u32[]{:S(2)}) collective-permute-start(bf16[8,64,576]{2,1,0:T(8,128)(2,1)S(1)} %collective-permute-done.7), channel_id=1, source_target_pairs={{0,17},{1,16},{16,1},{17,0},{2,19},{3,18},{18,3},{19,2},{4,21},{5,... | collective-permute-start | bytes 1769480 | tf_op jit(solution)/shard_map/ppermute | solution.py:107
  125.2 28.1 %collective-permute-start.12 = (bf16[1024,1792]{0,1:T(8,128)(2,1)}, bf16[1024,1792]{0,1:T(8,128)(2,1)}, u32[]{:S(2)}, u32[]{:S(2)}) collective-permute-start(bf16[1024,1792]{0,1:T(8,128)(2,1)} %all-gather.2.cloned.1.call-done), channel_id=1, source_target_pairs={{0,8},{8,0},{1,9},{9,1},{2,10},{10,2},{3,11},{11,3},{4,12},{12,4},... | collective-permute-start | bytes 11010056 | tf_op jit(solution)/shard_map/ppermute | solution.py:207
  128.0 7.5 %copy-start.3 = (bf16[64,1024]{1,0:T(8,128)(2,1)S(1)}, bf16[64,1024]{1,0:T(8,128)(2,1)}, u32[]{:S(2)}) copy-start(bf16[64,1024]{1,0:T(8,128)(2,1)} %param.8) | copy-start | bytes 393220
  129.9 7.7 %collective-permute-start.10 = (bf16[32,64,576]{2,1,0:T(8,128)(2,1)}, bf16[32,64,576]{2,1,0:T(8,128)(2,1)}, u32[]{:S(2)}, u32[]{:S(2)}) collective-permute-start(bf16[32,64,576]{2,1,0:T(8,128)(2,1)} %constant_dynamic-update-slice_fusion), channel_id=1, source_target_pairs={{0,8},{8,0},{1,9},{9,1},{2,10},{10,2},{3,11},{11,3},{4,12},{12,4},... | collective-permute-start | bytes 7077896 | tf_op jit(solution)/shard_map/ppermute | solution.py:104
  149.6 3.7 %copy-start.1 = (bf16[64,1024]{1,0:T(8,128)(2,1)S(1)}, bf16[64,1024]{1,0:T(8,128)(2,1)}, u32[]{:S(2)}) copy-start(bf16[64,1024]{1,0:T(8,128)(2,1)} %shard_map.82) | copy-start | bytes 393220
  157.9 10.5 %collective-permute-start.13 = (bf16[2,64,448]{2,1,0:T(8,128)(2,1)S(1)}, bf16[2,64,448]{2,1,0:T(8,128)(2,1)S(1)}, u32[]{:S(2)}, u32[]{:S(2)}) collective-permute-start(bf16[2,64,448]{2,1,0:T(8,128)(2,1)S(1)} %get-tuple-element.9), channel_id=1, source_target_pairs={{0,2},{2,0},{4,6},{6,4},{1,3},{3,1},{5,7},{7,5},{8,10},{10,8},{12,... | collective-permute-start | bytes 344072 | tf_op jit(solution)/shard_map/ppermute | solution.py:160
  160.3 8.7 %collective-permute-start.14 = (bf16[2,64,448]{2,1,0:T(8,128)(2,1)S(1)}, bf16[2,64,448]{2,1,0:T(8,128)(2,1)S(1)}, u32[]{:S(2)}, u32[]{:S(2)}) collective-permute-start(bf16[2,64,448]{2,1,0:T(8,128)(2,1)S(1)} %get-tuple-element.11), channel_id=1, source_target_pairs={{0,4},{2,6},{4,0},{6,2},{1,5},{3,7},{5,1},{7,3},{8,12},{10,14},{12... | collective-permute-start | bytes 344072 | tf_op jit(solution)/shard_map/ppermute | solution.py:160
  163.4 8.4 %collective-permute-start.15 = (bf16[2,64,448]{2,1,0:T(8,128)(2,1)S(1)}, bf16[2,64,448]{2,1,0:T(8,128)(2,1)S(1)}, u32[]{:S(2)}, u32[]{:S(2)}) collective-permute-start(bf16[2,64,448]{2,1,0:T(8,128)(2,1)S(1)} %get-tuple-element.10), channel_id=1, source_target_pairs={{0,6},{2,4},{4,2},{6,0},{1,7},{3,5},{5,3},{7,1},{8,14},{10,12},{12... | collective-permute-start | bytes 344072 | tf_op jit(solution)/shard_map/ppermute | solution.py:160
  171.9 7.7 %collective-permute-start.16 = (bf16[64,448]{1,0:T(8,128)(2,1)S(1)}, bf16[64,448]{1,0:T(8,128)(2,1)S(1)}, u32[]{:S(2)}, u32[]{:S(2)}) collective-permute-start(bf16[64,448]{1,0:T(8,128)(2,1)S(1)} %fusion.11), channel_id=1, source_target_pairs={{0,1},{1,0},{2,3},{3,2},{4,5},{5,4},{6,7},{7,6},{8,9},{9,8},{10,11... | collective-permute-start | bytes 172040 | tf_op jit(solution)/shard_map/ppermute | solution.py:166
Sparse Core Ops, SparseCore 0:
  15.4 109.7 all-gather.1

commit v18 on v17

--- a/solution.py
+++ b/solution.py
@@ -155,7 +155,7 @@
     yh = lax.axis_index("yh")
     blocks = blocks.reshape((columns, rows) + blocks.shape[1:])
     row_sums = blocks[x]
-    for shift in range(1, columns):
+    for shift in sorted(range(1, columns), key=lambda d: -bin(d).count("0")):
         sent = blocks[x ^ shift].astype(jnp.bfloat16)
         row_sums = row_sums + lax.ppermute(
             sent, "x", [(i, i ^ shift) for i in range(columns)]

time: 191 us -> 190 us (level)
  no operation moved by 1% of the time
where the time goes in v18:
time: 190 us; the launch traced here: 187 us
  waiting for transfers between devices  71.3 us (38%)
  starting transfers between devices  62.6 us (33%)
  between operations  13.8 us (7%)
  local copies, waits for them, and re-layouts  13.4 us (7%)
  Pallas kernels  12 us (6%)
  matrix products  7.11 us (4%)
  other arithmetic  6.87 us (4%)
    ppermute x3, waiting for transfers between devices, exchange(): return lax.ppermute(acc, axis, pairs)  29.2 us
    ppermute x7, starting transfers between devices, gather_earlier_keys(): lax.ppermute(local, 'zh', [(i, i + shift) for i in range(cubes - shift)])  29.2 us
    ppermute x7, waiting for transfers between devices, gather_earlier_keys(): lax.ppermute(local, 'zh', [(i, i + shift) for i in range(cubes - shift)])  21.4 us
    all_gather x1, waiting for transfers between devices, body(): own = lax.all_gather(pair, ('zh', 'zl'), axis=1, tiled=True)  14.7 us
    pallas_call x1, Pallas kernels, attend(): pl.pallas_call(attention_kernel, out_shape=jax.ShapeDtypeStruct((tokens,...  12 us
    ppermute x3, starting transfers between devices, scatter_sum(): lax.ppermute(sent, 'x', [(i, i ^ shift) for i in range(columns)])  9.82 us
    ppermute x3, starting transfers between devices, exchange(): return lax.ppermute(acc, axis, pairs)  7.91 us
    unnamed x17, local copies, waits for them, and re-layouts  6.76 us
  transfers between devices with their start and end apart: 18, of which 10 were waited for; matrix products, arithmetic and copies ran while one was open for 11% of the time, Pallas kernels for 6%

profile of v18, /device:TPU:6, one launch (start us, length us, event | category | flops | bytes accessed | tf_op | source)
XLA Modules:
  0.0 187.0 jit_solution(12231842867220399051)
XLA Ops:
  6.5 3.6 %collective-permute-start.11 = (bf16[1,56,1024]{2,1,0:T(8,128)(2,1)}, bf16[1,56,1024]{2,1,0:T(8,128)(2,1)S(1)}, u32[]{:S(2)}, u32[]{:S(2)}) collective-permute-start(bf16[1,56,1024]{2,1,0:T(8,128)(2,1)} %bitcast.93), channel_id=1, source_target_pairs={{0,16},{16,0},{1,17},{17,1},{2,18},{18,2},{3,19},{19,3},{4,20},{20... | collective-permute-start | bytes 344072 | tf_op jit(solution)/shard_map/ppermute | solution.py:104
  10.2 3.5 %collective-permute-done.11 = bf16[1,56,1024]{2,1,0:T(8,128)(2,1)S(1)} collective-permute-done((bf16[1,56,1024]{2,1,0:T(8,128)(2,1)}, bf16[1,56,1024]{2,1,0:T(8,128)(2,1)S(1)}, u32[]{:S(2)}, u32[]{:S(2)}) %collective-permute-start.11) | collective-permute-done | bytes 114720 | tf_op jit(solution)/shard_map/ppermute | solution.py:104
  17.9 5.2 %collective-permute-start = (bf16[64,576]{1,0:T(8,128)(2,1)S(1)}, bf16[64,576]{1,0:T(8,128)(2,1)S(1)}, u32[]{:S(2)}, u32[]{:S(2)}) collective-permute-start(bf16[64,576]{1,0:T(8,128)(2,1)S(1)} %pad_maximum_fusion.2), channel_id=1, source_target_pairs={{0,64},{64,128},{128,192},{192,256},{256,320},{320,384},{384,448},... | collective-permute-start | bytes 221192 | tf_op jit(solution)/shard_map/ppermute | solution.py:135
  23.1 9.1 %collective-permute-start.1 = (bf16[64,576]{1,0:T(8,128)(2,1)S(1)}, bf16[64,576]{1,0:T(8,128)(2,1)S(1)}, u32[]{:S(2)}, u32[]{:S(2)}) collective-permute-start(bf16[64,576]{1,0:T(8,128)(2,1)S(1)} %pad_maximum_fusion.2), channel_id=1, source_target_pairs={{0,128},{64,192},{128,256},{192,320},{256,384},{320,448},{1,129},{... | collective-permute-start | bytes 221192 | tf_op jit(solution)/shard_map/ppermute | solution.py:135
  32.2 8.2 %collective-permute-start.2 = (bf16[64,576]{1,0:T(8,128)(2,1)S(1)}, bf16[64,576]{1,0:T(8,128)(2,1)S(1)}, u32[]{:S(2)}, u32[]{:S(2)}) collective-permute-start(bf16[64,576]{1,0:T(8,128)(2,1)S(1)} %pad_maximum_fusion.2), channel_id=1, source_target_pairs={{0,192},{64,256},{128,320},{192,384},{256,448},{1,193},{65,257},{1... | collective-permute-start | bytes 221192 | tf_op jit(solution)/shard_map/ppermute | solution.py:135
  40.4 2.8 %collective-permute-start.3 = (bf16[64,576]{1,0:T(8,128)(2,1)S(1)}, bf16[64,576]{1,0:T(8,128)(2,1)S(1)}, u32[]{:S(2)}, u32[]{:S(2)}) collective-permute-start(bf16[64,576]{1,0:T(8,128)(2,1)S(1)} %pad_maximum_fusion.2), channel_id=1, source_target_pairs={{0,256},{64,320},{128,384},{192,448},{1,257},{65,321},{129,385},{1... | collective-permute-start | bytes 221192 | tf_op jit(solution)/shard_map/ppermute | solution.py:135
  51.4 12.3 %collective-permute-done.4 = bf16[64,576]{1,0:T(8,128)(2,1)S(1)} collective-permute-done((bf16[64,576]{1,0:T(8,128)(2,1)S(1)}, bf16[64,576]{1,0:T(8,128)(2,1)S(1)}, u32[]{:S(2)}, u32[]{:S(2)}) %collective-permute-start.4) | collective-permute-done | bytes 73760 | tf_op jit(solution)/shard_map/ppermute | solution.py:135
  64.4 5.2 %collective-permute-done.5 = bf16[64,576]{1,0:T(8,128)(2,1)S(1)} collective-permute-done((bf16[64,576]{1,0:T(8,128)(2,1)S(1)}, bf16[64,576]{1,0:T(8,128)(2,1)S(1)}, u32[]{:S(2)}, u32[]{:S(2)}) %collective-permute-start.5) | collective-permute-done | bytes 73760 | tf_op jit(solution)/shard_map/ppermute | solution.py:135
  70.3 3.9 %collective-permute-done.6 = bf16[64,576]{1,0:T(8,128)(2,1)S(1)} collective-permute-done((bf16[64,576]{1,0:T(8,128)(2,1)S(1)}, bf16[64,576]{1,0:T(8,128)(2,1)S(1)}, u32[]{:S(2)}, u32[]{:S(2)}) %collective-permute-start.6) | collective-permute-done | bytes 73760 | tf_op jit(solution)/shard_map/ppermute | solution.py:135
  76.8 3.5 %collective-permute-start.8 = (bf16[8,64,576]{2,1,0:T(8,128)(2,1)}, bf16[8,64,576]{2,1,0:T(8,128)(2,1)S(1)}, u32[]{:S(2)}, u32[]{:S(2)}) collective-permute-start(bf16[8,64,576]{2,1,0:T(8,128)(2,1)} %get-tuple-element.18), channel_id=1, source_target_pairs={{0,16},{16,0},{1,17},{17,1},{2,18},{18,2},{3,19},{19,3},{4,20},{20... | collective-permute-start | bytes 1769480 | tf_op jit(solution)/shard_map/ppermute | solution.py:106
  80.3 25.1 %collective-permute-done.7 = bf16[8,64,576]{2,1,0:T(8,128)(2,1)S(1)} collective-permute-done((bf16[8,64,576]{2,1,0:T(8,128)(2,1)}, bf16[8,64,576]{2,1,0:T(8,128)(2,1)S(1)}, u32[]{:S(2)}, u32[]{:S(2)}) %collective-permute-start.7) | collective-permute-done | bytes 589856 | tf_op jit(solution)/shard_map/ppermute | solution.py:104
  105.4 5.1 %collective-permute-start.9 = (bf16[8,64,576]{2,1,0:T(8,128)(2,1)S(1)}, bf16[8,64,576]{2,1,0:T(8,128)(2,1)S(1)}, u32[]{:S(2)}, u32[]{:S(2)}) collective-permute-start(bf16[8,64,576]{2,1,0:T(8,128)(2,1)S(1)} %collective-permute-done.7), channel_id=1, source_target_pairs={{0,17},{1,16},{16,1},{17,0},{2,19},{3,18},{18,3},{19,2},{4,21},{5,... | collective-permute-start | bytes 1769480 | tf_op jit(solution)/shard_map/ppermute | solution.py:107
  110.5 14.7 %all-gather.2.cloned.1.call-done = bf16[1024,1792]{0,1:T(8,128)(2,1)} async-done(((bf16[1024,112]{0,1:T(8,128)(2,1)}), bf16[1024,1792]{0,1:T(8,128)(2,1)}) %all-gather.2.cloned.1.call-update) | async-done | bytes 3670032 | tf_op jit(solution)/shard_map/all_gather | solution.py:206
  125.2 1.9 %collective-permute-start.12 = (bf16[1024,1792]{0,1:T(8,128)(2,1)}, bf16[1024,1792]{0,1:T(8,128)(2,1)}, u32[]{:S(2)}, u32[]{:S(2)}) collective-permute-start(bf16[1024,1792]{0,1:T(8,128)(2,1)} %all-gather.2.cloned.1.call-done), channel_id=1, source_target_pairs={{0,8},{8,0},{1,9},{9,1},{2,10},{10,2},{3,11},{11,3},{4,12},{12,4},... | collective-permute-start | bytes 11010056 | tf_op jit(solution)/shard_map/ppermute | solution.py:207
  129.9 2.4 %collective-permute-start.10 = (bf16[32,64,576]{2,1,0:T(8,128)(2,1)}, bf16[32,64,576]{2,1,0:T(8,128)(2,1)}, u32[]{:S(2)}, u32[]{:S(2)}) collective-permute-start(bf16[32,64,576]{2,1,0:T(8,128)(2,1)} %constant_dynamic-update-slice_fusion), channel_id=1, source_target_pairs={{0,8},{8,0},{1,9},{9,1},{2,10},{10,2},{3,11},{11,3},{4,12},{12,4},... | collective-permute-start | bytes 7077896 | tf_op jit(solution)/shard_map/ppermute | solution.py:104
  137.6 12.0 %shard_map.82 = bf16[64,1024]{1,0:T(8,128)(2,1)} custom-call(bf16[512,576]{1,0:T(8,128)(2,1)} %bitcast.91, s32[512,1]{1,0:T(8,128)} %reshape_tile.4.qi_ref, bf16[2048,576]{1,0:T(8,128)(2,1)} %bitcast.94, s32[1,2048]{1,0:T(1,128)} %add.134.ia_ref, bf16[2048,576]{1,0:T(8,128)(2,1)} %bitcast.15.kb_ref, s32[1,2048]{1,0:T(1,128)} %add.138.ib_ref, ...), custom_call_target="tpu_custom_call" | custom-call | flops 4563402752 | bytes 5832704 | tf_op jit(solution)/shard_map/pallas_call | solution.py:94
  149.6 3.4 %fusion.23 = f32[64,1792]{1,0:T(8,128)S(1)} fusion(bf16[64,1024]{1,0:T(8,128)(2,1)} %shard_map.82, bf16[1024,1792]{0,1:T(8,128)(2,1)} %all-gather.2.cloned.1.call-done), kind=kOutput, calls=%fused_computation.75 | convolution fusion | flops 234881024 | bytes 4259840 | tf_op jit(solution)/shard_map/dot_general | solution.py:211
  153.3 3.3 %fusion.24 = f32[64,1792]{1,0:T(8,128)S(1)} fusion(bf16[64,1024]{1,0:T(8,128)(2,1)S(1)} %copy-done.1, bf16[1024,1792]{0,1:T(8,128)(2,1)} %collective-permute-done.12), kind=kOutput, calls=%fused_computation.76 | convolution fusion | flops 234881024 | bytes 4259840 | tf_op jit(solution)/shard_map/dot_general | solution.py:211
  157.9 3.0 %collective-permute-start.13 = (bf16[2,64,448]{2,1,0:T(8,128)(2,1)S(1)}, bf16[2,64,448]{2,1,0:T(8,128)(2,1)S(1)}, u32[]{:S(2)}, u32[]{:S(2)}) collective-permute-start(bf16[2,64,448]{2,1,0:T(8,128)(2,1)S(1)} %get-tuple-element.9), channel_id=1, source_target_pairs={{0,4},{2,6},{4,0},{6,2},{1,5},{3,7},{5,1},{7,3},{8,12},{10,14},{12... | collective-permute-start | bytes 344072 | tf_op jit(solution)/shard_map/ppermute | solution.py:160
  160.9 1.9 %collective-permute-start.14 = (bf16[2,64,448]{2,1,0:T(8,128)(2,1)S(1)}, bf16[2,64,448]{2,1,0:T(8,128)(2,1)S(1)}, u32[]{:S(2)}, u32[]{:S(2)}) collective-permute-start(bf16[2,64,448]{2,1,0:T(8,128)(2,1)S(1)} %get-tuple-element.11), channel_id=1, source_target_pairs={{0,2},{2,0},{4,6},{6,4},{1,3},{3,1},{5,7},{7,5},{8,10},{10,8},{12,... | collective-permute-start | bytes 344072 | tf_op jit(solution)/shard_map/ppermute | solution.py:160
  162.8 4.9 %collective-permute-start.15 = (bf16[2,64,448]{2,1,0:T(8,128)(2,1)S(1)}, bf16[2,64,448]{2,1,0:T(8,128)(2,1)S(1)}, u32[]{:S(2)}, u32[]{:S(2)}) collective-permute-start(bf16[2,64,448]{2,1,0:T(8,128)(2,1)S(1)} %get-tuple-element.10), channel_id=1, source_target_pairs={{0,6},{2,4},{4,2},{6,0},{1,7},{3,5},{5,3},{7,1},{8,14},{10,12},{12... | collective-permute-start | bytes 344072 | tf_op jit(solution)/shard_map/ppermute | solution.py:160
  168.1 3.1 %collective-permute-done.15 = bf16[2,64,448]{2,1,0:T(8,128)(2,1)S(1)} collective-permute-done((bf16[2,64,448]{2,1,0:T(8,128)(2,1)S(1)}, bf16[2,64,448]{2,1,0:T(8,128)(2,1)S(1)}, u32[]{:S(2)}, u32[]{:S(2)}) %collective-permute-start.15) | collective-permute-done | bytes 114720 | tf_op jit(solution)/shard_map/ppermute | solution.py:160
  171.3 5.2 %collective-permute-start.16 = (bf16[64,448]{1,0:T(8,128)(2,1)S(1)}, bf16[64,448]{1,0:T(8,128)(2,1)S(1)}, u32[]{:S(2)}, u32[]{:S(2)}) collective-permute-start(bf16[64,448]{1,0:T(8,128)(2,1)S(1)} %fusion.11), channel_id=1, source_target_pairs={{0,1},{1,0},{2,3},{3,2},{4,5},{5,4},{6,7},{7,6},{8,9},{9,8},{10,11... | collective-permute-start | bytes 172040 | tf_op jit(solution)/shard_map/ppermute | solution.py:166
  176.5 2.5 %collective-permute-done.16 = bf16[64,448]{1,0:T(8,128)(2,1)S(1)} collective-permute-done((bf16[64,448]{1,0:T(8,128)(2,1)S(1)}, bf16[64,448]{1,0:T(8,128)(2,1)S(1)}, u32[]{:S(2)}, u32[]{:S(2)}) %collective-permute-start.16) | collective-permute-done | bytes 57376 | tf_op jit(solution)/shard_map/ppermute | solution.py:166
  (75 shorter events, 27.6 us)
Async XLA Ops:
  6.5 128.9 %copy-start = (bf16[512,1024]{1,0:T(8,128)(2,1)S(1)}, bf16[512,1024]{1,0:T(8,128)(2,1)}, u32[]{:S(2)}) copy-start(bf16[512,1024]{1,0:T(8,128)(2,1)} %param.13) | copy-start | bytes 3145732
  6.5 118.7 %all-gather.2.cloned.1.call-start = ((), (), s32[]{:S(2)}) async-start(), calls=%async_computation | async-start | bytes 3899392 | tf_op jit(solution)/shard_map/all_gather | solution.py:206
  6.5 7.1 %collective-permute-start.11 = (bf16[1,56,1024]{2,1,0:T(8,128)(2,1)}, bf16[1,56,1024]{2,1,0:T(8,128)(2,1)S(1)}, u32[]{:S(2)}, u32[]{:S(2)}) collective-permute-start(bf16[1,56,1024]{2,1,0:T(8,128)(2,1)} %bitcast.93), channel_id=1, source_target_pairs={{0,16},{16,0},{1,17},{17,1},{2,18},{18,2},{3,19},{19,3},{4,20},{20... | collective-permute-start | bytes 344072 | tf_op jit(solution)/shard_map/ppermute | solution.py:104
  17.9 28.2 %collective-permute-start = (bf16[64,576]{1,0:T(8,128)(2,1)S(1)}, bf16[64,576]{1,0:T(8,128)(2,1)S(1)}, u32[]{:S(2)}, u32[]{:S(2)}) collective-permute-start(bf16[64,576]{1,0:T(8,128)(2,1)S(1)} %pad_maximum_fusion.2), channel_id=1, source_target_pairs={{0,64},{64,128},{128,192},{192,256},{256,320},{320,384},{384,448},... | collective-permute-start | bytes 221192 | tf_op jit(solution)/shard_map/ppermute | solution.py:135
  23.1 25.0 %collective-permute-start.1 = (bf16[64,576]{1,0:T(8,128)(2,1)S(1)}, bf16[64,576]{1,0:T(8,128)(2,1)S(1)}, u32[]{:S(2)}, u32[]{:S(2)}) collective-permute-start(bf16[64,576]{1,0:T(8,128)(2,1)S(1)} %pad_maximum_fusion.2), channel_id=1, source_target_pairs={{0,128},{64,192},{128,256},{192,320},{256,384},{320,448},{1,129},{... | collective-permute-start | bytes 221192 | tf_op jit(solution)/shard_map/ppermute | solution.py:135
  32.2 17.8 %collective-permute-start.2 = (bf16[64,576]{1,0:T(8,128)(2,1)S(1)}, bf16[64,576]{1,0:T(8,128)(2,1)S(1)}, u32[]{:S(2)}, u32[]{:S(2)}) collective-permute-start(bf16[64,576]{1,0:T(8,128)(2,1)S(1)} %pad_maximum_fusion.2), channel_id=1, source_target_pairs={{0,192},{64,256},{128,320},{192,384},{256,448},{1,193},{65,257},{1... | collective-permute-start | bytes 221192 | tf_op jit(solution)/shard_map/ppermute | solution.py:135
  40.4 10.3 %collective-permute-start.3 = (bf16[64,576]{1,0:T(8,128)(2,1)S(1)}, bf16[64,576]{1,0:T(8,128)(2,1)S(1)}, u32[]{:S(2)}, u32[]{:S(2)}) collective-permute-start(bf16[64,576]{1,0:T(8,128)(2,1)S(1)} %pad_maximum_fusion.2), channel_id=1, source_target_pairs={{0,256},{64,320},{128,384},{192,448},{1,257},{65,321},{129,385},{1... | collective-permute-start | bytes 221192 | tf_op jit(solution)/shard_map/ppermute | solution.py:135
  43.2 20.4 %collective-permute-start.4 = (bf16[64,576]{1,0:T(8,128)(2,1)S(1)}, bf16[64,576]{1,0:T(8,128)(2,1)S(1)}, u32[]{:S(2)}, u32[]{:S(2)}) collective-permute-start(bf16[64,576]{1,0:T(8,128)(2,1)S(1)} %pad_maximum_fusion.2), channel_id=1, source_target_pairs={{0,320},{64,384},{128,448},{1,321},{65,385},{129,449},{2,322},{66,... | collective-permute-start | bytes 221192 | tf_op jit(solution)/shard_map/ppermute | solution.py:135
  46.1 23.5 %collective-permute-start.5 = (bf16[64,576]{1,0:T(8,128)(2,1)S(1)}, bf16[64,576]{1,0:T(8,128)(2,1)S(1)}, u32[]{:S(2)}, u32[]{:S(2)}) collective-permute-start(bf16[64,576]{1,0:T(8,128)(2,1)S(1)} %pad_maximum_fusion.2), channel_id=1, source_target_pairs={{0,384},{64,448},{1,385},{65,449},{2,386},{66,450},{3,387},{67,451... | collective-permute-start | bytes 221192 | tf_op jit(solution)/shard_map/ppermute | solution.py:135
  48.1 26.2 %collective-permute-start.6 = (bf16[64,576]{1,0:T(8,128)(2,1)S(1)}, bf16[64,576]{1,0:T(8,128)(2,1)S(1)}, u32[]{:S(2)}, u32[]{:S(2)}) collective-permute-start(bf16[64,576]{1,0:T(8,128)(2,1)S(1)} %pad_maximum_fusion.2), channel_id=1, source_target_pairs={{0,448},{1,449},{2,450},{3,451},{4,452},{5,453},{6,454},{7,455},{8... | collective-permute-start | bytes 221192 | tf_op jit(solution)/shard_map/ppermute | solution.py:135
  50.7 84.1 %copy-start.2 = (bf16[64,512]{1,0:T(8,128)(2,1)S(1)}, bf16[64,512]{1,0:T(8,128)(2,1)}, u32[]{:S(2)}) copy-start(bf16[64,512]{1,0:T(8,128)(2,1)} %param.9) | copy-start | bytes 196612
  74.9 30.5 %collective-permute-start.7 = (bf16[8,64,576]{2,1,0:T(8,128)(2,1)}, bf16[8,64,576]{2,1,0:T(8,128)(2,1)S(1)}, u32[]{:S(2)}, u32[]{:S(2)}) collective-permute-start(bf16[8,64,576]{2,1,0:T(8,128)(2,1)} %get-tuple-element.18), channel_id=1, source_target_pairs={{0,32},{32,0},{1,33},{33,1},{2,34},{34,2},{3,35},{35,3},{4,36},{36... | collective-permute-start | bytes 1769480 | tf_op jit(solution)/shard_map/ppermute | solution.py:104
  76.8 51.2 %collective-permute-start.8 = (bf16[8,64,576]{2,1,0:T(8,128)(2,1)}, bf16[8,64,576]{2,1,0:T(8,128)(2,1)S(1)}, u32[]{:S(2)}, u32[]{:S(2)}) collective-permute-start(bf16[8,64,576]{2,1,0:T(8,128)(2,1)} %get-tuple-element.18), channel_id=1, source_target_pairs={{0,16},{16,0},{1,17},{17,1},{2,18},{18,2},{3,19},{19,3},{4,20},{20... | collective-permute-start | bytes 1769480 | tf_op jit(solution)/shard_map/ppermute | solution.py:106
  105.4 23.5 %collective-permute-start.9 = (bf16[8,64,576]{2,1,0:T(8,128)(2,1)S(1)}, bf16[8,64,576]{2,1,0:T(8,128)(2,1)S(1)}, u32[]{:S(2)}, u32[]{:S(2)}) collective-permute-start(bf16[8,64,576]{2,1,0:T(8,128)(2,1)S(1)} %collective-permute-done.7), channel_id=1, source_target_pairs={{0,17},{1,16},{16,1},{17,0},{2,19},{3,18},{18,3},{19,2},{4,21},{5,... | collective-permute-start | bytes 1769480 | tf_op jit(solution)/shard_map/ppermute | solution.py:107
  125.2 28.1 %collective-permute-start.12 = (bf16[1024,1792]{0,1:T(8,128)(2,1)}, bf16[1024,1792]{0,1:T(8,128)(2,1)}, u32[]{:S(2)}, u32[]{:S(2)}) collective-permute-start(bf16[1024,1792]{0,1:T(8,128)(2,1)} %all-gather.2.cloned.1.call-done), channel_id=1, source_target_pairs={{0,8},{8,0},{1,9},{9,1},{2,10},{10,2},{3,11},{11,3},{4,12},{12,4},... | collective-permute-start | bytes 11010056 | tf_op jit(solution)/shard_map/ppermute | solution.py:207
  128.0 7.5 %copy-start.3 = (bf16[64,1024]{1,0:T(8,128)(2,1)S(1)}, bf16[64,1024]{1,0:T(8,128)(2,1)}, u32[]{:S(2)}) copy-start(bf16[64,1024]{1,0:T(8,128)(2,1)} %param.8) | copy-start | bytes 393220
  129.9 7.7 %collective-permute-start.10 = (bf16[32,64,576]{2,1,0:T(8,128)(2,1)}, bf16[32,64,576]{2,1,0:T(8,128)(2,1)}, u32[]{:S(2)}, u32[]{:S(2)}) collective-permute-start(bf16[32,64,576]{2,1,0:T(8,128)(2,1)} %constant_dynamic-update-slice_fusion), channel_id=1, source_target_pairs={{0,8},{8,0},{1,9},{9,1},{2,10},{10,2},{3,11},{11,3},{4,12},{12,4},... | collective-permute-start | bytes 7077896 | tf_op jit(solution)/shard_map/ppermute | solution.py:104
  149.6 3.7 %copy-start.1 = (bf16[64,1024]{1,0:T(8,128)(2,1)S(1)}, bf16[64,1024]{1,0:T(8,128)(2,1)}, u32[]{:S(2)}) copy-start(bf16[64,1024]{1,0:T(8,128)(2,1)} %shard_map.82) | copy-start | bytes 393220
  157.9 9.9 %collective-permute-start.13 = (bf16[2,64,448]{2,1,0:T(8,128)(2,1)S(1)}, bf16[2,64,448]{2,1,0:T(8,128)(2,1)S(1)}, u32[]{:S(2)}, u32[]{:S(2)}) collective-permute-start(bf16[2,64,448]{2,1,0:T(8,128)(2,1)S(1)} %get-tuple-element.9), channel_id=1, source_target_pairs={{0,4},{2,6},{4,0},{6,2},{1,5},{3,7},{5,1},{7,3},{8,12},{10,14},{12... | collective-permute-start | bytes 344072 | tf_op jit(solution)/shard_map/ppermute | solution.py:160
  160.9 7.1 %collective-permute-start.14 = (bf16[2,64,448]{2,1,0:T(8,128)(2,1)S(1)}, bf16[2,64,448]{2,1,0:T(8,128)(2,1)S(1)}, u32[]{:S(2)}, u32[]{:S(2)}) collective-permute-start(bf16[2,64,448]{2,1,0:T(8,128)(2,1)S(1)} %get-tuple-element.11), channel_id=1, source_target_pairs={{0,2},{2,0},{4,6},{6,4},{1,3},{3,1},{5,7},{7,5},{8,10},{10,8},{12,... | collective-permute-start | bytes 344072 | tf_op jit(solution)/shard_map/ppermute | solution.py:160
  162.8 8.4 %collective-permute-start.15 = (bf16[2,64,448]{2,1,0:T(8,128)(2,1)S(1)}, bf16[2,64,448]{2,1,0:T(8,128)(2,1)S(1)}, u32[]{:S(2)}, u32[]{:S(2)}) collective-permute-start(bf16[2,64,448]{2,1,0:T(8,128)(2,1)S(1)} %get-tuple-element.10), channel_id=1, source_target_pairs={{0,6},{2,4},{4,2},{6,0},{1,7},{3,5},{5,3},{7,1},{8,14},{10,12},{12... | collective-permute-start | bytes 344072 | tf_op jit(solution)/shard_map/ppermute | solution.py:160
  171.3 7.7 %collective-permute-start.16 = (bf16[64,448]{1,0:T(8,128)(2,1)S(1)}, bf16[64,448]{1,0:T(8,128)(2,1)S(1)}, u32[]{:S(2)}, u32[]{:S(2)}) collective-permute-start(bf16[64,448]{1,0:T(8,128)(2,1)S(1)} %fusion.11), channel_id=1, source_target_pairs={{0,1},{1,0},{2,3},{3,2},{4,5},{5,4},{6,7},{7,6},{8,9},{9,8},{10,11... | collective-permute-start | bytes 172040 | tf_op jit(solution)/shard_map/ppermute | solution.py:166
Sparse Core Ops, SparseCore 0:
  15.4 109.7 all-gather.1
